TPU v7x, 256 devices: a whole 4x4x8 slice. The times are simulated.
256 devices in a mesh: row: 16 (over z, y_hi), col: 16 (over x, y_lo, core).
Axes of the slice: x: 4, y: 4 (y_hi: 2, y_lo: 2; y = y_hi * 2 + y_lo), z: 8, core: 2. Of those that a mesh axis runs over, the one named last changes fastest.
Arguments:
- features: bfloat16 [512, 512, 256], P('row', 'col'), may hold values from -6 to 6
- dw_kernel: bfloat16 [7, 7, 256], replicated, may hold values from -0.875 to 0.875
- dw_bias: float32 [256], replicated, may hold values from -4 to 4
- norm_gain: float32 [256], replicated, may hold values from 0.5 to 2
- norm_bias: float32 [256], replicated, may hold values from -3 to 3
- w_expand: bfloat16 [256, 1024], replicated, may hold values from -0.375 to 0.375
- b_expand: float32 [1024], replicated, may hold values from -3 to 3
- w_reduce: bfloat16 [1024, 256], replicated, may hold values from -0.1875 to 0.1875
- b_reduce: float32 [256], replicated, may hold values from -3 to 3
- layer_scale: float32 [256], replicated, may hold values from 0.5 to 2
- w_query: bfloat16 [256, 256], replicated, may hold values from -2 to 2
- w_keyval: bfloat16 [256, 512], replicated, may hold values from -0.375 to 0.375
- rel_bias: float32 [8, 7, 127], replicated, may hold values from -8 to 250, as said below
- w_out: bfloat16 [256, 256], replicated, may hold values from -0.75 to 0.75
Outputs:
- result: bfloat16 [512, 512, 256], P('row', 'col')
Inputs may be any that keep to these rules, and one draw needn't show every extreme that they name: `rel_bias`: relative position bias of moderate size, with possibly a few much larger entries.
All inputs are finite; a program needn't handle non-finite values.
Results may differ from a plain program's by a relative error of at most 0.014.
Values may be sent and summed in bfloat16 or wider, within the bound.
No kernel may reach another device: no remote copies, remote signals or barrier semaphores. Data moves between devices by JAX's collectives and lax.ppermute only.
A program may use at most 64 MiB of HBM per device.

v0:
```python
import jax
import jax.numpy as jnp
from jax import lax
from jax.sharding import PartitionSpec as P

HEADS = 8


def padded_2(array, sides, width):
    for axis, dim in sides:
        devices, length = (lax.axis_size(axis), array.shape[dim])
        up = [(i, (i + 1) % devices) for i in range(devices - 1)]
        down = [(j, i) for i, j in up]
        last = lax.slice_in_dim(array, length - width, length, axis=dim)
        leading = lax.slice_in_dim(array, 0, width, axis=dim)
        before = lax.ppermute(last, axis, up)
        after = lax.ppermute(leading, axis, down)
        array = jnp.concatenate([before, array, after], axis=dim)
    return array


def block_pass(
    padded,
    features,
    dw_kernel,
    dw_bias,
    norm_gain,
    norm_bias,
    w_expand,
    b_expand,
    w_reduce,
    b_reduce,
    layer_scale,
):
    tile_rows, tile_cols, channels = features.shape
    convolved = jnp.zeros((tile_rows, tile_cols, channels), jnp.float32)
    for tap_row in range(7):
        for tap_col in range(7):
            convolved = convolved + padded[
                tap_row : tap_row + tile_rows, tap_col : tap_col + tile_cols
            ].astype(jnp.float32) * dw_kernel[tap_row, tap_col].astype(jnp.float32)
    convolved = convolved + dw_bias
    average = jnp.mean(convolved, axis=-1, keepdims=True)
    centred = convolved - average
    variance = jnp.mean(centred * centred, axis=-1, keepdims=True)
    normed = (
        (centred * lax.rsqrt(variance + 1e-06) * norm_gain + norm_bias)
        .astype(jnp.bfloat16)
        .reshape(-1, channels)
    )
    hidden = jax.nn.gelu(
        jnp.dot(normed, w_expand, preferred_element_type=jnp.float32) + b_expand, approximate=False
    ).astype(jnp.bfloat16)
    reduced = jnp.dot(hidden, w_reduce, preferred_element_type=jnp.float32) + b_reduce
    summed = features.astype(jnp.float32).reshape(-1, channels) + layer_scale * reduced
    return summed.astype(jnp.bfloat16).reshape(tile_rows, tile_cols, channels)


def shards(
    features,
    dw_kernel,
    dw_bias,
    norm_gain,
    norm_bias,
    w_expand,
    b_expand,
    w_reduce,
    b_reduce,
    layer_scale,
    w_query,
    w_keyval,
    rel_bias,
    w_out,
):
    tile_rows, tile_cols, channels = features.shape
    head_dim = channels // HEADS
    extended = padded_2(features, (("row", 0),), 3)
    padded = padded_2(extended, (("col", 1),), 3)
    block_out = block_pass(
        padded,
        features,
        dw_kernel,
        dw_bias,
        norm_gain,
        norm_bias,
        w_expand,
        b_expand,
        w_reduce,
        b_reduce,
        layer_scale,
    )
    region_side = tile_rows // 8
    local_count = region_side * region_side
    pooled = (
        block_out.astype(jnp.float32)
        .reshape(region_side, 8, region_side, 8, channels)
        .mean(axis=(1, 3))
    )
    pooled = pooled.astype(jnp.bfloat16).reshape(local_count, channels)
    queries = jnp.dot(pooled, w_query, preferred_element_type=jnp.float32).astype(jnp.bfloat16)
    keyval = jnp.dot(pooled, w_keyval, preferred_element_type=jnp.float32).astype(jnp.bfloat16)
    band_keyval = lax.all_gather(keyval, "col", axis=0, tiled=True)
    columns = lax.axis_size("col")
    position = lax.axis_index("col")
    span_cols = region_side * columns
    key_count = local_count * columns
    side_index = jnp.arange(region_side, dtype=jnp.int32)
    row_offsets = side_index[None, :] - side_index[:, None] + region_side - 1
    row_onehot = (
        row_offsets[:, :, None] == jnp.arange(2 * region_side - 1, dtype=jnp.int32)[None, None, :]
    ).astype(jnp.float32)
    row_picked = jnp.einsum("rso,hoc->hrsc", row_onehot, rel_bias, precision=lax.Precision.HIGHEST)
    query_cols = position * region_side + side_index
    span_index = jnp.arange(span_cols, dtype=jnp.int32)
    col_offsets = span_index[None, :] - query_cols[:, None] + span_cols - 1
    col_onehot = (
        col_offsets[:, :, None] == jnp.arange(2 * span_cols - 1, dtype=jnp.int32)[None, None, :]
    ).astype(jnp.float32)
    both_picked = jnp.einsum(
        "hrsc,qkc->hrqsk", row_picked, col_onehot, precision=lax.Precision.HIGHEST
    )
    both_picked = both_picked.reshape(
        HEADS, region_side, region_side, region_side, columns, region_side
    )
    bias_block = jnp.transpose(both_picked, (0, 1, 2, 4, 3, 5)).reshape(
        HEADS, local_count, key_count
    )
    query_heads = queries.reshape(local_count, HEADS, head_dim)
    key_heads = band_keyval[:, :channels].reshape(key_count, HEADS, head_dim)
    value_heads = band_keyval[:, channels:].reshape(key_count, HEADS, head_dim)
    scores = (
        jnp.einsum("qhd,khd->hqk", query_heads, key_heads, preferred_element_type=jnp.float32)
        / jnp.sqrt(jnp.float32(head_dim))
        + bias_block
    )
    attn = jax.nn.softmax(scores, axis=-1).astype(jnp.bfloat16)
    context = (
        jnp.einsum("hqk,khd->qhd", attn, value_heads, preferred_element_type=jnp.float32)
        .reshape(local_count, channels)
        .astype(jnp.bfloat16)
    )
    lifted = jnp.dot(context, w_out, preferred_element_type=jnp.float32).reshape(
        region_side, 1, region_side, 1, channels
    )
    spread = jnp.broadcast_to(lifted, (region_side, 8, region_side, 8, channels)).reshape(
        tile_rows, tile_cols, channels
    )
    return (block_out.astype(jnp.float32) + spread).astype(jnp.bfloat16)


def solution(mesh):
    return jax.shard_map(
        shards,
        mesh=mesh,
        in_specs=(
            P("row", "col", None),
            P(),
            P(),
            P(),
            P(),
            P(),
            P(),
            P(),
            P(),
            P(),
            P(),
            P(),
            P(),
            P(),
        ),
        out_specs=P("row", "col", None),
        check_vma=False,
    )
```

profile of v0, /device:TPU:113, one launch (start us, length us, event | category | flops | bytes accessed | tf_op | source)
XLA Modules:
  0.0 77.9 jit_solution(13312583361902755873)
XLA Ops:
  0.0 0.9 %fusion.106 = (bf16[3,32,256]{2,1,0:T(8,128)(2,1)S(1)}, bf16[3,32,256]{2,1,0:T(8,128)(2,1)S(1)}) fusion(bf16[32,32,256]{2,1,0:T(8,128)(2,1)} %param.14), kind=kLoop, calls=%fused_computation.266 | loop fusion | bytes 196608 | tf_op jit(solution)/shard_map/slice | solution.py:15
  0.9 4.5 %collective-permute-start = (bf16[3,32,256]{2,1,0:T(8,128)(2,1)S(1)}, bf16[3,32,256]{2,1,0:T(8,128)(2,1)S(1)}, u32[]{:S(2)}, u32[]{:S(2)}) collective-permute-start(bf16[3,32,256]{2,1,0:T(8,128)(2,1)S(1)} %get-tuple-element.13), channel_id=1, source_target_pairs={{0,16},{16,32},{32,48},{48,64},{64,80},{80,96},{96,112},{112,128},... | collective-permute-start | bytes 147464 | tf_op jit(solution)/shard_map/ppermute | solution.py:16
  5.4 2.3 %collective-permute-start.1 = (bf16[3,32,256]{2,1,0:T(8,128)(2,1)S(1)}, bf16[3,32,256]{2,1,0:T(8,128)(2,1)S(1)}, u32[]{:S(2)}, u32[]{:S(2)}) collective-permute-start(bf16[3,32,256]{2,1,0:T(8,128)(2,1)S(1)} %get-tuple-element.12), channel_id=1, source_target_pairs={{16,0},{32,16},{48,32},{64,48},{80,64},{96,80},{112,96},{128,112},... | collective-permute-start | bytes 147464 | tf_op jit(solution)/shard_map/ppermute | solution.py:17
  7.7 1.6 %slice_convert_fusion.48 = (f32[1,1,256]{2,1,0:T(1,128)S(1)}, f32[1,1,256]{2,1,0:T(1,128)S(1)}, f32[1,1,256]{2,1,0:T(1,128)S(1)}, f32[1,1,256]{2,1,0:T(1,128)S(1...) fusion(bf16[7,7,256]{2,1,0:T(8,128)(2,1)} %param.15), kind=kLoop, calls=%fused_computation.231 | loop fusion | flops 4864 | bytes 29184 | tf_op jit(solution)/shard_map/mul | solution.py:39
  9.4 1.0 %fusion.67 = f32[4,4,8,127]{3,1,2,0:T(4,128)S(1)} fusion(f32[8,7,127,1]{2,0,1,3:T(8,128)} %bitcast.105, s32[4,4]{1,0:T(4,128)S(1)} %subtract_add_fusion), kind=kOutput, calls=%fused_computation.165 | convolution fusion | flops 1365616 | bytes 93536 | tf_op jit(solution)/shard_map/rso,hoc->hrsc/dot_general | solution.py:112
  10.4 0.4 convolution_bitcast_fusion
  10.8 1.7 %slice_convert_fusion.47 = (f32[1,1,256]{2,1,0:T(1,128)}, f32[1,1,256]{2,1,0:T(1,128)}, f32[1,1,256]{2,1,0:T(1,128)}, f32[1,1,256]{2,1,0:T(1,128)}, f32[1,1,256]...) fusion(bf16[7,7,256]{2,1,0:T(8,128)(2,1)} %param.15), kind=kLoop, calls=%fused_computation.230 | loop fusion | flops 4864 | bytes 29184 | tf_op jit(solution)/shard_map/mul | solution.py:39
  12.5 1.2 %constant_dynamic-update-slice_fusion.3 = (bf16[35,32,256]{2,1,0:T(8,128)(2,1)S(1)}, bf16[38,32,256]{2,1,0:T(8,128)(2,1)S(1)}, bf16[35,32,256]{2,1,0:T(8,128)(2,1)S(1)}) fusion(bf16[35,32,256]{2,1,0:T(8,128)(2,1)S(1)} %get-tuple-element.16, bf16[32,32,256]{2,1,0:T(8,128)(2,1)} %param.14, bf16[38,32,256]{2,1,0:T(8,128)(2,1)S(1)} %get-tuple-element.17), kind=kLoop, calls=%fused_computation.171 | loop fusion | bytes 2097152 | tf_op jit(solution)/shard_map/concatenate | solution.py:18
  13.9 0.9 %fusion.105 = (bf16[38,3,256]{2,1,0:T(4,128)(2,1)}, bf16[38,3,256]{2,1,0:T(4,128)(2,1)}) fusion(bf16[38,32,256]{2,1,0:T(8,128)(2,1)S(1)} %get-tuple-element.19), kind=kLoop, calls=%fused_computation.265 | loop fusion | bytes 233472 | tf_op jit(solution)/shard_map/slice | solution.py:14
  14.8 3.9 %collective-permute-start.3 = (bf16[38,3,256]{2,1,0:T(4,128)(2,1)}, bf16[38,3,256]{2,1,0:T(4,128)(2,1)S(1)}, u32[]{:S(2)}, u32[]{:S(2)}) collective-permute-start(bf16[38,3,256]{2,1,0:T(4,128)(2,1)} %get-tuple-element.8), channel_id=1, source_target_pairs={{1,0},{2,1},{3,2},{4,3},{5,4},{6,5},{7,6},{8,7},{9,8},{10,9},{11,1... | collective-permute-start | bytes 175112 | tf_op jit(solution)/shard_map/ppermute | solution.py:17
  18.7 3.7 %collective-permute-start.2 = (bf16[38,3,256]{2,1,0:T(4,128)(2,1)}, bf16[38,3,256]{2,1,0:T(4,128)(2,1)}, u32[]{:S(2)}, u32[]{:S(2)}) collective-permute-start(bf16[38,3,256]{2,1,0:T(4,128)(2,1)} %get-tuple-element.7), channel_id=1, source_target_pairs={{0,1},{1,2},{2,3},{3,4},{4,5},{5,6},{6,7},{7,8},{8,9},{9,10},{10,1... | collective-permute-start | bytes 175112 | tf_op jit(solution)/shard_map/ppermute | solution.py:16
  22.4 1.5 %slice_convert_fusion.46 = (f32[1,1,256]{2,1,0:T(1,128)}, f32[1,1,256]{2,1,0:T(1,128)}, f32[1,1,256]{2,1,0:T(1,128)}, f32[1,1,256]{2,1,0:T(1,128)}, f32[1,1,256]...) fusion(bf16[7,7,256]{2,1,0:T(8,128)(2,1)} %param.15), kind=kLoop, calls=%fused_computation.229 | loop fusion | flops 2816 | bytes 16896 | tf_op jit(solution)/shard_map/mul | solution.py:39
  24.0 0.6 copy.22
  24.6 1.8 %copy.23 = f32[8,4,4,16,4,4]{0,5,4,3,2,1:T(4,128)} copy(f32[8,4,4,16,4,4]{0,5,3,4,2,1:T(4,128)S(1)} %bitcast.96) | data formatting | bytes 262144 | tf_op jit(solution)/shard_map/transpose | solution.py:125
  26.7 2.5 %copy.24 = f32[8,16,256]{2,1,0:T(8,128)S(1)} copy(f32[8,16,256]{0,2,1:T(8,128)} %bitcast.97) | data formatting | bytes 262144 | tf_op jit(solution)/shard_map/reshape | solution.py:125
  29.6 13.4 %fusion.104 = (f32[32,32]{1,0:T(8,128)S(1)}, f32[32,32,256]{2,1,0:T(8,128)S(1)}) fusion(f32[256]{0:T(256)} %param.16, f32[256]{0:T(256)} %bitcast.153, bf16[38,3,256]{2,1,0:T(4,128)(2,1)S(1)} %collective-permute-done.3, bf16[38,32,256]{2,1,0:T(8,128)(2,1)S(1)} %copy-done.5, f32[256]{0:T(256)} %bitcast.154, f32[256]{0:T(256)S(1)} %bitcast.107, ...), kind=kLoop, calls=%fused_computation.264 | loop fusion | flops 71826432 | bytes 5513216 | tf_op jit(solution)/shard_map/reduce_sum | solution.py:43
  43.0 0.4 multiply_reduce_fusion
  43.4 1.0 %add_convert_fusion.1 = bf16[32,32,256]{2,1,0:T(8,128)(2,1)S(1)} fusion(f32[32,32,256]{2,1,0:T(8,128)S(1)} %get-tuple-element.6, f32[256]{0:T(256)} %param.18, f32[256]{0:T(256)} %param.17, f32[32,32]{1,0:T(8,128)S(1)} %add_rsqrt_fusion, f32[32,32]{1,0:T(8,128)S(1)} %broadcast_multiply_fusion), kind=kLoop, calls=%fused_computation.75 | loop fusion | flops 1310720 | bytes 1583104 | tf_op jit(solution)/shard_map/convert_element_type | solution.py:48
  44.5 10.9 %fusion.14 = f32[1024,256]{1,0:T(8,128)S(1)} fusion(bf16[1024,256]{1,0:T(8,128)(2,1)S(1)} %copy-done, bf16[1024,256]{1,0:T(8,128)(2,1)S(1)} %bitcast.102, bf16[256,1024]{1,0:T(8,128)(2,1)} %param.19, f32[1024]{0:T(1024)S(1)} %copy-done.45, f32[256]{0:T(256)S(1)} %copy-done.46, f32[256]{0:T(256)S(1)} %copy-done.47, bf16[1024,256]{1,0:T(8,128)(2,1)S(1)} %bitcast.101), kind=kOutput, calls=%fused_computation.64 | convolution fusion | flops 1144520704 | bytes 3151872 | tf_op jit(solution)/shard_map/dot_general | solution.py:54
  55.7 19.7 %all_gather.3 = bf16[256,512]{1,0:T(8,128)(2,1)S(1)} all-gather(bf16[16,512]{1,0:T(8,128)(2,1)S(1)} %convolution_convert_fusion.1), channel_id=1, replica_groups=mesh['row'=16,'col'=16] {'col'}, dimensions={0}, use_global_device_ids=true | all-gather | bytes 278528 | tf_op jit(solution)/shard_map/all_gather | solution.py:102
  75.9 0.1 fusion.17
  76.1 0.2 fusion.108
  76.2 0.3 fusion.18
  76.9 0.9 %add_convert_fusion = bf16[32,32,256]{2,1,0:T(8,128)(2,1)} fusion(f32[32,32,256]{2,1,0:T(8,128)S(1)} %bitcast.99, f32[32,32,256]{2,1,0:T(8,128)S(1)} %bitcast.100), kind=kLoop, calls=%fused_computation.74 | loop fusion | flops 524288 | bytes 2621440 | tf_op jit(solution)/shard_map/convert_element_type | solution.py:148
  (120 shorter events, 1.5 us)
Async XLA Ops:
  0.0 44.5 %copy-start = (bf16[1024,256]{1,0:T(8,128)(2,1)S(1)}, bf16[1024,256]{1,0:T(8,128)(2,1)}, u32[]{:S(2)}) copy-start(bf16[1024,256]{1,0:T(8,128)(2,1)} %param.21) | copy-start | bytes 1572868
  0.9 11.6 %collective-permute-start = (bf16[3,32,256]{2,1,0:T(8,128)(2,1)S(1)}, bf16[3,32,256]{2,1,0:T(8,128)(2,1)S(1)}, u32[]{:S(2)}, u32[]{:S(2)}) collective-permute-start(bf16[3,32,256]{2,1,0:T(8,128)(2,1)S(1)} %get-tuple-element.13), channel_id=1, source_target_pairs={{0,16},{16,32},{32,48},{48,64},{64,80},{80,96},{96,112},{112,128},... | collective-permute-start | bytes 147464 | tf_op jit(solution)/shard_map/ppermute | solution.py:16
  5.4 8.4 %collective-permute-start.1 = (bf16[3,32,256]{2,1,0:T(8,128)(2,1)S(1)}, bf16[3,32,256]{2,1,0:T(8,128)(2,1)S(1)}, u32[]{:S(2)}, u32[]{:S(2)}) collective-permute-start(bf16[3,32,256]{2,1,0:T(8,128)(2,1)S(1)} %get-tuple-element.12), channel_id=1, source_target_pairs={{16,0},{32,16},{48,32},{64,48},{80,64},{96,80},{112,96},{128,112},... | collective-permute-start | bytes 147464 | tf_op jit(solution)/shard_map/ppermute | solution.py:17
  13.7 8.7 %copy-start.1 = (bf16[35,32,256]{2,1,0:T(8,128)(2,1)}, bf16[35,32,256]{2,1,0:T(8,128)(2,1)S(1)}, u32[]{:S(2)}) copy-start(bf16[35,32,256]{2,1,0:T(8,128)(2,1)S(1)} %get-tuple-element.9) | copy-start | bytes 1720324
  13.9 8.6 %copy-start.4 = (bf16[38,32,256]{2,1,0:T(8,128)(2,1)}, bf16[38,32,256]{2,1,0:T(8,128)(2,1)S(1)}, u32[]{:S(2)}) copy-start(bf16[38,32,256]{2,1,0:T(8,128)(2,1)S(1)} %get-tuple-element.19) | copy-start | bytes 1867780
  14.8 14.4 %collective-permute-start.3 = (bf16[38,3,256]{2,1,0:T(4,128)(2,1)}, bf16[38,3,256]{2,1,0:T(4,128)(2,1)S(1)}, u32[]{:S(2)}, u32[]{:S(2)}) collective-permute-start(bf16[38,3,256]{2,1,0:T(4,128)(2,1)} %get-tuple-element.8), channel_id=1, source_target_pairs={{1,0},{2,1},{3,2},{4,3},{5,4},{6,5},{7,6},{8,7},{9,8},{10,9},{11,1... | collective-permute-start | bytes 175112 | tf_op jit(solution)/shard_map/ppermute | solution.py:17
  18.7 10.5 %collective-permute-start.2 = (bf16[38,3,256]{2,1,0:T(4,128)(2,1)}, bf16[38,3,256]{2,1,0:T(4,128)(2,1)}, u32[]{:S(2)}, u32[]{:S(2)}) collective-permute-start(bf16[38,3,256]{2,1,0:T(4,128)(2,1)} %get-tuple-element.7), channel_id=1, source_target_pairs={{0,1},{1,2},{2,3},{3,4},{4,5},{5,6},{6,7},{7,8},{8,9},{9,10},{10,1... | collective-permute-start | bytes 175112 | tf_op jit(solution)/shard_map/ppermute | solution.py:16
  26.3 2.9 %copy-start.10 = (f32[1,1,256]{2,1,0:T(1,128)S(1)}, f32[1,1,256]{2,1,0:T(1,128)}, u32[]{:S(2)}) copy-start(f32[1,1,256]{2,1,0:T(1,128)} %get-tuple-element.26) | copy-start | bytes 3076
  26.4 2.9 %copy-start.11 = (f32[1,1,256]{2,1,0:T(1,128)S(1)}, f32[1,1,256]{2,1,0:T(1,128)}, u32[]{:S(2)}) copy-start(f32[1,1,256]{2,1,0:T(1,128)} %get-tuple-element.27) | copy-start | bytes 3076
  26.4 2.9 %copy-start.12 = (f32[1,1,256]{2,1,0:T(1,128)S(1)}, f32[1,1,256]{2,1,0:T(1,128)}, u32[]{:S(2)}) copy-start(f32[1,1,256]{2,1,0:T(1,128)} %get-tuple-element.28) | copy-start | bytes 3076
  26.4 2.9 %copy-start.13 = (f32[1,1,256]{2,1,0:T(1,128)S(1)}, f32[1,1,256]{2,1,0:T(1,128)}, u32[]{:S(2)}) copy-start(f32[1,1,256]{2,1,0:T(1,128)} %get-tuple-element.29) | copy-start | bytes 3076
  26.4 2.9 %copy-start.14 = (f32[1,1,256]{2,1,0:T(1,128)S(1)}, f32[1,1,256]{2,1,0:T(1,128)}, u32[]{:S(2)}) copy-start(f32[1,1,256]{2,1,0:T(1,128)} %get-tuple-element.30) | copy-start | bytes 3076
  26.4 2.9 %copy-start.15 = (f32[1,1,256]{2,1,0:T(1,128)S(1)}, f32[1,1,256]{2,1,0:T(1,128)}, u32[]{:S(2)}) copy-start(f32[1,1,256]{2,1,0:T(1,128)} %get-tuple-element.31) | copy-start | bytes 3076
  26.4 2.9 %copy-start.16 = (f32[1,1,256]{2,1,0:T(1,128)S(1)}, f32[1,1,256]{2,1,0:T(1,128)}, u32[]{:S(2)}) copy-start(f32[1,1,256]{2,1,0:T(1,128)} %get-tuple-element.32) | copy-start | bytes 3076
  26.4 2.9 %copy-start.17 = (f32[1,1,256]{2,1,0:T(1,128)S(1)}, f32[1,1,256]{2,1,0:T(1,128)}, u32[]{:S(2)}) copy-start(f32[1,1,256]{2,1,0:T(1,128)} %get-tuple-element.33) | copy-start | bytes 3076
  26.4 2.9 %copy-start.18 = (f32[1,1,256]{2,1,0:T(1,128)S(1)}, f32[1,1,256]{2,1,0:T(1,128)}, u32[]{:S(2)}) copy-start(f32[1,1,256]{2,1,0:T(1,128)} %get-tuple-element.34) | copy-start | bytes 3076
  26.4 2.9 %copy-start.19 = (f32[1,1,256]{2,1,0:T(1,128)S(1)}, f32[1,1,256]{2,1,0:T(1,128)}, u32[]{:S(2)}) copy-start(f32[1,1,256]{2,1,0:T(1,128)} %get-tuple-element.35) | copy-start | bytes 3076
  26.4 2.9 %copy-start.20 = (f32[1,1,256]{2,1,0:T(1,128)S(1)}, f32[1,1,256]{2,1,0:T(1,128)}, u32[]{:S(2)}) copy-start(f32[1,1,256]{2,1,0:T(1,128)} %get-tuple-element.36) | copy-start | bytes 3076
  26.5 2.9 %copy-start.21 = (f32[1,1,256]{2,1,0:T(1,128)S(1)}, f32[1,1,256]{2,1,0:T(1,128)}, u32[]{:S(2)}) copy-start(f32[1,1,256]{2,1,0:T(1,128)} %get-tuple-element.37) | copy-start | bytes 3076
  26.5 2.9 %copy-start.22 = (f32[1,1,256]{2,1,0:T(1,128)S(1)}, f32[1,1,256]{2,1,0:T(1,128)}, u32[]{:S(2)}) copy-start(f32[1,1,256]{2,1,0:T(1,128)} %get-tuple-element.38) | copy-start | bytes 3076
  26.5 2.9 %copy-start.23 = (f32[1,1,256]{2,1,0:T(1,128)S(1)}, f32[1,1,256]{2,1,0:T(1,128)}, u32[]{:S(2)}) copy-start(f32[1,1,256]{2,1,0:T(1,128)} %get-tuple-element.39) | copy-start | bytes 3076
  44.5 11.1 %copy-start.6 = (bf16[256,512]{1,0:T(8,128)(2,1)S(1)}, bf16[256,512]{1,0:T(8,128)(2,1)}, u32[]{:S(2)}) copy-start(bf16[256,512]{1,0:T(8,128)(2,1)} %param.25) | copy-start | bytes 786436
  55.4 20.2 %copy-start.7 = (bf16[256,256]{1,0:T(8,128)(2,1)S(1)}, bf16[256,256]{1,0:T(8,128)(2,1)}, u32[]{:S(2)}) copy-start(bf16[256,256]{1,0:T(8,128)(2,1)} %param.24) | copy-start | bytes 393220
  55.4 21.2 %copy-start.8 = (bf16[256,256]{1,0:T(8,128)(2,1)S(1)}, bf16[256,256]{1,0:T(8,128)(2,1)}, u32[]{:S(2)}) copy-start(bf16[256,256]{1,0:T(8,128)(2,1)} %param.27) | copy-start | bytes 393220
  (28 other events, 76.6 us)
where the time goes:
time: 79.1 us; the launch traced here: 77.9 us
  other arithmetic  20.9 us (26%)
  blocking collectives  19.7 us (25%)
  starting transfers between devices  14.4 us (18%)
  matrix products  13.2 us (17%)
  local copies, waits for them, and re-layouts  8.63 us (11%)
  between operations  0.97 us (1%)
    all_gather x1, blocking collectives, shards(): band_keyval = lax.all_gather(keyval, 'col', axis=0, tiled=True)  19.7 us
    reduce_sum x1, other arithmetic, block_pass(): average = jnp.mean(convolved, axis=-1, keepdims=True)  13.4 us
    dot_general x1, matrix products, block_pass(): jnp.dot(hidden, w_reduce, preferred_element_type=jnp.float32) + b_reduce  10.9 us
    ppermute x2, starting transfers between devices, padded_2(): before = lax.ppermute(last, axis, up)  8.23 us
    ppermute x2, starting transfers between devices, padded_2(): after = lax.ppermute(leading, axis, down)  6.19 us
    mul x3, other arithmetic, block_pass(): padded[tap_row:tap_row + tile_rows, tap_col:tap_col + tile_cols]  4.79 us
    reshape x1, local copies, waits for them, and re-layouts, shards(): jnp.transpose(both_picked, (0, 1, 2, 4, 3, 5))  2.47 us
    transpose x1, local copies, waits for them, and re-layouts, shards(): jnp.transpose(both_picked, (0, 1, 2, 4, 3, 5))  1.76 us
  transfers between devices with their start and end apart: 4, of which 1 were waited for; matrix products, arithmetic and copies ran while one was open for 16% of the time, Pallas kernels for 0%

commit v1 on v0

--- a/solution.py
+++ b/solution.py
@@ -98,33 +98,33 @@
     )
     pooled = pooled.astype(jnp.bfloat16).reshape(local_count, channels)
     queries = jnp.dot(pooled, w_query, preferred_element_type=jnp.float32).astype(jnp.bfloat16)
-    keyval = jnp.dot(pooled, w_keyval, preferred_element_type=jnp.float32).astype(jnp.bfloat16)
-    band_keyval = lax.all_gather(keyval, "col", axis=0, tiled=True)
     columns = lax.axis_size("col")
     position = lax.axis_index("col")
     span_cols = region_side * columns
     key_count = local_count * columns
-    side_index = jnp.arange(region_side, dtype=jnp.int32)
-    row_offsets = side_index[None, :] - side_index[:, None] + region_side - 1
-    row_onehot = (
-        row_offsets[:, :, None] == jnp.arange(2 * region_side - 1, dtype=jnp.int32)[None, None, :]
-    ).astype(jnp.float32)
-    row_picked = jnp.einsum("rso,hoc->hrsc", row_onehot, rel_bias, precision=lax.Precision.HIGHEST)
-    query_cols = position * region_side + side_index
-    span_index = jnp.arange(span_cols, dtype=jnp.int32)
-    col_offsets = span_index[None, :] - query_cols[:, None] + span_cols - 1
-    col_onehot = (
-        col_offsets[:, :, None] == jnp.arange(2 * span_cols - 1, dtype=jnp.int32)[None, None, :]
-    ).astype(jnp.float32)
-    both_picked = jnp.einsum(
-        "hrsc,qkc->hrqsk", row_picked, col_onehot, precision=lax.Precision.HIGHEST
+    sent = jnp.broadcast_to(pooled[None], (columns, local_count, channels)).reshape(
+        columns * local_count, channels
     )
-    both_picked = both_picked.reshape(
-        HEADS, region_side, region_side, region_side, columns, region_side
+    band_pooled = lax.all_to_all(sent, "col", 0, 0, tiled=True)
+    band_pooled = (
+        band_pooled.reshape(columns, region_side, region_side, channels)
+        .transpose(1, 0, 2, 3)
+        .reshape(key_count, channels)
     )
-    bias_block = jnp.transpose(both_picked, (0, 1, 2, 4, 3, 5)).reshape(
-        HEADS, local_count, key_count
+    band_keyval = jnp.dot(band_pooled, w_keyval, preferred_element_type=jnp.float32).astype(
+        jnp.bfloat16
     )
+    windows = []
+    for query_col in range(region_side):
+        first = span_cols - 1 - (position * region_side + query_col)
+        windows.append(lax.dynamic_slice_in_dim(rel_bias, first, span_cols, axis=2))
+    rows_of = []
+    for query_row in range(region_side):
+        per_col = [
+            w[:, region_side - 1 - query_row : 2 * region_side - 1 - query_row, :] for w in windows
+        ]
+        rows_of.append(jnp.stack(per_col, axis=1))
+    bias_block = jnp.stack(rows_of, axis=1).reshape(HEADS, local_count, key_count)
     query_heads = queries.reshape(local_count, HEADS, head_dim)
     key_heads = band_keyval[:, :channels].reshape(key_count, HEADS, head_dim)
     value_heads = band_keyval[:, channels:].reshape(key_count, HEADS, head_dim)

time: 79.1 us -> 64.4 us (0.81)
  the two profiles are of different devices: /device:TPU:113 before, /device:TPU:129 now
where the time goes in v1:
time: 64.4 us; the launch traced here: 63.8 us
  starting transfers between devices  22 us (34%)
  other arithmetic  18.7 us (29%)
  matrix products  10.8 us (17%)
  waiting for transfers between devices  7.04 us (11%)
  local copies, waits for them, and re-layouts  4.97 us (8%)
    reduce_sum x1, other arithmetic, block_pass(): average = jnp.mean(convolved, axis=-1, keepdims=True)  12 us
    dot_general x1, matrix products, block_pass(): jnp.dot(hidden, w_reduce, preferred_element_type=jnp.float32) + b_reduce  9.83 us
    ppermute x2, starting transfers between devices, padded_2(): before = lax.ppermute(last, axis, up)  7.91 us
    ppermute x2, starting transfers between devices, padded_2(): after = lax.ppermute(leading, axis, down)  7.22 us
    all_to_all x1, starting transfers between devices, shards(): band_pooled = lax.all_to_all(sent, 'col', 0, 0, tiled=True)  6.85 us
    all_to_all x1, waiting for transfers between devices, shards(): band_pooled = lax.all_to_all(sent, 'col', 0, 0, tiled=True)  5.92 us
    mul x3, other arithmetic, block_pass(): padded[tap_row:tap_row + tile_rows, tap_col:tap_col + tile_cols]  4.73 us
    another operation x1, local copies, waits for them, and re-layouts, shards(): rows_of.append(jnp.stack(per_col, axis=1))  1.44 us
  transfers between devices with their start and end apart: 5, of which 2 were waited for; matrix products, arithmetic and copies ran while one was open for 11% of the time, Pallas kernels for 0%

profile of v1, /device:TPU:129, one launch (start us, length us, event | category | flops | bytes accessed | tf_op | source)
XLA Modules:
  0.0 63.8 jit_solution(827272639975056236)
XLA Ops:
  0.0 0.9 %fusion.96 = (bf16[3,32,256]{2,1,0:T(8,128)(2,1)S(1)}, bf16[3,32,256]{2,1,0:T(8,128)(2,1)S(1)}) fusion(bf16[32,32,256]{2,1,0:T(8,128)(2,1)} %param.14), kind=kLoop, calls=%fused_computation.273 | loop fusion | bytes 196608 | tf_op jit(solution)/shard_map/slice | solution.py:15
  0.9 4.8 %collective-permute-start = (bf16[3,32,256]{2,1,0:T(8,128)(2,1)S(1)}, bf16[3,32,256]{2,1,0:T(8,128)(2,1)S(1)}, u32[]{:S(2)}, u32[]{:S(2)}) collective-permute-start(bf16[3,32,256]{2,1,0:T(8,128)(2,1)S(1)} %get-tuple-element.13), channel_id=1, source_target_pairs={{0,16},{16,32},{32,48},{48,64},{64,80},{80,96},{96,112},{112,128},... | collective-permute-start | bytes 147464 | tf_op jit(solution)/shard_map/ppermute | solution.py:16
  5.7 4.1 %collective-permute-start.1 = (bf16[3,32,256]{2,1,0:T(8,128)(2,1)S(1)}, bf16[3,32,256]{2,1,0:T(8,128)(2,1)S(1)}, u32[]{:S(2)}, u32[]{:S(2)}) collective-permute-start(bf16[3,32,256]{2,1,0:T(8,128)(2,1)S(1)} %get-tuple-element.12), channel_id=1, source_target_pairs={{16,0},{32,16},{48,32},{64,48},{80,64},{96,80},{112,96},{128,112},... | collective-permute-start | bytes 147464 | tf_op jit(solution)/shard_map/ppermute | solution.py:17
  9.8 1.5 %slice_convert_fusion.46 = (f32[1,1,256]{2,1,0:T(1,128)S(1)}, f32[1,1,256]{2,1,0:T(1,128)S(1)}, f32[1,1,256]{2,1,0:T(1,128)S(1)}, f32[1,1,256]{2,1,0:T(1,128)S(1...) fusion(bf16[7,7,256]{2,1,0:T(8,128)(2,1)} %param.15), kind=kLoop, calls=%fused_computation.237 | loop fusion | flops 2816 | bytes 16896 | tf_op jit(solution)/shard_map/mul | solution.py:39
  11.3 1.6 %slice_convert_fusion.48 = (f32[1,1,256]{2,1,0:T(1,128)}, f32[1,1,256]{2,1,0:T(1,128)}, f32[1,1,256]{2,1,0:T(1,128)}, f32[1,1,256]{2,1,0:T(1,128)}, f32[1,1,256]...) fusion(bf16[7,7,256]{2,1,0:T(8,128)(2,1)} %param.15), kind=kLoop, calls=%fused_computation.239 | loop fusion | flops 4864 | bytes 29184 | tf_op jit(solution)/shard_map/mul | solution.py:39
  12.9 1.6 %slice_convert_fusion.47 = (f32[1,1,256]{2,1,0:T(1,128)}, f32[1,1,256]{2,1,0:T(1,128)}, f32[1,1,256]{2,1,0:T(1,128)}, f32[1,1,256]{2,1,0:T(1,128)}, f32[1,1,256]...) fusion(bf16[7,7,256]{2,1,0:T(8,128)(2,1)} %param.15), kind=kLoop, calls=%fused_computation.238 | loop fusion | flops 4864 | bytes 29184 | tf_op jit(solution)/shard_map/mul | solution.py:39
  14.6 1.4 %dynamic-slice_bitcast_fusion.15 = (f32[8,1,4,64]{3,0,2,1:T(8,128)S(1)}, f32[8,1,4,64]{3,0,2,1:T(8,128)S(1)}, f32[8,1,4,64]{3,0,2,1:T(8,128)S(1)}, f32[8,1,4,64]...) fusion(f32[8,7,127]{2,0,1:T(8,128)} %param.26, ...), kind=kLoop, calls=%fused_computation.180 | loop fusion | bytes 262172 | tf_op jit(solution)/shard_map/stack | solution.py:126
  16.1 0.2 constant_dynamic-update-slice_fusion.3
  16.4 3.1 %collective-permute-start.3 = (bf16[38,3,256]{2,1,0:T(4,128)(2,1)S(1)}, bf16[38,3,256]{2,1,0:T(4,128)(2,1)S(1)}, u32[]{:S(2)}, u32[]{:S(2)}) collective-permute-start(bf16[38,3,256]{2,1,0:T(4,128)(2,1)S(1)} %get-tuple-element.8), channel_id=1, source_target_pairs={{1,0},{2,1},{3,2},{4,3},{5,4},{6,5},{7,6},{8,7},{9,8},{10,9},{11,1... | collective-permute-start | bytes 175112 | tf_op jit(solution)/shard_map/ppermute | solution.py:17
  19.6 3.1 %collective-permute-start.2 = (bf16[38,3,256]{2,1,0:T(4,128)(2,1)S(1)}, bf16[38,3,256]{2,1,0:T(4,128)(2,1)S(1)}, u32[]{:S(2)}, u32[]{:S(2)}) collective-permute-start(bf16[38,3,256]{2,1,0:T(4,128)(2,1)S(1)} %get-tuple-element.7), channel_id=1, source_target_pairs={{0,1},{1,2},{2,3},{3,4},{4,5},{5,6},{6,7},{7,8},{8,9},{9,10},{10,1... | collective-permute-start | bytes 175112 | tf_op jit(solution)/shard_map/ppermute | solution.py:16
  22.8 0.2 reshape.91
  23.0 1.1 %collective-permute-done.2 = bf16[38,3,256]{2,1,0:T(4,128)(2,1)S(1)} collective-permute-done((bf16[38,3,256]{2,1,0:T(4,128)(2,1)S(1)}, bf16[38,3,256]{2,1,0:T(4,128)(2,1)S(1)}, u32[]{:S(2)}, u32[]{:S(2)}) %collective-permute-start.2) | collective-permute-done | bytes 58400 | tf_op jit(solution)/shard_map/ppermute | solution.py:16
  24.1 12.0 %fusion.94 = (f32[32,32]{1,0:T(8,128)S(1)}, f32[32,32,256]{2,1,0:T(8,128)S(1)}) fusion(f32[256]{0:T(256)} %param.16, f32[256]{0:T(256)} %bitcast.134, bf16[38,3,256]{2,1,0:T(4,128)(2,1)S(1)} %collective-permute-done.3, bf16[38,32,256]{2,1,0:T(8,128)(2,1)S(1)} %get-tuple-element.19, f32[256]{0:T(256)} %bitcast.135, f32[256]{0:T(256)} %bitcast.137, ...), kind=kLoop, calls=%fused_computation.271 | loop fusion | flops 71826432 | bytes 5513216 | tf_op jit(solution)/shard_map/reduce_sum | solution.py:43
  36.1 0.4 multiply_reduce_fusion
  36.5 0.2 copy-done.5
  36.8 0.3 add_convert_fusion.1
  37.1 0.4 copy-done.7
  37.5 9.8 %fusion.14 = f32[1024,256]{1,0:T(8,128)S(1)} fusion(bf16[1024,256]{1,0:T(8,128)(2,1)S(1)} %copy-done, bf16[1024,256]{1,0:T(8,128)(2,1)S(1)} %bitcast.121, bf16[256,1024]{1,0:T(8,128)(2,1)S(1)} %copy-done.7, f32[1024]{0:T(1024)S(1)} %copy-done.8, f32[256]{0:T(256)S(1)} %copy-done.9, f32[256]{0:T(256)S(1)} %copy-done.10, bf16[1024,256]{1,0:T(8,128)(2,1)S(1)} %bitcast.120), kind=kOutput, calls=%fused_computation.64 | convolution fusion | flops 1144520704 | bytes 3151872 | tf_op jit(solution)/shard_map/dot_general | solution.py:54
  47.5 0.7 %broadcast_in_dim.4 = bf16[16,16,256]{2,1,0:T(8,128)(2,1)} broadcast(bf16[16,256]{1,0:T(8,128)(2,1)S(1)} %convert_element_type.356), dimensions={1,2} | broadcast | bytes 139264 | tf_op jit(solution)/shard_map/broadcast_in_dim | solution.py:105
  48.2 6.8 %all-to-all-start = ((bf16[16,16,256]{2,1,0:T(8,128)(2,1)}), bf16[16,16,256]{2,1,0:T(8,128)(2,1)S(1)}, u32[]{:S(2)}, u32[]{:S(2)}) async-start(bf16[16,16,256]{2,1,0:T(8,128)(2,1)} %broadcast_in_dim.4), calls=%async_computation | async-start | bytes 262144 | tf_op jit(solution)/shard_map/all_to_all | solution.py:108
  55.3 5.9 %all-to-all-done = bf16[16,16,256]{2,1,0:T(8,128)(2,1)S(1)} async-done(((bf16[16,16,256]{2,1,0:T(8,128)(2,1)}), bf16[16,16,256]{2,1,0:T(8,128)(2,1)S(1)}, u32[]{:S(2)}, u32[]{:S(2)}) %all-to-all-start) | async-done | bytes 131104 | tf_op jit(solution)/shard_map/all_to_all | solution.py:108
  61.4 0.2 convolution_convert_fusion
  62.2 0.3 fusion.18
  62.9 1.0 %add_convert_fusion = bf16[32,32,256]{2,1,0:T(8,128)(2,1)} fusion(f32[32,32,256]{2,1,0:T(8,128)S(1)} %bitcast.118, f32[32,32,256]{2,1,0:T(8,128)S(1)} %bitcast.119), kind=kLoop, calls=%fused_computation.73 | loop fusion | flops 524288 | bytes 2621440 | tf_op jit(solution)/shard_map/convert_element_type | solution.py:148
  (49 shorter events, 1.7 us)
Async XLA Ops:
  0.0 37.1 %copy-start = (bf16[1024,256]{1,0:T(8,128)(2,1)S(1)}, bf16[1024,256]{1,0:T(8,128)(2,1)}, u32[]{:S(2)}) copy-start(bf16[1024,256]{1,0:T(8,128)(2,1)} %param.21) | copy-start | bytes 1572868
  0.0 16.1 %copy-start.1 = (bf16[32,32,256]{2,1,0:T(8,128)(2,1)S(1)}, bf16[32,32,256]{2,1,0:T(8,128)(2,1)}, u32[]{:S(2)}) copy-start(bf16[32,32,256]{2,1,0:T(8,128)(2,1)} %param.14) | copy-start | bytes 1572868
  0.9 15.1 %collective-permute-start = (bf16[3,32,256]{2,1,0:T(8,128)(2,1)S(1)}, bf16[3,32,256]{2,1,0:T(8,128)(2,1)S(1)}, u32[]{:S(2)}, u32[]{:S(2)}) collective-permute-start(bf16[3,32,256]{2,1,0:T(8,128)(2,1)S(1)} %get-tuple-element.13), channel_id=1, source_target_pairs={{0,16},{16,32},{32,48},{48,64},{64,80},{80,96},{96,112},{112,128},... | collective-permute-start | bytes 147464 | tf_op jit(solution)/shard_map/ppermute | solution.py:16
  5.7 10.6 %collective-permute-start.1 = (bf16[3,32,256]{2,1,0:T(8,128)(2,1)S(1)}, bf16[3,32,256]{2,1,0:T(8,128)(2,1)S(1)}, u32[]{:S(2)}, u32[]{:S(2)}) collective-permute-start(bf16[3,32,256]{2,1,0:T(8,128)(2,1)S(1)} %get-tuple-element.12), channel_id=1, source_target_pairs={{16,0},{32,16},{48,32},{64,48},{80,64},{96,80},{112,96},{128,112},... | collective-permute-start | bytes 147464 | tf_op jit(solution)/shard_map/ppermute | solution.py:17
  16.4 6.6 %collective-permute-start.3 = (bf16[38,3,256]{2,1,0:T(4,128)(2,1)S(1)}, bf16[38,3,256]{2,1,0:T(4,128)(2,1)S(1)}, u32[]{:S(2)}, u32[]{:S(2)}) collective-permute-start(bf16[38,3,256]{2,1,0:T(4,128)(2,1)S(1)} %get-tuple-element.8), channel_id=1, source_target_pairs={{1,0},{2,1},{3,2},{4,3},{5,4},{6,5},{7,6},{8,7},{9,8},{10,9},{11,1... | collective-permute-start | bytes 175112 | tf_op jit(solution)/shard_map/ppermute | solution.py:17
  19.6 4.5 %collective-permute-start.2 = (bf16[38,3,256]{2,1,0:T(4,128)(2,1)S(1)}, bf16[38,3,256]{2,1,0:T(4,128)(2,1)S(1)}, u32[]{:S(2)}, u32[]{:S(2)}) collective-permute-start(bf16[38,3,256]{2,1,0:T(4,128)(2,1)S(1)} %get-tuple-element.7), channel_id=1, source_target_pairs={{0,1},{1,2},{2,3},{3,4},{4,5},{5,6},{6,7},{7,8},{8,9},{9,10},{10,1... | collective-permute-start | bytes 175112 | tf_op jit(solution)/shard_map/ppermute | solution.py:16
  36.1 0.7 %copy-start.5 = (f32[256]{0:T(256)S(1)}, f32[256]{0:T(256)}, u32[]{:S(2)}) copy-start(f32[256]{0:T(256)} %param.18) | copy-start | bytes 3076
  36.1 0.7 %copy-start.6 = (f32[256]{0:T(256)S(1)}, f32[256]{0:T(256)}, u32[]{:S(2)}) copy-start(f32[256]{0:T(256)} %param.17) | copy-start | bytes 3076
  36.5 1.0 %copy-start.7 = (bf16[256,1024]{1,0:T(8,128)(2,1)S(1)}, bf16[256,1024]{1,0:T(8,128)(2,1)}, u32[]{:S(2)}) copy-start(bf16[256,1024]{1,0:T(8,128)(2,1)} %param.19) | copy-start | bytes 1572868
  36.5 1.0 %copy-start.8 = (f32[1024]{0:T(1024)S(1)}, f32[1024]{0:T(1024)}, u32[]{:S(2)}) copy-start(f32[1024]{0:T(1024)} %param.20) | copy-start | bytes 12292
  36.5 1.0 %copy-start.9 = (f32[256]{0:T(256)S(1)}, f32[256]{0:T(256)}, u32[]{:S(2)}) copy-start(f32[256]{0:T(256)} %param.22) | copy-start | bytes 3076
  36.5 1.0 %copy-start.10 = (f32[256]{0:T(256)S(1)}, f32[256]{0:T(256)}, u32[]{:S(2)}) copy-start(f32[256]{0:T(256)} %param.23) | copy-start | bytes 3076
  47.4 7.7 %copy-start.3 = (bf16[256,256]{1,0:T(8,128)(2,1)S(1)}, bf16[256,256]{1,0:T(8,128)(2,1)}, u32[]{:S(2)}) copy-start(bf16[256,256]{1,0:T(8,128)(2,1)} %param.24) | copy-start | bytes 393220
  47.4 14.0 %copy-start.2 = (bf16[256,512]{1,0:T(8,128)(2,1)S(1)}, bf16[256,512]{1,0:T(8,128)(2,1)}, u32[]{:S(2)}) copy-start(bf16[256,512]{1,0:T(8,128)(2,1)} %param.25) | copy-start | bytes 786436
  48.2 13.0 %all-to-all-start = ((bf16[16,16,256]{2,1,0:T(8,128)(2,1)}), bf16[16,16,256]{2,1,0:T(8,128)(2,1)S(1)}, u32[]{:S(2)}, u32[]{:S(2)}) async-start(bf16[16,16,256]{2,1,0:T(8,128)(2,1)} %broadcast_in_dim.4), calls=%async_computation | async-start | bytes 262144 | tf_op jit(solution)/shard_map/all_to_all | solution.py:108
  61.6 1.0 %copy-start.4 = (bf16[256,256]{1,0:T(8,128)(2,1)S(1)}, bf16[256,256]{1,0:T(8,128)(2,1)}, u32[]{:S(2)}) copy-start(bf16[256,256]{1,0:T(8,128)(2,1)} %param.27) | copy-start | bytes 393220

commit v2 on v1

--- a/solution.py
+++ b/solution.py
@@ -2,6 +2,8 @@
 import jax.numpy as jnp
 from jax import lax
 from jax.sharding import PartitionSpec as P
+from jax.experimental import pallas as pl
+from jax.experimental.pallas import tpu as pltpu
 
 HEADS = 8
 
@@ -17,6 +19,67 @@
         after = lax.ppermute(leading, axis, down)
         array = jnp.concatenate([before, array, after], axis=dim)
     return array
+
+
+TAPS = 7
+ROW_BLOCK = 2
+
+
+def conv_norm_kernel(x_ref, k_ref, db_ref, g_ref, nb_ref, o_ref, xf_ref, sh_ref):
+    rows_p = x_ref.shape[0]
+    tile_rows, tile_cols, channels = o_ref.shape
+
+    def widen(r, carry):
+        xf_ref[r] = x_ref[r].astype(jnp.float32)
+        for b in range(TAPS):
+            sh_ref[b, r] = xf_ref[r, pl.ds(b, tile_cols), :]
+        return carry
+
+    lax.fori_loop(0, rows_p, widen, 0)
+    db = db_ref[...]
+    g = g_ref[...]
+    nb = nb_ref[...]
+
+    def body(i, carry):
+        r0 = pl.multiple_of(i * ROW_BLOCK, ROW_BLOCK)
+        acc = jnp.zeros((ROW_BLOCK, tile_cols, channels), jnp.float32)
+        for a in range(TAPS):
+            for b in range(TAPS):
+                acc = acc + sh_ref[b, pl.ds(r0 + a, ROW_BLOCK)] * k_ref[pl.ds(a * TAPS + b, 1), :]
+        acc = acc + db
+        mean = jnp.mean(acc, axis=-1, keepdims=True)
+        cen = acc - mean
+        var = jnp.mean(cen * cen, axis=-1, keepdims=True)
+        o_ref[pl.ds(r0, ROW_BLOCK)] = (cen * lax.rsqrt(var + 1e-06) * g + nb).astype(o_ref.dtype)
+        return carry
+
+    lax.fori_loop(0, tile_rows // ROW_BLOCK, body, 0)
+
+
+def conv_norm(padded, dw_kernel, dw_bias, norm_gain, norm_bias, tile_rows, tile_cols):
+    rows_p, cols_p, channels = padded.shape
+    vmem = pl.BlockSpec(memory_space=pltpu.VMEM)
+    return pl.pallas_call(
+        conv_norm_kernel,
+        out_shape=jax.ShapeDtypeStruct((tile_rows, tile_cols, channels), jnp.bfloat16),
+        in_specs=[vmem] * 5,
+        out_specs=vmem,
+        scratch_shapes=[
+            pltpu.VMEM((rows_p, cols_p, channels), jnp.float32),
+            pltpu.VMEM((TAPS, rows_p, tile_cols, channels), jnp.float32),
+        ],
+        cost_estimate=pl.CostEstimate(
+            flops=2 * TAPS * TAPS * tile_rows * tile_cols * channels,
+            bytes_accessed=2 * (rows_p * cols_p + tile_rows * tile_cols) * channels,
+            transcendentals=tile_rows * tile_cols,
+        ),
+    )(
+        padded,
+        dw_kernel.astype(jnp.float32).reshape(TAPS * TAPS, channels),
+        dw_bias.reshape(1, channels),
+        norm_gain.reshape(1, channels),
+        norm_bias.reshape(1, channels),
+    )
 
 
 def block_pass(
@@ -33,21 +96,10 @@
     layer_scale,
 ):
     tile_rows, tile_cols, channels = features.shape
-    convolved = jnp.zeros((tile_rows, tile_cols, channels), jnp.float32)
-    for tap_row in range(7):
-        for tap_col in range(7):
-            convolved = convolved + padded[
-                tap_row : tap_row + tile_rows, tap_col : tap_col + tile_cols
-            ].astype(jnp.float32) * dw_kernel[tap_row, tap_col].astype(jnp.float32)
-    convolved = convolved + dw_bias
-    average = jnp.mean(convolved, axis=-1, keepdims=True)
-    centred = convolved - average
-    variance = jnp.mean(centred * centred, axis=-1, keepdims=True)
-    normed = (
-        (centred * lax.rsqrt(variance + 1e-06) * norm_gain + norm_bias)
-        .astype(jnp.bfloat16)
-        .reshape(-1, channels)
-    )
+    padded = jnp.pad(padded, ((0, 0), (0, 8 - padded.shape[1] % 8), (0, 0)))
+    normed = conv_norm(
+        padded, dw_kernel, dw_bias, norm_gain, norm_bias, tile_rows, tile_cols
+    ).reshape(-1, channels)
     hidden = jax.nn.gelu(
         jnp.dot(normed, w_expand, preferred_element_type=jnp.float32) + b_expand, approximate=False
     ).astype(jnp.bfloat16)

time: 64.4 us -> 63.2 us (0.981)
  other arithmetic: 18.7 us -> 2.63 us
  Pallas kernels: 0 us -> 10.2 us
  waiting for transfers between devices: 7.04 us -> 13.2 us
  starting transfers between devices: 22 us -> 19.7 us
  matrix products: 10.8 us -> 11.8 us
    reduce_sum x2 -> x0, other arithmetic: 12.3 us -> none  [the longest x1 12 us: block_pass(): average = jnp.mean(convolved, axis=-1, keepdims=True)]
    pallas_call x0 -> x1, Pallas kernels: none -> 10.2 us  [conv_norm(): pl.pallas_call(conv_norm_kernel, out_shape=jax.ShapeDtypeStruct((tile_row...]
    mul x3 -> x0, other arithmetic: 4.73 us -> none  [block_pass(): padded[tap_row:tap_row + tile_rows, tap_col:tap_col + tile_cols]]
    ppermute x2, waiting for transfers between devices: 1.11 us -> 4.51 us  [padded_2(): before = lax.ppermute(last, axis, up)]
    ppermute x2, waiting for transfers between devices: 0.01 us -> 2.82 us  [padded_2(): after = lax.ppermute(leading, axis, down)]
    concatenate x0 -> x1, other arithmetic: none -> 1.34 us  [padded_2(): array = jnp.concatenate([before, array, after], axis=dim)]
    ppermute x2, starting transfers between devices: 7.91 us -> 6.72 us  [padded_2(): before = lax.ppermute(last, axis, up)]
    dot_general x1, matrix products: 9.83 us -> 10.9 us  [block_pass(): jnp.dot(hidden, w_reduce, preferred_element_type=jnp.float32) + b_reduce]
  transfers between devices with their start and end apart: 5 -> 5, of which waited for: 2 -> 3; matrix products, arithmetic and copies ran while one was open for 11% -> 4% of each run, Pallas kernels for 0% -> 0%
where the time goes in v2:
time: 63.2 us; the launch traced here: 62.7 us
  starting transfers between devices  19.7 us (31%)
  waiting for transfers between devices  13.2 us (21%)
  matrix products  11.8 us (19%)
  Pallas kernels  10.2 us (16%)
  local copies, waits for them, and re-layouts  4.83 us (8%)
  other arithmetic  2.63 us (4%)
    dot_general x1, matrix products, block_pass(): jnp.dot(hidden, w_reduce, preferred_element_type=jnp.float32) + b_reduce  10.9 us
    pallas_call x1, Pallas kernels, conv_norm(): pl.pallas_call(conv_norm_kernel, out_shape=jax.ShapeDtypeStruct((tile_row...  10.2 us
    all_to_all x1, starting transfers between devices, shards(): band_pooled = lax.all_to_all(sent, 'col', 0, 0, tiled=True)  6.74 us
    ppermute x2, starting transfers between devices, padded_2(): before = lax.ppermute(last, axis, up)  6.72 us
    ppermute x2, starting transfers between devices, padded_2(): after = lax.ppermute(leading, axis, down)  6.28 us
    all_to_all x1, waiting for transfers between devices, shards(): band_pooled = lax.all_to_all(sent, 'col', 0, 0, tiled=True)  5.92 us
    ppermute x2, waiting for transfers between devices, padded_2(): before = lax.ppermute(last, axis, up)  4.51 us
    ppermute x2, waiting for transfers between devices, padded_2(): after = lax.ppermute(leading, axis, down)  2.82 us
  transfers between devices with their start and end apart: 5, of which 3 were waited for; matrix products, arithmetic and copies ran while one was open for 4% of the time, Pallas kernels for 0%

profile of v2, /device:TPU:129, one launch (start us, length us, event | category | flops | bytes accessed | tf_op | source)
XLA Modules:
  0.0 62.7 jit_solution(1917182992499735129)
XLA Ops:
  0.0 0.9 %fusion.60 = (bf16[3,32,256]{2,1,0:T(8,128)(2,1)S(1)}, bf16[3,32,256]{2,1,0:T(8,128)(2,1)S(1)}) fusion(bf16[32,32,256]{2,1,0:T(8,128)(2,1)} %param.14), kind=kLoop, calls=%fused_computation.102 | loop fusion | bytes 196608 | tf_op jit(solution)/shard_map/slice | solution.py:17
  0.9 4.4 %collective-permute-start.1 = (bf16[3,32,256]{2,1,0:T(8,128)(2,1)S(1)}, bf16[3,32,256]{2,1,0:T(8,128)(2,1)S(1)}, u32[]{:S(2)}, u32[]{:S(2)}) collective-permute-start(bf16[3,32,256]{2,1,0:T(8,128)(2,1)S(1)} %get-tuple-element.7), channel_id=1, source_target_pairs={{16,0},{32,16},{48,32},{64,48},{80,64},{96,80},{112,96},{128,112},... | collective-permute-start | bytes 147464 | tf_op jit(solution)/shard_map/ppermute | solution.py:19
  5.3 2.4 %collective-permute-start = (bf16[3,32,256]{2,1,0:T(8,128)(2,1)S(1)}, bf16[3,32,256]{2,1,0:T(8,128)(2,1)S(1)}, u32[]{:S(2)}, u32[]{:S(2)}) collective-permute-start(bf16[3,32,256]{2,1,0:T(8,128)(2,1)S(1)} %get-tuple-element.8), channel_id=1, source_target_pairs={{0,16},{16,32},{32,48},{48,64},{64,80},{80,96},{96,112},{112,128},... | collective-permute-start | bytes 147464 | tf_op jit(solution)/shard_map/ppermute | solution.py:18
  7.7 1.4 %dynamic-slice_bitcast_fusion.15 = (f32[8,1,4,64]{3,0,2,1:T(8,128)S(1)}, f32[8,1,4,64]{3,0,2,1:T(8,128)S(1)}, f32[8,1,4,64]{3,0,2,1:T(8,128)S(1)}, f32[8,1,4,64]...) fusion(f32[8,7,127]{2,0,1:T(8,128)} %param.26, ...), kind=kLoop, calls=%fused_computation.65 | loop fusion | bytes 262172 | tf_op jit(solution)/shard_map/stack | solution.py:178
  9.2 4.5 %collective-permute-done = bf16[3,32,256]{2,1,0:T(8,128)(2,1)S(1)} collective-permute-done((bf16[3,32,256]{2,1,0:T(8,128)(2,1)S(1)}, bf16[3,32,256]{2,1,0:T(8,128)(2,1)S(1)}, u32[]{:S(2)}, u32[]{:S(2)}) %collective-permute-start) | collective-permute-done | bytes 49184 | tf_op jit(solution)/shard_map/ppermute | solution.py:18
  13.9 4.3 %collective-permute-start.2 = (bf16[38,3,256]{2,1,0:T(4,128)(2,1)S(1)}, bf16[38,3,256]{2,1,0:T(4,128)(2,1)S(1)}, u32[]{:S(2)}, u32[]{:S(2)}) collective-permute-start(bf16[38,3,256]{2,1,0:T(4,128)(2,1)S(1)} %get-tuple-element.5), channel_id=1, source_target_pairs={{0,1},{1,2},{2,3},{3,4},{4,5},{5,6},{6,7},{7,8},{8,9},{9,10},{10,1... | collective-permute-start | bytes 175112 | tf_op jit(solution)/shard_map/ppermute | solution.py:18
  18.2 1.9 %collective-permute-start.3 = (bf16[38,3,256]{2,1,0:T(4,128)(2,1)S(1)}, bf16[38,3,256]{2,1,0:T(4,128)(2,1)S(1)}, u32[]{:S(2)}, u32[]{:S(2)}) collective-permute-start(bf16[38,3,256]{2,1,0:T(4,128)(2,1)S(1)} %get-tuple-element.6), channel_id=1, source_target_pairs={{1,0},{2,1},{3,2},{4,3},{5,4},{6,5},{7,6},{8,7},{9,8},{10,9},{11,1... | collective-permute-start | bytes 175112 | tf_op jit(solution)/shard_map/ppermute | solution.py:19
  20.2 0.7 %reshape.105.k_ref = f32[49,256]{1,0:T(8,128)} reshape(bf16[7,7,256]{2,1,0:T(8,128)(2,1)S(1)} %copy-done.5) | data formatting | bytes 75264 | tf_op jit(solution)/shard_map/reshape | solution.py:78
  20.9 0.2 reshape.99
  21.1 2.8 %collective-permute-done.3 = bf16[38,3,256]{2,1,0:T(4,128)(2,1)S(1)} collective-permute-done((bf16[38,3,256]{2,1,0:T(4,128)(2,1)S(1)}, bf16[38,3,256]{2,1,0:T(4,128)(2,1)S(1)}, u32[]{:S(2)}, u32[]{:S(2)}) %collective-permute-start.3) | collective-permute-done | bytes 58400 | tf_op jit(solution)/shard_map/ppermute | solution.py:19
  23.9 1.3 %fusion.23.x_ref = bf16[38,40,256]{2,1,0:T(8,128)(2,1)} fusion(bf16[38,3,256]{2,1,0:T(4,128)(2,1)S(1)} %collective-permute-done.3, bf16[38,32,256]{2,1,0:T(8,128)(2,1)S(1)} %constant_dynamic-update-slice_fusion, bf16[38,3,256]{2,1,0:T(4,128)(2,1)S(1)} %collective-permute-done.2), kind=kLoop, calls=%fused_computation.39 | loop fusion | flops 3891200 | bytes 1517568 | tf_op jit(solution)/shard_map/concatenate | solution.py:20
  25.2 10.2 %shard_map.136 = bf16[32,32,256]{2,1,0:T(8,128)(2,1)} custom-call(bf16[38,40,256]{2,1,0:T(8,128)(2,1)} %fusion.23.x_ref, f32[49,256]{1,0:T(8,128)} %reshape.105.k_ref, f32[1,256]{1,0:T(1,128)} %bitcast.79, f32[1,256]{1,0:T(1,128)} %bitcast.80, f32[1,256]{1,0:T(1,128)} %bitcast.81), custom_call_target="tpu_custom_call" | custom-call | flops 25690112 | bytes 1302528 | tf_op jit(solution)/shard_map/pallas_call | solution.py:62
  35.4 10.9 %fusion.17 = f32[1024,256]{1,0:T(8,128)S(1)} fusion(bf16[1024,256]{1,0:T(8,128)(2,1)S(1)} %copy-done, bf16[1024,256]{1,0:T(8,128)(2,1)} %bitcast.75, bf16[256,1024]{1,0:T(8,128)(2,1)S(1)} %copy-done.6, f32[1024]{0:T(1024)S(1)} %copy-done.7, bf16[1024,256]{1,0:T(8,128)(2,1)S(1)} %bitcast.74, f32[256]{0:T(256)S(1)} %copy-done.8, f32[256]{0:T(256)S(1)} %copy-done.9), kind=kOutput, calls=%fused_computation.28 | convolution fusion | flops 1144520704 | bytes 3151872 | tf_op jit(solution)/shard_map/dot_general | solution.py:106
  46.5 0.7 %broadcast_in_dim.4 = bf16[16,16,256]{2,1,0:T(8,128)(2,1)} broadcast(bf16[16,256]{1,0:T(8,128)(2,1)S(1)} %convert_element_type.61), dimensions={1,2} | broadcast | bytes 139264 | tf_op jit(solution)/shard_map/broadcast_in_dim | solution.py:157
  47.1 6.7 %all-to-all-start = ((bf16[16,16,256]{2,1,0:T(8,128)(2,1)}), bf16[16,16,256]{2,1,0:T(8,128)(2,1)S(1)}, u32[]{:S(2)}, u32[]{:S(2)}) async-start(bf16[16,16,256]{2,1,0:T(8,128)(2,1)} %broadcast_in_dim.4), calls=%async_computation | async-start | bytes 262144 | tf_op jit(solution)/shard_map/all_to_all | solution.py:160
  53.9 0.1 convolution_convert_fusion.2
  54.1 5.9 %all-to-all-done = bf16[16,16,256]{2,1,0:T(8,128)(2,1)S(1)} async-done(((bf16[16,16,256]{2,1,0:T(8,128)(2,1)}), bf16[16,16,256]{2,1,0:T(8,128)(2,1)S(1)}, u32[]{:S(2)}, u32[]{:S(2)}) %all-to-all-start) | async-done | bytes 131104 | tf_op jit(solution)/shard_map/all_to_all | solution.py:160
  60.2 0.2 convolution_convert_fusion
  60.6 0.1 fusion.20
  60.7 0.2 fusion.62
  61.0 0.3 fusion.21
  61.4 0.1 fusion.24
  61.6 0.1 broadcast_in_dim.5
  61.7 1.0 %add_convert_fusion = bf16[32,32,256]{2,1,0:T(8,128)(2,1)} fusion(f32[32,32,256]{2,1,0:T(8,128)S(1)} %bitcast.72, f32[32,32,256]{2,1,0:T(8,128)S(1)} %bitcast.73), kind=kLoop, calls=%fused_computation.37 | loop fusion | flops 524288 | bytes 2621440 | tf_op jit(solution)/shard_map/convert_element_type | solution.py:200
  (42 shorter events, 1.0 us)
Async XLA Ops:
  0.0 35.4 %copy-start = (bf16[1024,256]{1,0:T(8,128)(2,1)S(1)}, bf16[1024,256]{1,0:T(8,128)(2,1)}, u32[]{:S(2)}) copy-start(bf16[1024,256]{1,0:T(8,128)(2,1)} %param.21) | copy-start | bytes 1572868
  0.0 13.7 %copy-start.1 = (bf16[32,32,256]{2,1,0:T(8,128)(2,1)S(1)}, bf16[32,32,256]{2,1,0:T(8,128)(2,1)}, u32[]{:S(2)}) copy-start(bf16[32,32,256]{2,1,0:T(8,128)(2,1)} %param.14) | copy-start | bytes 1572868
  0.9 12.9 %collective-permute-start.1 = (bf16[3,32,256]{2,1,0:T(8,128)(2,1)S(1)}, bf16[3,32,256]{2,1,0:T(8,128)(2,1)S(1)}, u32[]{:S(2)}, u32[]{:S(2)}) collective-permute-start(bf16[3,32,256]{2,1,0:T(8,128)(2,1)S(1)} %get-tuple-element.7), channel_id=1, source_target_pairs={{16,0},{32,16},{48,32},{64,48},{80,64},{96,80},{112,96},{128,112},... | collective-permute-start | bytes 147464 | tf_op jit(solution)/shard_map/ppermute | solution.py:19
  5.3 8.4 %collective-permute-start = (bf16[3,32,256]{2,1,0:T(8,128)(2,1)S(1)}, bf16[3,32,256]{2,1,0:T(8,128)(2,1)S(1)}, u32[]{:S(2)}, u32[]{:S(2)}) collective-permute-start(bf16[3,32,256]{2,1,0:T(8,128)(2,1)S(1)} %get-tuple-element.8), channel_id=1, source_target_pairs={{0,16},{16,32},{32,48},{48,64},{64,80},{80,96},{96,112},{112,128},... | collective-permute-start | bytes 147464 | tf_op jit(solution)/shard_map/ppermute | solution.py:18
  9.2 10.9 %copy-start.5 = (bf16[7,7,256]{2,1,0:T(8,128)(2,1)S(1)}, bf16[7,7,256]{2,1,0:T(8,128)(2,1)}, u32[]{:S(2)}) copy-start(bf16[7,7,256]{2,1,0:T(8,128)(2,1)} %param.15) | copy-start | bytes 75268
  13.9 7.2 %collective-permute-start.2 = (bf16[38,3,256]{2,1,0:T(4,128)(2,1)S(1)}, bf16[38,3,256]{2,1,0:T(4,128)(2,1)S(1)}, u32[]{:S(2)}, u32[]{:S(2)}) collective-permute-start(bf16[38,3,256]{2,1,0:T(4,128)(2,1)S(1)} %get-tuple-element.5), channel_id=1, source_target_pairs={{0,1},{1,2},{2,3},{3,4},{4,5},{5,6},{6,7},{7,8},{8,9},{9,10},{10,1... | collective-permute-start | bytes 175112 | tf_op jit(solution)/shard_map/ppermute | solution.py:18
  18.2 5.7 %collective-permute-start.3 = (bf16[38,3,256]{2,1,0:T(4,128)(2,1)S(1)}, bf16[38,3,256]{2,1,0:T(4,128)(2,1)S(1)}, u32[]{:S(2)}, u32[]{:S(2)}) collective-permute-start(bf16[38,3,256]{2,1,0:T(4,128)(2,1)S(1)} %get-tuple-element.6), channel_id=1, source_target_pairs={{1,0},{2,1},{3,2},{4,3},{5,4},{6,5},{7,6},{8,7},{9,8},{10,9},{11,1... | collective-permute-start | bytes 175112 | tf_op jit(solution)/shard_map/ppermute | solution.py:19
  25.2 10.2 %copy-start.6 = (bf16[256,1024]{1,0:T(8,128)(2,1)S(1)}, bf16[256,1024]{1,0:T(8,128)(2,1)}, u32[]{:S(2)}) copy-start(bf16[256,1024]{1,0:T(8,128)(2,1)} %param.19) | copy-start | bytes 1572868
  25.2 10.2 %copy-start.7 = (f32[1024]{0:T(1024)S(1)}, f32[1024]{0:T(1024)}, u32[]{:S(2)}) copy-start(f32[1024]{0:T(1024)} %param.20) | copy-start | bytes 12292
  25.2 10.2 %copy-start.8 = (f32[256]{0:T(256)S(1)}, f32[256]{0:T(256)}, u32[]{:S(2)}) copy-start(f32[256]{0:T(256)} %param.22) | copy-start | bytes 3076
  25.2 10.2 %copy-start.9 = (f32[256]{0:T(256)S(1)}, f32[256]{0:T(256)}, u32[]{:S(2)}) copy-start(f32[256]{0:T(256)} %param.23) | copy-start | bytes 3076
  46.3 7.6 %copy-start.3 = (bf16[256,256]{1,0:T(8,128)(2,1)S(1)}, bf16[256,256]{1,0:T(8,128)(2,1)}, u32[]{:S(2)}) copy-start(bf16[256,256]{1,0:T(8,128)(2,1)} %param.24) | copy-start | bytes 393220
  46.3 13.9 %copy-start.2 = (bf16[256,512]{1,0:T(8,128)(2,1)S(1)}, bf16[256,512]{1,0:T(8,128)(2,1)}, u32[]{:S(2)}) copy-start(bf16[256,512]{1,0:T(8,128)(2,1)} %param.25) | copy-start | bytes 786436
  47.1 12.9 %all-to-all-start = ((bf16[16,16,256]{2,1,0:T(8,128)(2,1)}), bf16[16,16,256]{2,1,0:T(8,128)(2,1)S(1)}, u32[]{:S(2)}, u32[]{:S(2)}) async-start(bf16[16,16,256]{2,1,0:T(8,128)(2,1)} %broadcast_in_dim.4), calls=%async_computation | async-start | bytes 262144 | tf_op jit(solution)/shard_map/all_to_all | solution.py:160
  60.5 1.0 %copy-start.4 = (bf16[256,256]{1,0:T(8,128)(2,1)S(1)}, bf16[256,256]{1,0:T(8,128)(2,1)}, u32[]{:S(2)}) copy-start(bf16[256,256]{1,0:T(8,128)(2,1)} %param.27) | copy-start | bytes 393220

commit v3 on v2

--- a/solution.py
+++ b/solution.py
@@ -154,22 +154,34 @@
     position = lax.axis_index("col")
     span_cols = region_side * columns
     key_count = local_count * columns
-    sent = jnp.broadcast_to(pooled[None], (columns, local_count, channels)).reshape(
-        columns * local_count, channels
-    )
-    band_pooled = lax.all_to_all(sent, "col", 0, 0, tiled=True)
-    band_pooled = (
-        band_pooled.reshape(columns, region_side, region_side, channels)
-        .transpose(1, 0, 2, 3)
-        .reshape(key_count, channels)
-    )
+    block = pooled[None]
+    bits = []
+    distance = columns // 2
+    while distance >= 1:
+        pairs = [(i, i ^ distance) for i in range(columns)]
+        theirs = lax.ppermute(block, "col", pairs)
+        upper = (position & distance) != 0
+        block = jnp.where(
+            upper,
+            jnp.concatenate([theirs, block], axis=0),
+            jnp.concatenate([block, theirs], axis=0),
+        )
+        bits.append(distance)
+        distance //= 2
+    steps = len(bits)
+    band_pooled = block.reshape((2,) * steps + (region_side, region_side, channels))
+    order = (steps,) + tuple(range(steps - 1, -1, -1)) + (steps + 1, steps + 2)
+    band_pooled = band_pooled.transpose(order).reshape(key_count, channels)
     band_keyval = jnp.dot(band_pooled, w_keyval, preferred_element_type=jnp.float32).astype(
         jnp.bfloat16
     )
-    windows = []
-    for query_col in range(region_side):
-        first = span_cols - 1 - (position * region_side + query_col)
-        windows.append(lax.dynamic_slice_in_dim(rel_bias, first, span_cols, axis=2))
+    window_all = lax.dynamic_slice_in_dim(
+        rel_bias, span_cols - region_side - position * region_side, span_cols + region_side - 1, axis=2
+    )
+    windows = [
+        window_all[:, :, region_side - 1 - query_col : region_side - 1 - query_col + span_cols]
+        for query_col in range(region_side)
+    ]
     rows_of = []
     for query_row in range(region_side):
         per_col = [

time: 63.2 us -> 64 us (1.013)
  the two profiles are of different devices: /device:TPU:129 before, /device:TPU:113 now
where the time goes in v3:
time: 64 us; the launch traced here: 63.3 us
  starting transfers between devices  21.5 us (34%)
  waiting for transfers between devices  12.9 us (20%)
  matrix products  11.8 us (18%)
  Pallas kernels  10.2 us (16%)
  local copies, waits for them, and re-layouts  3.86 us (6%)
  other arithmetic  2.67 us (4%)
    dot_general x1, matrix products, block_pass(): jnp.dot(hidden, w_reduce, preferred_element_type=jnp.float32) + b_reduce  10.9 us
    ppermute x2, starting transfers between devices, padded_2(): before = lax.ppermute(last, axis, up)  10.3 us
    pallas_call x1, Pallas kernels, conv_norm(): pl.pallas_call(conv_norm_kernel, out_shape=jax.ShapeDtypeStruct((tile_row...  10.2 us
    ppermute x2, waiting for transfers between devices, padded_2(): after = lax.ppermute(leading, axis, down)  8.04 us
    ppermute x4, starting transfers between devices, shards(): theirs = lax.ppermute(block, 'col', pairs)  7.01 us
    ppermute x4, waiting for transfers between devices, shards(): theirs = lax.ppermute(block, 'col', pairs)  4.88 us
    ppermute x2, starting transfers between devices, padded_2(): after = lax.ppermute(leading, axis, down)  4.18 us
    concatenate x1, other arithmetic, padded_2(): array = jnp.concatenate([before, array, after], axis=dim)  1.34 us
  transfers between devices with their start and end apart: 8, of which 6 were waited for; matrix products, arithmetic and copies ran while one was open for 4% of the time, Pallas kernels for 0%

profile of v3, /device:TPU:113, one launch (start us, length us, event | category | flops | bytes accessed | tf_op | source)
XLA Modules:
  0.0 63.3 jit_solution(8121746833476799101)
XLA Ops:
  0.0 0.9 %fusion.60 = (bf16[3,32,256]{2,1,0:T(8,128)(2,1)S(1)}, bf16[3,32,256]{2,1,0:T(8,128)(2,1)S(1)}) fusion(bf16[32,32,256]{2,1,0:T(8,128)(2,1)} %param.14), kind=kLoop, calls=%fused_computation.106 | loop fusion | bytes 196608 | tf_op jit(solution)/shard_map/slice | solution.py:17
  0.9 4.5 %collective-permute-start = (bf16[3,32,256]{2,1,0:T(8,128)(2,1)S(1)}, bf16[3,32,256]{2,1,0:T(8,128)(2,1)S(1)}, u32[]{:S(2)}, u32[]{:S(2)}) collective-permute-start(bf16[3,32,256]{2,1,0:T(8,128)(2,1)S(1)} %get-tuple-element.8), channel_id=1, source_target_pairs={{0,16},{16,32},{32,48},{48,64},{64,80},{80,96},{96,112},{112,128},... | collective-permute-start | bytes 147464 | tf_op jit(solution)/shard_map/ppermute | solution.py:18
  5.4 2.3 %collective-permute-start.1 = (bf16[3,32,256]{2,1,0:T(8,128)(2,1)S(1)}, bf16[3,32,256]{2,1,0:T(8,128)(2,1)S(1)}, u32[]{:S(2)}, u32[]{:S(2)}) collective-permute-start(bf16[3,32,256]{2,1,0:T(8,128)(2,1)S(1)} %get-tuple-element.7), channel_id=1, source_target_pairs={{16,0},{32,16},{48,32},{64,48},{80,64},{96,80},{112,96},{128,112},... | collective-permute-start | bytes 147464 | tf_op jit(solution)/shard_map/ppermute | solution.py:19
  7.7 1.1 %constant_dynamic-update-slice_fusion.1 = bf16[38,32,256]{2,1,0:T(8,128)(2,1)S(1)} fusion(bf16[38,32,256]{2,1,0:T(8,128)(2,1)S(1)} %constant_dynamic-update-slice_fusion.2, bf16[32,32,256]{2,1,0:T(8,128)(2,1)} %param.14), kind=kLoop, calls=%fused_computation.72 | loop fusion | bytes 1048576
  8.8 5.1 %collective-permute-done.1 = bf16[3,32,256]{2,1,0:T(8,128)(2,1)S(1)} collective-permute-done((bf16[3,32,256]{2,1,0:T(8,128)(2,1)S(1)}, bf16[3,32,256]{2,1,0:T(8,128)(2,1)S(1)}, u32[]{:S(2)}, u32[]{:S(2)}) %collective-permute-start.1) | collective-permute-done | bytes 49184 | tf_op jit(solution)/shard_map/ppermute | solution.py:19
  14.0 5.8 %collective-permute-start.2 = (bf16[38,3,256]{2,1,0:T(4,128)(2,1)S(1)}, bf16[38,3,256]{2,1,0:T(4,128)(2,1)S(1)}, u32[]{:S(2)}, u32[]{:S(2)}) collective-permute-start(bf16[38,3,256]{2,1,0:T(4,128)(2,1)S(1)} %get-tuple-element.5), channel_id=1, source_target_pairs={{0,1},{1,2},{2,3},{3,4},{4,5},{5,6},{6,7},{7,8},{8,9},{9,10},{10,1... | collective-permute-start | bytes 175112 | tf_op jit(solution)/shard_map/ppermute | solution.py:18
  19.8 1.9 %collective-permute-start.3 = (bf16[38,3,256]{2,1,0:T(4,128)(2,1)S(1)}, bf16[38,3,256]{2,1,0:T(4,128)(2,1)S(1)}, u32[]{:S(2)}, u32[]{:S(2)}) collective-permute-start(bf16[38,3,256]{2,1,0:T(4,128)(2,1)S(1)} %get-tuple-element.6), channel_id=1, source_target_pairs={{1,0},{2,1},{3,2},{4,3},{5,4},{6,5},{7,6},{8,7},{9,8},{10,9},{11,1... | collective-permute-start | bytes 175112 | tf_op jit(solution)/shard_map/ppermute | solution.py:19
  21.9 0.6 reshape.111.k_ref
  22.5 3.0 %collective-permute-done.3 = bf16[38,3,256]{2,1,0:T(4,128)(2,1)S(1)} collective-permute-done((bf16[38,3,256]{2,1,0:T(4,128)(2,1)S(1)}, bf16[38,3,256]{2,1,0:T(4,128)(2,1)S(1)}, u32[]{:S(2)}, u32[]{:S(2)}) %collective-permute-start.3) | collective-permute-done | bytes 58400 | tf_op jit(solution)/shard_map/ppermute | solution.py:19
  25.5 1.3 %fusion.23.x_ref = bf16[38,40,256]{2,1,0:T(8,128)(2,1)} fusion(bf16[38,3,256]{2,1,0:T(4,128)(2,1)S(1)} %collective-permute-done.3, bf16[38,32,256]{2,1,0:T(8,128)(2,1)S(1)} %constant_dynamic-update-slice_fusion, bf16[38,3,256]{2,1,0:T(4,128)(2,1)S(1)} %collective-permute-done.2), kind=kLoop, calls=%fused_computation.39 | loop fusion | flops 3891200 | bytes 1517568 | tf_op jit(solution)/shard_map/concatenate | solution.py:20
  26.8 10.2 %shard_map.136 = bf16[32,32,256]{2,1,0:T(8,128)(2,1)} custom-call(bf16[38,40,256]{2,1,0:T(8,128)(2,1)} %fusion.23.x_ref, f32[49,256]{1,0:T(8,128)} %reshape.111.k_ref, f32[1,256]{1,0:T(1,128)} %bitcast.77, f32[1,256]{1,0:T(1,128)} %bitcast.78, f32[1,256]{1,0:T(1,128)} %bitcast.79), custom_call_target="tpu_custom_call" | custom-call | flops 25690112 | bytes 1302528 | tf_op jit(solution)/shard_map/pallas_call | solution.py:62
  37.1 10.9 %fusion.17 = f32[1024,256]{1,0:T(8,128)S(1)} fusion(bf16[1024,256]{1,0:T(8,128)(2,1)S(1)} %copy-done, bf16[1024,256]{1,0:T(8,128)(2,1)} %bitcast.73, bf16[256,1024]{1,0:T(8,128)(2,1)S(1)} %copy-done.7, f32[1024]{0:T(1024)S(1)} %copy-done.8, bf16[1024,256]{1,0:T(8,128)(2,1)S(1)} %bitcast.72, f32[256]{0:T(256)S(1)} %copy-done.9, f32[256]{0:T(256)S(1)} %copy-done.10), kind=kOutput, calls=%fused_computation.28 | convolution fusion | flops 1144520704 | bytes 3151872 | tf_op jit(solution)/shard_map/dot_general | solution.py:106
  48.1 2.8 %collective-permute-start.4 = (bf16[1,16,256]{2,1,0:T(8,128)(2,1)S(1)}, bf16[1,16,256]{2,1,0:T(8,128)(2,1)S(1)}, u32[]{:S(2)}, u32[]{:S(2)}) collective-permute-start(bf16[1,16,256]{2,1,0:T(8,128)(2,1)S(1)} %convert_element_type.67), channel_id=1, source_target_pairs={{0,8},{1,9},{2,10},{3,11},{4,12},{5,13},{6,14},{7,15},{8,0},{9,1},... | collective-permute-start | bytes 24584 | tf_op jit(solution)/shard_map/ppermute | solution.py:162
  50.9 1.2 %collective-permute-done.4 = bf16[1,16,256]{2,1,0:T(8,128)(2,1)S(1)} collective-permute-done((bf16[1,16,256]{2,1,0:T(8,128)(2,1)S(1)}, bf16[1,16,256]{2,1,0:T(8,128)(2,1)S(1)}, u32[]{:S(2)}, u32[]{:S(2)}) %collective-permute-start.4) | collective-permute-done | bytes 8224 | tf_op jit(solution)/shard_map/ppermute | solution.py:162
  52.2 1.2 %collective-permute-start.5 = (bf16[2,16,256]{2,1,0:T(8,128)(2,1)S(1)}, bf16[2,16,256]{2,1,0:T(8,128)(2,1)S(1)}, u32[]{:S(2)}, u32[]{:S(2)}) collective-permute-start(bf16[2,16,256]{2,1,0:T(8,128)(2,1)S(1)} %maximum_select_fusion.3), channel_id=1, source_target_pairs={{0,4},{1,5},{2,6},{3,7},{4,0},{5,1},{6,2},{7,3},{8,12},{9,13},{10,... | collective-permute-start | bytes 49160 | tf_op jit(solution)/shard_map/ppermute | solution.py:162
  53.4 1.7 %collective-permute-done.5 = bf16[2,16,256]{2,1,0:T(8,128)(2,1)S(1)} collective-permute-done((bf16[2,16,256]{2,1,0:T(8,128)(2,1)S(1)}, bf16[2,16,256]{2,1,0:T(8,128)(2,1)S(1)}, u32[]{:S(2)}, u32[]{:S(2)}) %collective-permute-start.5) | collective-permute-done | bytes 16416 | tf_op jit(solution)/shard_map/ppermute | solution.py:162
  55.1 1.2 %collective-permute-start.6 = (bf16[4,16,256]{2,1,0:T(8,128)(2,1)S(1)}, bf16[4,16,256]{2,1,0:T(8,128)(2,1)S(1)}, u32[]{:S(2)}, u32[]{:S(2)}) collective-permute-start(bf16[4,16,256]{2,1,0:T(8,128)(2,1)S(1)} %maximum_select_fusion.2), channel_id=1, source_target_pairs={{0,2},{1,3},{2,0},{3,1},{4,6},{5,7},{6,4},{7,5},{8,10},{9,11},{10,... | collective-permute-start | bytes 98312 | tf_op jit(solution)/shard_map/ppermute | solution.py:162
  56.4 0.2 reshape.105
  56.6 1.3 %collective-permute-done.6 = bf16[4,16,256]{2,1,0:T(8,128)(2,1)S(1)} collective-permute-done((bf16[4,16,256]{2,1,0:T(8,128)(2,1)S(1)}, bf16[4,16,256]{2,1,0:T(8,128)(2,1)S(1)}, u32[]{:S(2)}, u32[]{:S(2)}) %collective-permute-start.6) | collective-permute-done | bytes 32800 | tf_op jit(solution)/shard_map/ppermute | solution.py:162
  57.9 1.8 %collective-permute-start.7 = (bf16[8,16,256]{2,1,0:T(8,128)(2,1)S(1)}, bf16[8,16,256]{2,1,0:T(8,128)(2,1)S(1)}, u32[]{:S(2)}, u32[]{:S(2)}) collective-permute-start(bf16[8,16,256]{2,1,0:T(8,128)(2,1)S(1)} %maximum_select_fusion.1), channel_id=1, source_target_pairs={{0,1},{1,0},{2,3},{3,2},{4,5},{5,4},{6,7},{7,6},{8,9},{9,8},{10,11... | collective-permute-start | bytes 196616 | tf_op jit(solution)/shard_map/ppermute | solution.py:162
  60.0 0.7 %collective-permute-done.7 = bf16[8,16,256]{2,1,0:T(8,128)(2,1)S(1)} collective-permute-done((bf16[8,16,256]{2,1,0:T(8,128)(2,1)S(1)}, bf16[8,16,256]{2,1,0:T(8,128)(2,1)S(1)}, u32[]{:S(2)}, u32[]{:S(2)}) %collective-permute-start.7) | collective-permute-done | bytes 65568 | tf_op jit(solution)/shard_map/ppermute | solution.py:162
  60.8 0.2 convolution_convert_fusion
  61.6 0.3 fusion.21
  62.3 1.0 %add_convert_fusion = bf16[32,32,256]{2,1,0:T(8,128)(2,1)} fusion(f32[32,32,256]{2,1,0:T(8,128)S(1)} %bitcast.70, f32[32,32,256]{2,1,0:T(8,128)S(1)} %bitcast.71), kind=kLoop, calls=%fused_computation.37 | loop fusion | flops 524288 | bytes 2621440 | tf_op jit(solution)/shard_map/convert_element_type | solution.py:212
  (54 shorter events, 1.8 us)
Async XLA Ops:
  0.0 37.0 %copy-start = (bf16[1024,256]{1,0:T(8,128)(2,1)S(1)}, bf16[1024,256]{1,0:T(8,128)(2,1)}, u32[]{:S(2)}) copy-start(bf16[1024,256]{1,0:T(8,128)(2,1)} %param.21) | copy-start | bytes 1572868
  0.0 21.7 %copy-start.1 = (f32[8,7,127]{2,0,1:T(8,128)S(1)}, f32[8,7,127]{2,0,1:T(8,128)}, u32[]{:S(2)}) copy-start(f32[8,7,127]{2,0,1:T(8,128)} %param.26) | copy-start | bytes 85348
  0.9 6.8 %collective-permute-start = (bf16[3,32,256]{2,1,0:T(8,128)(2,1)S(1)}, bf16[3,32,256]{2,1,0:T(8,128)(2,1)S(1)}, u32[]{:S(2)}, u32[]{:S(2)}) collective-permute-start(bf16[3,32,256]{2,1,0:T(8,128)(2,1)S(1)} %get-tuple-element.8), channel_id=1, source_target_pairs={{0,16},{16,32},{32,48},{48,64},{64,80},{80,96},{96,112},{112,128},... | collective-permute-start | bytes 147464 | tf_op jit(solution)/shard_map/ppermute | solution.py:18
  5.4 8.4 %collective-permute-start.1 = (bf16[3,32,256]{2,1,0:T(8,128)(2,1)S(1)}, bf16[3,32,256]{2,1,0:T(8,128)(2,1)S(1)}, u32[]{:S(2)}, u32[]{:S(2)}) collective-permute-start(bf16[3,32,256]{2,1,0:T(8,128)(2,1)S(1)} %get-tuple-element.7), channel_id=1, source_target_pairs={{16,0},{32,16},{48,32},{64,48},{80,64},{96,80},{112,96},{128,112},... | collective-permute-start | bytes 147464 | tf_op jit(solution)/shard_map/ppermute | solution.py:19
  7.7 14.2 %copy-start.6 = (bf16[7,7,256]{2,1,0:T(8,128)(2,1)S(1)}, bf16[7,7,256]{2,1,0:T(8,128)(2,1)}, u32[]{:S(2)}) copy-start(bf16[7,7,256]{2,1,0:T(8,128)(2,1)} %param.15) | copy-start | bytes 75268
  14.0 8.5 %collective-permute-start.2 = (bf16[38,3,256]{2,1,0:T(4,128)(2,1)S(1)}, bf16[38,3,256]{2,1,0:T(4,128)(2,1)S(1)}, u32[]{:S(2)}, u32[]{:S(2)}) collective-permute-start(bf16[38,3,256]{2,1,0:T(4,128)(2,1)S(1)} %get-tuple-element.5), channel_id=1, source_target_pairs={{0,1},{1,2},{2,3},{3,4},{4,5},{5,6},{6,7},{7,8},{8,9},{9,10},{10,1... | collective-permute-start | bytes 175112 | tf_op jit(solution)/shard_map/ppermute | solution.py:18
  19.8 5.7 %collective-permute-start.3 = (bf16[38,3,256]{2,1,0:T(4,128)(2,1)S(1)}, bf16[38,3,256]{2,1,0:T(4,128)(2,1)S(1)}, u32[]{:S(2)}, u32[]{:S(2)}) collective-permute-start(bf16[38,3,256]{2,1,0:T(4,128)(2,1)S(1)} %get-tuple-element.6), channel_id=1, source_target_pairs={{1,0},{2,1},{3,2},{4,3},{5,4},{6,5},{7,6},{8,7},{9,8},{10,9},{11,1... | collective-permute-start | bytes 175112 | tf_op jit(solution)/shard_map/ppermute | solution.py:19
  26.8 10.2 %copy-start.2 = (bf16[32,32,256]{2,1,0:T(8,128)(2,1)S(1)}, bf16[32,32,256]{2,1,0:T(8,128)(2,1)}, u32[]{:S(2)}) copy-start(bf16[32,32,256]{2,1,0:T(8,128)(2,1)} %param.14) | copy-start | bytes 1572868
  26.8 10.2 %copy-start.7 = (bf16[256,1024]{1,0:T(8,128)(2,1)S(1)}, bf16[256,1024]{1,0:T(8,128)(2,1)}, u32[]{:S(2)}) copy-start(bf16[256,1024]{1,0:T(8,128)(2,1)} %param.19) | copy-start | bytes 1572868
  26.8 10.2 %copy-start.8 = (f32[1024]{0:T(1024)S(1)}, f32[1024]{0:T(1024)}, u32[]{:S(2)}) copy-start(f32[1024]{0:T(1024)} %param.20) | copy-start | bytes 12292
  26.8 10.2 %copy-start.9 = (f32[256]{0:T(256)S(1)}, f32[256]{0:T(256)}, u32[]{:S(2)}) copy-start(f32[256]{0:T(256)} %param.22) | copy-start | bytes 3076
  26.8 10.2 %copy-start.10 = (f32[256]{0:T(256)S(1)}, f32[256]{0:T(256)}, u32[]{:S(2)}) copy-start(f32[256]{0:T(256)} %param.23) | copy-start | bytes 3076
  48.1 4.1 %collective-permute-start.4 = (bf16[1,16,256]{2,1,0:T(8,128)(2,1)S(1)}, bf16[1,16,256]{2,1,0:T(8,128)(2,1)S(1)}, u32[]{:S(2)}, u32[]{:S(2)}) collective-permute-start(bf16[1,16,256]{2,1,0:T(8,128)(2,1)S(1)} %convert_element_type.67), channel_id=1, source_target_pairs={{0,8},{1,9},{2,10},{3,11},{4,12},{5,13},{6,14},{7,15},{8,0},{9,1},... | collective-permute-start | bytes 24584 | tf_op jit(solution)/shard_map/ppermute | solution.py:162
  50.9 8.8 %copy-start.4 = (bf16[256,256]{1,0:T(8,128)(2,1)S(1)}, bf16[256,256]{1,0:T(8,128)(2,1)}, u32[]{:S(2)}) copy-start(bf16[256,256]{1,0:T(8,128)(2,1)} %param.24) | copy-start | bytes 393220
  52.2 2.9 %collective-permute-start.5 = (bf16[2,16,256]{2,1,0:T(8,128)(2,1)S(1)}, bf16[2,16,256]{2,1,0:T(8,128)(2,1)S(1)}, u32[]{:S(2)}, u32[]{:S(2)}) collective-permute-start(bf16[2,16,256]{2,1,0:T(8,128)(2,1)S(1)} %maximum_select_fusion.3), channel_id=1, source_target_pairs={{0,4},{1,5},{2,6},{3,7},{4,0},{5,1},{6,2},{7,3},{8,12},{9,13},{10,... | collective-permute-start | bytes 49160 | tf_op jit(solution)/shard_map/ppermute | solution.py:162
  55.1 2.8 %collective-permute-start.6 = (bf16[4,16,256]{2,1,0:T(8,128)(2,1)S(1)}, bf16[4,16,256]{2,1,0:T(8,128)(2,1)S(1)}, u32[]{:S(2)}, u32[]{:S(2)}) collective-permute-start(bf16[4,16,256]{2,1,0:T(8,128)(2,1)S(1)} %maximum_select_fusion.2), channel_id=1, source_target_pairs={{0,2},{1,3},{2,0},{3,1},{4,6},{5,7},{6,4},{7,5},{8,10},{9,11},{10,... | collective-permute-start | bytes 98312 | tf_op jit(solution)/shard_map/ppermute | solution.py:162
  56.3 4.5 %copy-start.3 = (bf16[256,512]{1,0:T(8,128)(2,1)S(1)}, bf16[256,512]{1,0:T(8,128)(2,1)}, u32[]{:S(2)}) copy-start(bf16[256,512]{1,0:T(8,128)(2,1)} %param.25) | copy-start | bytes 786436
  57.9 2.7 %collective-permute-start.7 = (bf16[8,16,256]{2,1,0:T(8,128)(2,1)S(1)}, bf16[8,16,256]{2,1,0:T(8,128)(2,1)S(1)}, u32[]{:S(2)}, u32[]{:S(2)}) collective-permute-start(bf16[8,16,256]{2,1,0:T(8,128)(2,1)S(1)} %maximum_select_fusion.1), channel_id=1, source_target_pairs={{0,1},{1,0},{2,3},{3,2},{4,5},{5,4},{6,7},{7,6},{8,9},{9,8},{10,11... | collective-permute-start | bytes 196616 | tf_op jit(solution)/shard_map/ppermute | solution.py:162
  61.1 1.0 %copy-start.5 = (bf16[256,256]{1,0:T(8,128)(2,1)S(1)}, bf16[256,256]{1,0:T(8,128)(2,1)}, u32[]{:S(2)}) copy-start(bf16[256,256]{1,0:T(8,128)(2,1)} %param.27) | copy-start | bytes 393220

commit v4 on v2

--- a/solution.py
+++ b/solution.py
@@ -82,6 +82,83 @@
     )
 
 
+ERFC_COEFFS = (
+    -1.26551223,
+    1.00002368,
+    0.37409196,
+    0.09678418,
+    -0.18628806,
+    0.27886807,
+    -1.13520398,
+    1.48851587,
+    -0.82215223,
+    0.17087277,
+)
+PIXEL_BLOCK = 256
+HIDDEN_BLOCK = 256
+
+
+def gelu_exact(pre):
+    z = jnp.abs(pre) * jnp.float32(0.7071067811865476)
+    t = 1.0 / (1.0 + 0.5 * z)
+    poly = jnp.float32(ERFC_COEFFS[-1])
+    for coeff in ERFC_COEFFS[-2::-1]:
+        poly = poly * t + jnp.float32(coeff)
+    tail = t * jnp.exp(poly - z * z)
+    one_plus_erf = jnp.where(pre >= 0, 2.0 - tail, tail)
+    return 0.5 * pre * one_plus_erf
+
+
+def mlp_kernel(n_ref, f_ref, we_ref, be_ref, wr_ref, br_ref, ls_ref, o_ref):
+    normed = n_ref[...]
+    hidden_total = we_ref.shape[1]
+    acc = jnp.zeros(o_ref.shape, jnp.float32)
+    for h0 in range(0, hidden_total, HIDDEN_BLOCK):
+        pre = (
+            jnp.dot(normed, we_ref[:, h0 : h0 + HIDDEN_BLOCK], preferred_element_type=jnp.float32)
+            + be_ref[:, h0 : h0 + HIDDEN_BLOCK]
+        )
+        hidden = gelu_exact(pre).astype(jnp.bfloat16)
+        acc = acc + jnp.dot(hidden, wr_ref[h0 : h0 + HIDDEN_BLOCK, :], preferred_element_type=jnp.float32)
+    reduced = acc + br_ref[...]
+    o_ref[...] = (f_ref[...].astype(jnp.float32) + ls_ref[...] * reduced).astype(o_ref.dtype)
+
+
+def mlp(normed, features, w_expand, b_expand, w_reduce, b_reduce, layer_scale):
+    pixels, channels = normed.shape
+    hidden_total = w_expand.shape[1]
+    rows = pl.BlockSpec((PIXEL_BLOCK, channels), lambda i: (i, 0))
+    whole = lambda shape: pl.BlockSpec(shape, lambda i: (0, 0))
+    return pl.pallas_call(
+        mlp_kernel,
+        out_shape=jax.ShapeDtypeStruct((pixels, channels), jnp.bfloat16),
+        grid=(pixels // PIXEL_BLOCK,),
+        in_specs=[
+            rows,
+            rows,
+            whole((channels, hidden_total)),
+            whole((1, hidden_total)),
+            whole((hidden_total, channels)),
+            whole((1, channels)),
+            whole((1, channels)),
+        ],
+        out_specs=rows,
+        cost_estimate=pl.CostEstimate(
+            flops=4 * pixels * channels * hidden_total,
+            bytes_accessed=2 * (3 * pixels * channels + 2 * channels * hidden_total),
+            transcendentals=2 * pixels * hidden_total,
+        ),
+    )(
+        normed,
+        features,
+        w_expand,
+        b_expand.reshape(1, hidden_total),
+        w_reduce,
+        b_reduce.reshape(1, channels),
+        layer_scale.reshape(1, channels),
+    )
+
+
 def block_pass(
     padded,
     features,
@@ -100,12 +177,16 @@
     normed = conv_norm(
         padded, dw_kernel, dw_bias, norm_gain, norm_bias, tile_rows, tile_cols
     ).reshape(-1, channels)
-    hidden = jax.nn.gelu(
-        jnp.dot(normed, w_expand, preferred_element_type=jnp.float32) + b_expand, approximate=False
-    ).astype(jnp.bfloat16)
-    reduced = jnp.dot(hidden, w_reduce, preferred_element_type=jnp.float32) + b_reduce
-    summed = features.astype(jnp.float32).reshape(-1, channels) + layer_scale * reduced
-    return summed.astype(jnp.bfloat16).reshape(tile_rows, tile_cols, channels)
+    summed = mlp(
+        normed,
+        features.reshape(-1, channels),
+        w_expand,
+        b_expand,
+        w_reduce,
+        b_reduce,
+        layer_scale,
+    )
+    return summed.reshape(tile_rows, tile_cols, channels)
 
 
 def shards(

time: 63.2 us -> 61.4 us (0.972)
  matrix products: 11.8 us -> 0.93 us
  Pallas kernels: 10.2 us -> 18.2 us
  other arithmetic: 2.63 us -> 3.74 us
    dot_general x1 -> x0, matrix products: 10.9 us -> none  [block_pass(): jnp.dot(hidden, w_reduce, preferred_element_type=jnp.float32) + b_reduce]
    pallas_call x0 -> x1, Pallas kernels: none -> 8.13 us  [mlp(): pl.pallas_call(mlp_kernel, out_shape=jax.ShapeDtypeStruct((pixels, channe...]
    convert_element_type x1 -> x2, other arithmetic: 0.96 us -> 2.07 us  [shards(): return (block_out.astype(jnp.float32) + spread).astype(jnp.bfloat16)]
where the time goes in v4:
time: 61.4 us; the launch traced here: 60.9 us
  starting transfers between devices  19.7 us (32%)
  Pallas kernels  18.2 us (30%)
  waiting for transfers between devices  13.3 us (22%)
  local copies, waits for them, and re-layouts  4.78 us (8%)
  other arithmetic  3.74 us (6%)
  matrix products  0.93 us (2%)
    pallas_call x1, Pallas kernels, conv_norm(): pl.pallas_call(conv_norm_kernel, out_shape=jax.ShapeDtypeStruct((tile_row...  10.1 us
    pallas_call x1, Pallas kernels, mlp(): pl.pallas_call(mlp_kernel, out_shape=jax.ShapeDtypeStruct((pixels, channe...  8.13 us
    all_to_all x1, starting transfers between devices, shards(): band_pooled = lax.all_to_all(sent, 'col', 0, 0, tiled=True)  6.74 us
    ppermute x2, starting transfers between devices, padded_2(): before = lax.ppermute(last, axis, up)  6.72 us
    ppermute x2, starting transfers between devices, padded_2(): after = lax.ppermute(leading, axis, down)  6.28 us
    all_to_all x1, waiting for transfers between devices, shards(): band_pooled = lax.all_to_all(sent, 'col', 0, 0, tiled=True)  5.92 us
    ppermute x2, waiting for transfers between devices, padded_2(): before = lax.ppermute(last, axis, up)  4.51 us
    ppermute x2, waiting for transfers between devices, padded_2(): after = lax.ppermute(leading, axis, down)  2.83 us
  transfers between devices with their start and end apart: 5, of which 3 were waited for; matrix products, arithmetic and copies ran while one was open for 4% of the time, Pallas kernels for 0%

profile of v4, /device:TPU:129, one launch (start us, length us, event | category | flops | bytes accessed | tf_op | source)
XLA Modules:
  0.0 60.9 jit_solution(2762059430604640744)
XLA Ops:
  0.0 0.9 %fusion.16 = (bf16[3,32,256]{2,1,0:T(8,128)(2,1)S(1)}, bf16[3,32,256]{2,1,0:T(8,128)(2,1)S(1)}) fusion(bf16[32,32,256]{2,1,0:T(8,128)(2,1)} %param.14), kind=kLoop, calls=%fused_computation.48 | loop fusion | bytes 196608 | tf_op jit(solution)/shard_map/slice | solution.py:17
  0.9 4.4 %collective-permute-start.1 = (bf16[3,32,256]{2,1,0:T(8,128)(2,1)S(1)}, bf16[3,32,256]{2,1,0:T(8,128)(2,1)S(1)}, u32[]{:S(2)}, u32[]{:S(2)}) collective-permute-start(bf16[3,32,256]{2,1,0:T(8,128)(2,1)S(1)} %get-tuple-element.7), channel_id=1, source_target_pairs={{16,0},{32,16},{48,32},{64,48},{80,64},{96,80},{112,96},{128,112},... | collective-permute-start | bytes 147464 | tf_op jit(solution)/shard_map/ppermute | solution.py:19
  5.3 2.4 %collective-permute-start = (bf16[3,32,256]{2,1,0:T(8,128)(2,1)S(1)}, bf16[3,32,256]{2,1,0:T(8,128)(2,1)S(1)}, u32[]{:S(2)}, u32[]{:S(2)}) collective-permute-start(bf16[3,32,256]{2,1,0:T(8,128)(2,1)S(1)} %get-tuple-element.8), channel_id=1, source_target_pairs={{0,16},{16,32},{32,48},{48,64},{64,80},{80,96},{96,112},{112,128},... | collective-permute-start | bytes 147464 | tf_op jit(solution)/shard_map/ppermute | solution.py:18
  7.7 1.4 %dynamic-slice_bitcast_fusion.15 = (f32[8,1,4,64]{3,0,2,1:T(8,128)S(1)}, f32[8,1,4,64]{3,0,2,1:T(8,128)S(1)}, f32[8,1,4,64]{3,0,2,1:T(8,128)S(1)}, f32[8,1,4,64]...) fusion(f32[8,7,127]{2,0,1:T(8,128)} %param.26, ...), kind=kLoop, calls=%fused_computation.41 | loop fusion | bytes 262172 | tf_op jit(solution)/shard_map/stack | solution.py:259
  9.2 4.5 %collective-permute-done = bf16[3,32,256]{2,1,0:T(8,128)(2,1)S(1)} collective-permute-done((bf16[3,32,256]{2,1,0:T(8,128)(2,1)S(1)}, bf16[3,32,256]{2,1,0:T(8,128)(2,1)S(1)}, u32[]{:S(2)}, u32[]{:S(2)}) %collective-permute-start) | collective-permute-done | bytes 49184 | tf_op jit(solution)/shard_map/ppermute | solution.py:18
  13.9 4.3 %collective-permute-start.2 = (bf16[38,3,256]{2,1,0:T(4,128)(2,1)S(1)}, bf16[38,3,256]{2,1,0:T(4,128)(2,1)S(1)}, u32[]{:S(2)}, u32[]{:S(2)}) collective-permute-start(bf16[38,3,256]{2,1,0:T(4,128)(2,1)S(1)} %get-tuple-element.5), channel_id=1, source_target_pairs={{0,1},{1,2},{2,3},{3,4},{4,5},{5,6},{6,7},{7,8},{8,9},{9,10},{10,1... | collective-permute-start | bytes 175112 | tf_op jit(solution)/shard_map/ppermute | solution.py:18
  18.2 1.9 %collective-permute-start.3 = (bf16[38,3,256]{2,1,0:T(4,128)(2,1)S(1)}, bf16[38,3,256]{2,1,0:T(4,128)(2,1)S(1)}, u32[]{:S(2)}, u32[]{:S(2)}) collective-permute-start(bf16[38,3,256]{2,1,0:T(4,128)(2,1)S(1)} %get-tuple-element.6), channel_id=1, source_target_pairs={{1,0},{2,1},{3,2},{4,3},{5,4},{6,5},{7,6},{8,7},{9,8},{10,9},{11,1... | collective-permute-start | bytes 175112 | tf_op jit(solution)/shard_map/ppermute | solution.py:19
  20.1 0.6 %reshape.108.k_ref = f32[49,256]{1,0:T(8,128)} reshape(bf16[7,7,256]{2,1,0:T(8,128)(2,1)S(1)} %copy-done.4) | data formatting | bytes 75264 | tf_op jit(solution)/shard_map/reshape | solution.py:78
  20.8 0.2 reshape.104
  21.1 2.8 %collective-permute-done.3 = bf16[38,3,256]{2,1,0:T(4,128)(2,1)S(1)} collective-permute-done((bf16[38,3,256]{2,1,0:T(4,128)(2,1)S(1)}, bf16[38,3,256]{2,1,0:T(4,128)(2,1)S(1)}, u32[]{:S(2)}, u32[]{:S(2)}) %collective-permute-start.3) | collective-permute-done | bytes 58400 | tf_op jit(solution)/shard_map/ppermute | solution.py:19
  23.9 1.3 %fusion.9.x_ref = bf16[38,40,256]{2,1,0:T(8,128)(2,1)} fusion(bf16[38,3,256]{2,1,0:T(4,128)(2,1)S(1)} %collective-permute-done.3, bf16[38,32,256]{2,1,0:T(8,128)(2,1)S(1)} %constant_dynamic-update-slice_fusion, bf16[38,3,256]{2,1,0:T(4,128)(2,1)S(1)} %collective-permute-done.2), kind=kLoop, calls=%fused_computation.15 | loop fusion | flops 3891200 | bytes 1517568 | tf_op jit(solution)/shard_map/concatenate | solution.py:20
  25.2 10.1 %shard_map.136 = bf16[32,32,256]{2,1,0:T(8,128)(2,1)} custom-call(bf16[38,40,256]{2,1,0:T(8,128)(2,1)} %fusion.9.x_ref, f32[49,256]{1,0:T(8,128)} %reshape.108.k_ref, f32[1,256]{1,0:T(1,128)} %bitcast.78, f32[1,256]{1,0:T(1,128)} %bitcast.79, f32[1,256]{1,0:T(1,128)} %bitcast.80), custom_call_target="tpu_custom_call" | custom-call | flops 25690112 | bytes 1302528 | tf_op jit(solution)/shard_map/pallas_call | solution.py:62
  35.3 8.1 %shard_map.137 = bf16[1024,256]{1,0:T(8,128)(2,1)} custom-call(bf16[1024,256]{1,0:T(8,128)(2,1)} %bitcast.74, bf16[1024,256]{1,0:T(8,128)(2,1)} %bitcast.73, bf16[256,1024]{1,0:T(8,128)(2,1)} %we_ref.1, f32[1,1024]{1,0:T(1,128)} %bitcast.81, bf16[1024,256]{1,0:T(8,128)(2,1)} %wr_ref.1, f32[1,256]{1,0:T(1,128)} %bitcast.82, f32[1,256]{1,0:T(1,128)} %bitcast.83), custom_call_target="tpu_custom_call" | custom-call | flops 1073741824 | bytes 2621440 | tf_op jit(solution)/shard_map/pallas_call | solution.py:132
  43.5 1.1 %convert_element_type.59 = f32[1024,256]{1,0:T(8,128)S(1)} convert(bf16[1024,256]{1,0:T(8,128)(2,1)} %shard_map.137) | non-fusion elementwise | flops 262144 | bytes 1572864 | tf_op jit(solution)/shard_map/convert_element_type | solution.py:281
  44.7 0.7 %broadcast_in_dim.4 = bf16[16,16,256]{2,1,0:T(8,128)(2,1)} broadcast(bf16[16,256]{1,0:T(8,128)(2,1)S(1)} %convert_element_type.52), dimensions={1,2} | broadcast | bytes 139264 | tf_op jit(solution)/shard_map/broadcast_in_dim | solution.py:238
  45.4 6.7 %all-to-all-start = ((bf16[16,16,256]{2,1,0:T(8,128)(2,1)}), bf16[16,16,256]{2,1,0:T(8,128)(2,1)S(1)}, u32[]{:S(2)}, u32[]{:S(2)}) async-start(bf16[16,16,256]{2,1,0:T(8,128)(2,1)} %broadcast_in_dim.4), calls=%async_computation | async-start | bytes 262144 | tf_op jit(solution)/shard_map/all_to_all | solution.py:241
  52.1 0.1 convolution_convert_fusion.2
  52.4 5.9 %all-to-all-done = bf16[16,16,256]{2,1,0:T(8,128)(2,1)S(1)} async-done(((bf16[16,16,256]{2,1,0:T(8,128)(2,1)}), bf16[16,16,256]{2,1,0:T(8,128)(2,1)S(1)}, u32[]{:S(2)}, u32[]{:S(2)}) %all-to-all-start) | async-done | bytes 131104 | tf_op jit(solution)/shard_map/all_to_all | solution.py:241
  58.5 0.2 convolution_convert_fusion
  58.8 0.1 fusion.6
  59.0 0.2 fusion.18
  59.3 0.3 fusion.7
  59.7 0.1 fusion.10
  60.0 1.0 %add_convert_fusion = bf16[32,32,256]{2,1,0:T(8,128)(2,1)} fusion(f32[32,32,256]{2,1,0:T(8,128)S(1)} %bitcast.71, f32[32,32,256]{2,1,0:T(8,128)S(1)} %bitcast.72), kind=kLoop, calls=%fused_computation.13 | loop fusion | flops 524288 | bytes 2621440 | tf_op jit(solution)/shard_map/convert_element_type | solution.py:281
  (33 shorter events, 1.1 us)
Async XLA Ops:
  0.0 58.5 %copy-start = (bf16[256,512]{1,0:T(8,128)(2,1)S(1)}, bf16[256,512]{1,0:T(8,128)(2,1)}, u32[]{:S(2)}) copy-start(bf16[256,512]{1,0:T(8,128)(2,1)} %param.25) | copy-start | bytes 786436
  0.0 13.7 %copy-start.1 = (bf16[32,32,256]{2,1,0:T(8,128)(2,1)S(1)}, bf16[32,32,256]{2,1,0:T(8,128)(2,1)}, u32[]{:S(2)}) copy-start(bf16[32,32,256]{2,1,0:T(8,128)(2,1)} %param.14) | copy-start | bytes 1572868
  0.9 12.9 %collective-permute-start.1 = (bf16[3,32,256]{2,1,0:T(8,128)(2,1)S(1)}, bf16[3,32,256]{2,1,0:T(8,128)(2,1)S(1)}, u32[]{:S(2)}, u32[]{:S(2)}) collective-permute-start(bf16[3,32,256]{2,1,0:T(8,128)(2,1)S(1)} %get-tuple-element.7), channel_id=1, source_target_pairs={{16,0},{32,16},{48,32},{64,48},{80,64},{96,80},{112,96},{128,112},... | collective-permute-start | bytes 147464 | tf_op jit(solution)/shard_map/ppermute | solution.py:19
  5.3 8.4 %collective-permute-start = (bf16[3,32,256]{2,1,0:T(8,128)(2,1)S(1)}, bf16[3,32,256]{2,1,0:T(8,128)(2,1)S(1)}, u32[]{:S(2)}, u32[]{:S(2)}) collective-permute-start(bf16[3,32,256]{2,1,0:T(8,128)(2,1)S(1)} %get-tuple-element.8), channel_id=1, source_target_pairs={{0,16},{16,32},{32,48},{48,64},{64,80},{80,96},{96,112},{112,128},... | collective-permute-start | bytes 147464 | tf_op jit(solution)/shard_map/ppermute | solution.py:18
  9.2 10.9 %copy-start.4 = (bf16[7,7,256]{2,1,0:T(8,128)(2,1)S(1)}, bf16[7,7,256]{2,1,0:T(8,128)(2,1)}, u32[]{:S(2)}) copy-start(bf16[7,7,256]{2,1,0:T(8,128)(2,1)} %param.15) | copy-start | bytes 75268
  13.9 7.2 %collective-permute-start.2 = (bf16[38,3,256]{2,1,0:T(4,128)(2,1)S(1)}, bf16[38,3,256]{2,1,0:T(4,128)(2,1)S(1)}, u32[]{:S(2)}, u32[]{:S(2)}) collective-permute-start(bf16[38,3,256]{2,1,0:T(4,128)(2,1)S(1)} %get-tuple-element.5), channel_id=1, source_target_pairs={{0,1},{1,2},{2,3},{3,4},{4,5},{5,6},{6,7},{7,8},{8,9},{9,10},{10,1... | collective-permute-start | bytes 175112 | tf_op jit(solution)/shard_map/ppermute | solution.py:18
  18.2 5.7 %collective-permute-start.3 = (bf16[38,3,256]{2,1,0:T(4,128)(2,1)S(1)}, bf16[38,3,256]{2,1,0:T(4,128)(2,1)S(1)}, u32[]{:S(2)}, u32[]{:S(2)}) collective-permute-start(bf16[38,3,256]{2,1,0:T(4,128)(2,1)S(1)} %get-tuple-element.6), channel_id=1, source_target_pairs={{1,0},{2,1},{3,2},{4,3},{5,4},{6,5},{7,6},{8,7},{9,8},{10,9},{11,1... | collective-permute-start | bytes 175112 | tf_op jit(solution)/shard_map/ppermute | solution.py:19
  44.6 7.5 %copy-start.2 = (bf16[256,256]{1,0:T(8,128)(2,1)S(1)}, bf16[256,256]{1,0:T(8,128)(2,1)}, u32[]{:S(2)}) copy-start(bf16[256,256]{1,0:T(8,128)(2,1)} %param.24) | copy-start | bytes 393220
  45.4 12.9 %all-to-all-start = ((bf16[16,16,256]{2,1,0:T(8,128)(2,1)}), bf16[16,16,256]{2,1,0:T(8,128)(2,1)S(1)}, u32[]{:S(2)}, u32[]{:S(2)}) async-start(bf16[16,16,256]{2,1,0:T(8,128)(2,1)} %broadcast_in_dim.4), calls=%async_computation | async-start | bytes 262144 | tf_op jit(solution)/shard_map/all_to_all | solution.py:241
  58.7 1.0 %copy-start.3 = (bf16[256,256]{1,0:T(8,128)(2,1)S(1)}, bf16[256,256]{1,0:T(8,128)(2,1)}, u32[]{:S(2)}) copy-start(bf16[256,256]{1,0:T(8,128)(2,1)} %param.27) | copy-start | bytes 393220

commit v5 on v4

--- a/solution.py
+++ b/solution.py
@@ -8,34 +8,54 @@
 HEADS = 8
 
 
-def padded_2(array, sides, width):
-    for axis, dim in sides:
-        devices, length = (lax.axis_size(axis), array.shape[dim])
-        up = [(i, (i + 1) % devices) for i in range(devices - 1)]
-        down = [(j, i) for i, j in up]
-        last = lax.slice_in_dim(array, length - width, length, axis=dim)
-        leading = lax.slice_in_dim(array, 0, width, axis=dim)
-        before = lax.ppermute(last, axis, up)
-        after = lax.ppermute(leading, axis, down)
-        array = jnp.concatenate([before, array, after], axis=dim)
-    return array
-
+def shifted(piece, axis):
+    devices = lax.axis_size(axis)
+    up = [(i, i + 1) for i in range(devices - 1)]
+    down = [(i + 1, i) for i in range(devices - 1)]
+    return lax.ppermute(piece, axis, up), lax.ppermute(piece, axis, down)
+
+
+def halo_pieces(features, width):
+    rows, cols = features.shape[:2]
+    top, _ = shifted(features[rows - width :], "row")
+    _, bottom = shifted(features[:width], "row")
+    last_cols = jnp.concatenate(
+        [top[:, cols - width :], features[:, cols - width :], bottom[:, cols - width :]], axis=0
+    )
+    first_cols = jnp.concatenate([top[:, :width], features[:, :width], bottom[:, :width]], axis=0)
+    left, _ = shifted(last_cols, "col")
+    _, right = shifted(first_cols, "col")
+    return top, bottom, left, right
 
 TAPS = 7
 ROW_BLOCK = 2
 
 
-def conv_norm_kernel(x_ref, k_ref, db_ref, g_ref, nb_ref, o_ref, xf_ref, sh_ref):
-    rows_p = x_ref.shape[0]
+def conv_norm_kernel(
+    c_ref, t_ref, b_ref, l_ref, r_ref, k_ref, db_ref, g_ref, nb_ref, o_ref, xf_ref, kf_ref, sh_ref
+):
     tile_rows, tile_cols, channels = o_ref.shape
-
-    def widen(r, carry):
-        xf_ref[r] = x_ref[r].astype(jnp.float32)
+    halo = t_ref.shape[0]
+    rows_p = tile_rows + 2 * halo
+    for a in range(TAPS):
+        kf_ref[a, pl.ds(0, TAPS), :] = k_ref[a].astype(jnp.float32)
+
+    def put(r, mid):
+        xf_ref[r, pl.ds(0, halo), :] = l_ref[r].astype(jnp.float32)
+        xf_ref[r, pl.ds(halo, tile_cols), :] = mid.astype(jnp.float32)
+        xf_ref[r, pl.ds(halo + tile_cols, halo), :] = r_ref[r].astype(jnp.float32)
         for b in range(TAPS):
             sh_ref[b, r] = xf_ref[r, pl.ds(b, tile_cols), :]
+
+    for r in range(halo):
+        put(r, t_ref[r])
+        put(rows_p - halo + r, b_ref[r])
+
+    def widen(r, carry):
+        put(r, c_ref[r - halo])
         return carry
 
-    lax.fori_loop(0, rows_p, widen, 0)
+    lax.fori_loop(halo, rows_p - halo, widen, 0)
     db = db_ref[...]
     g = g_ref[...]
     nb = nb_ref[...]
@@ -45,7 +65,7 @@
         acc = jnp.zeros((ROW_BLOCK, tile_cols, channels), jnp.float32)
         for a in range(TAPS):
             for b in range(TAPS):
-                acc = acc + sh_ref[b, pl.ds(r0 + a, ROW_BLOCK)] * k_ref[pl.ds(a * TAPS + b, 1), :]
+                acc = acc + sh_ref[b, pl.ds(r0 + a, ROW_BLOCK)] * kf_ref[a, pl.ds(b, 1), :]
         acc = acc + db
         mean = jnp.mean(acc, axis=-1, keepdims=True)
         cen = acc - mean
@@ -56,16 +76,21 @@
     lax.fori_loop(0, tile_rows // ROW_BLOCK, body, 0)
 
 
-def conv_norm(padded, dw_kernel, dw_bias, norm_gain, norm_bias, tile_rows, tile_cols):
-    rows_p, cols_p, channels = padded.shape
+def conv_norm(centre, top, bottom, left, right, dw_kernel, dw_bias, norm_gain, norm_bias):
+    tile_rows, tile_cols, channels = centre.shape
+    halo = top.shape[0]
+    rows_p = tile_rows + 2 * halo
+    cols_p = tile_cols + 2 * halo
+    cols_p += -cols_p % 8
     vmem = pl.BlockSpec(memory_space=pltpu.VMEM)
     return pl.pallas_call(
         conv_norm_kernel,
         out_shape=jax.ShapeDtypeStruct((tile_rows, tile_cols, channels), jnp.bfloat16),
-        in_specs=[vmem] * 5,
+        in_specs=[vmem] * 9,
         out_specs=vmem,
         scratch_shapes=[
             pltpu.VMEM((rows_p, cols_p, channels), jnp.float32),
+            pltpu.VMEM((TAPS, 8, channels), jnp.float32),
             pltpu.VMEM((TAPS, rows_p, tile_cols, channels), jnp.float32),
         ],
         cost_estimate=pl.CostEstimate(
@@ -74,8 +99,12 @@
             transcendentals=tile_rows * tile_cols,
         ),
     )(
-        padded,
-        dw_kernel.astype(jnp.float32).reshape(TAPS * TAPS, channels),
+        centre,
+        top,
+        bottom,
+        left,
+        right,
+        dw_kernel,
         dw_bias.reshape(1, channels),
         norm_gain.reshape(1, channels),
         norm_bias.reshape(1, channels),
@@ -109,7 +138,7 @@
     return 0.5 * pre * one_plus_erf
 
 
-def mlp_kernel(n_ref, f_ref, we_ref, be_ref, wr_ref, br_ref, ls_ref, o_ref):
+def mlp_kernel(n_ref, f_ref, we_ref, be_ref, wr_ref, br_ref, ls_ref, o_ref, p_ref):
     normed = n_ref[...]
     hidden_total = we_ref.shape[1]
     acc = jnp.zeros(o_ref.shape, jnp.float32)
@@ -121,18 +150,29 @@
         hidden = gelu_exact(pre).astype(jnp.bfloat16)
         acc = acc + jnp.dot(hidden, wr_ref[h0 : h0 + HIDDEN_BLOCK, :], preferred_element_type=jnp.float32)
     reduced = acc + br_ref[...]
-    o_ref[...] = (f_ref[...].astype(jnp.float32) + ls_ref[...] * reduced).astype(o_ref.dtype)
-
-
-def mlp(normed, features, w_expand, b_expand, w_reduce, b_reduce, layer_scale):
+    out = (f_ref[...].astype(jnp.float32) + ls_ref[...] * reduced).astype(o_ref.dtype)
+    o_ref[...] = out
+    pixels, channels = o_ref.shape
+    tile_cols = pixels // 8
+    column_sums = out.astype(jnp.float32).reshape(8, tile_cols, channels).sum(axis=0)
+    region_sums = column_sums.reshape(tile_cols // 8, 8, channels).sum(axis=1)
+    p_ref[0] = (region_sums * jnp.float32(1.0 / 64.0)).astype(p_ref.dtype)
+
+
+def mlp(normed, features, w_expand, b_expand, w_reduce, b_reduce, layer_scale, tile_cols):
     pixels, channels = normed.shape
     hidden_total = w_expand.shape[1]
-    rows = pl.BlockSpec((PIXEL_BLOCK, channels), lambda i: (i, 0))
+    block = 8 * tile_cols
+    steps = pixels // block
+    rows = pl.BlockSpec((block, channels), lambda i: (i, 0))
     whole = lambda shape: pl.BlockSpec(shape, lambda i: (0, 0))
     return pl.pallas_call(
         mlp_kernel,
-        out_shape=jax.ShapeDtypeStruct((pixels, channels), jnp.bfloat16),
-        grid=(pixels // PIXEL_BLOCK,),
+        out_shape=(
+            jax.ShapeDtypeStruct((pixels, channels), jnp.bfloat16),
+            jax.ShapeDtypeStruct((steps, tile_cols // 8, channels), jnp.bfloat16),
+        ),
+        grid=(steps,),
         in_specs=[
             rows,
             rows,
@@ -142,7 +182,7 @@
             whole((1, channels)),
             whole((1, channels)),
         ],
-        out_specs=rows,
+        out_specs=(rows, pl.BlockSpec((1, tile_cols // 8, channels), lambda i: (i, 0, 0))),
         cost_estimate=pl.CostEstimate(
             flops=4 * pixels * channels * hidden_total,
             bytes_accessed=2 * (3 * pixels * channels + 2 * channels * hidden_total),
@@ -158,9 +198,8 @@
         layer_scale.reshape(1, channels),
     )
 
-
 def block_pass(
-    padded,
+    pieces,
     features,
     dw_kernel,
     dw_bias,
@@ -173,11 +212,10 @@
     layer_scale,
 ):
     tile_rows, tile_cols, channels = features.shape
-    padded = jnp.pad(padded, ((0, 0), (0, 8 - padded.shape[1] % 8), (0, 0)))
-    normed = conv_norm(
-        padded, dw_kernel, dw_bias, norm_gain, norm_bias, tile_rows, tile_cols
-    ).reshape(-1, channels)
-    summed = mlp(
+    normed = conv_norm(features, *pieces, dw_kernel, dw_bias, norm_gain, norm_bias).reshape(
+        -1, channels
+    )
+    summed, pooled = mlp(
         normed,
         features.reshape(-1, channels),
         w_expand,
@@ -185,8 +223,9 @@
         w_reduce,
         b_reduce,
         layer_scale,
-    )
-    return summed.reshape(tile_rows, tile_cols, channels)
+        tile_cols,
+    )
+    return summed.reshape(tile_rows, tile_cols, channels), pooled
 
 
 def shards(
@@ -207,10 +246,9 @@
 ):
     tile_rows, tile_cols, channels = features.shape
     head_dim = channels // HEADS
-    extended = padded_2(features, (("row", 0),), 3)
-    padded = padded_2(extended, (("col", 1),), 3)
-    block_out = block_pass(
-        padded,
+    pieces = halo_pieces(features, 3)
+    block_out, pooled = block_pass(
+        pieces,
         features,
         dw_kernel,
         dw_bias,
@@ -224,12 +262,7 @@
     )
     region_side = tile_rows // 8
     local_count = region_side * region_side
-    pooled = (
-        block_out.astype(jnp.float32)
-        .reshape(region_side, 8, region_side, 8, channels)
-        .mean(axis=(1, 3))
-    )
-    pooled = pooled.astype(jnp.bfloat16).reshape(local_count, channels)
+    pooled = pooled.reshape(local_count, channels)
     queries = jnp.dot(pooled, w_query, preferred_element_type=jnp.float32).astype(jnp.bfloat16)
     columns = lax.axis_size("col")
     position = lax.axis_index("col")

time: 61.4 us -> 63.8 us (1.039)
  local copies, waits for them, and re-layouts: 4.78 us -> 7.73 us
  other arithmetic: 3.74 us -> 1.32 us
  Pallas kernels: 18.2 us -> 19.9 us
    unnamed x12 -> x18, local copies, waits for them, and re-layouts: 0.07 us -> 3.32 us
    pallas_call x1, Pallas kernels: 10.1 us -> 11.7 us  [conv_norm(): pl.pallas_call(conv_norm_kernel, out_shape=jax.ShapeDtypeStruct((tile_row...]
    another operation x1, local copies, waits for them, and re-layouts: 1.44 us -> 0.14 us  [shards(): rows_of.append(jnp.stack(per_col, axis=1))]
    concatenate x1 -> x2, other arithmetic: 1.34 us -> 0.12 us  [the longest x1 0.06 us: halo_pieces(): jnp.concatenate([top[:, :width], features[:, :width], bottom[:, :width]],...]
    convert_element_type x2 -> x1, other arithmetic: 2.07 us -> 0.97 us  [shards(): return (block_out.astype(jnp.float32) + spread).astype(jnp.bfloat16)]
    slice x2 -> x4, local copies, waits for them, and re-layouts: 0.97 us -> 1.92 us  [the longest x1 1.03 us: halo_pieces(): features[:, :width]]
    broadcast_in_dim x1 -> x2, local copies, waits for them, and re-layouts: 0.66 us -> 1.37 us  [shards(): jnp.broadcast_to(pooled[None], (columns, local_count, channels))]
    reshape x1 -> x0, local copies, waits for them, and re-layouts: 0.64 us -> none  [conv_norm(): dw_kernel.astype(jnp.float32).reshape(TAPS * TAPS, channels)]
  transfers between devices with their start and end apart: 5 -> 5, of which waited for: 3 -> 3; matrix products, arithmetic and copies ran while one was open for 4% -> 3% of each run, Pallas kernels for 0% -> 0%
where the time goes in v5:
time: 63.8 us; the launch traced here: 63.3 us
  starting transfers between devices  19.9 us (31%)
  Pallas kernels  19.9 us (31%)
  waiting for transfers between devices  13.4 us (21%)
  local copies, waits for them, and re-layouts  7.73 us (12%)
  other arithmetic  1.32 us (2%)
  matrix products  0.93 us (1%)
    ppermute x4, starting transfers between devices, shifted(): return (lax.ppermute(piece, axis, up), lax.ppermute(piece, axis, down))  13 us
    pallas_call x1, Pallas kernels, conv_norm(): pl.pallas_call(conv_norm_kernel, out_shape=jax.ShapeDtypeStruct((tile_row...  11.7 us
    pallas_call x1, Pallas kernels, mlp(): pl.pallas_call(mlp_kernel, out_shape=(jax.ShapeDtypeStruct((pixels, chann...  8.19 us
    ppermute x4, waiting for transfers between devices, shifted(): return (lax.ppermute(piece, axis, up), lax.ppermute(piece, axis, down))  7.46 us
    all_to_all x1, starting transfers between devices, shards(): band_pooled = lax.all_to_all(sent, 'col', 0, 0, tiled=True)  6.88 us
    all_to_all x1, waiting for transfers between devices, shards(): band_pooled = lax.all_to_all(sent, 'col', 0, 0, tiled=True)  5.92 us
    unnamed x18, local copies, waits for them, and re-layouts  3.32 us
    broadcast_in_dim x2, local copies, waits for them, and re-layouts, shards(): jnp.broadcast_to(pooled[None], (columns, local_count, channels))  1.37 us
  transfers between devices with their start and end apart: 5, of which 3 were waited for; matrix products, arithmetic and copies ran while one was open for 3% of the time, Pallas kernels for 0%

profile of v5, /device:TPU:129, one launch (start us, length us, event | category | flops | bytes accessed | tf_op | source)
XLA Modules:
  0.0 63.3 jit_solution(7746380335326428004)
XLA Ops:
  0.0 0.9 %fusion.12 = (bf16[3,32,256]{2,1,0:T(8,128)(2,1)S(1)}, bf16[3,32,256]{2,1,0:T(8,128)(2,1)S(1)}) fusion(bf16[32,32,256]{2,1,0:T(8,128)(2,1)} %c_ref.1), kind=kLoop, calls=%fused_computation.41 | loop fusion | bytes 196608 | tf_op jit(solution)/shard_map/slice | solution.py:21
  0.9 4.4 %collective-permute-start.1 = (bf16[3,32,256]{2,1,0:T(8,128)(2,1)S(1)}, bf16[3,32,256]{2,1,0:T(8,128)(2,1)S(1)}, u32[]{:S(2)}, u32[]{:S(2)}) collective-permute-start(bf16[3,32,256]{2,1,0:T(8,128)(2,1)S(1)} %get-tuple-element.11), channel_id=1, source_target_pairs={{16,0},{32,16},{48,32},{64,48},{80,64},{96,80},{112,96},{128,112},... | collective-permute-start | bytes 147464 | tf_op jit(solution)/shard_map/ppermute | solution.py:15
  5.2 2.4 %collective-permute-start = (bf16[3,32,256]{2,1,0:T(8,128)(2,1)S(1)}, bf16[3,32,256]{2,1,0:T(8,128)(2,1)S(1)}, u32[]{:S(2)}, u32[]{:S(2)}) collective-permute-start(bf16[3,32,256]{2,1,0:T(8,128)(2,1)S(1)} %get-tuple-element.12), channel_id=1, source_target_pairs={{0,16},{16,32},{32,48},{48,64},{64,80},{80,96},{96,112},{112,128},... | collective-permute-start | bytes 147464 | tf_op jit(solution)/shard_map/ppermute | solution.py:15
  7.7 1.0 %fusion.11 = (bf16[32,3,256]{2,1,0:T(4,128)(2,1)S(1)}, bf16[32,3,256]{2,1,0:T(4,128)(2,1)S(1)}) fusion(bf16[32,32,256]{2,1,0:T(8,128)(2,1)} %c_ref.1), kind=kLoop, calls=%fused_computation.40 | loop fusion | bytes 196608 | tf_op jit(solution)/shard_map/slice | solution.py:25
  8.7 0.7 %copy-done.1 = f32[8,7,127]{2,0,1:T(8,128)S(1)} copy-done((f32[8,7,127]{2,0,1:T(8,128)S(1)}, f32[8,7,127]{2,0,1:T(8,128)}, u32[]{:S(2)}) %copy-start.1) | copy-done | bytes 28472
  9.7 4.0 %collective-permute-done.t_ref = bf16[3,32,256]{2,1,0:T(8,128)(2,1)S(1)} collective-permute-done((bf16[3,32,256]{2,1,0:T(8,128)(2,1)S(1)}, bf16[3,32,256]{2,1,0:T(8,128)(2,1)S(1)}, u32[]{:S(2)}, u32[]{:S(2)}) %collective-permute-start) | collective-permute-done | bytes 49184 | tf_op jit(solution)/shard_map/ppermute | solution.py:15
  13.8 0.5 copy-done.8
  14.3 4.3 %collective-permute-start.2 = (bf16[38,3,256]{2,1,0:T(4,128)(2,1)S(1)}, bf16[38,3,256]{2,1,0:T(4,128)(2,1)S(1)}, u32[]{:S(2)}, u32[]{:S(2)}) collective-permute-start(bf16[38,3,256]{2,1,0:T(4,128)(2,1)S(1)} %pad_maximum_fusion.1), channel_id=1, source_target_pairs={{0,1},{1,2},{2,3},{3,4},{4,5},{5,6},{6,7},{7,8},{8,9},{9,10},{10,1... | collective-permute-start | bytes 175112 | tf_op jit(solution)/shard_map/ppermute | solution.py:15
  18.7 1.9 %collective-permute-start.3 = (bf16[38,3,256]{2,1,0:T(4,128)(2,1)S(1)}, bf16[38,3,256]{2,1,0:T(4,128)(2,1)S(1)}, u32[]{:S(2)}, u32[]{:S(2)}) collective-permute-start(bf16[38,3,256]{2,1,0:T(4,128)(2,1)S(1)} %pad_maximum_fusion.2), channel_id=1, source_target_pairs={{1,0},{2,1},{3,2},{4,3},{5,4},{6,5},{7,6},{8,7},{9,8},{10,9},{11,1... | collective-permute-start | bytes 175112 | tf_op jit(solution)/shard_map/ppermute | solution.py:15
  20.7 0.2 reshape.84
  20.9 3.5 %collective-permute-done.3.r_ref = bf16[38,3,256]{2,1,0:T(4,128)(2,1)S(1)} collective-permute-done((bf16[38,3,256]{2,1,0:T(4,128)(2,1)S(1)}, bf16[38,3,256]{2,1,0:T(4,128)(2,1)S(1)}, u32[]{:S(2)}, u32[]{:S(2)}) %collective-permute-start.3) | collective-permute-done | bytes 58400 | tf_op jit(solution)/shard_map/ppermute | solution.py:15
  24.4 0.6 copy-done.6
  25.0 11.7 %shard_map.136 = bf16[32,32,256]{2,1,0:T(8,128)(2,1)} custom-call(bf16[32,32,256]{2,1,0:T(8,128)(2,1)} %c_ref.1, bf16[3,32,256]{2,1,0:T(8,128)(2,1)} %copy-done.8, bf16[3,32,256]{2,1,0:T(8,128)(2,1)} %copy-done.7, bf16[38,3,256]{2,1,0:T(4,128)(2,1)} %copy-done.5, bf16[38,3,256]{2,1,0:T(4,128)(2,1)} %copy-done.6, bf16[7,7,256]{2,1,0:T(8,128)(2,1)} %k_ref.1, ...), custom_call_target="tpu_custom_call" | custom-call | flops 25690112 | bytes 1302528 | tf_op jit(solution)/shard_map/pallas_call | solution.py:86
  36.7 8.2 %shard_map.137 = (bf16[1024,256]{1,0:T(8,128)(2,1)}, bf16[4,4,256]{2,1,0:T(4,128)(2,1)}) custom-call(bf16[1024,256]{1,0:T(8,128)(2,1)} %bitcast.72, bf16[1024,256]{1,0:T(8,128)(2,1)} %bitcast.71, bf16[256,1024]{1,0:T(8,128)(2,1)} %we_ref.1, f32[1,1024]{1,0:T(1,128)} %bitcast.80, bf16[1024,256]{1,0:T(8,128)(2,1)} %wr_ref.1, f32[1,256]{1,0:T(1,128)} %bitcast.81, ...), custom_call_target="tpu_custom_call" | custom-call | flops 1073741824 | bytes 2621440 | tf_op jit(solution)/shard_map/pallas_call | solution.py:169
  44.9 0.7 %broadcast_in_dim.6 = bf16[16,256]{1,0:T(8,128)(2,1)S(1)} reshape(bf16[4,4,256]{2,1,0:T(4,128)(2,1)} %get-tuple-element.8) | data formatting | bytes 16384 | tf_op jit(solution)/shard_map/broadcast_in_dim | solution.py:271
  45.6 0.7 %broadcast_in_dim.7 = bf16[16,16,256]{2,1,0:T(8,128)(2,1)} broadcast(bf16[16,256]{1,0:T(8,128)(2,1)S(1)} %broadcast_in_dim.6), dimensions={1,2} | broadcast | bytes 139264 | tf_op jit(solution)/shard_map/broadcast_in_dim | solution.py:271
  46.2 6.9 %all-to-all-start = ((bf16[16,16,256]{2,1,0:T(8,128)(2,1)}), bf16[16,16,256]{2,1,0:T(8,128)(2,1)S(1)}, u32[]{:S(2)}, u32[]{:S(2)}) async-start(bf16[16,16,256]{2,1,0:T(8,128)(2,1)} %broadcast_in_dim.7), calls=%async_computation | async-start | bytes 262144 | tf_op jit(solution)/shard_map/all_to_all | solution.py:274
  53.4 5.9 %all-to-all-done = bf16[16,16,256]{2,1,0:T(8,128)(2,1)S(1)} async-done(((bf16[16,16,256]{2,1,0:T(8,128)(2,1)}), bf16[16,16,256]{2,1,0:T(8,128)(2,1)S(1)}, u32[]{:S(2)}, u32[]{:S(2)}) %all-to-all-start) | async-done | bytes 131104 | tf_op jit(solution)/shard_map/all_to_all | solution.py:274
  59.5 0.2 convolution_convert_fusion
  60.0 0.2 fusion.16
  60.3 0.3 fusion.4
  60.7 0.5 copy-done.4
  61.4 0.9 %copy-done.2 = bf16[1024,256]{1,0:T(8,128)(2,1)S(1)} copy-done((bf16[1024,256]{1,0:T(8,128)(2,1)S(1)}, bf16[1024,256]{1,0:T(8,128)(2,1)}, u32[]{:S(2)}) %copy-start.2) | copy-done | bytes 524312
  62.4 1.0 %fusion.5 = bf16[32,32,256]{2,1,0:T(8,128)(2,1)} fusion(f32[32,32,256]{2,1,0:T(8,128)S(1)} %bitcast.70, bf16[32,32,256]{2,1,0:T(8,128)(2,1)S(1)} %bitcast.75), kind=kLoop, calls=%fused_computation.10 | loop fusion | flops 786432 | bytes 2097152 | tf_op jit(solution)/shard_map/convert_element_type | solution.py:314
  (37 shorter events, 1.6 us)
Async XLA Ops:
  0.0 59.5 %copy-start = (bf16[256,512]{1,0:T(8,128)(2,1)S(1)}, bf16[256,512]{1,0:T(8,128)(2,1)}, u32[]{:S(2)}) copy-start(bf16[256,512]{1,0:T(8,128)(2,1)} %param.25) | copy-start | bytes 786436
  0.9 8.8 %collective-permute-start.1 = (bf16[3,32,256]{2,1,0:T(8,128)(2,1)S(1)}, bf16[3,32,256]{2,1,0:T(8,128)(2,1)S(1)}, u32[]{:S(2)}, u32[]{:S(2)}) collective-permute-start(bf16[3,32,256]{2,1,0:T(8,128)(2,1)S(1)} %get-tuple-element.11), channel_id=1, source_target_pairs={{16,0},{32,16},{48,32},{64,48},{80,64},{96,80},{112,96},{128,112},... | collective-permute-start | bytes 147464 | tf_op jit(solution)/shard_map/ppermute | solution.py:15
  5.2 8.4 %collective-permute-start = (bf16[3,32,256]{2,1,0:T(8,128)(2,1)S(1)}, bf16[3,32,256]{2,1,0:T(8,128)(2,1)S(1)}, u32[]{:S(2)}, u32[]{:S(2)}) collective-permute-start(bf16[3,32,256]{2,1,0:T(8,128)(2,1)S(1)} %get-tuple-element.12), channel_id=1, source_target_pairs={{0,16},{16,32},{32,48},{48,64},{64,80},{80,96},{96,112},{112,128},... | collective-permute-start | bytes 147464 | tf_op jit(solution)/shard_map/ppermute | solution.py:15
  8.7 0.8 %copy-start.1 = (f32[8,7,127]{2,0,1:T(8,128)S(1)}, f32[8,7,127]{2,0,1:T(8,128)}, u32[]{:S(2)}) copy-start(f32[8,7,127]{2,0,1:T(8,128)} %param.26) | copy-start | bytes 85348
  9.7 4.1 %copy-start.7 = (bf16[3,32,256]{2,1,0:T(8,128)(2,1)}, bf16[3,32,256]{2,1,0:T(8,128)(2,1)S(1)}, u32[]{:S(2)}) copy-start(bf16[3,32,256]{2,1,0:T(8,128)(2,1)S(1)} %collective-permute-done.1.b_ref) | copy-start | bytes 147460
  13.7 0.6 copy-start.8
  14.3 6.6 %collective-permute-start.2 = (bf16[38,3,256]{2,1,0:T(4,128)(2,1)S(1)}, bf16[38,3,256]{2,1,0:T(4,128)(2,1)S(1)}, u32[]{:S(2)}, u32[]{:S(2)}) collective-permute-start(bf16[38,3,256]{2,1,0:T(4,128)(2,1)S(1)} %pad_maximum_fusion.1), channel_id=1, source_target_pairs={{0,1},{1,2},{2,3},{3,4},{4,5},{5,6},{6,7},{7,8},{8,9},{9,10},{10,1... | collective-permute-start | bytes 175112 | tf_op jit(solution)/shard_map/ppermute | solution.py:15
  18.7 5.7 %collective-permute-start.3 = (bf16[38,3,256]{2,1,0:T(4,128)(2,1)S(1)}, bf16[38,3,256]{2,1,0:T(4,128)(2,1)S(1)}, u32[]{:S(2)}, u32[]{:S(2)}) collective-permute-start(bf16[38,3,256]{2,1,0:T(4,128)(2,1)S(1)} %pad_maximum_fusion.2), channel_id=1, source_target_pairs={{1,0},{2,1},{3,2},{4,3},{5,4},{6,5},{7,6},{8,7},{9,8},{10,9},{11,1... | collective-permute-start | bytes 175112 | tf_op jit(solution)/shard_map/ppermute | solution.py:15
  20.9 3.5 %copy-start.5 = (bf16[38,3,256]{2,1,0:T(4,128)(2,1)}, bf16[38,3,256]{2,1,0:T(4,128)(2,1)S(1)}, u32[]{:S(2)}) copy-start(bf16[38,3,256]{2,1,0:T(4,128)(2,1)S(1)} %collective-permute-done.2.l_ref) | copy-start | bytes 175108
  24.4 0.6 copy-start.6
  46.2 6.9 %copy-start.3 = (bf16[256,256]{1,0:T(8,128)(2,1)S(1)}, bf16[256,256]{1,0:T(8,128)(2,1)}, u32[]{:S(2)}) copy-start(bf16[256,256]{1,0:T(8,128)(2,1)} %param.24) | copy-start | bytes 393220
  46.2 13.0 %all-to-all-start = ((bf16[16,16,256]{2,1,0:T(8,128)(2,1)}), bf16[16,16,256]{2,1,0:T(8,128)(2,1)S(1)}, u32[]{:S(2)}, u32[]{:S(2)}) async-start(bf16[16,16,256]{2,1,0:T(8,128)(2,1)} %broadcast_in_dim.7), calls=%async_computation | async-start | bytes 262144 | tf_op jit(solution)/shard_map/all_to_all | solution.py:274
  60.3 0.9 %copy-start.4 = (bf16[256,256]{1,0:T(8,128)(2,1)S(1)}, bf16[256,256]{1,0:T(8,128)(2,1)}, u32[]{:S(2)}) copy-start(bf16[256,256]{1,0:T(8,128)(2,1)} %param.27) | copy-start | bytes 393220
  61.3 1.1 %copy-start.2 = (bf16[1024,256]{1,0:T(8,128)(2,1)S(1)}, bf16[1024,256]{1,0:T(8,128)(2,1)}, u32[]{:S(2)}) copy-start(bf16[1024,256]{1,0:T(8,128)(2,1)} %get-tuple-element.7) | copy-start | bytes 1572868

commit v6 on v5

--- a/solution.py
+++ b/solution.py
@@ -28,68 +28,60 @@
     return top, bottom, left, right
 
 TAPS = 7
-ROW_BLOCK = 2
-
-
-def conv_norm_kernel(
-    c_ref, t_ref, b_ref, l_ref, r_ref, k_ref, db_ref, g_ref, nb_ref, o_ref, xf_ref, kf_ref, sh_ref
-):
+ROW_BLOCK = 8
+
+
+def conv_norm_kernel(x_ref, k_ref, db_ref, g_ref, nb_ref, o_ref, kf_ref, sh_ref):
+    rows_p = x_ref.shape[0]
     tile_rows, tile_cols, channels = o_ref.shape
-    halo = t_ref.shape[0]
-    rows_p = tile_rows + 2 * halo
     for a in range(TAPS):
         kf_ref[a, pl.ds(0, TAPS), :] = k_ref[a].astype(jnp.float32)
 
-    def put(r, mid):
-        xf_ref[r, pl.ds(0, halo), :] = l_ref[r].astype(jnp.float32)
-        xf_ref[r, pl.ds(halo, tile_cols), :] = mid.astype(jnp.float32)
-        xf_ref[r, pl.ds(halo + tile_cols, halo), :] = r_ref[r].astype(jnp.float32)
+    def widen(r, carry):
+        row = x_ref[r].astype(jnp.float32)
         for b in range(TAPS):
-            sh_ref[b, r] = xf_ref[r, pl.ds(b, tile_cols), :]
-
-    for r in range(halo):
-        put(r, t_ref[r])
-        put(rows_p - halo + r, b_ref[r])
-
-    def widen(r, carry):
-        put(r, c_ref[r - halo])
+            sh_ref[b, r] = row[b : b + tile_cols]
         return carry
 
-    lax.fori_loop(halo, rows_p - halo, widen, 0)
+    lax.fori_loop(0, rows_p, widen, 0)
     db = db_ref[...]
     g = g_ref[...]
     nb = nb_ref[...]
+    lanes = 128
+    halves = channels // lanes
 
     def body(i, carry):
         r0 = pl.multiple_of(i * ROW_BLOCK, ROW_BLOCK)
-        acc = jnp.zeros((ROW_BLOCK, tile_cols, channels), jnp.float32)
-        for a in range(TAPS):
-            for b in range(TAPS):
-                acc = acc + sh_ref[b, pl.ds(r0 + a, ROW_BLOCK)] * kf_ref[a, pl.ds(b, 1), :]
-        acc = acc + db
-        mean = jnp.mean(acc, axis=-1, keepdims=True)
-        cen = acc - mean
-        var = jnp.mean(cen * cen, axis=-1, keepdims=True)
-        o_ref[pl.ds(r0, ROW_BLOCK)] = (cen * lax.rsqrt(var + 1e-06) * g + nb).astype(o_ref.dtype)
+        for s0 in range(0, tile_cols, 8):
+            parts = []
+            for h in range(halves):
+                lane = pl.ds(h * lanes, lanes)
+                acc = jnp.zeros((ROW_BLOCK, 8, lanes), jnp.float32)
+                for b in range(TAPS):
+                    x = sh_ref[b, pl.ds(r0, ROW_BLOCK + TAPS - 1), pl.ds(s0, 8), lane]
+                    for a in range(TAPS):
+                        acc = acc + x[a : a + ROW_BLOCK] * kf_ref[a, pl.ds(b, 1), lane]
+                parts.append(acc)
+            acc = jnp.concatenate(parts, axis=-1) + db
+            mean = jnp.mean(acc, axis=-1, keepdims=True)
+            cen = acc - mean
+            var = jnp.mean(cen * cen, axis=-1, keepdims=True)
+            normed = cen * lax.rsqrt(var + 1e-06) * g + nb
+            o_ref[pl.ds(r0, ROW_BLOCK), pl.ds(s0, 8), :] = normed.astype(o_ref.dtype)
         return carry
 
     lax.fori_loop(0, tile_rows // ROW_BLOCK, body, 0)
 
 
-def conv_norm(centre, top, bottom, left, right, dw_kernel, dw_bias, norm_gain, norm_bias):
-    tile_rows, tile_cols, channels = centre.shape
-    halo = top.shape[0]
-    rows_p = tile_rows + 2 * halo
-    cols_p = tile_cols + 2 * halo
-    cols_p += -cols_p % 8
+def conv_norm(padded, dw_kernel, dw_bias, norm_gain, norm_bias, tile_rows, tile_cols):
+    rows_p, cols_p, channels = padded.shape
     vmem = pl.BlockSpec(memory_space=pltpu.VMEM)
     return pl.pallas_call(
         conv_norm_kernel,
         out_shape=jax.ShapeDtypeStruct((tile_rows, tile_cols, channels), jnp.bfloat16),
-        in_specs=[vmem] * 9,
+        in_specs=[vmem] * 5,
         out_specs=vmem,
         scratch_shapes=[
-            pltpu.VMEM((rows_p, cols_p, channels), jnp.float32),
             pltpu.VMEM((TAPS, 8, channels), jnp.float32),
             pltpu.VMEM((TAPS, rows_p, tile_cols, channels), jnp.float32),
         ],
@@ -99,11 +91,7 @@
             transcendentals=tile_rows * tile_cols,
         ),
     )(
-        centre,
-        top,
-        bottom,
-        left,
-        right,
+        padded,
         dw_kernel,
         dw_bias.reshape(1, channels),
         norm_gain.reshape(1, channels),
@@ -212,9 +200,14 @@
     layer_scale,
 ):
     tile_rows, tile_cols, channels = features.shape
-    normed = conv_norm(features, *pieces, dw_kernel, dw_bias, norm_gain, norm_bias).reshape(
-        -1, channels
-    )
+    top, bottom, left, right = pieces
+    extended = jnp.concatenate([top, features, bottom], axis=0)
+    padded = jnp.concatenate(
+        [left, extended, right, jnp.zeros_like(right)[:, : -(tile_cols + 3 * 3) % 8]], axis=1
+    )
+    normed = conv_norm(
+        padded, dw_kernel, dw_bias, norm_gain, norm_bias, tile_rows, tile_cols
+    ).reshape(-1, channels)
     summed, pooled = mlp(
         normed,
         features.reshape(-1, channels),
@@ -262,16 +255,14 @@
     )
     region_side = tile_rows // 8
     local_count = region_side * region_side
-    pooled = pooled.reshape(local_count, channels)
-    queries = jnp.dot(pooled, w_query, preferred_element_type=jnp.float32).astype(jnp.bfloat16)
+    queries = jnp.einsum("rcd,de->rce", pooled, w_query, preferred_element_type=jnp.float32)
+    queries = queries.astype(jnp.bfloat16).reshape(local_count, channels)
     columns = lax.axis_size("col")
     position = lax.axis_index("col")
     span_cols = region_side * columns
     key_count = local_count * columns
-    sent = jnp.broadcast_to(pooled[None], (columns, local_count, channels)).reshape(
-        columns * local_count, channels
-    )
-    band_pooled = lax.all_to_all(sent, "col", 0, 0, tiled=True)
+    sent = jnp.broadcast_to(pooled[None], (columns,) + pooled.shape)
+    band_pooled = lax.all_to_all(sent, "col", 0, 0)
     band_pooled = (
         band_pooled.reshape(columns, region_side, region_side, channels)
         .transpose(1, 0, 2, 3)

time: 63.8 us -> 59.8 us (0.937)
  the two profiles are of different devices: /device:TPU:129 before, /device:TPU:113 now
where the time goes in v6:
time: 59.8 us; the launch traced here: 59.3 us
  starting transfers between devices  21 us (35%)
  Pallas kernels  17.7 us (30%)
  waiting for transfers between devices  9.86 us (16%)
  local copies, waits for them, and re-layouts  6.13 us (10%)
  other arithmetic  2.72 us (5%)
  matrix products  1.62 us (3%)
    ppermute x4, starting transfers between devices, shifted(): return (lax.ppermute(piece, axis, up), lax.ppermute(piece, axis, down))  14.5 us
    pallas_call x1, Pallas kernels, conv_norm(): pl.pallas_call(conv_norm_kernel, out_shape=jax.ShapeDtypeStruct((tile_row...  9.46 us
    pallas_call x1, Pallas kernels, mlp(): pl.pallas_call(mlp_kernel, out_shape=(jax.ShapeDtypeStruct((pixels, chann...  8.22 us
    all_to_all x1, starting transfers between devices, shards(): band_pooled = lax.all_to_all(sent, 'col', 0, 0)  6.52 us
    all_to_all x1, waiting for transfers between devices, shards(): band_pooled = lax.all_to_all(sent, 'col', 0, 0)  5.23 us
    ppermute x4, waiting for transfers between devices, shifted(): return (lax.ppermute(piece, axis, up), lax.ppermute(piece, axis, down))  4.63 us
    another operation x1, local copies, waits for them, and re-layouts, shards(): rows_of.append(jnp.stack(per_col, axis=1))  1.45 us
    concatenate x1, other arithmetic, block_pass(): jnp.concatenate([left, extended, right, jnp.zeros_like(right)[:, :-(tile_...  1.4 us
  transfers between devices with their start and end apart: 5, of which 3 were waited for; matrix products, arithmetic and copies ran while one was open for 7% of the time, Pallas kernels for 0%

profile of v6, /device:TPU:113, one launch (start us, length us, event | category | flops | bytes accessed | tf_op | source)
XLA Modules:
  0.0 59.3 jit_solution(1028920841741334394)
XLA Ops:
  0.0 0.9 %fusion.13 = (bf16[3,32,256]{2,1,0:T(8,128)(2,1)S(1)}, bf16[3,32,256]{2,1,0:T(8,128)(2,1)S(1)}) fusion(bf16[32,32,256]{2,1,0:T(8,128)(2,1)} %param.14), kind=kLoop, calls=%fused_computation.43 | loop fusion | bytes 196608 | tf_op jit(solution)/shard_map/slice | solution.py:20
  0.9 4.5 %collective-permute-start = (bf16[3,32,256]{2,1,0:T(8,128)(2,1)S(1)}, bf16[3,32,256]{2,1,0:T(8,128)(2,1)S(1)}, u32[]{:S(2)}, u32[]{:S(2)}) collective-permute-start(bf16[3,32,256]{2,1,0:T(8,128)(2,1)S(1)} %get-tuple-element.11), channel_id=1, source_target_pairs={{0,16},{16,32},{32,48},{48,64},{64,80},{80,96},{96,112},{112,128},... | collective-permute-start | bytes 147464 | tf_op jit(solution)/shard_map/ppermute | solution.py:15
  5.4 2.3 %collective-permute-start.1 = (bf16[3,32,256]{2,1,0:T(8,128)(2,1)S(1)}, bf16[3,32,256]{2,1,0:T(8,128)(2,1)S(1)}, u32[]{:S(2)}, u32[]{:S(2)}) collective-permute-start(bf16[3,32,256]{2,1,0:T(8,128)(2,1)S(1)} %get-tuple-element.12), channel_id=1, source_target_pairs={{16,0},{32,16},{48,32},{64,48},{80,64},{96,80},{112,96},{128,112},... | collective-permute-start | bytes 147464 | tf_op jit(solution)/shard_map/ppermute | solution.py:15
  7.7 1.0 %fusion.12 = (bf16[32,3,256]{2,1,0:T(4,128)(2,1)S(1)}, bf16[32,3,256]{2,1,0:T(4,128)(2,1)S(1)}) fusion(bf16[32,32,256]{2,1,0:T(8,128)(2,1)} %param.14), kind=kLoop, calls=%fused_computation.42 | loop fusion | bytes 196608 | tf_op jit(solution)/shard_map/slice | solution.py:23
  8.7 1.4 %dynamic-slice_bitcast_fusion.15 = (f32[8,1,4,64]{3,0,2,1:T(8,128)S(1)}, f32[8,1,4,64]{3,0,2,1:T(8,128)S(1)}, f32[8,1,4,64]{3,0,2,1:T(8,128)S(1)}, f32[8,1,4,64]...) fusion(f32[8,7,127]{2,0,1:T(8,128)} %param.26, ...), kind=kLoop, calls=%fused_computation.40 | loop fusion | bytes 262172 | tf_op jit(solution)/shard_map/stack | solution.py:283
  10.2 3.6 %collective-permute-done.1 = bf16[3,32,256]{2,1,0:T(8,128)(2,1)S(1)} collective-permute-done((bf16[3,32,256]{2,1,0:T(8,128)(2,1)S(1)}, bf16[3,32,256]{2,1,0:T(8,128)(2,1)S(1)}, u32[]{:S(2)}, u32[]{:S(2)}) %collective-permute-start.1) | collective-permute-done | bytes 49184 | tf_op jit(solution)/shard_map/ppermute | solution.py:15
  13.9 4.0 %collective-permute-start.3 = (bf16[38,3,256]{2,1,0:T(4,128)(2,1)S(1)}, bf16[38,3,256]{2,1,0:T(4,128)(2,1)S(1)}, u32[]{:S(2)}, u32[]{:S(2)}) collective-permute-start(bf16[38,3,256]{2,1,0:T(4,128)(2,1)S(1)} %pad_maximum_fusion.2), channel_id=1, source_target_pairs={{1,0},{2,1},{3,2},{4,3},{5,4},{6,5},{7,6},{8,7},{9,8},{10,9},{11,1... | collective-permute-start | bytes 175112 | tf_op jit(solution)/shard_map/ppermute | solution.py:15
  18.0 3.7 %collective-permute-start.2 = (bf16[38,3,256]{2,1,0:T(4,128)(2,1)S(1)}, bf16[38,3,256]{2,1,0:T(4,128)(2,1)S(1)}, u32[]{:S(2)}, u32[]{:S(2)}) collective-permute-start(bf16[38,3,256]{2,1,0:T(4,128)(2,1)S(1)} %pad_maximum_fusion.1), channel_id=1, source_target_pairs={{0,1},{1,2},{2,3},{3,4},{4,5},{5,6},{6,7},{7,8},{8,9},{9,10},{10,1... | collective-permute-start | bytes 175112 | tf_op jit(solution)/shard_map/ppermute | solution.py:15
  21.8 0.2 reshape.70
  22.1 1.0 %collective-permute-done.2 = bf16[38,3,256]{2,1,0:T(4,128)(2,1)S(1)} collective-permute-done((bf16[38,3,256]{2,1,0:T(4,128)(2,1)S(1)}, bf16[38,3,256]{2,1,0:T(4,128)(2,1)S(1)}, u32[]{:S(2)}, u32[]{:S(2)}) %collective-permute-start.2) | collective-permute-done | bytes 58400 | tf_op jit(solution)/shard_map/ppermute | solution.py:15
  23.2 1.4 %maximum_maximum_fusion.x_ref = bf16[38,41,256]{2,1,0:T(8,128)(2,1)} fusion(bf16[38,3,256]{2,1,0:T(4,128)(2,1)S(1)} %collective-permute-done.3, bf16[3,32,256]{2,1,0:T(8,128)(2,1)S(1)} %collective-permute-done.1, bf16[32,32,256]{2,1,0:T(8,128)(2,1)S(1)} %copy-done.1, bf16[3,32,256]{2,1,0:T(8,128)(2,1)S(1)} %collective-permute-done, ...), kind=kLoop, calls=%fused_computation.11 | loop fusion | flops 4786176 | bytes 1537106 | tf_op jit(solution)/shard_map/concatenate | solution.py:205
  24.6 9.5 %shard_map.136 = bf16[32,32,256]{2,1,0:T(8,128)(2,1)} custom-call(bf16[38,41,256]{2,1,0:T(8,128)(2,1)} %maximum_maximum_fusion.x_ref, bf16[7,7,256]{2,1,0:T(8,128)(2,1)} %k_ref.1, f32[1,256]{1,0:T(1,128)} %bitcast.77, f32[1,256]{1,0:T(1,128)} %bitcast.78, f32[1,256]{1,0:T(1,128)} %bitcast.79), custom_call_target="tpu_custom_call" | custom-call | flops 25690112 | bytes 1321984 | tf_op jit(solution)/shard_map/pallas_call | solution.py:79
  34.0 8.2 %shard_map.137 = (bf16[1024,256]{1,0:T(8,128)(2,1)}, bf16[4,4,256]{2,1,0:T(4,128)(2,1)}) custom-call(bf16[1024,256]{1,0:T(8,128)(2,1)} %bitcast.72, bf16[1024,256]{1,0:T(8,128)(2,1)} %bitcast.71, bf16[256,1024]{1,0:T(8,128)(2,1)} %we_ref.1, f32[1,1024]{1,0:T(1,128)} %bitcast.80, bf16[1024,256]{1,0:T(8,128)(2,1)} %wr_ref.1, f32[1,256]{1,0:T(1,128)} %bitcast.81, ...), custom_call_target="tpu_custom_call" | custom-call | flops 1073741824 | bytes 2621440 | tf_op jit(solution)/shard_map/pallas_call | solution.py:157
  42.2 1.4 %broadcast_in_dim.7 = bf16[16,4,4,256]{3,2,1,0:T(4,128)(2,1)} broadcast(bf16[4,4,256]{2,1,0:T(4,128)(2,1)} %get-tuple-element.8), dimensions={1,2,3} | broadcast | bytes 139264 | tf_op jit(solution)/shard_map/broadcast_in_dim | solution.py:264
  43.6 6.5 %all-to-all-start = ((bf16[16,4,4,256]{3,2,1,0:T(4,128)(2,1)}), bf16[16,4,4,256]{3,2,1,0:T(4,128)(2,1)S(1)}, u32[]{:S(2)}, u32[]{:S(2)}) async-start(bf16[16,4,4,256]{3,2,1,0:T(4,128)(2,1)} %broadcast_in_dim.7), calls=%async_computation | async-start | bytes 262144 | tf_op jit(solution)/shard_map/all_to_all | solution.py:265
  50.2 0.8 %convolution_convert_fusion.2 = bf16[4,4,256]{2,1,0:T(4,128)(2,1)S(1)} fusion(bf16[4,4,256]{2,1,0:T(4,128)(2,1)} %get-tuple-element.8, bf16[256,256]{1,0:T(8,128)(2,1)S(1)} %copy-done.3), kind=kOutput, calls=%fused_computation.8 | convolution fusion | flops 2101248 | bytes 147456 | tf_op jit(solution)/shard_map/rcd,de->rce/dot_general | solution.py:258
  51.1 5.2 %all-to-all-done = bf16[16,4,4,256]{3,2,1,0:T(4,128)(2,1)S(1)} async-done(((bf16[16,4,4,256]{3,2,1,0:T(4,128)(2,1)}), bf16[16,4,4,256]{3,2,1,0:T(4,128)(2,1)S(1)}, u32[]{:S(2)}, u32[]{:S(2)}) %all-to-all-start) | async-done | bytes 131104 | tf_op jit(solution)/shard_map/all_to_all | solution.py:265
  56.4 0.2 convolution_convert_fusion
  56.8 0.1 fusion.3
  56.9 0.2 fusion.17
  57.2 0.3 fusion.4
  57.7 0.1 fusion.6
  57.9 0.4 copy-done.2
  58.3 1.0 %fusion.5 = bf16[32,32,256]{2,1,0:T(8,128)(2,1)} fusion(f32[32,32,256]{2,1,0:T(8,128)S(1)} %bitcast.70, bf16[32,32,256]{2,1,0:T(8,128)(2,1)S(1)} %bitcast.75), kind=kLoop, calls=%fused_computation.10 | loop fusion | flops 786432 | bytes 2097152 | tf_op jit(solution)/shard_map/convert_element_type | solution.py:305
  (30 shorter events, 1.0 us)
Async XLA Ops:
  0.0 56.4 %copy-start = (bf16[256,512]{1,0:T(8,128)(2,1)S(1)}, bf16[256,512]{1,0:T(8,128)(2,1)}, u32[]{:S(2)}) copy-start(bf16[256,512]{1,0:T(8,128)(2,1)} %param.25) | copy-start | bytes 786436
  0.9 9.3 %collective-permute-start = (bf16[3,32,256]{2,1,0:T(8,128)(2,1)S(1)}, bf16[3,32,256]{2,1,0:T(8,128)(2,1)S(1)}, u32[]{:S(2)}, u32[]{:S(2)}) collective-permute-start(bf16[3,32,256]{2,1,0:T(8,128)(2,1)S(1)} %get-tuple-element.11), channel_id=1, source_target_pairs={{0,16},{16,32},{32,48},{48,64},{64,80},{80,96},{96,112},{112,128},... | collective-permute-start | bytes 147464 | tf_op jit(solution)/shard_map/ppermute | solution.py:15
  5.4 8.4 %collective-permute-start.1 = (bf16[3,32,256]{2,1,0:T(8,128)(2,1)S(1)}, bf16[3,32,256]{2,1,0:T(8,128)(2,1)S(1)}, u32[]{:S(2)}, u32[]{:S(2)}) collective-permute-start(bf16[3,32,256]{2,1,0:T(8,128)(2,1)S(1)} %get-tuple-element.12), channel_id=1, source_target_pairs={{16,0},{32,16},{48,32},{64,48},{80,64},{96,80},{112,96},{128,112},... | collective-permute-start | bytes 147464 | tf_op jit(solution)/shard_map/ppermute | solution.py:15
  10.2 13.0 %copy-start.1 = (bf16[32,32,256]{2,1,0:T(8,128)(2,1)S(1)}, bf16[32,32,256]{2,1,0:T(8,128)(2,1)}, u32[]{:S(2)}) copy-start(bf16[32,32,256]{2,1,0:T(8,128)(2,1)} %param.14) | copy-start | bytes 1572868
  13.9 8.2 %collective-permute-start.3 = (bf16[38,3,256]{2,1,0:T(4,128)(2,1)S(1)}, bf16[38,3,256]{2,1,0:T(4,128)(2,1)S(1)}, u32[]{:S(2)}, u32[]{:S(2)}) collective-permute-start(bf16[38,3,256]{2,1,0:T(4,128)(2,1)S(1)} %pad_maximum_fusion.2), channel_id=1, source_target_pairs={{1,0},{2,1},{3,2},{4,3},{5,4},{6,5},{7,6},{8,7},{9,8},{10,9},{11,1... | collective-permute-start | bytes 175112 | tf_op jit(solution)/shard_map/ppermute | solution.py:15
  18.0 5.1 %collective-permute-start.2 = (bf16[38,3,256]{2,1,0:T(4,128)(2,1)S(1)}, bf16[38,3,256]{2,1,0:T(4,128)(2,1)S(1)}, u32[]{:S(2)}, u32[]{:S(2)}) collective-permute-start(bf16[38,3,256]{2,1,0:T(4,128)(2,1)S(1)} %pad_maximum_fusion.1), channel_id=1, source_target_pairs={{0,1},{1,2},{2,3},{3,4},{4,5},{5,6},{6,7},{7,8},{8,9},{9,10},{10,1... | collective-permute-start | bytes 175112 | tf_op jit(solution)/shard_map/ppermute | solution.py:15
  34.0 16.1 %copy-start.3 = (bf16[256,256]{1,0:T(8,128)(2,1)S(1)}, bf16[256,256]{1,0:T(8,128)(2,1)}, u32[]{:S(2)}) copy-start(bf16[256,256]{1,0:T(8,128)(2,1)} %param.24) | copy-start | bytes 393220
  43.6 12.7 %all-to-all-start = ((bf16[16,4,4,256]{3,2,1,0:T(4,128)(2,1)}), bf16[16,4,4,256]{3,2,1,0:T(4,128)(2,1)S(1)}, u32[]{:S(2)}, u32[]{:S(2)}) async-start(bf16[16,4,4,256]{3,2,1,0:T(4,128)(2,1)} %broadcast_in_dim.7), calls=%async_computation | async-start | bytes 262144 | tf_op jit(solution)/shard_map/all_to_all | solution.py:265
  56.7 1.0 %copy-start.4 = (bf16[256,256]{1,0:T(8,128)(2,1)S(1)}, bf16[256,256]{1,0:T(8,128)(2,1)}, u32[]{:S(2)}) copy-start(bf16[256,256]{1,0:T(8,128)(2,1)} %param.27) | copy-start | bytes 393220
  57.2 1.1 %copy-start.2 = (bf16[1024,256]{1,0:T(8,128)(2,1)S(1)}, bf16[1024,256]{1,0:T(8,128)(2,1)}, u32[]{:S(2)}) copy-start(bf16[1024,256]{1,0:T(8,128)(2,1)} %get-tuple-element.7) | copy-start | bytes 1572868

commit v7 on v6

--- a/solution.py
+++ b/solution.py
@@ -17,81 +17,89 @@
 
 def halo_pieces(features, width):
     rows, cols = features.shape[:2]
-    top, _ = shifted(features[rows - width :], "row")
-    _, bottom = shifted(features[:width], "row")
-    last_cols = jnp.concatenate(
-        [top[:, cols - width :], features[:, cols - width :], bottom[:, cols - width :]], axis=0
-    )
-    first_cols = jnp.concatenate([top[:, :width], features[:, :width], bottom[:, :width]], axis=0)
-    left, _ = shifted(last_cols, "col")
-    _, right = shifted(first_cols, "col")
-    return top, bottom, left, right
+    left, _ = shifted(features[:, cols - width :], "col")
+    _, right = shifted(features[:, :width], "col")
+    spare = -(cols + 2 * width) % 8
+    extended = jnp.concatenate([left, features, right, jnp.zeros_like(left)[:, :spare]], axis=1)
+    top, _ = shifted(extended[rows - width :], "row")
+    _, bottom = shifted(extended[:width], "row")
+    return extended, top, bottom
 
 TAPS = 7
 ROW_BLOCK = 8
 
 
 def conv_norm_kernel(x_ref, k_ref, db_ref, g_ref, nb_ref, o_ref, kf_ref, sh_ref):
-    rows_p = x_ref.shape[0]
-    tile_rows, tile_cols, channels = o_ref.shape
+    slabs, rows_in = x_ref.shape[:2]
+    n_out, tile_cols, channels = o_ref.shape[1:]
     for a in range(TAPS):
         kf_ref[a, pl.ds(0, TAPS), :] = k_ref[a].astype(jnp.float32)
-
-    def widen(r, carry):
-        row = x_ref[r].astype(jnp.float32)
-        for b in range(TAPS):
-            sh_ref[b, r] = row[b : b + tile_cols]
-        return carry
-
-    lax.fori_loop(0, rows_p, widen, 0)
     db = db_ref[...]
     g = g_ref[...]
     nb = nb_ref[...]
     lanes = 128
     halves = channels // lanes
 
-    def body(i, carry):
-        r0 = pl.multiple_of(i * ROW_BLOCK, ROW_BLOCK)
-        for s0 in range(0, tile_cols, 8):
-            parts = []
-            for h in range(halves):
-                lane = pl.ds(h * lanes, lanes)
-                acc = jnp.zeros((ROW_BLOCK, 8, lanes), jnp.float32)
-                for b in range(TAPS):
-                    x = sh_ref[b, pl.ds(r0, ROW_BLOCK + TAPS - 1), pl.ds(s0, 8), lane]
-                    for a in range(TAPS):
-                        acc = acc + x[a : a + ROW_BLOCK] * kf_ref[a, pl.ds(b, 1), lane]
-                parts.append(acc)
-            acc = jnp.concatenate(parts, axis=-1) + db
-            mean = jnp.mean(acc, axis=-1, keepdims=True)
-            cen = acc - mean
-            var = jnp.mean(cen * cen, axis=-1, keepdims=True)
-            normed = cen * lax.rsqrt(var + 1e-06) * g + nb
-            o_ref[pl.ds(r0, ROW_BLOCK), pl.ds(s0, 8), :] = normed.astype(o_ref.dtype)
-        return carry
-
-    lax.fori_loop(0, tile_rows // ROW_BLOCK, body, 0)
-
-
-def conv_norm(padded, dw_kernel, dw_bias, norm_gain, norm_bias, tile_rows, tile_cols):
-    rows_p, cols_p, channels = padded.shape
+    for slab in range(slabs):
+
+        def widen(r, carry):
+            row = x_ref[slab, r].astype(jnp.float32)
+            for b in range(TAPS):
+                sh_ref[b, r] = row[b : b + tile_cols]
+            return carry
+
+        lax.fori_loop(0, rows_in, widen, 0)
+
+        def rows_block(r0, count):
+            for s0 in range(0, tile_cols, 8):
+                parts = []
+                for h in range(halves):
+                    lane = pl.ds(h * lanes, lanes)
+                    acc = jnp.zeros((count, 8, lanes), jnp.float32)
+                    for b in range(TAPS):
+                        x = sh_ref[b, pl.ds(r0, count + TAPS - 1), pl.ds(s0, 8), lane]
+                        for a in range(TAPS):
+                            acc = acc + x[a : a + count] * kf_ref[a, pl.ds(b, 1), lane]
+                    parts.append(acc)
+                acc = jnp.concatenate(parts, axis=-1) + db
+                mean = jnp.mean(acc, axis=-1, keepdims=True)
+                cen = acc - mean
+                var = jnp.mean(cen * cen, axis=-1, keepdims=True)
+                normed = cen * lax.rsqrt(var + 1e-06) * g + nb
+                o_ref[slab, pl.ds(r0, count), pl.ds(s0, 8), :] = normed.astype(o_ref.dtype)
+
+        full = n_out // ROW_BLOCK
+
+        def body(i, carry):
+            rows_block(pl.multiple_of(i * ROW_BLOCK, ROW_BLOCK), ROW_BLOCK)
+            return carry
+
+        if full:
+            lax.fori_loop(0, full, body, 0)
+        if n_out % ROW_BLOCK:
+            rows_block(full * ROW_BLOCK, n_out % ROW_BLOCK)
+
+
+def conv_norm(slabs_in, dw_kernel, dw_bias, norm_gain, norm_bias, tile_cols):
+    slabs, rows_in, cols_p, channels = slabs_in.shape
+    n_out = rows_in - (TAPS - 1)
     vmem = pl.BlockSpec(memory_space=pltpu.VMEM)
     return pl.pallas_call(
         conv_norm_kernel,
-        out_shape=jax.ShapeDtypeStruct((tile_rows, tile_cols, channels), jnp.bfloat16),
+        out_shape=jax.ShapeDtypeStruct((slabs, n_out, tile_cols, channels), jnp.bfloat16),
         in_specs=[vmem] * 5,
         out_specs=vmem,
         scratch_shapes=[
             pltpu.VMEM((TAPS, 8, channels), jnp.float32),
-            pltpu.VMEM((TAPS, rows_p, tile_cols, channels), jnp.float32),
+            pltpu.VMEM((TAPS, rows_in, tile_cols, channels), jnp.float32),
         ],
         cost_estimate=pl.CostEstimate(
-            flops=2 * TAPS * TAPS * tile_rows * tile_cols * channels,
-            bytes_accessed=2 * (rows_p * cols_p + tile_rows * tile_cols) * channels,
-            transcendentals=tile_rows * tile_cols,
+            flops=2 * TAPS * TAPS * slabs * n_out * tile_cols * channels,
+            bytes_accessed=2 * slabs * (rows_in * cols_p + n_out * tile_cols) * channels,
+            transcendentals=slabs * n_out * tile_cols,
         ),
     )(
-        padded,
+        slabs_in,
         dw_kernel,
         dw_bias.reshape(1, channels),
         norm_gain.reshape(1, channels),
@@ -200,14 +208,17 @@
     layer_scale,
 ):
     tile_rows, tile_cols, channels = features.shape
-    top, bottom, left, right = pieces
-    extended = jnp.concatenate([top, features, bottom], axis=0)
-    padded = jnp.concatenate(
-        [left, extended, right, jnp.zeros_like(right)[:, : -(tile_cols + 3 * 3) % 8]], axis=1
-    )
-    normed = conv_norm(
-        padded, dw_kernel, dw_bias, norm_gain, norm_bias, tile_rows, tile_cols
-    ).reshape(-1, channels)
+    extended, top, bottom = pieces
+    reach = TAPS - 1
+    inner = conv_norm(extended[None], dw_kernel, dw_bias, norm_gain, norm_bias, tile_cols)
+    edge_in = jnp.stack(
+        [
+            jnp.concatenate([top, extended[:reach]], axis=0),
+            jnp.concatenate([extended[tile_rows - reach :], bottom], axis=0),
+        ]
+    )
+    edges = conv_norm(edge_in, dw_kernel, dw_bias, norm_gain, norm_bias, tile_cols)
+    normed = jnp.concatenate([edges[0], inner[0], edges[1]], axis=0).reshape(-1, channels)
     summed, pooled = mlp(
         normed,
         features.reshape(-1, channels),

time: 59.8 us -> 60.1 us (level)
  the two profiles are of different devices: /device:TPU:113 before, /device:TPU:129 now
where the time goes in v7:
time: 60.1 us; the launch traced here: 59.5 us
  starting transfers between devices  20.4 us (34%)
  Pallas kernels  19.5 us (32%)
  waiting for transfers between devices  6.98 us (12%)
  local copies, waits for them, and re-layouts  6.13 us (10%)
  other arithmetic  4.58 us (8%)
  matrix products  1.62 us (3%)
    ppermute x4, starting transfers between devices, shifted(): return (lax.ppermute(piece, axis, up), lax.ppermute(piece, axis, down))  14.6 us
    pallas_call x2, Pallas kernels, conv_norm(): pl.pallas_call(conv_norm_kernel, out_shape=jax.ShapeDtypeStruct((slabs, n...  11.3 us
    pallas_call x1, Pallas kernels, mlp(): pl.pallas_call(mlp_kernel, out_shape=(jax.ShapeDtypeStruct((pixels, chann...  8.23 us
    all_to_all x1, starting transfers between devices, shards(): band_pooled = lax.all_to_all(sent, 'col', 0, 0)  5.85 us
    all_to_all x1, waiting for transfers between devices, shards(): band_pooled = lax.all_to_all(sent, 'col', 0, 0)  5.23 us
    ppermute x4, waiting for transfers between devices, shifted(): return (lax.ppermute(piece, axis, up), lax.ppermute(piece, axis, down))  1.75 us
    another operation x1, local copies, waits for them, and re-layouts, shards(): rows_of.append(jnp.stack(per_col, axis=1))  1.44 us
    broadcast_in_dim x1, local copies, waits for them, and re-layouts, shards(): sent = jnp.broadcast_to(pooled[None], (columns,) + pooled.shape)  1.39 us
  transfers between devices with their start and end apart: 5, of which 2 were waited for; matrix products, arithmetic and copies ran while one was open for 7% of the time, Pallas kernels for 13%

profile of v7, /device:TPU:129, one launch (start us, length us, event | category | flops | bytes accessed | tf_op | source)
XLA Modules:
  0.0 59.5 jit_solution(9773119875146974177)
XLA Ops:
  0.0 1.1 %fusion.14 = (bf16[32,3,256]{2,1,0:T(4,128)(2,1)S(1)}, bf16[32,3,256]{2,1,0:T(4,128)(2,1)S(1)}) fusion(bf16[32,32,256]{2,1,0:T(8,128)(2,1)} %param.14), kind=kLoop, calls=%fused_computation.48 | loop fusion | bytes 196608 | tf_op jit(solution)/shard_map/slice | solution.py:20
  1.1 3.8 %collective-permute-start = (bf16[32,3,256]{2,1,0:T(4,128)(2,1)S(1)}, bf16[32,3,256]{2,1,0:T(4,128)(2,1)S(1)}, u32[]{:S(2)}, u32[]{:S(2)}) collective-permute-start(bf16[32,3,256]{2,1,0:T(4,128)(2,1)S(1)} %get-tuple-element.13), channel_id=1, source_target_pairs={{0,1},{1,2},{2,3},{3,4},{4,5},{5,6},{6,7},{7,8},{8,9},{9,10},{10,1... | collective-permute-start | bytes 147464 | tf_op jit(solution)/shard_map/ppermute | solution.py:15
  4.8 1.9 %collective-permute-start.1 = (bf16[32,3,256]{2,1,0:T(4,128)(2,1)S(1)}, bf16[32,3,256]{2,1,0:T(4,128)(2,1)S(1)}, u32[]{:S(2)}, u32[]{:S(2)}) collective-permute-start(bf16[32,3,256]{2,1,0:T(4,128)(2,1)S(1)} %get-tuple-element.14), channel_id=1, source_target_pairs={{1,0},{2,1},{3,2},{4,3},{5,4},{6,5},{7,6},{8,7},{9,8},{10,9},{11,1... | collective-permute-start | bytes 147464 | tf_op jit(solution)/shard_map/ppermute | solution.py:15
  6.8 1.4 %dynamic-slice_bitcast_fusion.15 = (f32[8,1,4,64]{3,0,2,1:T(8,128)S(1)}, f32[8,1,4,64]{3,0,2,1:T(8,128)S(1)}, f32[8,1,4,64]{3,0,2,1:T(8,128)S(1)}, f32[8,1,4,64]...) fusion(f32[8,7,127]{2,0,1:T(8,128)} %param.26, ...), kind=kLoop, calls=%fused_computation.44 | loop fusion | bytes 262172 | tf_op jit(solution)/shard_map/stack | solution.py:294
  8.4 0.2 reshape.73
  8.7 1.7 %collective-permute-done.1 = bf16[32,3,256]{2,1,0:T(4,128)(2,1)S(1)} collective-permute-done((bf16[32,3,256]{2,1,0:T(4,128)(2,1)S(1)}, bf16[32,3,256]{2,1,0:T(4,128)(2,1)S(1)}, u32[]{:S(2)}, u32[]{:S(2)}) %collective-permute-start.1) | collective-permute-done | bytes 49184 | tf_op jit(solution)/shard_map/ppermute | solution.py:15
  10.4 0.4 maximum_maximum_fusion
  10.9 4.5 %collective-permute-start.2 = (bf16[3,40,256]{2,1,0:T(8,128)(2,1)S(1)}, bf16[3,40,256]{2,1,0:T(8,128)(2,1)S(1)}, u32[]{:S(2)}, u32[]{:S(2)}) collective-permute-start(bf16[3,40,256]{2,1,0:T(8,128)(2,1)S(1)} %get-tuple-element.9), channel_id=1, source_target_pairs={{0,16},{16,32},{32,48},{48,64},{64,80},{80,96},{96,112},{112,128},... | collective-permute-start | bytes 184328 | tf_op jit(solution)/shard_map/ppermute | solution.py:15
  15.5 4.4 %collective-permute-start.3 = (bf16[3,40,256]{2,1,0:T(8,128)(2,1)S(1)}, bf16[3,40,256]{2,1,0:T(8,128)(2,1)S(1)}, u32[]{:S(2)}, u32[]{:S(2)}) collective-permute-start(bf16[3,40,256]{2,1,0:T(8,128)(2,1)S(1)} %get-tuple-element.10), channel_id=1, source_target_pairs={{16,0},{32,16},{48,32},{64,48},{80,64},{96,80},{112,96},{128,112},... | collective-permute-start | bytes 184328 | tf_op jit(solution)/shard_map/ppermute | solution.py:15
  19.8 1.3 %fusion.25.x_ref = bf16[1,32,40,256]{3,2,1,0:T(8,128)(2,1)} fusion(bf16[40]{0:T(256)(128)(2,1)S(1)} %pad.32.clone, bf16[32,3,256]{2,1,0:T(4,128)(2,1)S(1)} %collective-permute-done.1, bf16[32,32,256]{2,1,0:T(8,128)(2,1)S(1)} %copy-done.1, bf16[32,3,256]{2,1,0:T(4,128)(2,1)S(1)} %collective-permute-done), kind=kLoop, calls=%fused_computation.51 | loop fusion | flops 2621440 | bytes 1278032 | tf_op jit(solution)/shard_map/broadcast_in_dim | solution.py:213
  21.1 8.0 %shard_map.137 = bf16[1,26,32,256]{3,2,1,0:T(8,128)(2,1)} custom-call(bf16[1,32,40,256]{3,2,1,0:T(8,128)(2,1)} %fusion.25.x_ref, bf16[7,7,256]{2,1,0:T(8,128)(2,1)} %k_ref.3, f32[1,256]{1,0:T(1,128)} %bitcast.89, f32[1,256]{1,0:T(1,128)} %bitcast.91, f32[1,256]{1,0:T(1,128)} %bitcast.93), custom_call_target="tpu_custom_call" | custom-call | flops 20873216 | bytes 1081344 | tf_op jit(solution)/shard_map/pallas_call | solution.py:87
  29.2 0.8 %pad_maximum_fusion.1.x_ref = bf16[2,9,40,256]{3,2,1,0:T(8,128)(2,1)} fusion(bf16[1,9,40,256]{3,2,1,0:T(8,128)(2,1)S(1)} %maximum_bitcast_fusion.1, bf16[1,9,40,256]{3,2,1,0:T(8,128)(2,1)S(1)} %maximum_bitcast_fusion), kind=kLoop, calls=%fused_computation.13 | loop fusion | flops 184320 | bytes 737280 | tf_op jit(solution)/shard_map/stack | solution.py:214
  29.9 3.3 %shard_map.136 = bf16[2,3,32,256]{3,2,1,0:T(8,128)(2,1)} custom-call(bf16[2,9,40,256]{3,2,1,0:T(8,128)(2,1)} %pad_maximum_fusion.1.x_ref, bf16[7,7,256]{2,1,0:T(8,128)(2,1)} %k_ref.3, f32[1,256]{1,0:T(1,128)} %bitcast.90, f32[1,256]{1,0:T(1,128)} %bitcast.92, f32[1,256]{1,0:T(1,128)} %bitcast.94), custom_call_target="tpu_custom_call" | custom-call | flops 4816896 | bytes 466944 | tf_op jit(solution)/shard_map/pallas_call | solution.py:87
  33.2 0.8 %slice_bitcast_fusion.1 = (bf16[3,32,256]{2,1,0:T(8,128)(2,1)S(1)}, bf16[3,32,256]{2,1,0:T(8,128)(2,1)S(1)}) fusion(bf16[2,3,32,256]{3,2,1,0:T(8,128)(2,1)} %shard_map.136), kind=kLoop, calls=%fused_computation.27 | loop fusion | bytes 196608 | tf_op jit(solution)/shard_map/squeeze | solution.py:221
  34.0 0.9 %pad_maximum_fusion = bf16[32,32,256]{2,1,0:T(8,128)(2,1)} fusion(bf16[3,32,256]{2,1,0:T(8,128)(2,1)S(1)} %get-tuple-element.18, bf16[26,32,256]{2,1,0:T(8,128)(2,1)S(1)} %bitcast.83, bf16[3,32,256]{2,1,0:T(8,128)(2,1)S(1)} %get-tuple-element.17), kind=kLoop, calls=%fused_computation.12 | loop fusion | flops 524288 | bytes 1048576 | tf_op jit(solution)/shard_map/concatenate | solution.py:221
  34.9 8.2 %shard_map.138 = (bf16[1024,256]{1,0:T(8,128)(2,1)}, bf16[4,4,256]{2,1,0:T(4,128)(2,1)}) custom-call(bf16[1024,256]{1,0:T(8,128)(2,1)} %bitcast.84, bf16[1024,256]{1,0:T(8,128)(2,1)} %bitcast.82, bf16[256,1024]{1,0:T(8,128)(2,1)} %we_ref.1, f32[1,1024]{1,0:T(1,128)} %bitcast.95, bf16[1024,256]{1,0:T(8,128)(2,1)} %wr_ref.1, f32[1,256]{1,0:T(1,128)} %bitcast.96, ...), custom_call_target="tpu_custom_call" | custom-call | flops 1073741824 | bytes 2621440 | tf_op jit(solution)/shard_map/pallas_call | solution.py:165
  43.1 1.4 %broadcast_in_dim.7 = bf16[16,4,4,256]{3,2,1,0:T(4,128)(2,1)} broadcast(bf16[4,4,256]{2,1,0:T(4,128)(2,1)} %get-tuple-element.8), dimensions={1,2,3} | broadcast | bytes 139264 | tf_op jit(solution)/shard_map/broadcast_in_dim | solution.py:275
  44.5 5.8 %all-to-all-start = ((bf16[16,4,4,256]{3,2,1,0:T(4,128)(2,1)}), bf16[16,4,4,256]{3,2,1,0:T(4,128)(2,1)S(1)}, u32[]{:S(2)}, u32[]{:S(2)}) async-start(bf16[16,4,4,256]{3,2,1,0:T(4,128)(2,1)} %broadcast_in_dim.7), calls=%async_computation | async-start | bytes 262144 | tf_op jit(solution)/shard_map/all_to_all | solution.py:276
  50.4 0.8 %convolution_convert_fusion.2 = bf16[4,4,256]{2,1,0:T(4,128)(2,1)S(1)} fusion(bf16[4,4,256]{2,1,0:T(4,128)(2,1)} %get-tuple-element.8, bf16[256,256]{1,0:T(8,128)(2,1)S(1)} %copy-done.4), kind=kOutput, calls=%fused_computation.8 | convolution fusion | flops 2101248 | bytes 147456 | tf_op jit(solution)/shard_map/rcd,de->rce/dot_general | solution.py:269
  51.3 5.2 %all-to-all-done = bf16[16,4,4,256]{3,2,1,0:T(4,128)(2,1)S(1)} async-done(((bf16[16,4,4,256]{3,2,1,0:T(4,128)(2,1)}), bf16[16,4,4,256]{3,2,1,0:T(4,128)(2,1)S(1)}, u32[]{:S(2)}, u32[]{:S(2)}) %all-to-all-start) | async-done | bytes 131104 | tf_op jit(solution)/shard_map/all_to_all | solution.py:276
  56.6 0.2 convolution_convert_fusion
  57.5 0.3 fusion.4
  58.1 0.4 copy-done.3
  58.5 1.0 %fusion.5 = bf16[32,32,256]{2,1,0:T(8,128)(2,1)} fusion(f32[32,32,256]{2,1,0:T(8,128)S(1)} %bitcast.81, bf16[32,32,256]{2,1,0:T(8,128)(2,1)S(1)} %bitcast.87), kind=kLoop, calls=%fused_computation.10 | loop fusion | flops 786432 | bytes 2097152 | tf_op jit(solution)/shard_map/convert_element_type | solution.py:316
  (36 shorter events, 1.4 us)
Async XLA Ops:
  0.0 56.6 %copy-start = (bf16[256,512]{1,0:T(8,128)(2,1)S(1)}, bf16[256,512]{1,0:T(8,128)(2,1)}, u32[]{:S(2)}) copy-start(bf16[256,512]{1,0:T(8,128)(2,1)} %param.25) | copy-start | bytes 786436
  1.1 7.6 %collective-permute-start = (bf16[32,3,256]{2,1,0:T(4,128)(2,1)S(1)}, bf16[32,3,256]{2,1,0:T(4,128)(2,1)S(1)}, u32[]{:S(2)}, u32[]{:S(2)}) collective-permute-start(bf16[32,3,256]{2,1,0:T(4,128)(2,1)S(1)} %get-tuple-element.13), channel_id=1, source_target_pairs={{0,1},{1,2},{2,3},{3,4},{4,5},{5,6},{6,7},{7,8},{8,9},{9,10},{10,1... | collective-permute-start | bytes 147464 | tf_op jit(solution)/shard_map/ppermute | solution.py:15
  4.8 5.6 %collective-permute-start.1 = (bf16[32,3,256]{2,1,0:T(4,128)(2,1)S(1)}, bf16[32,3,256]{2,1,0:T(4,128)(2,1)S(1)}, u32[]{:S(2)}, u32[]{:S(2)}) collective-permute-start(bf16[32,3,256]{2,1,0:T(4,128)(2,1)S(1)} %get-tuple-element.14), channel_id=1, source_target_pairs={{1,0},{2,1},{3,2},{4,3},{5,4},{6,5},{7,6},{8,7},{9,8},{10,9},{11,1... | collective-permute-start | bytes 147464 | tf_op jit(solution)/shard_map/ppermute | solution.py:15
  8.2 2.2 %copy-start.1 = (bf16[32,32,256]{2,1,0:T(8,128)(2,1)S(1)}, bf16[32,32,256]{2,1,0:T(8,128)(2,1)}, u32[]{:S(2)}) copy-start(bf16[32,32,256]{2,1,0:T(8,128)(2,1)} %param.14) | copy-start | bytes 1572868
  10.9 18.2 %collective-permute-start.2 = (bf16[3,40,256]{2,1,0:T(8,128)(2,1)S(1)}, bf16[3,40,256]{2,1,0:T(8,128)(2,1)S(1)}, u32[]{:S(2)}, u32[]{:S(2)}) collective-permute-start(bf16[3,40,256]{2,1,0:T(8,128)(2,1)S(1)} %get-tuple-element.9), channel_id=1, source_target_pairs={{0,16},{16,32},{32,48},{48,64},{64,80},{80,96},{96,112},{112,128},... | collective-permute-start | bytes 184328 | tf_op jit(solution)/shard_map/ppermute | solution.py:15
  15.5 13.7 %collective-permute-start.3 = (bf16[3,40,256]{2,1,0:T(8,128)(2,1)S(1)}, bf16[3,40,256]{2,1,0:T(8,128)(2,1)S(1)}, u32[]{:S(2)}, u32[]{:S(2)}) collective-permute-start(bf16[3,40,256]{2,1,0:T(8,128)(2,1)S(1)} %get-tuple-element.10), channel_id=1, source_target_pairs={{16,0},{32,16},{48,32},{64,48},{80,64},{96,80},{112,96},{128,112},... | collective-permute-start | bytes 184328 | tf_op jit(solution)/shard_map/ppermute | solution.py:15
  29.1 4.9 %copy-start.2 = (bf16[1,26,32,256]{3,2,1,0:T(8,128)(2,1)S(1)}, bf16[1,26,32,256]{3,2,1,0:T(8,128)(2,1)}, u32[]{:S(2)}) copy-start(bf16[1,26,32,256]{3,2,1,0:T(8,128)(2,1)} %shard_map.137) | copy-start | bytes 1277956
  34.9 15.5 %copy-start.4 = (bf16[256,256]{1,0:T(8,128)(2,1)S(1)}, bf16[256,256]{1,0:T(8,128)(2,1)}, u32[]{:S(2)}) copy-start(bf16[256,256]{1,0:T(8,128)(2,1)} %param.24) | copy-start | bytes 393220
  44.5 12.0 %all-to-all-start = ((bf16[16,4,4,256]{3,2,1,0:T(4,128)(2,1)}), bf16[16,4,4,256]{3,2,1,0:T(4,128)(2,1)S(1)}, u32[]{:S(2)}, u32[]{:S(2)}) async-start(bf16[16,4,4,256]{3,2,1,0:T(4,128)(2,1)} %broadcast_in_dim.7), calls=%async_computation | async-start | bytes 262144 | tf_op jit(solution)/shard_map/all_to_all | solution.py:276
  56.9 1.0 %copy-start.5 = (bf16[256,256]{1,0:T(8,128)(2,1)S(1)}, bf16[256,256]{1,0:T(8,128)(2,1)}, u32[]{:S(2)}) copy-start(bf16[256,256]{1,0:T(8,128)(2,1)} %param.27) | copy-start | bytes 393220
  57.4 1.1 %copy-start.3 = (bf16[1024,256]{1,0:T(8,128)(2,1)S(1)}, bf16[1024,256]{1,0:T(8,128)(2,1)}, u32[]{:S(2)}) copy-start(bf16[1024,256]{1,0:T(8,128)(2,1)} %get-tuple-element.7) | copy-start | bytes 1572868

commit v8 on v6

--- a/solution.py
+++ b/solution.py
@@ -31,19 +31,29 @@
 ROW_BLOCK = 8
 
 
-def conv_norm_kernel(x_ref, k_ref, db_ref, g_ref, nb_ref, o_ref, kf_ref, sh_ref):
-    rows_p = x_ref.shape[0]
+def conv_norm_kernel(
+    c_ref, t_ref, b_ref, l_ref, r_ref, k_ref, db_ref, g_ref, nb_ref, o_ref, kf_ref, sh_ref
+):
     tile_rows, tile_cols, channels = o_ref.shape
+    halo = t_ref.shape[0]
+    rows_p = tile_rows + 2 * halo
     for a in range(TAPS):
         kf_ref[a, pl.ds(0, TAPS), :] = k_ref[a].astype(jnp.float32)
 
-    def widen(r, carry):
-        row = x_ref[r].astype(jnp.float32)
+    def put(r, mid):
+        row = jnp.concatenate([l_ref[r], mid, r_ref[r]], axis=0).astype(jnp.float32)
         for b in range(TAPS):
             sh_ref[b, r] = row[b : b + tile_cols]
+
+    for r in range(halo):
+        put(r, t_ref[r])
+        put(rows_p - halo + r, b_ref[r])
+
+    def widen(r, carry):
+        put(r, c_ref[r - halo])
         return carry
 
-    lax.fori_loop(0, rows_p, widen, 0)
+    lax.fori_loop(halo, rows_p - halo, widen, 0)
     db = db_ref[...]
     g = g_ref[...]
     nb = nb_ref[...]
@@ -73,13 +83,14 @@
     lax.fori_loop(0, tile_rows // ROW_BLOCK, body, 0)
 
 
-def conv_norm(padded, dw_kernel, dw_bias, norm_gain, norm_bias, tile_rows, tile_cols):
-    rows_p, cols_p, channels = padded.shape
+def conv_norm(centre, top, bottom, left, right, dw_kernel, dw_bias, norm_gain, norm_bias):
+    tile_rows, tile_cols, channels = centre.shape
+    rows_p = tile_rows + 2 * top.shape[0]
     vmem = pl.BlockSpec(memory_space=pltpu.VMEM)
     return pl.pallas_call(
         conv_norm_kernel,
         out_shape=jax.ShapeDtypeStruct((tile_rows, tile_cols, channels), jnp.bfloat16),
-        in_specs=[vmem] * 5,
+        in_specs=[vmem] * 9,
         out_specs=vmem,
         scratch_shapes=[
             pltpu.VMEM((TAPS, 8, channels), jnp.float32),
@@ -87,17 +98,20 @@
         ],
         cost_estimate=pl.CostEstimate(
             flops=2 * TAPS * TAPS * tile_rows * tile_cols * channels,
-            bytes_accessed=2 * (rows_p * cols_p + tile_rows * tile_cols) * channels,
+            bytes_accessed=2 * (rows_p * rows_p + tile_rows * tile_cols) * channels,
             transcendentals=tile_rows * tile_cols,
         ),
     )(
-        padded,
+        centre,
+        top,
+        bottom,
+        left,
+        right,
         dw_kernel,
         dw_bias.reshape(1, channels),
         norm_gain.reshape(1, channels),
         norm_bias.reshape(1, channels),
     )
-
 
 ERFC_COEFFS = (
     -1.26551223,
@@ -126,7 +140,7 @@
     return 0.5 * pre * one_plus_erf
 
 
-def mlp_kernel(n_ref, f_ref, we_ref, be_ref, wr_ref, br_ref, ls_ref, o_ref, p_ref):
+def mlp_kernel(n_ref, f_ref, we_ref, be_ref, wr_ref, br_ref, ls_ref, wq_ref, o_ref, q_ref, s_ref):
     normed = n_ref[...]
     hidden_total = we_ref.shape[1]
     acc = jnp.zeros(o_ref.shape, jnp.float32)
@@ -142,23 +156,36 @@
     o_ref[...] = out
     pixels, channels = o_ref.shape
     tile_cols = pixels // 8
+    per_row = tile_cols // 8
     column_sums = out.astype(jnp.float32).reshape(8, tile_cols, channels).sum(axis=0)
-    region_sums = column_sums.reshape(tile_cols // 8, 8, channels).sum(axis=1)
-    p_ref[0] = (region_sums * jnp.float32(1.0 / 64.0)).astype(p_ref.dtype)
-
-
-def mlp(normed, features, w_expand, b_expand, w_reduce, b_reduce, layer_scale, tile_cols):
+    region_sums = column_sums.reshape(per_row, 8, channels).sum(axis=1)
+    pooled = (region_sums * jnp.float32(1.0 / 64.0)).astype(jnp.bfloat16)
+    queries = jnp.dot(pooled, wq_ref[...], preferred_element_type=jnp.float32)
+    queries = queries.astype(jnp.bfloat16).astype(jnp.float32)
+    copies = jnp.broadcast_to(pooled.astype(jnp.float32)[None], (s_ref.shape[0], per_row, channels))
+    step = pl.program_id(0)
+    for k in range(s_ref.shape[1] // per_row):
+
+        @pl.when(step == k)
+        def _():
+            q_ref[pl.ds(k * per_row, per_row), :] = queries
+            s_ref[:, pl.ds(k * per_row, per_row), :] = copies
+
+
+def mlp(normed, features, w_expand, b_expand, w_reduce, b_reduce, layer_scale, w_query, tile_cols, copies):
     pixels, channels = normed.shape
     hidden_total = w_expand.shape[1]
     block = 8 * tile_cols
     steps = pixels // block
+    tokens = steps * (tile_cols // 8)
     rows = pl.BlockSpec((block, channels), lambda i: (i, 0))
-    whole = lambda shape: pl.BlockSpec(shape, lambda i: (0, 0))
+    whole = lambda shape: pl.BlockSpec(shape, lambda i: (0,) * len(shape))
     return pl.pallas_call(
         mlp_kernel,
         out_shape=(
             jax.ShapeDtypeStruct((pixels, channels), jnp.bfloat16),
-            jax.ShapeDtypeStruct((steps, tile_cols // 8, channels), jnp.bfloat16),
+            jax.ShapeDtypeStruct((tokens, channels), jnp.float32),
+            jax.ShapeDtypeStruct((copies, tokens, channels), jnp.float32),
         ),
         grid=(steps,),
         in_specs=[
@@ -169,8 +196,9 @@
             whole((hidden_total, channels)),
             whole((1, channels)),
             whole((1, channels)),
+            whole((channels, channels)),
         ],
-        out_specs=(rows, pl.BlockSpec((1, tile_cols // 8, channels), lambda i: (i, 0, 0))),
+        out_specs=(rows, whole((tokens, channels)), whole((copies, tokens, channels))),
         cost_estimate=pl.CostEstimate(
             flops=4 * pixels * channels * hidden_total,
             bytes_accessed=2 * (3 * pixels * channels + 2 * channels * hidden_total),
@@ -184,6 +212,7 @@
         w_reduce,
         b_reduce.reshape(1, channels),
         layer_scale.reshape(1, channels),
+        w_query,
     )
 
 def block_pass(
@@ -198,17 +227,14 @@
     w_reduce,
     b_reduce,
     layer_scale,
+    w_query,
+    copies,
 ):
     tile_rows, tile_cols, channels = features.shape
-    top, bottom, left, right = pieces
-    extended = jnp.concatenate([top, features, bottom], axis=0)
-    padded = jnp.concatenate(
-        [left, extended, right, jnp.zeros_like(right)[:, : -(tile_cols + 3 * 3) % 8]], axis=1
-    )
-    normed = conv_norm(
-        padded, dw_kernel, dw_bias, norm_gain, norm_bias, tile_rows, tile_cols
-    ).reshape(-1, channels)
-    summed, pooled = mlp(
+    normed = conv_norm(features, *pieces, dw_kernel, dw_bias, norm_gain, norm_bias).reshape(
+        -1, channels
+    )
+    summed, queries, sent = mlp(
         normed,
         features.reshape(-1, channels),
         w_expand,
@@ -216,9 +242,11 @@
         w_reduce,
         b_reduce,
         layer_scale,
+        w_query,
         tile_cols,
-    )
-    return summed.reshape(tile_rows, tile_cols, channels), pooled
+        copies,
+    )
+    return summed.reshape(tile_rows, tile_cols, channels), queries, sent
 
 
 def shards(
@@ -240,7 +268,9 @@
     tile_rows, tile_cols, channels = features.shape
     head_dim = channels // HEADS
     pieces = halo_pieces(features, 3)
-    block_out, pooled = block_pass(
+    columns = lax.axis_size("col")
+    position = lax.axis_index("col")
+    block_out, queries, sent = block_pass(
         pieces,
         features,
         dw_kernel,
@@ -252,21 +282,20 @@
         w_reduce,
         b_reduce,
         layer_scale,
+        w_query,
+        columns,
     )
     region_side = tile_rows // 8
     local_count = region_side * region_side
-    queries = jnp.einsum("rcd,de->rce", pooled, w_query, preferred_element_type=jnp.float32)
-    queries = queries.astype(jnp.bfloat16).reshape(local_count, channels)
-    columns = lax.axis_size("col")
-    position = lax.axis_index("col")
+    queries = queries.astype(jnp.bfloat16)
     span_cols = region_side * columns
     key_count = local_count * columns
-    sent = jnp.broadcast_to(pooled[None], (columns,) + pooled.shape)
     band_pooled = lax.all_to_all(sent, "col", 0, 0)
     band_pooled = (
         band_pooled.reshape(columns, region_side, region_side, channels)
         .transpose(1, 0, 2, 3)
         .reshape(key_count, channels)
+        .astype(jnp.bfloat16)
     )
     band_keyval = jnp.dot(band_pooled, w_keyval, preferred_element_type=jnp.float32).astype(
         jnp.bfloat16

time: 59.8 us -> 62.6 us (1.047)
  the two profiles are of different devices: /device:TPU:113 before, /device:TPU:129 now
where the time goes in v8:
time: 62.6 us; the launch traced here: 62 us
  starting transfers between devices  19.7 us (31%)
  Pallas kernels  18.5 us (30%)
  waiting for transfers between devices  13 us (21%)
  local copies, waits for them, and re-layouts  6.82 us (11%)
  other arithmetic  2.94 us (5%)
  matrix products  0.8 us (1%)
    ppermute x4, starting transfers between devices, shifted(): return (lax.ppermute(piece, axis, up), lax.ppermute(piece, axis, down))  13 us
    pallas_call x1, Pallas kernels, conv_norm(): pl.pallas_call(conv_norm_kernel, out_shape=jax.ShapeDtypeStruct((tile_row...  9.59 us
    pallas_call x1, Pallas kernels, mlp(): pl.pallas_call(mlp_kernel, out_shape=(jax.ShapeDtypeStruct((pixels, chann...  8.88 us
    ppermute x4, waiting for transfers between devices, shifted(): return (lax.ppermute(piece, axis, up), lax.ppermute(piece, axis, down))  7.79 us
    all_to_all x1, starting transfers between devices, shards(): band_pooled = lax.all_to_all(sent, 'col', 0, 0)  6.74 us
    all_to_all x1, waiting for transfers between devices, shards(): band_pooled = lax.all_to_all(sent, 'col', 0, 0)  5.23 us
    unnamed x18, local copies, waits for them, and re-layouts  3.82 us
    unnamed x1, other arithmetic  1.62 us
  transfers between devices with their start and end apart: 5, of which 3 were waited for; matrix products, arithmetic and copies ran while one was open for 3% of the time, Pallas kernels for 0%

profile of v8, /device:TPU:129, one launch (start us, length us, event | category | flops | bytes accessed | tf_op | source)
XLA Modules:
  0.0 62.0 jit_solution(2410177867211061667)
XLA Ops:
  0.0 0.9 %fusion.12 = (bf16[3,32,256]{2,1,0:T(8,128)(2,1)S(1)}, bf16[3,32,256]{2,1,0:T(8,128)(2,1)S(1)}) fusion(bf16[32,32,256]{2,1,0:T(8,128)(2,1)} %c_ref.1), kind=kLoop, calls=%fused_computation.41 | loop fusion | bytes 196608 | tf_op jit(solution)/shard_map/slice | solution.py:21
  0.9 4.4 %collective-permute-start.1 = (bf16[3,32,256]{2,1,0:T(8,128)(2,1)S(1)}, bf16[3,32,256]{2,1,0:T(8,128)(2,1)S(1)}, u32[]{:S(2)}, u32[]{:S(2)}) collective-permute-start(bf16[3,32,256]{2,1,0:T(8,128)(2,1)S(1)} %get-tuple-element.13), channel_id=1, source_target_pairs={{16,0},{32,16},{48,32},{64,48},{80,64},{96,80},{112,96},{128,112},... | collective-permute-start | bytes 147464 | tf_op jit(solution)/shard_map/ppermute | solution.py:15
  5.2 2.4 %collective-permute-start = (bf16[3,32,256]{2,1,0:T(8,128)(2,1)S(1)}, bf16[3,32,256]{2,1,0:T(8,128)(2,1)S(1)}, u32[]{:S(2)}, u32[]{:S(2)}) collective-permute-start(bf16[3,32,256]{2,1,0:T(8,128)(2,1)S(1)} %get-tuple-element.14), channel_id=1, source_target_pairs={{0,16},{16,32},{32,48},{48,64},{64,80},{80,96},{96,112},{112,128},... | collective-permute-start | bytes 147464 | tf_op jit(solution)/shard_map/ppermute | solution.py:15
  7.7 1.0 %fusion.11 = (bf16[32,3,256]{2,1,0:T(4,128)(2,1)S(1)}, bf16[32,3,256]{2,1,0:T(4,128)(2,1)S(1)}) fusion(bf16[32,32,256]{2,1,0:T(8,128)(2,1)} %c_ref.1), kind=kLoop, calls=%fused_computation.40 | loop fusion | bytes 196608 | tf_op jit(solution)/shard_map/slice | solution.py:25
  8.7 0.7 %copy-done.1 = f32[8,7,127]{2,0,1:T(8,128)S(1)} copy-done((f32[8,7,127]{2,0,1:T(8,128)S(1)}, f32[8,7,127]{2,0,1:T(8,128)}, u32[]{:S(2)}) %copy-start.1) | copy-done | bytes 28472
  9.6 4.0 %collective-permute-done.t_ref = bf16[3,32,256]{2,1,0:T(8,128)(2,1)S(1)} collective-permute-done((bf16[3,32,256]{2,1,0:T(8,128)(2,1)S(1)}, bf16[3,32,256]{2,1,0:T(8,128)(2,1)S(1)}, u32[]{:S(2)}, u32[]{:S(2)}) %collective-permute-start) | collective-permute-done | bytes 49184 | tf_op jit(solution)/shard_map/ppermute | solution.py:15
  13.8 0.5 copy-done.7
  14.3 4.3 %collective-permute-start.2 = (bf16[38,3,256]{2,1,0:T(4,128)(2,1)S(1)}, bf16[38,3,256]{2,1,0:T(4,128)(2,1)S(1)}, u32[]{:S(2)}, u32[]{:S(2)}) collective-permute-start(bf16[38,3,256]{2,1,0:T(4,128)(2,1)S(1)} %pad_maximum_fusion.1), channel_id=1, source_target_pairs={{0,1},{1,2},{2,3},{3,4},{4,5},{5,6},{6,7},{7,8},{8,9},{9,10},{10,1... | collective-permute-start | bytes 175112 | tf_op jit(solution)/shard_map/ppermute | solution.py:15
  18.7 1.9 %collective-permute-start.3 = (bf16[38,3,256]{2,1,0:T(4,128)(2,1)S(1)}, bf16[38,3,256]{2,1,0:T(4,128)(2,1)S(1)}, u32[]{:S(2)}, u32[]{:S(2)}) collective-permute-start(bf16[38,3,256]{2,1,0:T(4,128)(2,1)S(1)} %pad_maximum_fusion.2), channel_id=1, source_target_pairs={{1,0},{2,1},{3,2},{4,3},{5,4},{6,5},{7,6},{8,7},{9,8},{10,9},{11,1... | collective-permute-start | bytes 175112 | tf_op jit(solution)/shard_map/ppermute | solution.py:15
  20.6 3.7 %collective-permute-done.3.r_ref = bf16[38,3,256]{2,1,0:T(4,128)(2,1)S(1)} collective-permute-done((bf16[38,3,256]{2,1,0:T(4,128)(2,1)S(1)}, bf16[38,3,256]{2,1,0:T(4,128)(2,1)S(1)}, u32[]{:S(2)}, u32[]{:S(2)}) %collective-permute-start.3) | collective-permute-done | bytes 58400 | tf_op jit(solution)/shard_map/ppermute | solution.py:15
  24.4 0.6 %copy-done.5 = bf16[38,3,256]{2,1,0:T(4,128)(2,1)} copy-done((bf16[38,3,256]{2,1,0:T(4,128)(2,1)}, bf16[38,3,256]{2,1,0:T(4,128)(2,1)S(1)}, u32[]{:S(2)}) %copy-start.5) | copy-done | bytes 58392
  25.0 9.6 %shard_map.136 = bf16[32,32,256]{2,1,0:T(8,128)(2,1)} custom-call(bf16[32,32,256]{2,1,0:T(8,128)(2,1)} %c_ref.1, bf16[3,32,256]{2,1,0:T(8,128)(2,1)} %copy-done.7, bf16[3,32,256]{2,1,0:T(8,128)(2,1)} %copy-done.6, bf16[38,3,256]{2,1,0:T(4,128)(2,1)} %copy-done.4, bf16[38,3,256]{2,1,0:T(4,128)(2,1)} %copy-done.5, bf16[7,7,256]{2,1,0:T(8,128)(2,1)} %k_ref.1, ...), custom_call_target="tpu_custom_call" | custom-call | flops 25690112 | bytes 1263616 | tf_op jit(solution)/shard_map/pallas_call | solution.py:90
  34.6 8.9 %shard_map.137 = (bf16[1024,256]{1,0:T(8,128)(2,1)}, f32[16,256]{1,0:T(8,128)}, f32[16,16,256]{2,1,0:T(8,128)}) custom-call(bf16[1024,256]{1,0:T(8,128)(2,1)} %bitcast.70, bf16[1024,256]{1,0:T(8,128)(2,1)} %bitcast.69, bf16[256,1024]{1,0:T(8,128)(2,1)} %we_ref.1, f32[1,1024]{1,0:T(1,128)} %bitcast.78, bf16[1024,256]{1,0:T(8,128)(2,1)} %wr_ref.1, ...), custom_call_target="tpu_custom_call" | custom-call | flops 1073741824 | bytes 2621440 | tf_op jit(solution)/shard_map/pallas_call | solution.py:183
  43.5 1.6 %convert.5 = bf16[16,16,256]{2,1,0:T(8,128)(2,1)} convert(f32[16,16,256]{2,1,0:T(8,128)} %get-tuple-element.9) | non-fusion elementwise | flops 65536 | bytes 393216
  45.1 6.7 %all-to-all-start = ((bf16[16,16,256]{2,1,0:T(8,128)(2,1)}), bf16[16,16,256]{2,1,0:T(8,128)(2,1)S(1)}, u32[]{:S(2)}, u32[]{:S(2)}) async-start(bf16[16,16,256]{2,1,0:T(8,128)(2,1)} %convert.5), calls=%async_computation | async-start | bytes 262144 | tf_op jit(solution)/shard_map/all_to_all | solution.py:293
  52.0 0.2 reshape.73
  52.2 0.5 copy-done.8
  52.8 5.2 %all-to-all-done = bf16[16,16,256]{2,1,0:T(8,128)(2,1)S(1)} async-done(((bf16[16,16,256]{2,1,0:T(8,128)(2,1)}), bf16[16,16,256]{2,1,0:T(8,128)(2,1)S(1)}, u32[]{:S(2)}, u32[]{:S(2)}) %all-to-all-start) | async-done | bytes 131104 | tf_op jit(solution)/shard_map/all_to_all | solution.py:293
  58.2 0.2 convolution_convert_fusion
  58.7 0.2 fusion.16
  59.0 0.3 fusion.4
  59.4 0.5 copy-done.3
  60.1 0.9 %copy-done.2 = bf16[1024,256]{1,0:T(8,128)(2,1)S(1)} copy-done((bf16[1024,256]{1,0:T(8,128)(2,1)S(1)}, bf16[1024,256]{1,0:T(8,128)(2,1)}, u32[]{:S(2)}) %copy-start.2) | copy-done | bytes 524312
  61.1 1.0 %fusion.5 = bf16[32,32,256]{2,1,0:T(8,128)(2,1)} fusion(f32[32,32,256]{2,1,0:T(8,128)S(1)} %bitcast.68, bf16[32,32,256]{2,1,0:T(8,128)(2,1)S(1)} %bitcast.73), kind=kLoop, calls=%fused_computation.9 | loop fusion | flops 786432 | bytes 2097152 | tf_op jit(solution)/shard_map/convert_element_type | solution.py:334
  (36 shorter events, 1.4 us)
Async XLA Ops:
  0.0 58.2 %copy-start = (bf16[256,512]{1,0:T(8,128)(2,1)S(1)}, bf16[256,512]{1,0:T(8,128)(2,1)}, u32[]{:S(2)}) copy-start(bf16[256,512]{1,0:T(8,128)(2,1)} %param.25) | copy-start | bytes 786436
  0.9 8.7 %collective-permute-start.1 = (bf16[3,32,256]{2,1,0:T(8,128)(2,1)S(1)}, bf16[3,32,256]{2,1,0:T(8,128)(2,1)S(1)}, u32[]{:S(2)}, u32[]{:S(2)}) collective-permute-start(bf16[3,32,256]{2,1,0:T(8,128)(2,1)S(1)} %get-tuple-element.13), channel_id=1, source_target_pairs={{16,0},{32,16},{48,32},{64,48},{80,64},{96,80},{112,96},{128,112},... | collective-permute-start | bytes 147464 | tf_op jit(solution)/shard_map/ppermute | solution.py:15
  5.2 8.4 %collective-permute-start = (bf16[3,32,256]{2,1,0:T(8,128)(2,1)S(1)}, bf16[3,32,256]{2,1,0:T(8,128)(2,1)S(1)}, u32[]{:S(2)}, u32[]{:S(2)}) collective-permute-start(bf16[3,32,256]{2,1,0:T(8,128)(2,1)S(1)} %get-tuple-element.14), channel_id=1, source_target_pairs={{0,16},{16,32},{32,48},{48,64},{64,80},{80,96},{96,112},{112,128},... | collective-permute-start | bytes 147464 | tf_op jit(solution)/shard_map/ppermute | solution.py:15
  8.7 0.8 %copy-start.1 = (f32[8,7,127]{2,0,1:T(8,128)S(1)}, f32[8,7,127]{2,0,1:T(8,128)}, u32[]{:S(2)}) copy-start(f32[8,7,127]{2,0,1:T(8,128)} %param.26) | copy-start | bytes 85348
  9.6 4.2 %copy-start.6 = (bf16[3,32,256]{2,1,0:T(8,128)(2,1)}, bf16[3,32,256]{2,1,0:T(8,128)(2,1)S(1)}, u32[]{:S(2)}) copy-start(bf16[3,32,256]{2,1,0:T(8,128)(2,1)S(1)} %collective-permute-done.1.b_ref) | copy-start | bytes 147460
  13.7 0.6 copy-start.7
  14.3 6.3 %collective-permute-start.2 = (bf16[38,3,256]{2,1,0:T(4,128)(2,1)S(1)}, bf16[38,3,256]{2,1,0:T(4,128)(2,1)S(1)}, u32[]{:S(2)}, u32[]{:S(2)}) collective-permute-start(bf16[38,3,256]{2,1,0:T(4,128)(2,1)S(1)} %pad_maximum_fusion.1), channel_id=1, source_target_pairs={{0,1},{1,2},{2,3},{3,4},{4,5},{5,6},{6,7},{7,8},{8,9},{9,10},{10,1... | collective-permute-start | bytes 175112 | tf_op jit(solution)/shard_map/ppermute | solution.py:15
  18.7 5.7 %collective-permute-start.3 = (bf16[38,3,256]{2,1,0:T(4,128)(2,1)S(1)}, bf16[38,3,256]{2,1,0:T(4,128)(2,1)S(1)}, u32[]{:S(2)}, u32[]{:S(2)}) collective-permute-start(bf16[38,3,256]{2,1,0:T(4,128)(2,1)S(1)} %pad_maximum_fusion.2), channel_id=1, source_target_pairs={{1,0},{2,1},{3,2},{4,3},{5,4},{6,5},{7,6},{8,7},{9,8},{10,9},{11,1... | collective-permute-start | bytes 175112 | tf_op jit(solution)/shard_map/ppermute | solution.py:15
  20.6 3.8 %copy-start.4 = (bf16[38,3,256]{2,1,0:T(4,128)(2,1)}, bf16[38,3,256]{2,1,0:T(4,128)(2,1)S(1)}, u32[]{:S(2)}) copy-start(bf16[38,3,256]{2,1,0:T(4,128)(2,1)S(1)} %collective-permute-done.2.l_ref) | copy-start | bytes 175108
  24.4 0.6 %copy-start.5 = (bf16[38,3,256]{2,1,0:T(4,128)(2,1)}, bf16[38,3,256]{2,1,0:T(4,128)(2,1)S(1)}, u32[]{:S(2)}) copy-start(bf16[38,3,256]{2,1,0:T(4,128)(2,1)S(1)} %collective-permute-done.3.r_ref) | copy-start | bytes 175108
  45.1 12.9 %all-to-all-start = ((bf16[16,16,256]{2,1,0:T(8,128)(2,1)}), bf16[16,16,256]{2,1,0:T(8,128)(2,1)S(1)}, u32[]{:S(2)}, u32[]{:S(2)}) async-start(bf16[16,16,256]{2,1,0:T(8,128)(2,1)} %convert.5), calls=%async_computation | async-start | bytes 262144 | tf_op jit(solution)/shard_map/all_to_all | solution.py:293
  52.0 0.7 %copy-start.8 = (f32[16,256]{1,0:T(8,128)S(1)}, f32[16,256]{1,0:T(8,128)}, u32[]{:S(2)}) copy-start(f32[16,256]{1,0:T(8,128)} %get-tuple-element.10) | copy-start | bytes 49156
  59.0 0.9 %copy-start.3 = (bf16[256,256]{1,0:T(8,128)(2,1)S(1)}, bf16[256,256]{1,0:T(8,128)(2,1)}, u32[]{:S(2)}) copy-start(bf16[256,256]{1,0:T(8,128)(2,1)} %param.27) | copy-start | bytes 393220
  60.0 1.1 %copy-start.2 = (bf16[1024,256]{1,0:T(8,128)(2,1)S(1)}, bf16[1024,256]{1,0:T(8,128)(2,1)}, u32[]{:S(2)}) copy-start(bf16[1024,256]{1,0:T(8,128)(2,1)} %get-tuple-element.8) | copy-start | bytes 1572868

commit v9 on v8

--- a/solution.py
+++ b/solution.py
@@ -162,7 +162,7 @@
     pooled = (region_sums * jnp.float32(1.0 / 64.0)).astype(jnp.bfloat16)
     queries = jnp.dot(pooled, wq_ref[...], preferred_element_type=jnp.float32)
     queries = queries.astype(jnp.bfloat16).astype(jnp.float32)
-    copies = jnp.broadcast_to(pooled.astype(jnp.float32)[None], (s_ref.shape[0], per_row, channels))
+    copies = jnp.broadcast_to(pooled[None], (s_ref.shape[0], per_row, channels))
     step = pl.program_id(0)
     for k in range(s_ref.shape[1] // per_row):
 
@@ -185,7 +185,7 @@
         out_shape=(
             jax.ShapeDtypeStruct((pixels, channels), jnp.bfloat16),
             jax.ShapeDtypeStruct((tokens, channels), jnp.float32),
-            jax.ShapeDtypeStruct((copies, tokens, channels), jnp.float32),
+            jax.ShapeDtypeStruct((copies, tokens, channels), jnp.bfloat16),
         ),
         grid=(steps,),
         in_specs=[
@@ -295,7 +295,6 @@
         band_pooled.reshape(columns, region_side, region_side, channels)
         .transpose(1, 0, 2, 3)
         .reshape(key_count, channels)
-        .astype(jnp.bfloat16)
     )
     band_keyval = jnp.dot(band_pooled, w_keyval, preferred_element_type=jnp.float32).astype(
         jnp.bfloat16

time: 62.6 us -> 60.8 us (0.971)
  other arithmetic: 2.94 us -> 1.33 us
    unnamed x1 -> x0, other arithmetic: 1.62 us -> none
where the time goes in v9:
time: 60.8 us; the launch traced here: 60.3 us
  starting transfers between devices  19.7 us (32%)
  Pallas kernels  18.3 us (30%)
  waiting for transfers between devices  13 us (21%)
  local copies, waits for them, and re-layouts  6.82 us (11%)
  other arithmetic  1.33 us (2%)
  matrix products  0.79 us (1%)
    ppermute x4, starting transfers between devices, shifted(): return (lax.ppermute(piece, axis, up), lax.ppermute(piece, axis, down))  13 us
    pallas_call x1, Pallas kernels, conv_norm(): pl.pallas_call(conv_norm_kernel, out_shape=jax.ShapeDtypeStruct((tile_row...  9.59 us
    pallas_call x1, Pallas kernels, mlp(): pl.pallas_call(mlp_kernel, out_shape=(jax.ShapeDtypeStruct((pixels, chann...  8.76 us
    ppermute x4, waiting for transfers between devices, shifted(): return (lax.ppermute(piece, axis, up), lax.ppermute(piece, axis, down))  7.79 us
    all_to_all x1, starting transfers between devices, shards(): band_pooled = lax.all_to_all(sent, 'col', 0, 0)  6.75 us
    all_to_all x1, waiting for transfers between devices, shards(): band_pooled = lax.all_to_all(sent, 'col', 0, 0)  5.23 us
    unnamed x18, local copies, waits for them, and re-layouts  3.82 us
  transfers between devices with their start and end apart: 5, of which 3 were waited for; matrix products, arithmetic and copies ran while one was open for 3% of the time, Pallas kernels for 0%

profile of v9, /device:TPU:129, one launch (start us, length us, event | category | flops | bytes accessed | tf_op | source)
XLA Modules:
  0.0 60.3 jit_solution(4343947574407538059)
XLA Ops:
  0.0 0.9 %fusion.12 = (bf16[3,32,256]{2,1,0:T(8,128)(2,1)S(1)}, bf16[3,32,256]{2,1,0:T(8,128)(2,1)S(1)}) fusion(bf16[32,32,256]{2,1,0:T(8,128)(2,1)} %c_ref.1), kind=kLoop, calls=%fused_computation.41 | loop fusion | bytes 196608 | tf_op jit(solution)/shard_map/slice | solution.py:21
  0.9 4.4 %collective-permute-start.1 = (bf16[3,32,256]{2,1,0:T(8,128)(2,1)S(1)}, bf16[3,32,256]{2,1,0:T(8,128)(2,1)S(1)}, u32[]{:S(2)}, u32[]{:S(2)}) collective-permute-start(bf16[3,32,256]{2,1,0:T(8,128)(2,1)S(1)} %get-tuple-element.13), channel_id=1, source_target_pairs={{16,0},{32,16},{48,32},{64,48},{80,64},{96,80},{112,96},{128,112},... | collective-permute-start | bytes 147464 | tf_op jit(solution)/shard_map/ppermute | solution.py:15
  5.2 2.4 %collective-permute-start = (bf16[3,32,256]{2,1,0:T(8,128)(2,1)S(1)}, bf16[3,32,256]{2,1,0:T(8,128)(2,1)S(1)}, u32[]{:S(2)}, u32[]{:S(2)}) collective-permute-start(bf16[3,32,256]{2,1,0:T(8,128)(2,1)S(1)} %get-tuple-element.14), channel_id=1, source_target_pairs={{0,16},{16,32},{32,48},{48,64},{64,80},{80,96},{96,112},{112,128},... | collective-permute-start | bytes 147464 | tf_op jit(solution)/shard_map/ppermute | solution.py:15
  7.7 1.0 %fusion.11 = (bf16[32,3,256]{2,1,0:T(4,128)(2,1)S(1)}, bf16[32,3,256]{2,1,0:T(4,128)(2,1)S(1)}) fusion(bf16[32,32,256]{2,1,0:T(8,128)(2,1)} %c_ref.1), kind=kLoop, calls=%fused_computation.40 | loop fusion | bytes 196608 | tf_op jit(solution)/shard_map/slice | solution.py:25
  8.7 0.7 %copy-done.1 = f32[8,7,127]{2,0,1:T(8,128)S(1)} copy-done((f32[8,7,127]{2,0,1:T(8,128)S(1)}, f32[8,7,127]{2,0,1:T(8,128)}, u32[]{:S(2)}) %copy-start.1) | copy-done | bytes 28472
  9.6 4.0 %collective-permute-done.t_ref = bf16[3,32,256]{2,1,0:T(8,128)(2,1)S(1)} collective-permute-done((bf16[3,32,256]{2,1,0:T(8,128)(2,1)S(1)}, bf16[3,32,256]{2,1,0:T(8,128)(2,1)S(1)}, u32[]{:S(2)}, u32[]{:S(2)}) %collective-permute-start) | collective-permute-done | bytes 49184 | tf_op jit(solution)/shard_map/ppermute | solution.py:15
  13.8 0.5 copy-done.7
  14.3 4.3 %collective-permute-start.2 = (bf16[38,3,256]{2,1,0:T(4,128)(2,1)S(1)}, bf16[38,3,256]{2,1,0:T(4,128)(2,1)S(1)}, u32[]{:S(2)}, u32[]{:S(2)}) collective-permute-start(bf16[38,3,256]{2,1,0:T(4,128)(2,1)S(1)} %pad_maximum_fusion.1), channel_id=1, source_target_pairs={{0,1},{1,2},{2,3},{3,4},{4,5},{5,6},{6,7},{7,8},{8,9},{9,10},{10,1... | collective-permute-start | bytes 175112 | tf_op jit(solution)/shard_map/ppermute | solution.py:15
  18.7 1.9 %collective-permute-start.3 = (bf16[38,3,256]{2,1,0:T(4,128)(2,1)S(1)}, bf16[38,3,256]{2,1,0:T(4,128)(2,1)S(1)}, u32[]{:S(2)}, u32[]{:S(2)}) collective-permute-start(bf16[38,3,256]{2,1,0:T(4,128)(2,1)S(1)} %pad_maximum_fusion.2), channel_id=1, source_target_pairs={{1,0},{2,1},{3,2},{4,3},{5,4},{6,5},{7,6},{8,7},{9,8},{10,9},{11,1... | collective-permute-start | bytes 175112 | tf_op jit(solution)/shard_map/ppermute | solution.py:15
  20.6 3.7 %collective-permute-done.3.r_ref = bf16[38,3,256]{2,1,0:T(4,128)(2,1)S(1)} collective-permute-done((bf16[38,3,256]{2,1,0:T(4,128)(2,1)S(1)}, bf16[38,3,256]{2,1,0:T(4,128)(2,1)S(1)}, u32[]{:S(2)}, u32[]{:S(2)}) %collective-permute-start.3) | collective-permute-done | bytes 58400 | tf_op jit(solution)/shard_map/ppermute | solution.py:15
  24.4 0.6 %copy-done.5 = bf16[38,3,256]{2,1,0:T(4,128)(2,1)} copy-done((bf16[38,3,256]{2,1,0:T(4,128)(2,1)}, bf16[38,3,256]{2,1,0:T(4,128)(2,1)S(1)}, u32[]{:S(2)}) %copy-start.5) | copy-done | bytes 58392
  25.0 9.6 %shard_map.136 = bf16[32,32,256]{2,1,0:T(8,128)(2,1)} custom-call(bf16[32,32,256]{2,1,0:T(8,128)(2,1)} %c_ref.1, bf16[3,32,256]{2,1,0:T(8,128)(2,1)} %copy-done.7, bf16[3,32,256]{2,1,0:T(8,128)(2,1)} %copy-done.6, bf16[38,3,256]{2,1,0:T(4,128)(2,1)} %copy-done.4, bf16[38,3,256]{2,1,0:T(4,128)(2,1)} %copy-done.5, bf16[7,7,256]{2,1,0:T(8,128)(2,1)} %k_ref.1, ...), custom_call_target="tpu_custom_call" | custom-call | flops 25690112 | bytes 1263616 | tf_op jit(solution)/shard_map/pallas_call | solution.py:90
  34.6 8.8 %shard_map.137 = (bf16[1024,256]{1,0:T(8,128)(2,1)}, f32[16,256]{1,0:T(8,128)}, bf16[16,16,256]{2,1,0:T(8,128)(2,1)}) custom-call(bf16[1024,256]{1,0:T(8,128)(2,1)} %bitcast.70, bf16[1024,256]{1,0:T(8,128)(2,1)} %bitcast.69, bf16[256,1024]{1,0:T(8,128)(2,1)} %we_ref.1, f32[1,1024]{1,0:T(1,128)} %bitcast.78, bf16[1024,256]{1,0:T(8,128)(2,1)} %wr_ref.1, ...), custom_call_target="tpu_custom_call" | custom-call | flops 1073741824 | bytes 2621440 | tf_op jit(solution)/shard_map/pallas_call | solution.py:183
  43.4 6.8 %all-to-all-start = ((bf16[16,16,256]{2,1,0:T(8,128)(2,1)}), bf16[16,16,256]{2,1,0:T(8,128)(2,1)S(1)}, u32[]{:S(2)}, u32[]{:S(2)}) async-start(bf16[16,16,256]{2,1,0:T(8,128)(2,1)} %get-tuple-element.9), calls=%async_computation | async-start | bytes 262144 | tf_op jit(solution)/shard_map/all_to_all | solution.py:293
  50.2 0.2 reshape.77
  50.4 0.5 copy-done.8
  51.0 5.2 %all-to-all-done = bf16[16,16,256]{2,1,0:T(8,128)(2,1)S(1)} async-done(((bf16[16,16,256]{2,1,0:T(8,128)(2,1)}), bf16[16,16,256]{2,1,0:T(8,128)(2,1)S(1)}, u32[]{:S(2)}, u32[]{:S(2)}) %all-to-all-start) | async-done | bytes 131104 | tf_op jit(solution)/shard_map/all_to_all | solution.py:293
  56.4 0.2 convolution_convert_fusion
  56.8 0.1 fusion.3
  56.9 0.2 fusion.16
  57.2 0.3 fusion.4
  57.6 0.5 copy-done.3
  58.4 0.9 %copy-done.2 = bf16[1024,256]{1,0:T(8,128)(2,1)S(1)} copy-done((bf16[1024,256]{1,0:T(8,128)(2,1)S(1)}, bf16[1024,256]{1,0:T(8,128)(2,1)}, u32[]{:S(2)}) %copy-start.2) | copy-done | bytes 524312
  59.3 1.0 %fusion.5 = bf16[32,32,256]{2,1,0:T(8,128)(2,1)} fusion(f32[32,32,256]{2,1,0:T(8,128)S(1)} %bitcast.68, bf16[32,32,256]{2,1,0:T(8,128)(2,1)S(1)} %bitcast.73), kind=kLoop, calls=%fused_computation.9 | loop fusion | flops 786432 | bytes 2097152 | tf_op jit(solution)/shard_map/convert_element_type | solution.py:333
  (35 shorter events, 1.2 us)
Async XLA Ops:
  0.0 56.4 %copy-start = (bf16[256,512]{1,0:T(8,128)(2,1)S(1)}, bf16[256,512]{1,0:T(8,128)(2,1)}, u32[]{:S(2)}) copy-start(bf16[256,512]{1,0:T(8,128)(2,1)} %param.25) | copy-start | bytes 786436
  0.9 8.7 %collective-permute-start.1 = (bf16[3,32,256]{2,1,0:T(8,128)(2,1)S(1)}, bf16[3,32,256]{2,1,0:T(8,128)(2,1)S(1)}, u32[]{:S(2)}, u32[]{:S(2)}) collective-permute-start(bf16[3,32,256]{2,1,0:T(8,128)(2,1)S(1)} %get-tuple-element.13), channel_id=1, source_target_pairs={{16,0},{32,16},{48,32},{64,48},{80,64},{96,80},{112,96},{128,112},... | collective-permute-start | bytes 147464 | tf_op jit(solution)/shard_map/ppermute | solution.py:15
  5.2 8.4 %collective-permute-start = (bf16[3,32,256]{2,1,0:T(8,128)(2,1)S(1)}, bf16[3,32,256]{2,1,0:T(8,128)(2,1)S(1)}, u32[]{:S(2)}, u32[]{:S(2)}) collective-permute-start(bf16[3,32,256]{2,1,0:T(8,128)(2,1)S(1)} %get-tuple-element.14), channel_id=1, source_target_pairs={{0,16},{16,32},{32,48},{48,64},{64,80},{80,96},{96,112},{112,128},... | collective-permute-start | bytes 147464 | tf_op jit(solution)/shard_map/ppermute | solution.py:15
  8.7 0.8 %copy-start.1 = (f32[8,7,127]{2,0,1:T(8,128)S(1)}, f32[8,7,127]{2,0,1:T(8,128)}, u32[]{:S(2)}) copy-start(f32[8,7,127]{2,0,1:T(8,128)} %param.26) | copy-start | bytes 85348
  9.6 4.2 %copy-start.6 = (bf16[3,32,256]{2,1,0:T(8,128)(2,1)}, bf16[3,32,256]{2,1,0:T(8,128)(2,1)S(1)}, u32[]{:S(2)}) copy-start(bf16[3,32,256]{2,1,0:T(8,128)(2,1)S(1)} %collective-permute-done.1.b_ref) | copy-start | bytes 147460
  13.7 0.6 %copy-start.7 = (bf16[3,32,256]{2,1,0:T(8,128)(2,1)}, bf16[3,32,256]{2,1,0:T(8,128)(2,1)S(1)}, u32[]{:S(2)}) copy-start(bf16[3,32,256]{2,1,0:T(8,128)(2,1)S(1)} %collective-permute-done.t_ref) | copy-start | bytes 147460
  14.3 6.3 %collective-permute-start.2 = (bf16[38,3,256]{2,1,0:T(4,128)(2,1)S(1)}, bf16[38,3,256]{2,1,0:T(4,128)(2,1)S(1)}, u32[]{:S(2)}, u32[]{:S(2)}) collective-permute-start(bf16[38,3,256]{2,1,0:T(4,128)(2,1)S(1)} %pad_maximum_fusion.1), channel_id=1, source_target_pairs={{0,1},{1,2},{2,3},{3,4},{4,5},{5,6},{6,7},{7,8},{8,9},{9,10},{10,1... | collective-permute-start | bytes 175112 | tf_op jit(solution)/shard_map/ppermute | solution.py:15
  18.7 5.7 %collective-permute-start.3 = (bf16[38,3,256]{2,1,0:T(4,128)(2,1)S(1)}, bf16[38,3,256]{2,1,0:T(4,128)(2,1)S(1)}, u32[]{:S(2)}, u32[]{:S(2)}) collective-permute-start(bf16[38,3,256]{2,1,0:T(4,128)(2,1)S(1)} %pad_maximum_fusion.2), channel_id=1, source_target_pairs={{1,0},{2,1},{3,2},{4,3},{5,4},{6,5},{7,6},{8,7},{9,8},{10,9},{11,1... | collective-permute-start | bytes 175112 | tf_op jit(solution)/shard_map/ppermute | solution.py:15
  20.6 3.8 %copy-start.4 = (bf16[38,3,256]{2,1,0:T(4,128)(2,1)}, bf16[38,3,256]{2,1,0:T(4,128)(2,1)S(1)}, u32[]{:S(2)}) copy-start(bf16[38,3,256]{2,1,0:T(4,128)(2,1)S(1)} %collective-permute-done.2.l_ref) | copy-start | bytes 175108
  24.4 0.6 %copy-start.5 = (bf16[38,3,256]{2,1,0:T(4,128)(2,1)}, bf16[38,3,256]{2,1,0:T(4,128)(2,1)S(1)}, u32[]{:S(2)}) copy-start(bf16[38,3,256]{2,1,0:T(4,128)(2,1)S(1)} %collective-permute-done.3.r_ref) | copy-start | bytes 175108
  43.4 12.9 %all-to-all-start = ((bf16[16,16,256]{2,1,0:T(8,128)(2,1)}), bf16[16,16,256]{2,1,0:T(8,128)(2,1)S(1)}, u32[]{:S(2)}, u32[]{:S(2)}) async-start(bf16[16,16,256]{2,1,0:T(8,128)(2,1)} %get-tuple-element.9), calls=%async_computation | async-start | bytes 262144 | tf_op jit(solution)/shard_map/all_to_all | solution.py:293
  50.2 0.7 %copy-start.8 = (f32[16,256]{1,0:T(8,128)S(1)}, f32[16,256]{1,0:T(8,128)}, u32[]{:S(2)}) copy-start(f32[16,256]{1,0:T(8,128)} %get-tuple-element.10) | copy-start | bytes 49156
  57.2 0.9 %copy-start.3 = (bf16[256,256]{1,0:T(8,128)(2,1)S(1)}, bf16[256,256]{1,0:T(8,128)(2,1)}, u32[]{:S(2)}) copy-start(bf16[256,256]{1,0:T(8,128)(2,1)} %param.27) | copy-start | bytes 393220
  58.3 1.1 %copy-start.2 = (bf16[1024,256]{1,0:T(8,128)(2,1)S(1)}, bf16[1024,256]{1,0:T(8,128)(2,1)}, u32[]{:S(2)}) copy-start(bf16[1024,256]{1,0:T(8,128)(2,1)} %get-tuple-element.8) | copy-start | bytes 1572868

commit v10 on v9

--- a/solution.py
+++ b/solution.py
@@ -214,6 +214,61 @@
         layer_scale.reshape(1, channels),
         w_query,
     )
+
+def attention_kernel(band_ref, wkv_ref, q_ref, bias_ref, wo_ref, bo_ref, o_ref):
+    tokens, channels = q_ref.shape
+    heads = bias_ref.shape[0]
+    head_dim = channels // heads
+    keyval = jnp.dot(band_ref[...], wkv_ref[...], preferred_element_type=jnp.float32)
+    keyval = keyval.astype(jnp.bfloat16)
+    keys = keyval[:, :channels]
+    values = keyval[:, channels:]
+    queries = q_ref[...]
+    head_of = lax.broadcasted_iota(jnp.int32, (1, channels), 1) // head_dim
+    zero = jnp.zeros((), jnp.bfloat16)
+    context = jnp.zeros((tokens, channels), jnp.float32)
+    for h in range(heads):
+        mine = head_of == h
+        scores = lax.dot_general(
+            jnp.where(mine, queries, zero),
+            keys,
+            (((1,), (1,)), ((), ())),
+            preferred_element_type=jnp.float32,
+        )
+        scores = scores / jnp.sqrt(jnp.float32(head_dim)) + bias_ref[h]
+        top = jnp.max(scores, axis=-1, keepdims=True)
+        weights = jnp.exp(scores - top)
+        attn = (weights / jnp.sum(weights, axis=-1, keepdims=True)).astype(jnp.bfloat16)
+        context = context + jnp.dot(
+            attn, jnp.where(mine, values, zero), preferred_element_type=jnp.float32
+        )
+    lifted = jnp.dot(context.astype(jnp.bfloat16), wo_ref[...], preferred_element_type=jnp.float32)
+    tile_rows, tile_cols = o_ref.shape[:2]
+    per_row = tile_cols // 8
+    for i in range(tile_rows // 8):
+        spread = jnp.broadcast_to(
+            lifted[i * per_row : (i + 1) * per_row][:, None, :], (per_row, 8, channels)
+        ).reshape(tile_cols, channels)
+        rows = pl.ds(i * 8, 8)
+        o_ref[rows] = (bo_ref[rows].astype(jnp.float32) + spread[None]).astype(o_ref.dtype)
+
+
+def attention(band, w_keyval, queries, bias, w_out, block_out):
+    vmem = pl.BlockSpec(memory_space=pltpu.VMEM)
+    keys, channels = band.shape
+    tokens = queries.shape[0]
+    return pl.pallas_call(
+        attention_kernel,
+        out_shape=jax.ShapeDtypeStruct(block_out.shape, jnp.bfloat16),
+        in_specs=[vmem] * 6,
+        out_specs=vmem,
+        cost_estimate=pl.CostEstimate(
+            flops=2 * keys * channels * 2 * channels + 4 * bias.shape[0] * tokens * keys * channels,
+            bytes_accessed=2 * (keys * channels + 2 * block_out.size),
+            transcendentals=bias.shape[0] * tokens * keys,
+        ),
+    )(band, w_keyval, queries, bias, w_out, block_out)
+
 
 def block_pass(
     pieces,
@@ -296,9 +351,6 @@
         .transpose(1, 0, 2, 3)
         .reshape(key_count, channels)
     )
-    band_keyval = jnp.dot(band_pooled, w_keyval, preferred_element_type=jnp.float32).astype(
-        jnp.bfloat16
-    )
     windows = []
     for query_col in range(region_side):
         first = span_cols - 1 - (position * region_side + query_col)
@@ -310,27 +362,7 @@
         ]
         rows_of.append(jnp.stack(per_col, axis=1))
     bias_block = jnp.stack(rows_of, axis=1).reshape(HEADS, local_count, key_count)
-    query_heads = queries.reshape(local_count, HEADS, head_dim)
-    key_heads = band_keyval[:, :channels].reshape(key_count, HEADS, head_dim)
-    value_heads = band_keyval[:, channels:].reshape(key_count, HEADS, head_dim)
-    scores = (
-        jnp.einsum("qhd,khd->hqk", query_heads, key_heads, preferred_element_type=jnp.float32)
-        / jnp.sqrt(jnp.float32(head_dim))
-        + bias_block
-    )
-    attn = jax.nn.softmax(scores, axis=-1).astype(jnp.bfloat16)
-    context = (
-        jnp.einsum("hqk,khd->qhd", attn, value_heads, preferred_element_type=jnp.float32)
-        .reshape(local_count, channels)
-        .astype(jnp.bfloat16)
-    )
-    lifted = jnp.dot(context, w_out, preferred_element_type=jnp.float32).reshape(
-        region_side, 1, region_side, 1, channels
-    )
-    spread = jnp.broadcast_to(lifted, (region_side, 8, region_side, 8, channels)).reshape(
-        tile_rows, tile_cols, channels
-    )
-    return (block_out.astype(jnp.float32) + spread).astype(jnp.bfloat16)
+    return attention(band_pooled, w_keyval, queries, bias_block, w_out, block_out)
 
 
 def solution(mesh):

time: 60.8 us -> 61.2 us (level)
  the two profiles are of different devices: /device:TPU:129 before, /device:TPU:113 now
where the time goes in v10:
time: 61.2 us; the launch traced here: 60.7 us
  Pallas kernels  21.9 us (36%)
  starting transfers between devices  19.7 us (32%)
  waiting for transfers between devices  12.6 us (21%)
  local copies, waits for them, and re-layouts  5.59 us (9%)
  other arithmetic  0.79 us (1%)
    ppermute x4, starting transfers between devices, shifted(): return (lax.ppermute(piece, axis, up), lax.ppermute(piece, axis, down))  14.5 us
    pallas_call x1, Pallas kernels, conv_norm(): pl.pallas_call(conv_norm_kernel, out_shape=jax.ShapeDtypeStruct((tile_row...  9.59 us
    pallas_call x1, Pallas kernels, mlp(): pl.pallas_call(mlp_kernel, out_shape=(jax.ShapeDtypeStruct((pixels, chann...  8.74 us
    ppermute x4, waiting for transfers between devices, shifted(): return (lax.ppermute(piece, axis, up), lax.ppermute(piece, axis, down))  8 us
    all_to_all x1, starting transfers between devices, shards(): band_pooled = lax.all_to_all(sent, 'col', 0, 0)  5.25 us
    all_to_all x1, waiting for transfers between devices, shards(): band_pooled = lax.all_to_all(sent, 'col', 0, 0)  4.58 us
    pallas_call x1, Pallas kernels, attention(): pl.pallas_call(attention_kernel, out_shape=jax.ShapeDtypeStruct(block_out...  3.57 us
    unnamed x12, local copies, waits for them, and re-layouts  1.88 us
  transfers between devices with their start and end apart: 5, of which 3 were waited for; matrix products, arithmetic and copies ran while one was open for 5% of the time, Pallas kernels for 0%

profile of v10, /device:TPU:113, one launch (start us, length us, event | category | flops | bytes accessed | tf_op | source)
XLA Modules:
  0.0 60.7 jit_solution(12530850709310817643)
XLA Ops:
  0.0 0.8 %fusion.1 = (bf16[3,32,256]{2,1,0:T(8,128)(2,1)S(1)}, bf16[3,32,256]{2,1,0:T(8,128)(2,1)S(1)}) fusion(bf16[32,32,256]{2,1,0:T(8,128)(2,1)} %c_ref.1), kind=kLoop, calls=%fused_computation.25 | loop fusion | bytes 196608 | tf_op jit(solution)/shard_map/slice | solution.py:21
  0.8 4.5 %collective-permute-start = (bf16[3,32,256]{2,1,0:T(8,128)(2,1)S(1)}, bf16[3,32,256]{2,1,0:T(8,128)(2,1)S(1)}, u32[]{:S(2)}, u32[]{:S(2)}) collective-permute-start(bf16[3,32,256]{2,1,0:T(8,128)(2,1)S(1)} %get-tuple-element.14), channel_id=1, source_target_pairs={{0,16},{16,32},{32,48},{48,64},{64,80},{80,96},{96,112},{112,128},... | collective-permute-start | bytes 147464 | tf_op jit(solution)/shard_map/ppermute | solution.py:15
  5.4 2.3 %collective-permute-start.1 = (bf16[3,32,256]{2,1,0:T(8,128)(2,1)S(1)}, bf16[3,32,256]{2,1,0:T(8,128)(2,1)S(1)}, u32[]{:S(2)}, u32[]{:S(2)}) collective-permute-start(bf16[3,32,256]{2,1,0:T(8,128)(2,1)S(1)} %get-tuple-element.13), channel_id=1, source_target_pairs={{16,0},{32,16},{48,32},{64,48},{80,64},{96,80},{112,96},{128,112},... | collective-permute-start | bytes 147464 | tf_op jit(solution)/shard_map/ppermute | solution.py:15
  7.6 1.0 %fusion = (bf16[32,3,256]{2,1,0:T(4,128)(2,1)S(1)}, bf16[32,3,256]{2,1,0:T(4,128)(2,1)S(1)}) fusion(bf16[32,32,256]{2,1,0:T(8,128)(2,1)} %c_ref.1), kind=kLoop, calls=%fused_computation.24 | loop fusion | bytes 196608 | tf_op jit(solution)/shard_map/slice | solution.py:25
  8.7 0.7 %copy-done = f32[8,7,127]{2,0,1:T(8,128)S(1)} copy-done((f32[8,7,127]{2,0,1:T(8,128)S(1)}, f32[8,7,127]{2,0,1:T(8,128)}, u32[]{:S(2)}) %copy-start) | copy-done | bytes 28472
  9.4 0.1 dynamic-slice_bitcast_fusion.15
  9.6 4.2 %collective-permute-done.1.b_ref = bf16[3,32,256]{2,1,0:T(8,128)(2,1)S(1)} collective-permute-done((bf16[3,32,256]{2,1,0:T(8,128)(2,1)S(1)}, bf16[3,32,256]{2,1,0:T(8,128)(2,1)S(1)}, u32[]{:S(2)}, u32[]{:S(2)}) %collective-permute-start.1) | collective-permute-done | bytes 49184 | tf_op jit(solution)/shard_map/ppermute | solution.py:15
  13.9 0.1 pad_maximum_fusion.1
  13.9 0.5 copy-done.4
  14.4 0.0 copy-done.3
  14.4 5.8 %collective-permute-start.2 = (bf16[38,3,256]{2,1,0:T(4,128)(2,1)S(1)}, bf16[38,3,256]{2,1,0:T(4,128)(2,1)S(1)}, u32[]{:S(2)}, u32[]{:S(2)}) collective-permute-start(bf16[38,3,256]{2,1,0:T(4,128)(2,1)S(1)} %pad_maximum_fusion.1), channel_id=1, source_target_pairs={{0,1},{1,2},{2,3},{3,4},{4,5},{5,6},{6,7},{7,8},{8,9},{9,10},{10,1... | collective-permute-start | bytes 175112 | tf_op jit(solution)/shard_map/ppermute | solution.py:15
  20.2 0.1 pad_maximum_fusion.2
  20.3 1.9 %collective-permute-start.3 = (bf16[38,3,256]{2,1,0:T(4,128)(2,1)S(1)}, bf16[38,3,256]{2,1,0:T(4,128)(2,1)S(1)}, u32[]{:S(2)}, u32[]{:S(2)}) collective-permute-start(bf16[38,3,256]{2,1,0:T(4,128)(2,1)S(1)} %pad_maximum_fusion.2), channel_id=1, source_target_pairs={{1,0},{2,1},{3,2},{4,3},{5,4},{6,5},{7,6},{8,7},{9,8},{10,9},{11,1... | collective-permute-start | bytes 175112 | tf_op jit(solution)/shard_map/ppermute | solution.py:15
  22.3 3.7 %collective-permute-done.3.r_ref = bf16[38,3,256]{2,1,0:T(4,128)(2,1)S(1)} collective-permute-done((bf16[38,3,256]{2,1,0:T(4,128)(2,1)S(1)}, bf16[38,3,256]{2,1,0:T(4,128)(2,1)S(1)}, u32[]{:S(2)}, u32[]{:S(2)}) %collective-permute-start.3) | collective-permute-done | bytes 58400 | tf_op jit(solution)/shard_map/ppermute | solution.py:15
  26.0 0.6 %copy-done.2 = bf16[38,3,256]{2,1,0:T(4,128)(2,1)} copy-done((bf16[38,3,256]{2,1,0:T(4,128)(2,1)}, bf16[38,3,256]{2,1,0:T(4,128)(2,1)S(1)}, u32[]{:S(2)}) %copy-start.2) | copy-done | bytes 58392
  26.6 9.6 %shard_map.136 = bf16[32,32,256]{2,1,0:T(8,128)(2,1)} custom-call(bf16[32,32,256]{2,1,0:T(8,128)(2,1)} %c_ref.1, bf16[3,32,256]{2,1,0:T(8,128)(2,1)} %copy-done.3, bf16[3,32,256]{2,1,0:T(8,128)(2,1)} %copy-done.4, bf16[38,3,256]{2,1,0:T(4,128)(2,1)} %copy-done.1, bf16[38,3,256]{2,1,0:T(4,128)(2,1)} %copy-done.2, bf16[7,7,256]{2,1,0:T(8,128)(2,1)} %k_ref.1, ...), custom_call_target="tpu_custom_call" | custom-call | flops 25690112 | bytes 1263616 | tf_op jit(solution)/shard_map/pallas_call | solution.py:90
  36.2 8.7 %shard_map.137 = (bf16[1024,256]{1,0:T(8,128)(2,1)}, f32[16,256]{1,0:T(8,128)}, bf16[16,16,256]{2,1,0:T(8,128)(2,1)}) custom-call(bf16[1024,256]{1,0:T(8,128)(2,1)} %bitcast.54, bf16[1024,256]{1,0:T(8,128)(2,1)} %bitcast.52, bf16[256,1024]{1,0:T(8,128)(2,1)} %we_ref.1, f32[1,1024]{1,0:T(1,128)} %bitcast.59, bf16[1024,256]{1,0:T(8,128)(2,1)} %wr_ref.1, ...), custom_call_target="tpu_custom_call" | custom-call | flops 1073741824 | bytes 2621440 | tf_op jit(solution)/shard_map/pallas_call | solution.py:183
  45.0 5.2 %all-to-all-start = ((bf16[16,16,256]{2,1,0:T(8,128)(2,1)}), bf16[16,16,256]{2,1,0:T(8,128)(2,1)S(1)}, u32[]{:S(2)}, u32[]{:S(2)}) async-start(bf16[16,16,256]{2,1,0:T(8,128)(2,1)} %get-tuple-element.8), calls=%async_computation | async-start | bytes 262144 | tf_op jit(solution)/shard_map/all_to_all | solution.py:348
  50.3 0.1 copy.16
  50.4 0.8 %reshape.46.bias_ref = f32[8,16,256]{2,1,0:T(8,128)} reshape(f32[8,4,4,4,64]{4,3,2,1,0:T(4,128)S(1)} %copy.16) | data formatting | bytes 262144 | tf_op jit(solution)/shard_map/reshape | solution.py:364
  51.2 0.6 %convert_element_type.3.q_ref = bf16[16,256]{1,0:T(8,128)(2,1)} convert(f32[16,256]{1,0:T(8,128)S(1)} %copy-done.5) | non-fusion elementwise | flops 4096 | bytes 24576 | tf_op jit(solution)/shard_map/convert_element_type | solution.py:345
  51.8 4.6 %all-to-all-done = bf16[16,16,256]{2,1,0:T(8,128)(2,1)S(1)} async-done(((bf16[16,16,256]{2,1,0:T(8,128)(2,1)}), bf16[16,16,256]{2,1,0:T(8,128)(2,1)S(1)}, u32[]{:S(2)}, u32[]{:S(2)}) %all-to-all-start) | async-done | bytes 131104 | tf_op jit(solution)/shard_map/all_to_all | solution.py:348
  56.5 0.7 %reshape.45.band_ref = bf16[256,256]{1,0:T(8,128)(2,1)} reshape(bf16[4,16,4,256]{3,2,1,0:T(4,128)(2,1)S(1)} %bitcast.55) | data formatting | bytes 262144 | tf_op jit(solution)/shard_map/reshape | solution.py:352
  57.2 3.6 %shard_map.138 = bf16[32,32,256]{2,1,0:T(8,128)(2,1)} custom-call(bf16[256,256]{1,0:T(8,128)(2,1)} %reshape.45.band_ref, bf16[256,512]{1,0:T(8,128)(2,1)} %wkv_ref.1, bf16[16,256]{1,0:T(8,128)(2,1)} %convert_element_type.3.q_ref, f32[8,16,256]{2,1,0:T(8,128)} %reshape.46.bias_ref, bf16[256,256]{1,0:T(8,128)(2,1)} %wo_ref.1, bf16[32,32,256]{2,1,0:T(8,128)(2,1)} %bitcast.53), custom_call_target="tpu_custom_call" | custom-call | flops 100663296 | bytes 1179648 | tf_op jit(solution)/shard_map/pallas_call | solution.py:260
  (17 shorter events, 0.2 us)
Async XLA Ops:
  0.8 13.0 %collective-permute-start = (bf16[3,32,256]{2,1,0:T(8,128)(2,1)S(1)}, bf16[3,32,256]{2,1,0:T(8,128)(2,1)S(1)}, u32[]{:S(2)}, u32[]{:S(2)}) collective-permute-start(bf16[3,32,256]{2,1,0:T(8,128)(2,1)S(1)} %get-tuple-element.14), channel_id=1, source_target_pairs={{0,16},{16,32},{32,48},{48,64},{64,80},{80,96},{96,112},{112,128},... | collective-permute-start | bytes 147464 | tf_op jit(solution)/shard_map/ppermute | solution.py:15
  5.4 8.4 %collective-permute-start.1 = (bf16[3,32,256]{2,1,0:T(8,128)(2,1)S(1)}, bf16[3,32,256]{2,1,0:T(8,128)(2,1)S(1)}, u32[]{:S(2)}, u32[]{:S(2)}) collective-permute-start(bf16[3,32,256]{2,1,0:T(8,128)(2,1)S(1)} %get-tuple-element.13), channel_id=1, source_target_pairs={{16,0},{32,16},{48,32},{64,48},{80,64},{96,80},{112,96},{128,112},... | collective-permute-start | bytes 147464 | tf_op jit(solution)/shard_map/ppermute | solution.py:15
  8.7 0.8 %copy-start = (f32[8,7,127]{2,0,1:T(8,128)S(1)}, f32[8,7,127]{2,0,1:T(8,128)}, u32[]{:S(2)}) copy-start(f32[8,7,127]{2,0,1:T(8,128)} %param.26) | copy-start | bytes 85348
  13.8 0.6 %copy-start.4 = (bf16[3,32,256]{2,1,0:T(8,128)(2,1)}, bf16[3,32,256]{2,1,0:T(8,128)(2,1)S(1)}, u32[]{:S(2)}) copy-start(bf16[3,32,256]{2,1,0:T(8,128)(2,1)S(1)} %collective-permute-done.1.b_ref) | copy-start | bytes 147460
  13.8 0.6 %copy-start.3 = (bf16[3,32,256]{2,1,0:T(8,128)(2,1)}, bf16[3,32,256]{2,1,0:T(8,128)(2,1)S(1)}, u32[]{:S(2)}) copy-start(bf16[3,32,256]{2,1,0:T(8,128)(2,1)S(1)} %collective-permute-done.t_ref) | copy-start | bytes 147460
  14.4 7.8 %collective-permute-start.2 = (bf16[38,3,256]{2,1,0:T(4,128)(2,1)S(1)}, bf16[38,3,256]{2,1,0:T(4,128)(2,1)S(1)}, u32[]{:S(2)}, u32[]{:S(2)}) collective-permute-start(bf16[38,3,256]{2,1,0:T(4,128)(2,1)S(1)} %pad_maximum_fusion.1), channel_id=1, source_target_pairs={{0,1},{1,2},{2,3},{3,4},{4,5},{5,6},{6,7},{7,8},{8,9},{9,10},{10,1... | collective-permute-start | bytes 175112 | tf_op jit(solution)/shard_map/ppermute | solution.py:15
  20.3 5.7 %collective-permute-start.3 = (bf16[38,3,256]{2,1,0:T(4,128)(2,1)S(1)}, bf16[38,3,256]{2,1,0:T(4,128)(2,1)S(1)}, u32[]{:S(2)}, u32[]{:S(2)}) collective-permute-start(bf16[38,3,256]{2,1,0:T(4,128)(2,1)S(1)} %pad_maximum_fusion.2), channel_id=1, source_target_pairs={{1,0},{2,1},{3,2},{4,3},{5,4},{6,5},{7,6},{8,7},{9,8},{10,9},{11,1... | collective-permute-start | bytes 175112 | tf_op jit(solution)/shard_map/ppermute | solution.py:15
  22.3 3.8 %copy-start.1 = (bf16[38,3,256]{2,1,0:T(4,128)(2,1)}, bf16[38,3,256]{2,1,0:T(4,128)(2,1)S(1)}, u32[]{:S(2)}) copy-start(bf16[38,3,256]{2,1,0:T(4,128)(2,1)S(1)} %collective-permute-done.2.l_ref) | copy-start | bytes 175108
  26.0 0.6 %copy-start.2 = (bf16[38,3,256]{2,1,0:T(4,128)(2,1)}, bf16[38,3,256]{2,1,0:T(4,128)(2,1)S(1)}, u32[]{:S(2)}) copy-start(bf16[38,3,256]{2,1,0:T(4,128)(2,1)S(1)} %collective-permute-done.3.r_ref) | copy-start | bytes 175108
  45.0 11.4 %all-to-all-start = ((bf16[16,16,256]{2,1,0:T(8,128)(2,1)}), bf16[16,16,256]{2,1,0:T(8,128)(2,1)S(1)}, u32[]{:S(2)}, u32[]{:S(2)}) async-start(bf16[16,16,256]{2,1,0:T(8,128)(2,1)} %get-tuple-element.8), calls=%async_computation | async-start | bytes 262144 | tf_op jit(solution)/shard_map/all_to_all | solution.py:348
  50.3 0.9 %copy-start.5 = (f32[16,256]{1,0:T(8,128)S(1)}, f32[16,256]{1,0:T(8,128)}, u32[]{:S(2)}) copy-start(f32[16,256]{1,0:T(8,128)} %get-tuple-element.9) | copy-start | bytes 49156

commit v11 on v9

--- a/solution.py
+++ b/solution.py
@@ -31,29 +31,19 @@
 ROW_BLOCK = 8
 
 
-def conv_norm_kernel(
-    c_ref, t_ref, b_ref, l_ref, r_ref, k_ref, db_ref, g_ref, nb_ref, o_ref, kf_ref, sh_ref
-):
+def conv_norm_kernel(x_ref, k_ref, db_ref, g_ref, nb_ref, o_ref, kf_ref, sh_ref):
+    rows_p = x_ref.shape[0]
     tile_rows, tile_cols, channels = o_ref.shape
-    halo = t_ref.shape[0]
-    rows_p = tile_rows + 2 * halo
     for a in range(TAPS):
         kf_ref[a, pl.ds(0, TAPS), :] = k_ref[a].astype(jnp.float32)
 
-    def put(r, mid):
-        row = jnp.concatenate([l_ref[r], mid, r_ref[r]], axis=0).astype(jnp.float32)
+    def widen(r, carry):
+        row = x_ref[r].astype(jnp.float32)
         for b in range(TAPS):
             sh_ref[b, r] = row[b : b + tile_cols]
-
-    for r in range(halo):
-        put(r, t_ref[r])
-        put(rows_p - halo + r, b_ref[r])
-
-    def widen(r, carry):
-        put(r, c_ref[r - halo])
         return carry
 
-    lax.fori_loop(halo, rows_p - halo, widen, 0)
+    lax.fori_loop(0, rows_p, widen, 0)
     db = db_ref[...]
     g = g_ref[...]
     nb = nb_ref[...]
@@ -83,14 +73,13 @@
     lax.fori_loop(0, tile_rows // ROW_BLOCK, body, 0)
 
 
-def conv_norm(centre, top, bottom, left, right, dw_kernel, dw_bias, norm_gain, norm_bias):
-    tile_rows, tile_cols, channels = centre.shape
-    rows_p = tile_rows + 2 * top.shape[0]
+def conv_norm(padded, dw_kernel, dw_bias, norm_gain, norm_bias, tile_rows, tile_cols):
+    rows_p, cols_p, channels = padded.shape
     vmem = pl.BlockSpec(memory_space=pltpu.VMEM)
     return pl.pallas_call(
         conv_norm_kernel,
         out_shape=jax.ShapeDtypeStruct((tile_rows, tile_cols, channels), jnp.bfloat16),
-        in_specs=[vmem] * 9,
+        in_specs=[vmem] * 5,
         out_specs=vmem,
         scratch_shapes=[
             pltpu.VMEM((TAPS, 8, channels), jnp.float32),
@@ -98,20 +87,17 @@
         ],
         cost_estimate=pl.CostEstimate(
             flops=2 * TAPS * TAPS * tile_rows * tile_cols * channels,
-            bytes_accessed=2 * (rows_p * rows_p + tile_rows * tile_cols) * channels,
+            bytes_accessed=2 * (rows_p * cols_p + tile_rows * tile_cols) * channels,
             transcendentals=tile_rows * tile_cols,
         ),
     )(
-        centre,
-        top,
-        bottom,
-        left,
-        right,
+        padded,
         dw_kernel,
         dw_bias.reshape(1, channels),
         norm_gain.reshape(1, channels),
         norm_bias.reshape(1, channels),
     )
+
 
 ERFC_COEFFS = (
     -1.26551223,
@@ -231,9 +217,14 @@
     copies,
 ):
     tile_rows, tile_cols, channels = features.shape
-    normed = conv_norm(features, *pieces, dw_kernel, dw_bias, norm_gain, norm_bias).reshape(
-        -1, channels
-    )
+    top, bottom, left, right = pieces
+    extended = jnp.concatenate([top, features, bottom], axis=0)
+    padded = jnp.concatenate(
+        [left, extended, right, jnp.zeros_like(right)[:, : -(tile_cols + 3 * 3) % 8]], axis=1
+    )
+    normed = conv_norm(
+        padded, dw_kernel, dw_bias, norm_gain, norm_bias, tile_rows, tile_cols
+    ).reshape(-1, channels)
     summed, queries, sent = mlp(
         normed,
         features.reshape(-1, channels),

time: 60.8 us -> 59 us (0.970)
  the two profiles are of different devices: /device:TPU:129 before, /device:TPU:113 now
where the time goes in v11:
time: 59 us; the launch traced here: 58.5 us
  starting transfers between devices  21 us (36%)
  Pallas kernels  18.2 us (31%)
  waiting for transfers between devices  10.7 us (18%)
  local copies, waits for them, and re-layouts  4.79 us (8%)
  other arithmetic  2.72 us (5%)
  matrix products  0.79 us (1%)
    ppermute x4, starting transfers between devices, shifted(): return (lax.ppermute(piece, axis, up), lax.ppermute(piece, axis, down))  14.5 us
    pallas_call x1, Pallas kernels, conv_norm(): pl.pallas_call(conv_norm_kernel, out_shape=jax.ShapeDtypeStruct((tile_row...  9.46 us
    pallas_call x1, Pallas kernels, mlp(): pl.pallas_call(mlp_kernel, out_shape=(jax.ShapeDtypeStruct((pixels, chann...  8.74 us
    all_to_all x1, starting transfers between devices, shards(): band_pooled = lax.all_to_all(sent, 'col', 0, 0)  6.53 us
    all_to_all x1, waiting for transfers between devices, shards(): band_pooled = lax.all_to_all(sent, 'col', 0, 0)  5.74 us
    ppermute x4, waiting for transfers between devices, shifted(): return (lax.ppermute(piece, axis, up), lax.ppermute(piece, axis, down))  4.99 us
    another operation x1, local copies, waits for them, and re-layouts, shards(): rows_of.append(jnp.stack(per_col, axis=1))  1.45 us
    concatenate x1, other arithmetic, block_pass(): jnp.concatenate([left, extended, right, jnp.zeros_like(right)[:, :-(tile_...  1.4 us
  transfers between devices with their start and end apart: 5, of which 3 were waited for; matrix products, arithmetic and copies ran while one was open for 5% of the time, Pallas kernels for 0%

profile of v11, /device:TPU:113, one launch (start us, length us, event | category | flops | bytes accessed | tf_op | source)
XLA Modules:
  0.0 58.5 jit_solution(7064450436173756738)
XLA Ops:
  0.0 0.9 %fusion.12 = (bf16[3,32,256]{2,1,0:T(8,128)(2,1)S(1)}, bf16[3,32,256]{2,1,0:T(8,128)(2,1)S(1)}) fusion(bf16[32,32,256]{2,1,0:T(8,128)(2,1)} %param.14), kind=kLoop, calls=%fused_computation.42 | loop fusion | bytes 196608 | tf_op jit(solution)/shard_map/slice | solution.py:20
  0.9 4.5 %collective-permute-start = (bf16[3,32,256]{2,1,0:T(8,128)(2,1)S(1)}, bf16[3,32,256]{2,1,0:T(8,128)(2,1)S(1)}, u32[]{:S(2)}, u32[]{:S(2)}) collective-permute-start(bf16[3,32,256]{2,1,0:T(8,128)(2,1)S(1)} %get-tuple-element.13), channel_id=1, source_target_pairs={{0,16},{16,32},{32,48},{48,64},{64,80},{80,96},{96,112},{112,128},... | collective-permute-start | bytes 147464 | tf_op jit(solution)/shard_map/ppermute | solution.py:15
  5.4 2.3 %collective-permute-start.1 = (bf16[3,32,256]{2,1,0:T(8,128)(2,1)S(1)}, bf16[3,32,256]{2,1,0:T(8,128)(2,1)S(1)}, u32[]{:S(2)}, u32[]{:S(2)}) collective-permute-start(bf16[3,32,256]{2,1,0:T(8,128)(2,1)S(1)} %get-tuple-element.14), channel_id=1, source_target_pairs={{16,0},{32,16},{48,32},{64,48},{80,64},{96,80},{112,96},{128,112},... | collective-permute-start | bytes 147464 | tf_op jit(solution)/shard_map/ppermute | solution.py:15
  7.7 1.0 %fusion.11 = (bf16[32,3,256]{2,1,0:T(4,128)(2,1)S(1)}, bf16[32,3,256]{2,1,0:T(4,128)(2,1)S(1)}) fusion(bf16[32,32,256]{2,1,0:T(8,128)(2,1)} %param.14), kind=kLoop, calls=%fused_computation.41 | loop fusion | bytes 196608 | tf_op jit(solution)/shard_map/slice | solution.py:23
  8.7 1.4 %dynamic-slice_bitcast_fusion.15 = (f32[8,1,4,64]{3,0,2,1:T(8,128)S(1)}, f32[8,1,4,64]{3,0,2,1:T(8,128)S(1)}, f32[8,1,4,64]{3,0,2,1:T(8,128)S(1)}, f32[8,1,4,64]...) fusion(f32[8,7,127]{2,0,1:T(8,128)} %param.26, ...), kind=kLoop, calls=%fused_computation.39 | loop fusion | bytes 262172 | tf_op jit(solution)/shard_map/stack | solution.py:302
  10.3 3.6 %collective-permute-done.1 = bf16[3,32,256]{2,1,0:T(8,128)(2,1)S(1)} collective-permute-done((bf16[3,32,256]{2,1,0:T(8,128)(2,1)S(1)}, bf16[3,32,256]{2,1,0:T(8,128)(2,1)S(1)}, u32[]{:S(2)}, u32[]{:S(2)}) %collective-permute-start.1) | collective-permute-done | bytes 49184 | tf_op jit(solution)/shard_map/ppermute | solution.py:15
  14.0 4.0 %collective-permute-start.3 = (bf16[38,3,256]{2,1,0:T(4,128)(2,1)S(1)}, bf16[38,3,256]{2,1,0:T(4,128)(2,1)S(1)}, u32[]{:S(2)}, u32[]{:S(2)}) collective-permute-start(bf16[38,3,256]{2,1,0:T(4,128)(2,1)S(1)} %pad_maximum_fusion.2), channel_id=1, source_target_pairs={{1,0},{2,1},{3,2},{4,3},{5,4},{6,5},{7,6},{8,7},{9,8},{10,9},{11,1... | collective-permute-start | bytes 175112 | tf_op jit(solution)/shard_map/ppermute | solution.py:15
  18.1 3.7 %collective-permute-start.2 = (bf16[38,3,256]{2,1,0:T(4,128)(2,1)S(1)}, bf16[38,3,256]{2,1,0:T(4,128)(2,1)S(1)}, u32[]{:S(2)}, u32[]{:S(2)}) collective-permute-start(bf16[38,3,256]{2,1,0:T(4,128)(2,1)S(1)} %pad_maximum_fusion.1), channel_id=1, source_target_pairs={{0,1},{1,2},{2,3},{3,4},{4,5},{5,6},{6,7},{7,8},{8,9},{9,10},{10,1... | collective-permute-start | bytes 175112 | tf_op jit(solution)/shard_map/ppermute | solution.py:15
  21.8 1.4 %collective-permute-done.2 = bf16[38,3,256]{2,1,0:T(4,128)(2,1)S(1)} collective-permute-done((bf16[38,3,256]{2,1,0:T(4,128)(2,1)S(1)}, bf16[38,3,256]{2,1,0:T(4,128)(2,1)S(1)}, u32[]{:S(2)}, u32[]{:S(2)}) %collective-permute-start.2) | collective-permute-done | bytes 58400 | tf_op jit(solution)/shard_map/ppermute | solution.py:15
  23.2 1.4 %maximum_maximum_fusion.x_ref = bf16[38,41,256]{2,1,0:T(8,128)(2,1)} fusion(bf16[38,3,256]{2,1,0:T(4,128)(2,1)S(1)} %collective-permute-done.3, bf16[3,32,256]{2,1,0:T(8,128)(2,1)S(1)} %collective-permute-done.1, bf16[32,32,256]{2,1,0:T(8,128)(2,1)S(1)} %copy-done.1, bf16[3,32,256]{2,1,0:T(8,128)(2,1)S(1)} %collective-permute-done, ...), kind=kLoop, calls=%fused_computation.10 | loop fusion | flops 4786176 | bytes 1537106 | tf_op jit(solution)/shard_map/concatenate | solution.py:222
  24.6 9.5 %shard_map.136 = bf16[32,32,256]{2,1,0:T(8,128)(2,1)} custom-call(bf16[38,41,256]{2,1,0:T(8,128)(2,1)} %maximum_maximum_fusion.x_ref, bf16[7,7,256]{2,1,0:T(8,128)(2,1)} %k_ref.1, f32[1,256]{1,0:T(1,128)} %bitcast.75, f32[1,256]{1,0:T(1,128)} %bitcast.76, f32[1,256]{1,0:T(1,128)} %bitcast.77), custom_call_target="tpu_custom_call" | custom-call | flops 25690112 | bytes 1321984 | tf_op jit(solution)/shard_map/pallas_call | solution.py:79
  34.1 8.7 %shard_map.137 = (bf16[1024,256]{1,0:T(8,128)(2,1)}, f32[16,256]{1,0:T(8,128)}, bf16[16,16,256]{2,1,0:T(8,128)(2,1)}) custom-call(bf16[1024,256]{1,0:T(8,128)(2,1)} %bitcast.70, bf16[1024,256]{1,0:T(8,128)(2,1)} %bitcast.69, bf16[256,1024]{1,0:T(8,128)(2,1)} %we_ref.1, f32[1,1024]{1,0:T(1,128)} %bitcast.78, bf16[1024,256]{1,0:T(8,128)(2,1)} %wr_ref.1, ...), custom_call_target="tpu_custom_call" | custom-call | flops 1073741824 | bytes 2621440 | tf_op jit(solution)/shard_map/pallas_call | solution.py:169
  42.8 6.5 %all-to-all-start = ((bf16[16,16,256]{2,1,0:T(8,128)(2,1)}), bf16[16,16,256]{2,1,0:T(8,128)(2,1)S(1)}, u32[]{:S(2)}, u32[]{:S(2)}) async-start(bf16[16,16,256]{2,1,0:T(8,128)(2,1)} %get-tuple-element.9), calls=%async_computation | async-start | bytes 262144 | tf_op jit(solution)/shard_map/all_to_all | solution.py:284
  49.5 0.2 reshape.77
  49.8 5.7 %all-to-all-done = bf16[16,16,256]{2,1,0:T(8,128)(2,1)S(1)} async-done(((bf16[16,16,256]{2,1,0:T(8,128)(2,1)}), bf16[16,16,256]{2,1,0:T(8,128)(2,1)S(1)}, u32[]{:S(2)}, u32[]{:S(2)}) %all-to-all-start) | async-done | bytes 131104 | tf_op jit(solution)/shard_map/all_to_all | solution.py:284
  55.7 0.2 convolution_convert_fusion
  55.9 0.1 copy.21
  56.0 0.1 fusion.3
  56.2 0.2 fusion.16
  56.5 0.3 fusion.4
  56.9 0.1 fusion.6
  57.0 0.1 broadcast_in_dim.5
  57.2 0.4 copy-done.2
  57.5 1.0 %fusion.5 = bf16[32,32,256]{2,1,0:T(8,128)(2,1)} fusion(f32[32,32,256]{2,1,0:T(8,128)S(1)} %bitcast.68, bf16[32,32,256]{2,1,0:T(8,128)(2,1)S(1)} %bitcast.73), kind=kLoop, calls=%fused_computation.9 | loop fusion | flops 786432 | bytes 2097152 | tf_op jit(solution)/shard_map/convert_element_type | solution.py:324
  (30 shorter events, 0.9 us)
Async XLA Ops:
  0.0 55.6 %copy-start = (bf16[256,512]{1,0:T(8,128)(2,1)S(1)}, bf16[256,512]{1,0:T(8,128)(2,1)}, u32[]{:S(2)}) copy-start(bf16[256,512]{1,0:T(8,128)(2,1)} %param.25) | copy-start | bytes 786436
  0.0 23.2 %copy-start.1 = (bf16[32,32,256]{2,1,0:T(8,128)(2,1)S(1)}, bf16[32,32,256]{2,1,0:T(8,128)(2,1)}, u32[]{:S(2)}) copy-start(bf16[32,32,256]{2,1,0:T(8,128)(2,1)} %param.14) | copy-start | bytes 1572868
  0.9 9.4 %collective-permute-start = (bf16[3,32,256]{2,1,0:T(8,128)(2,1)S(1)}, bf16[3,32,256]{2,1,0:T(8,128)(2,1)S(1)}, u32[]{:S(2)}, u32[]{:S(2)}) collective-permute-start(bf16[3,32,256]{2,1,0:T(8,128)(2,1)S(1)} %get-tuple-element.13), channel_id=1, source_target_pairs={{0,16},{16,32},{32,48},{48,64},{64,80},{80,96},{96,112},{112,128},... | collective-permute-start | bytes 147464 | tf_op jit(solution)/shard_map/ppermute | solution.py:15
  5.4 8.4 %collective-permute-start.1 = (bf16[3,32,256]{2,1,0:T(8,128)(2,1)S(1)}, bf16[3,32,256]{2,1,0:T(8,128)(2,1)S(1)}, u32[]{:S(2)}, u32[]{:S(2)}) collective-permute-start(bf16[3,32,256]{2,1,0:T(8,128)(2,1)S(1)} %get-tuple-element.14), channel_id=1, source_target_pairs={{16,0},{32,16},{48,32},{64,48},{80,64},{96,80},{112,96},{128,112},... | collective-permute-start | bytes 147464 | tf_op jit(solution)/shard_map/ppermute | solution.py:15
  14.0 7.9 %collective-permute-start.3 = (bf16[38,3,256]{2,1,0:T(4,128)(2,1)S(1)}, bf16[38,3,256]{2,1,0:T(4,128)(2,1)S(1)}, u32[]{:S(2)}, u32[]{:S(2)}) collective-permute-start(bf16[38,3,256]{2,1,0:T(4,128)(2,1)S(1)} %pad_maximum_fusion.2), channel_id=1, source_target_pairs={{1,0},{2,1},{3,2},{4,3},{5,4},{6,5},{7,6},{8,7},{9,8},{10,9},{11,1... | collective-permute-start | bytes 175112 | tf_op jit(solution)/shard_map/ppermute | solution.py:15
  18.1 5.1 %collective-permute-start.2 = (bf16[38,3,256]{2,1,0:T(4,128)(2,1)S(1)}, bf16[38,3,256]{2,1,0:T(4,128)(2,1)S(1)}, u32[]{:S(2)}, u32[]{:S(2)}) collective-permute-start(bf16[38,3,256]{2,1,0:T(4,128)(2,1)S(1)} %pad_maximum_fusion.1), channel_id=1, source_target_pairs={{0,1},{1,2},{2,3},{3,4},{4,5},{5,6},{6,7},{7,8},{8,9},{9,10},{10,1... | collective-permute-start | bytes 175112 | tf_op jit(solution)/shard_map/ppermute | solution.py:15
  42.8 6.9 %copy-start.4 = (f32[16,256]{1,0:T(8,128)S(1)}, f32[16,256]{1,0:T(8,128)}, u32[]{:S(2)}) copy-start(f32[16,256]{1,0:T(8,128)} %get-tuple-element.10) | copy-start | bytes 49156
  42.8 12.7 %all-to-all-start = ((bf16[16,16,256]{2,1,0:T(8,128)(2,1)}), bf16[16,16,256]{2,1,0:T(8,128)(2,1)S(1)}, u32[]{:S(2)}, u32[]{:S(2)}) async-start(bf16[16,16,256]{2,1,0:T(8,128)(2,1)} %get-tuple-element.9), calls=%async_computation | async-start | bytes 262144 | tf_op jit(solution)/shard_map/all_to_all | solution.py:284
  55.9 1.0 %copy-start.3 = (bf16[256,256]{1,0:T(8,128)(2,1)S(1)}, bf16[256,256]{1,0:T(8,128)(2,1)}, u32[]{:S(2)}) copy-start(bf16[256,256]{1,0:T(8,128)(2,1)} %param.27) | copy-start | bytes 393220
  56.5 1.1 %copy-start.2 = (bf16[1024,256]{1,0:T(8,128)(2,1)S(1)}, bf16[1024,256]{1,0:T(8,128)(2,1)}, u32[]{:S(2)}) copy-start(bf16[1024,256]{1,0:T(8,128)(2,1)} %get-tuple-element.8) | copy-start | bytes 1572868

commit v12 on v11

--- a/solution.py
+++ b/solution.py
@@ -35,7 +35,9 @@
     rows_p = x_ref.shape[0]
     tile_rows, tile_cols, channels = o_ref.shape
     for a in range(TAPS):
-        kf_ref[a, pl.ds(0, TAPS), :] = k_ref[a].astype(jnp.float32)
+        taps = k_ref[a].astype(jnp.float32)
+        for b in range(TAPS):
+            kf_ref[b, a] = jnp.broadcast_to(taps[b : b + 1], (8, channels))
 
     def widen(r, carry):
         row = x_ref[r].astype(jnp.float32)
@@ -50,27 +52,34 @@
     lanes = 128
     halves = channels // lanes
 
+    col_blocks = tile_cols // 8
+
     def body(i, carry):
-        r0 = pl.multiple_of(i * ROW_BLOCK, ROW_BLOCK)
-        for s0 in range(0, tile_cols, 8):
-            parts = []
+        r0 = pl.multiple_of((i // col_blocks) * ROW_BLOCK, ROW_BLOCK)
+        s0 = pl.multiple_of((i % col_blocks) * 8, 8)
+
+        def tap_column(b, accs):
+            new = []
             for h in range(halves):
                 lane = pl.ds(h * lanes, lanes)
-                acc = jnp.zeros((ROW_BLOCK, 8, lanes), jnp.float32)
-                for b in range(TAPS):
-                    x = sh_ref[b, pl.ds(r0, ROW_BLOCK + TAPS - 1), pl.ds(s0, 8), lane]
-                    for a in range(TAPS):
-                        acc = acc + x[a : a + ROW_BLOCK] * kf_ref[a, pl.ds(b, 1), lane]
-                parts.append(acc)
-            acc = jnp.concatenate(parts, axis=-1) + db
-            mean = jnp.mean(acc, axis=-1, keepdims=True)
-            cen = acc - mean
-            var = jnp.mean(cen * cen, axis=-1, keepdims=True)
-            normed = cen * lax.rsqrt(var + 1e-06) * g + nb
-            o_ref[pl.ds(r0, ROW_BLOCK), pl.ds(s0, 8), :] = normed.astype(o_ref.dtype)
+                x = sh_ref[b, pl.ds(r0, ROW_BLOCK + TAPS - 1), pl.ds(s0, 8), lane]
+                acc = accs[h]
+                for a in range(TAPS):
+                    acc = acc + x[a : a + ROW_BLOCK] * kf_ref[b, a, :, lane][None]
+                new.append(acc)
+            return tuple(new)
+
+        zero = jnp.zeros((ROW_BLOCK, 8, lanes), jnp.float32)
+        parts = lax.fori_loop(0, TAPS, tap_column, (zero,) * halves)
+        acc = jnp.concatenate(parts, axis=-1) + db
+        mean = jnp.mean(acc, axis=-1, keepdims=True)
+        cen = acc - mean
+        var = jnp.mean(cen * cen, axis=-1, keepdims=True)
+        normed = cen * lax.rsqrt(var + 1e-06) * g + nb
+        o_ref[pl.ds(r0, ROW_BLOCK), pl.ds(s0, 8), :] = normed.astype(o_ref.dtype)
         return carry
 
-    lax.fori_loop(0, tile_rows // ROW_BLOCK, body, 0)
+    lax.fori_loop(0, (tile_rows // ROW_BLOCK) * col_blocks, body, 0)
 
 
 def conv_norm(padded, dw_kernel, dw_bias, norm_gain, norm_bias, tile_rows, tile_cols):
@@ -82,7 +91,7 @@
         in_specs=[vmem] * 5,
         out_specs=vmem,
         scratch_shapes=[
-            pltpu.VMEM((TAPS, 8, channels), jnp.float32),
+            pltpu.VMEM((TAPS, TAPS, 8, channels), jnp.float32),
             pltpu.VMEM((TAPS, rows_p, tile_cols, channels), jnp.float32),
         ],
         cost_estimate=pl.CostEstimate(
@@ -290,10 +299,13 @@
     band_keyval = jnp.dot(band_pooled, w_keyval, preferred_element_type=jnp.float32).astype(
         jnp.bfloat16
     )
-    windows = []
-    for query_col in range(region_side):
-        first = span_cols - 1 - (position * region_side + query_col)
-        windows.append(lax.dynamic_slice_in_dim(rel_bias, first, span_cols, axis=2))
+    window_all = lax.dynamic_slice_in_dim(
+        rel_bias, span_cols - region_side - position * region_side, span_cols + region_side - 1, axis=2
+    )
+    windows = [
+        window_all[:, :, region_side - 1 - query_col : region_side - 1 - query_col + span_cols]
+        for query_col in range(region_side)
+    ]
     rows_of = []
     for query_row in range(region_side):
         per_col = [

time: 59 us -> 59.5 us (level)
  no operation moved by 1% of the time
where the time goes in v12:
time: 59.5 us; the launch traced here: 59 us
  starting transfers between devices  21 us (35%)
  Pallas kernels  18.7 us (31%)
  waiting for transfers between devices  10.7 us (18%)
  local copies, waits for them, and re-layouts  4.79 us (8%)
  other arithmetic  2.72 us (5%)
  matrix products  0.79 us (1%)
    ppermute x4, starting transfers between devices, shifted(): return (lax.ppermute(piece, axis, up), lax.ppermute(piece, axis, down))  14.5 us
    pallas_call x1, Pallas kernels, conv_norm(): pl.pallas_call(conv_norm_kernel, out_shape=jax.ShapeDtypeStruct((tile_row...  9.93 us
    pallas_call x1, Pallas kernels, mlp(): pl.pallas_call(mlp_kernel, out_shape=(jax.ShapeDtypeStruct((pixels, chann...  8.75 us
    all_to_all x1, starting transfers between devices, shards(): band_pooled = lax.all_to_all(sent, 'col', 0, 0)  6.53 us
    all_to_all x1, waiting for transfers between devices, shards(): band_pooled = lax.all_to_all(sent, 'col', 0, 0)  5.74 us
    ppermute x4, waiting for transfers between devices, shifted(): return (lax.ppermute(piece, axis, up), lax.ppermute(piece, axis, down))  4.99 us
    another operation x1, local copies, waits for them, and re-layouts, shards(): rows_of.append(jnp.stack(per_col, axis=1))  1.45 us
    concatenate x1, other arithmetic, block_pass(): jnp.concatenate([left, extended, right, jnp.zeros_like(right)[:, :-(tile_...  1.4 us
  transfers between devices with their start and end apart: 5, of which 3 were waited for; matrix products, arithmetic and copies ran while one was open for 5% of the time, Pallas kernels for 0%

profile of v12, /device:TPU:113, one launch (start us, length us, event | category | flops | bytes accessed | tf_op | source)
XLA Modules:
  0.0 59.0 jit_solution(9076537319735964172)
XLA Ops:
  0.0 0.9 %fusion.12 = (bf16[3,32,256]{2,1,0:T(8,128)(2,1)S(1)}, bf16[3,32,256]{2,1,0:T(8,128)(2,1)S(1)}) fusion(bf16[32,32,256]{2,1,0:T(8,128)(2,1)} %param.14), kind=kLoop, calls=%fused_computation.42 | loop fusion | bytes 196608 | tf_op jit(solution)/shard_map/slice | solution.py:20
  0.9 4.5 %collective-permute-start = (bf16[3,32,256]{2,1,0:T(8,128)(2,1)S(1)}, bf16[3,32,256]{2,1,0:T(8,128)(2,1)S(1)}, u32[]{:S(2)}, u32[]{:S(2)}) collective-permute-start(bf16[3,32,256]{2,1,0:T(8,128)(2,1)S(1)} %get-tuple-element.13), channel_id=1, source_target_pairs={{0,16},{16,32},{32,48},{48,64},{64,80},{80,96},{96,112},{112,128},... | collective-permute-start | bytes 147464 | tf_op jit(solution)/shard_map/ppermute | solution.py:15
  5.4 2.3 %collective-permute-start.1 = (bf16[3,32,256]{2,1,0:T(8,128)(2,1)S(1)}, bf16[3,32,256]{2,1,0:T(8,128)(2,1)S(1)}, u32[]{:S(2)}, u32[]{:S(2)}) collective-permute-start(bf16[3,32,256]{2,1,0:T(8,128)(2,1)S(1)} %get-tuple-element.14), channel_id=1, source_target_pairs={{16,0},{32,16},{48,32},{64,48},{80,64},{96,80},{112,96},{128,112},... | collective-permute-start | bytes 147464 | tf_op jit(solution)/shard_map/ppermute | solution.py:15
  7.7 1.0 %fusion.11 = (bf16[32,3,256]{2,1,0:T(4,128)(2,1)S(1)}, bf16[32,3,256]{2,1,0:T(4,128)(2,1)S(1)}) fusion(bf16[32,32,256]{2,1,0:T(8,128)(2,1)} %param.14), kind=kLoop, calls=%fused_computation.41 | loop fusion | bytes 196608 | tf_op jit(solution)/shard_map/slice | solution.py:23
  8.7 1.4 %dynamic-slice_bitcast_fusion.15 = (f32[8,1,4,64]{3,0,2,1:T(8,128)S(1)}, f32[8,1,4,64]{3,0,2,1:T(8,128)S(1)}, f32[8,1,4,64]{3,0,2,1:T(8,128)S(1)}, f32[8,1,4,64]...) fusion(f32[8,7,127]{2,0,1:T(8,128)} %param.26, ...), kind=kLoop, calls=%fused_computation.39 | loop fusion | bytes 262172 | tf_op jit(solution)/shard_map/stack | solution.py:314
  10.3 3.6 %collective-permute-done.1 = bf16[3,32,256]{2,1,0:T(8,128)(2,1)S(1)} collective-permute-done((bf16[3,32,256]{2,1,0:T(8,128)(2,1)S(1)}, bf16[3,32,256]{2,1,0:T(8,128)(2,1)S(1)}, u32[]{:S(2)}, u32[]{:S(2)}) %collective-permute-start.1) | collective-permute-done | bytes 49184 | tf_op jit(solution)/shard_map/ppermute | solution.py:15
  14.0 4.0 %collective-permute-start.3 = (bf16[38,3,256]{2,1,0:T(4,128)(2,1)S(1)}, bf16[38,3,256]{2,1,0:T(4,128)(2,1)S(1)}, u32[]{:S(2)}, u32[]{:S(2)}) collective-permute-start(bf16[38,3,256]{2,1,0:T(4,128)(2,1)S(1)} %pad_maximum_fusion.2), channel_id=1, source_target_pairs={{1,0},{2,1},{3,2},{4,3},{5,4},{6,5},{7,6},{8,7},{9,8},{10,9},{11,1... | collective-permute-start | bytes 175112 | tf_op jit(solution)/shard_map/ppermute | solution.py:15
  18.1 3.7 %collective-permute-start.2 = (bf16[38,3,256]{2,1,0:T(4,128)(2,1)S(1)}, bf16[38,3,256]{2,1,0:T(4,128)(2,1)S(1)}, u32[]{:S(2)}, u32[]{:S(2)}) collective-permute-start(bf16[38,3,256]{2,1,0:T(4,128)(2,1)S(1)} %pad_maximum_fusion.1), channel_id=1, source_target_pairs={{0,1},{1,2},{2,3},{3,4},{4,5},{5,6},{6,7},{7,8},{8,9},{9,10},{10,1... | collective-permute-start | bytes 175112 | tf_op jit(solution)/shard_map/ppermute | solution.py:15
  21.8 1.4 %collective-permute-done.2 = bf16[38,3,256]{2,1,0:T(4,128)(2,1)S(1)} collective-permute-done((bf16[38,3,256]{2,1,0:T(4,128)(2,1)S(1)}, bf16[38,3,256]{2,1,0:T(4,128)(2,1)S(1)}, u32[]{:S(2)}, u32[]{:S(2)}) %collective-permute-start.2) | collective-permute-done | bytes 58400 | tf_op jit(solution)/shard_map/ppermute | solution.py:15
  23.2 1.4 %maximum_maximum_fusion.x_ref = bf16[38,41,256]{2,1,0:T(8,128)(2,1)} fusion(bf16[38,3,256]{2,1,0:T(4,128)(2,1)S(1)} %collective-permute-done.3, bf16[3,32,256]{2,1,0:T(8,128)(2,1)S(1)} %collective-permute-done.1, bf16[32,32,256]{2,1,0:T(8,128)(2,1)S(1)} %copy-done.1, bf16[3,32,256]{2,1,0:T(8,128)(2,1)S(1)} %collective-permute-done, ...), kind=kLoop, calls=%fused_computation.10 | loop fusion | flops 4786176 | bytes 1537106 | tf_op jit(solution)/shard_map/concatenate | solution.py:231
  24.6 9.9 %shard_map.136 = bf16[32,32,256]{2,1,0:T(8,128)(2,1)} custom-call(bf16[38,41,256]{2,1,0:T(8,128)(2,1)} %maximum_maximum_fusion.x_ref, bf16[7,7,256]{2,1,0:T(8,128)(2,1)} %k_ref.1, f32[1,256]{1,0:T(1,128)} %bitcast.75, f32[1,256]{1,0:T(1,128)} %bitcast.76, f32[1,256]{1,0:T(1,128)} %bitcast.77), custom_call_target="tpu_custom_call" | custom-call | flops 25690112 | bytes 1321984 | tf_op jit(solution)/shard_map/pallas_call | solution.py:88
  34.5 8.7 %shard_map.137 = (bf16[1024,256]{1,0:T(8,128)(2,1)}, f32[16,256]{1,0:T(8,128)}, bf16[16,16,256]{2,1,0:T(8,128)(2,1)}) custom-call(bf16[1024,256]{1,0:T(8,128)(2,1)} %bitcast.70, bf16[1024,256]{1,0:T(8,128)(2,1)} %bitcast.69, bf16[256,1024]{1,0:T(8,128)(2,1)} %we_ref.1, f32[1,1024]{1,0:T(1,128)} %bitcast.78, bf16[1024,256]{1,0:T(8,128)(2,1)} %wr_ref.1, ...), custom_call_target="tpu_custom_call" | custom-call | flops 1073741824 | bytes 2621440 | tf_op jit(solution)/shard_map/pallas_call | solution.py:178
  43.3 6.5 %all-to-all-start = ((bf16[16,16,256]{2,1,0:T(8,128)(2,1)}), bf16[16,16,256]{2,1,0:T(8,128)(2,1)S(1)}, u32[]{:S(2)}, u32[]{:S(2)}) async-start(bf16[16,16,256]{2,1,0:T(8,128)(2,1)} %get-tuple-element.9), calls=%async_computation | async-start | bytes 262144 | tf_op jit(solution)/shard_map/all_to_all | solution.py:293
  49.9 0.2 reshape.77
  50.2 5.7 %all-to-all-done = bf16[16,16,256]{2,1,0:T(8,128)(2,1)S(1)} async-done(((bf16[16,16,256]{2,1,0:T(8,128)(2,1)}), bf16[16,16,256]{2,1,0:T(8,128)(2,1)S(1)}, u32[]{:S(2)}, u32[]{:S(2)}) %all-to-all-start) | async-done | bytes 131104 | tf_op jit(solution)/shard_map/all_to_all | solution.py:293
  56.1 0.2 convolution_convert_fusion
  56.4 0.1 copy.21
  56.5 0.1 fusion.3
  56.6 0.2 fusion.16
  57.0 0.3 fusion.4
  57.4 0.1 fusion.6
  57.5 0.1 broadcast_in_dim.5
  57.6 0.4 copy-done.2
  58.0 1.0 %fusion.5 = bf16[32,32,256]{2,1,0:T(8,128)(2,1)} fusion(f32[32,32,256]{2,1,0:T(8,128)S(1)} %bitcast.68, bf16[32,32,256]{2,1,0:T(8,128)(2,1)S(1)} %bitcast.73), kind=kLoop, calls=%fused_computation.9 | loop fusion | flops 786432 | bytes 2097152 | tf_op jit(solution)/shard_map/convert_element_type | solution.py:336
  (30 shorter events, 0.9 us)
Async XLA Ops:
  0.0 56.1 %copy-start = (bf16[256,512]{1,0:T(8,128)(2,1)S(1)}, bf16[256,512]{1,0:T(8,128)(2,1)}, u32[]{:S(2)}) copy-start(bf16[256,512]{1,0:T(8,128)(2,1)} %param.25) | copy-start | bytes 786436
  0.0 23.2 %copy-start.1 = (bf16[32,32,256]{2,1,0:T(8,128)(2,1)S(1)}, bf16[32,32,256]{2,1,0:T(8,128)(2,1)}, u32[]{:S(2)}) copy-start(bf16[32,32,256]{2,1,0:T(8,128)(2,1)} %param.14) | copy-start | bytes 1572868
  0.9 9.4 %collective-permute-start = (bf16[3,32,256]{2,1,0:T(8,128)(2,1)S(1)}, bf16[3,32,256]{2,1,0:T(8,128)(2,1)S(1)}, u32[]{:S(2)}, u32[]{:S(2)}) collective-permute-start(bf16[3,32,256]{2,1,0:T(8,128)(2,1)S(1)} %get-tuple-element.13), channel_id=1, source_target_pairs={{0,16},{16,32},{32,48},{48,64},{64,80},{80,96},{96,112},{112,128},... | collective-permute-start | bytes 147464 | tf_op jit(solution)/shard_map/ppermute | solution.py:15
  5.4 8.4 %collective-permute-start.1 = (bf16[3,32,256]{2,1,0:T(8,128)(2,1)S(1)}, bf16[3,32,256]{2,1,0:T(8,128)(2,1)S(1)}, u32[]{:S(2)}, u32[]{:S(2)}) collective-permute-start(bf16[3,32,256]{2,1,0:T(8,128)(2,1)S(1)} %get-tuple-element.14), channel_id=1, source_target_pairs={{16,0},{32,16},{48,32},{64,48},{80,64},{96,80},{112,96},{128,112},... | collective-permute-start | bytes 147464 | tf_op jit(solution)/shard_map/ppermute | solution.py:15
  14.0 7.9 %collective-permute-start.3 = (bf16[38,3,256]{2,1,0:T(4,128)(2,1)S(1)}, bf16[38,3,256]{2,1,0:T(4,128)(2,1)S(1)}, u32[]{:S(2)}, u32[]{:S(2)}) collective-permute-start(bf16[38,3,256]{2,1,0:T(4,128)(2,1)S(1)} %pad_maximum_fusion.2), channel_id=1, source_target_pairs={{1,0},{2,1},{3,2},{4,3},{5,4},{6,5},{7,6},{8,7},{9,8},{10,9},{11,1... | collective-permute-start | bytes 175112 | tf_op jit(solution)/shard_map/ppermute | solution.py:15
  18.1 5.1 %collective-permute-start.2 = (bf16[38,3,256]{2,1,0:T(4,128)(2,1)S(1)}, bf16[38,3,256]{2,1,0:T(4,128)(2,1)S(1)}, u32[]{:S(2)}, u32[]{:S(2)}) collective-permute-start(bf16[38,3,256]{2,1,0:T(4,128)(2,1)S(1)} %pad_maximum_fusion.1), channel_id=1, source_target_pairs={{0,1},{1,2},{2,3},{3,4},{4,5},{5,6},{6,7},{7,8},{8,9},{9,10},{10,1... | collective-permute-start | bytes 175112 | tf_op jit(solution)/shard_map/ppermute | solution.py:15
  43.3 6.9 %copy-start.4 = (f32[16,256]{1,0:T(8,128)S(1)}, f32[16,256]{1,0:T(8,128)}, u32[]{:S(2)}) copy-start(f32[16,256]{1,0:T(8,128)} %get-tuple-element.10) | copy-start | bytes 49156
  43.3 12.7 %all-to-all-start = ((bf16[16,16,256]{2,1,0:T(8,128)(2,1)}), bf16[16,16,256]{2,1,0:T(8,128)(2,1)S(1)}, u32[]{:S(2)}, u32[]{:S(2)}) async-start(bf16[16,16,256]{2,1,0:T(8,128)(2,1)} %get-tuple-element.9), calls=%async_computation | async-start | bytes 262144 | tf_op jit(solution)/shard_map/all_to_all | solution.py:293
  56.4 1.0 %copy-start.3 = (bf16[256,256]{1,0:T(8,128)(2,1)S(1)}, bf16[256,256]{1,0:T(8,128)(2,1)}, u32[]{:S(2)}) copy-start(bf16[256,256]{1,0:T(8,128)(2,1)} %param.27) | copy-start | bytes 393220
  56.9 1.1 %copy-start.2 = (bf16[1024,256]{1,0:T(8,128)(2,1)S(1)}, bf16[1024,256]{1,0:T(8,128)(2,1)}, u32[]{:S(2)}) copy-start(bf16[1024,256]{1,0:T(8,128)(2,1)} %get-tuple-element.8) | copy-start | bytes 1572868

commit v13 on v11

--- a/solution.py
+++ b/solution.py
@@ -72,33 +72,6 @@
 
     lax.fori_loop(0, tile_rows // ROW_BLOCK, body, 0)
 
-
-def conv_norm(padded, dw_kernel, dw_bias, norm_gain, norm_bias, tile_rows, tile_cols):
-    rows_p, cols_p, channels = padded.shape
-    vmem = pl.BlockSpec(memory_space=pltpu.VMEM)
-    return pl.pallas_call(
-        conv_norm_kernel,
-        out_shape=jax.ShapeDtypeStruct((tile_rows, tile_cols, channels), jnp.bfloat16),
-        in_specs=[vmem] * 5,
-        out_specs=vmem,
-        scratch_shapes=[
-            pltpu.VMEM((TAPS, 8, channels), jnp.float32),
-            pltpu.VMEM((TAPS, rows_p, tile_cols, channels), jnp.float32),
-        ],
-        cost_estimate=pl.CostEstimate(
-            flops=2 * TAPS * TAPS * tile_rows * tile_cols * channels,
-            bytes_accessed=2 * (rows_p * cols_p + tile_rows * tile_cols) * channels,
-            transcendentals=tile_rows * tile_cols,
-        ),
-    )(
-        padded,
-        dw_kernel,
-        dw_bias.reshape(1, channels),
-        norm_gain.reshape(1, channels),
-        norm_bias.reshape(1, channels),
-    )
-
-
 ERFC_COEFFS = (
     -1.26551223,
     1.00002368,
@@ -126,10 +99,9 @@
     return 0.5 * pre * one_plus_erf
 
 
-def mlp_kernel(n_ref, f_ref, we_ref, be_ref, wr_ref, br_ref, ls_ref, wq_ref, o_ref, q_ref, s_ref):
-    normed = n_ref[...]
+def mlp_block(normed, features, we_ref, be_ref, wr_ref, br_ref, ls_ref, out_dtype):
     hidden_total = we_ref.shape[1]
-    acc = jnp.zeros(o_ref.shape, jnp.float32)
+    acc = jnp.zeros(features.shape, jnp.float32)
     for h0 in range(0, hidden_total, HIDDEN_BLOCK):
         pre = (
             jnp.dot(normed, we_ref[:, h0 : h0 + HIDDEN_BLOCK], preferred_element_type=jnp.float32)
@@ -138,9 +110,11 @@
         hidden = gelu_exact(pre).astype(jnp.bfloat16)
         acc = acc + jnp.dot(hidden, wr_ref[h0 : h0 + HIDDEN_BLOCK, :], preferred_element_type=jnp.float32)
     reduced = acc + br_ref[...]
-    out = (f_ref[...].astype(jnp.float32) + ls_ref[...] * reduced).astype(o_ref.dtype)
-    o_ref[...] = out
-    pixels, channels = o_ref.shape
+    return (features.astype(jnp.float32) + ls_ref[...] * reduced).astype(out_dtype)
+
+
+def region_tokens(out, wq_ref, copies):
+    pixels, channels = out.shape
     tile_cols = pixels // 8
     per_row = tile_cols // 8
     column_sums = out.astype(jnp.float32).reshape(8, tile_cols, channels).sum(axis=0)
@@ -148,51 +122,76 @@
     pooled = (region_sums * jnp.float32(1.0 / 64.0)).astype(jnp.bfloat16)
     queries = jnp.dot(pooled, wq_ref[...], preferred_element_type=jnp.float32)
     queries = queries.astype(jnp.bfloat16).astype(jnp.float32)
-    copies = jnp.broadcast_to(pooled[None], (s_ref.shape[0], per_row, channels))
-    step = pl.program_id(0)
-    for k in range(s_ref.shape[1] // per_row):
-
-        @pl.when(step == k)
-        def _():
-            q_ref[pl.ds(k * per_row, per_row), :] = queries
-            s_ref[:, pl.ds(k * per_row, per_row), :] = copies
-
-
-def mlp(normed, features, w_expand, b_expand, w_reduce, b_reduce, layer_scale, w_query, tile_cols, copies):
-    pixels, channels = normed.shape
+    return queries, jnp.broadcast_to(pooled[None], (copies, per_row, channels))
+
+
+def block_kernel(
+    x_ref, k_ref, db_ref, g_ref, nb_ref, f_ref, we_hbm, be_ref, wr_hbm, br_ref, ls_ref, wq_hbm,
+    o_ref, q_ref, s_ref, kf_ref, sh_ref, n_ref, we_ref, wr_ref, wq_ref, sem,
+):
+    loads = [
+        pltpu.make_async_copy(source, target, sem.at[i])
+        for i, (source, target) in enumerate(((we_hbm, we_ref), (wr_hbm, wr_ref), (wq_hbm, wq_ref)))
+    ]
+    for load in loads:
+        load.start()
+    conv_norm_kernel(x_ref, k_ref, db_ref, g_ref, nb_ref, n_ref, kf_ref, sh_ref)
+    for load in loads:
+        load.wait()
+    tile_rows, tile_cols, channels = n_ref.shape
+    per_row = tile_cols // 8
+    block = 8 * tile_cols
+    for step in range(tile_rows // 8):
+        rows = pl.ds(step * block, block)
+        normed = n_ref[pl.ds(step * 8, 8)].reshape(block, channels)
+        out = mlp_block(normed, f_ref[rows], we_ref, be_ref, wr_ref, br_ref, ls_ref, o_ref.dtype)
+        o_ref[rows] = out
+        queries, copies = region_tokens(out, wq_ref, s_ref.shape[0])
+        q_ref[pl.ds(step * per_row, per_row), :] = queries
+        s_ref[:, pl.ds(step * per_row, per_row), :] = copies
+
+
+def block_call(
+    padded, features, dw_kernel, dw_bias, norm_gain, norm_bias, w_expand, b_expand, w_reduce,
+    b_reduce, layer_scale, w_query, copies,
+):
+    rows_p, cols_p, channels = padded.shape
+    tile_rows, tile_cols = features.shape[:2]
+    pixels = tile_rows * tile_cols
     hidden_total = w_expand.shape[1]
-    block = 8 * tile_cols
-    steps = pixels // block
-    tokens = steps * (tile_cols // 8)
-    rows = pl.BlockSpec((block, channels), lambda i: (i, 0))
-    whole = lambda shape: pl.BlockSpec(shape, lambda i: (0,) * len(shape))
+    tokens = pixels // 64
+    vmem = pl.BlockSpec(memory_space=pltpu.VMEM)
+    anywhere = pl.BlockSpec(memory_space=pl.ANY)
     return pl.pallas_call(
-        mlp_kernel,
+        block_kernel,
         out_shape=(
             jax.ShapeDtypeStruct((pixels, channels), jnp.bfloat16),
             jax.ShapeDtypeStruct((tokens, channels), jnp.float32),
             jax.ShapeDtypeStruct((copies, tokens, channels), jnp.bfloat16),
         ),
-        grid=(steps,),
-        in_specs=[
-            rows,
-            rows,
-            whole((channels, hidden_total)),
-            whole((1, hidden_total)),
-            whole((hidden_total, channels)),
-            whole((1, channels)),
-            whole((1, channels)),
-            whole((channels, channels)),
+        in_specs=[vmem] * 6 + [anywhere, vmem, anywhere, vmem, vmem, anywhere],
+        out_specs=(vmem, vmem, vmem),
+        scratch_shapes=[
+            pltpu.VMEM((TAPS, 8, channels), jnp.float32),
+            pltpu.VMEM((TAPS, rows_p, tile_cols, channels), jnp.float32),
+            pltpu.VMEM((tile_rows, tile_cols, channels), jnp.bfloat16),
+            pltpu.VMEM((channels, hidden_total), jnp.bfloat16),
+            pltpu.VMEM((hidden_total, channels), jnp.bfloat16),
+            pltpu.VMEM((channels, channels), jnp.bfloat16),
+            pltpu.SemaphoreType.DMA((3,)),
         ],
-        out_specs=(rows, whole((tokens, channels)), whole((copies, tokens, channels))),
         cost_estimate=pl.CostEstimate(
-            flops=4 * pixels * channels * hidden_total,
-            bytes_accessed=2 * (3 * pixels * channels + 2 * channels * hidden_total),
+            flops=2 * TAPS * TAPS * pixels * channels + 4 * pixels * channels * hidden_total,
+            bytes_accessed=2 * (rows_p * cols_p * channels + 2 * pixels * channels + 2 * channels * hidden_total),
             transcendentals=2 * pixels * hidden_total,
         ),
     )(
-        normed,
-        features,
+        padded,
+        dw_kernel,
+        dw_bias.reshape(1, channels),
+        norm_gain.reshape(1, channels),
+        norm_bias.reshape(1, channels),
+        features.reshape(pixels, channels),
         w_expand,
         b_expand.reshape(1, hidden_total),
         w_reduce,
@@ -222,19 +221,19 @@
     padded = jnp.concatenate(
         [left, extended, right, jnp.zeros_like(right)[:, : -(tile_cols + 3 * 3) % 8]], axis=1
     )
-    normed = conv_norm(
-        padded, dw_kernel, dw_bias, norm_gain, norm_bias, tile_rows, tile_cols
-    ).reshape(-1, channels)
-    summed, queries, sent = mlp(
-        normed,
-        features.reshape(-1, channels),
+    summed, queries, sent = block_call(
+        padded,
+        features,
+        dw_kernel,
+        dw_bias,
+        norm_gain,
+        norm_bias,
         w_expand,
         b_expand,
         w_reduce,
         b_reduce,
         layer_scale,
         w_query,
-        tile_cols,
         copies,
     )
     return summed.reshape(tile_rows, tile_cols, channels), queries, sent

time: 59 us -> 56.2 us (0.953)
  Pallas kernels: 18.2 us -> 15.4 us
    pallas_call x2 -> x1, Pallas kernels: 18.2 us -> 15.4 us  [block_call(): pl.pallas_call(block_kernel, out_shape=(jax.ShapeDtypeStruct((pixels, cha...]
where the time goes in v13:
time: 56.2 us; the launch traced here: 55.7 us
  starting transfers between devices  21 us (37%)
  Pallas kernels  15.4 us (27%)
  waiting for transfers between devices  10.7 us (19%)
  local copies, waits for them, and re-layouts  4.8 us (9%)
  other arithmetic  2.72 us (5%)
  matrix products  0.79 us (1%)
    pallas_call x1, Pallas kernels, block_call(): pl.pallas_call(block_kernel, out_shape=(jax.ShapeDtypeStruct((pixels, cha...  15.4 us
    ppermute x4, starting transfers between devices, shifted(): return (lax.ppermute(piece, axis, up), lax.ppermute(piece, axis, down))  14.5 us
    all_to_all x1, starting transfers between devices, shards(): band_pooled = lax.all_to_all(sent, 'col', 0, 0)  6.53 us
    all_to_all x1, waiting for transfers between devices, shards(): band_pooled = lax.all_to_all(sent, 'col', 0, 0)  5.74 us
    ppermute x4, waiting for transfers between devices, shifted(): return (lax.ppermute(piece, axis, up), lax.ppermute(piece, axis, down))  4.99 us
    another operation x1, local copies, waits for them, and re-layouts, shards(): rows_of.append(jnp.stack(per_col, axis=1))  1.45 us
    concatenate x1, other arithmetic, block_pass(): jnp.concatenate([left, extended, right, jnp.zeros_like(right)[:, :-(tile_...  1.4 us
  transfers between devices with their start and end apart: 5, of which 3 were waited for; matrix products, arithmetic and copies ran while one was open for 5% of the time, Pallas kernels for 0%

profile of v13, /device:TPU:113, one launch (start us, length us, event | category | flops | bytes accessed | tf_op | source)
XLA Modules:
  0.0 55.7 jit_solution(12966736486857929896)
XLA Ops:
  0.0 0.9 %fusion.12 = (bf16[3,32,256]{2,1,0:T(8,128)(2,1)S(1)}, bf16[3,32,256]{2,1,0:T(8,128)(2,1)S(1)}) fusion(bf16[32,32,256]{2,1,0:T(8,128)(2,1)} %param.14), kind=kLoop, calls=%fused_computation.42 | loop fusion | bytes 196608 | tf_op jit(solution)/shard_map/slice | solution.py:20
  0.9 4.5 %collective-permute-start = (bf16[3,32,256]{2,1,0:T(8,128)(2,1)S(1)}, bf16[3,32,256]{2,1,0:T(8,128)(2,1)S(1)}, u32[]{:S(2)}, u32[]{:S(2)}) collective-permute-start(bf16[3,32,256]{2,1,0:T(8,128)(2,1)S(1)} %get-tuple-element.13), channel_id=1, source_target_pairs={{0,16},{16,32},{32,48},{48,64},{64,80},{80,96},{96,112},{112,128},... | collective-permute-start | bytes 147464 | tf_op jit(solution)/shard_map/ppermute | solution.py:15
  5.4 2.3 %collective-permute-start.1 = (bf16[3,32,256]{2,1,0:T(8,128)(2,1)S(1)}, bf16[3,32,256]{2,1,0:T(8,128)(2,1)S(1)}, u32[]{:S(2)}, u32[]{:S(2)}) collective-permute-start(bf16[3,32,256]{2,1,0:T(8,128)(2,1)S(1)} %get-tuple-element.14), channel_id=1, source_target_pairs={{16,0},{32,16},{48,32},{64,48},{80,64},{96,80},{112,96},{128,112},... | collective-permute-start | bytes 147464 | tf_op jit(solution)/shard_map/ppermute | solution.py:15
  7.7 1.0 %fusion.11 = (bf16[32,3,256]{2,1,0:T(4,128)(2,1)S(1)}, bf16[32,3,256]{2,1,0:T(4,128)(2,1)S(1)}) fusion(bf16[32,32,256]{2,1,0:T(8,128)(2,1)} %param.14), kind=kLoop, calls=%fused_computation.41 | loop fusion | bytes 196608 | tf_op jit(solution)/shard_map/slice | solution.py:23
  8.7 1.4 %dynamic-slice_bitcast_fusion.15 = (f32[8,1,4,64]{3,0,2,1:T(8,128)S(1)}, f32[8,1,4,64]{3,0,2,1:T(8,128)S(1)}, f32[8,1,4,64]{3,0,2,1:T(8,128)S(1)}, f32[8,1,4,64]...) fusion(f32[8,7,127]{2,0,1:T(8,128)} %param.26, ...), kind=kLoop, calls=%fused_computation.39 | loop fusion | bytes 262172 | tf_op jit(solution)/shard_map/stack | solution.py:301
  10.3 3.6 %collective-permute-done.1 = bf16[3,32,256]{2,1,0:T(8,128)(2,1)S(1)} collective-permute-done((bf16[3,32,256]{2,1,0:T(8,128)(2,1)S(1)}, bf16[3,32,256]{2,1,0:T(8,128)(2,1)S(1)}, u32[]{:S(2)}, u32[]{:S(2)}) %collective-permute-start.1) | collective-permute-done | bytes 49184 | tf_op jit(solution)/shard_map/ppermute | solution.py:15
  14.0 4.0 %collective-permute-start.3 = (bf16[38,3,256]{2,1,0:T(4,128)(2,1)S(1)}, bf16[38,3,256]{2,1,0:T(4,128)(2,1)S(1)}, u32[]{:S(2)}, u32[]{:S(2)}) collective-permute-start(bf16[38,3,256]{2,1,0:T(4,128)(2,1)S(1)} %pad_maximum_fusion.2), channel_id=1, source_target_pairs={{1,0},{2,1},{3,2},{4,3},{5,4},{6,5},{7,6},{8,7},{9,8},{10,9},{11,1... | collective-permute-start | bytes 175112 | tf_op jit(solution)/shard_map/ppermute | solution.py:15
  18.1 3.7 %collective-permute-start.2 = (bf16[38,3,256]{2,1,0:T(4,128)(2,1)S(1)}, bf16[38,3,256]{2,1,0:T(4,128)(2,1)S(1)}, u32[]{:S(2)}, u32[]{:S(2)}) collective-permute-start(bf16[38,3,256]{2,1,0:T(4,128)(2,1)S(1)} %pad_maximum_fusion.1), channel_id=1, source_target_pairs={{0,1},{1,2},{2,3},{3,4},{4,5},{5,6},{6,7},{7,8},{8,9},{9,10},{10,1... | collective-permute-start | bytes 175112 | tf_op jit(solution)/shard_map/ppermute | solution.py:15
  21.8 1.4 %collective-permute-done.2 = bf16[38,3,256]{2,1,0:T(4,128)(2,1)S(1)} collective-permute-done((bf16[38,3,256]{2,1,0:T(4,128)(2,1)S(1)}, bf16[38,3,256]{2,1,0:T(4,128)(2,1)S(1)}, u32[]{:S(2)}, u32[]{:S(2)}) %collective-permute-start.2) | collective-permute-done | bytes 58400 | tf_op jit(solution)/shard_map/ppermute | solution.py:15
  23.2 1.4 %maximum_maximum_fusion.x_ref = bf16[38,41,256]{2,1,0:T(8,128)(2,1)} fusion(bf16[38,3,256]{2,1,0:T(4,128)(2,1)S(1)} %collective-permute-done.3, bf16[3,32,256]{2,1,0:T(8,128)(2,1)S(1)} %collective-permute-done.1, bf16[32,32,256]{2,1,0:T(8,128)(2,1)S(1)} %copy-done.1, bf16[3,32,256]{2,1,0:T(8,128)(2,1)S(1)} %collective-permute-done, ...), kind=kLoop, calls=%fused_computation.10 | loop fusion | flops 4786176 | bytes 1537106 | tf_op jit(solution)/shard_map/concatenate | solution.py:221
  24.6 15.4 %shard_map.136 = (bf16[1024,256]{1,0:T(8,128)(2,1)}, f32[16,256]{1,0:T(8,128)}, bf16[16,16,256]{2,1,0:T(8,128)(2,1)}) custom-call(bf16[38,41,256]{2,1,0:T(8,128)(2,1)} %maximum_maximum_fusion.x_ref, bf16[7,7,256]{2,1,0:T(8,128)(2,1)} %k_ref.1, f32[1,256]{1,0:T(1,128)} %bitcast.74, f32[1,256]{1,0:T(1,128)} %bitcast.75, f32[1,256]{1,0:T(1,128)} %bitcast.76, ...), custom_call_target="tpu_custom_call" | custom-call | flops 1099431936 | bytes 2894848 | tf_op jit(solution)/shard_map/pallas_call | solution.py:165
  40.1 6.5 %all-to-all-start = ((bf16[16,16,256]{2,1,0:T(8,128)(2,1)}), bf16[16,16,256]{2,1,0:T(8,128)(2,1)S(1)}, u32[]{:S(2)}, u32[]{:S(2)}) async-start(bf16[16,16,256]{2,1,0:T(8,128)(2,1)} %get-tuple-element.9), calls=%async_computation | async-start | bytes 262144 | tf_op jit(solution)/shard_map/all_to_all | solution.py:283
  46.7 0.2 reshape.73
  47.0 5.7 %all-to-all-done = bf16[16,16,256]{2,1,0:T(8,128)(2,1)S(1)} async-done(((bf16[16,16,256]{2,1,0:T(8,128)(2,1)}), bf16[16,16,256]{2,1,0:T(8,128)(2,1)S(1)}, u32[]{:S(2)}, u32[]{:S(2)}) %all-to-all-start) | async-done | bytes 131104 | tf_op jit(solution)/shard_map/all_to_all | solution.py:283
  52.9 0.2 convolution_convert_fusion
  53.2 0.1 copy.21
  53.3 0.1 fusion.3
  53.4 0.2 fusion.16
  53.6 0.1 copy.20
  53.7 0.3 fusion.4
  54.1 0.1 fusion.6
  54.3 0.1 broadcast_in_dim.5
  54.4 0.4 copy-done.2
  54.8 1.0 %fusion.5 = bf16[32,32,256]{2,1,0:T(8,128)(2,1)} fusion(f32[32,32,256]{2,1,0:T(8,128)S(1)} %bitcast.67, bf16[32,32,256]{2,1,0:T(8,128)(2,1)S(1)} %bitcast.71), kind=kLoop, calls=%fused_computation.9 | loop fusion | flops 786432 | bytes 2097152 | tf_op jit(solution)/shard_map/convert_element_type | solution.py:323
  (29 shorter events, 0.8 us)
Async XLA Ops:
  0.0 52.9 %copy-start = (bf16[256,512]{1,0:T(8,128)(2,1)S(1)}, bf16[256,512]{1,0:T(8,128)(2,1)}, u32[]{:S(2)}) copy-start(bf16[256,512]{1,0:T(8,128)(2,1)} %param.25) | copy-start | bytes 786436
  0.0 23.2 %copy-start.1 = (bf16[32,32,256]{2,1,0:T(8,128)(2,1)S(1)}, bf16[32,32,256]{2,1,0:T(8,128)(2,1)}, u32[]{:S(2)}) copy-start(bf16[32,32,256]{2,1,0:T(8,128)(2,1)} %param.14) | copy-start | bytes 1572868
  0.9 9.4 %collective-permute-start = (bf16[3,32,256]{2,1,0:T(8,128)(2,1)S(1)}, bf16[3,32,256]{2,1,0:T(8,128)(2,1)S(1)}, u32[]{:S(2)}, u32[]{:S(2)}) collective-permute-start(bf16[3,32,256]{2,1,0:T(8,128)(2,1)S(1)} %get-tuple-element.13), channel_id=1, source_target_pairs={{0,16},{16,32},{32,48},{48,64},{64,80},{80,96},{96,112},{112,128},... | collective-permute-start | bytes 147464 | tf_op jit(solution)/shard_map/ppermute | solution.py:15
  5.4 8.4 %collective-permute-start.1 = (bf16[3,32,256]{2,1,0:T(8,128)(2,1)S(1)}, bf16[3,32,256]{2,1,0:T(8,128)(2,1)S(1)}, u32[]{:S(2)}, u32[]{:S(2)}) collective-permute-start(bf16[3,32,256]{2,1,0:T(8,128)(2,1)S(1)} %get-tuple-element.14), channel_id=1, source_target_pairs={{16,0},{32,16},{48,32},{64,48},{80,64},{96,80},{112,96},{128,112},... | collective-permute-start | bytes 147464 | tf_op jit(solution)/shard_map/ppermute | solution.py:15
  14.0 7.9 %collective-permute-start.3 = (bf16[38,3,256]{2,1,0:T(4,128)(2,1)S(1)}, bf16[38,3,256]{2,1,0:T(4,128)(2,1)S(1)}, u32[]{:S(2)}, u32[]{:S(2)}) collective-permute-start(bf16[38,3,256]{2,1,0:T(4,128)(2,1)S(1)} %pad_maximum_fusion.2), channel_id=1, source_target_pairs={{1,0},{2,1},{3,2},{4,3},{5,4},{6,5},{7,6},{8,7},{9,8},{10,9},{11,1... | collective-permute-start | bytes 175112 | tf_op jit(solution)/shard_map/ppermute | solution.py:15
  18.1 5.1 %collective-permute-start.2 = (bf16[38,3,256]{2,1,0:T(4,128)(2,1)S(1)}, bf16[38,3,256]{2,1,0:T(4,128)(2,1)S(1)}, u32[]{:S(2)}, u32[]{:S(2)}) collective-permute-start(bf16[38,3,256]{2,1,0:T(4,128)(2,1)S(1)} %pad_maximum_fusion.1), channel_id=1, source_target_pairs={{0,1},{1,2},{2,3},{3,4},{4,5},{5,6},{6,7},{7,8},{8,9},{9,10},{10,1... | collective-permute-start | bytes 175112 | tf_op jit(solution)/shard_map/ppermute | solution.py:15
  40.0 6.9 %copy-start.4 = (f32[16,256]{1,0:T(8,128)S(1)}, f32[16,256]{1,0:T(8,128)}, u32[]{:S(2)}) copy-start(f32[16,256]{1,0:T(8,128)} %get-tuple-element.10) | copy-start | bytes 49156
  40.1 12.7 %all-to-all-start = ((bf16[16,16,256]{2,1,0:T(8,128)(2,1)}), bf16[16,16,256]{2,1,0:T(8,128)(2,1)S(1)}, u32[]{:S(2)}, u32[]{:S(2)}) async-start(bf16[16,16,256]{2,1,0:T(8,128)(2,1)} %get-tuple-element.9), calls=%async_computation | async-start | bytes 262144 | tf_op jit(solution)/shard_map/all_to_all | solution.py:283
  53.2 1.0 %copy-start.3 = (bf16[256,256]{1,0:T(8,128)(2,1)S(1)}, bf16[256,256]{1,0:T(8,128)(2,1)}, u32[]{:S(2)}) copy-start(bf16[256,256]{1,0:T(8,128)(2,1)} %param.27) | copy-start | bytes 393220
  53.7 1.1 %copy-start.2 = (bf16[1024,256]{1,0:T(8,128)(2,1)S(1)}, bf16[1024,256]{1,0:T(8,128)(2,1)}, u32[]{:S(2)}) copy-start(bf16[1024,256]{1,0:T(8,128)(2,1)} %get-tuple-element.8) | copy-start | bytes 1572868

commit v14 on v13

--- a/solution.py
+++ b/solution.py
@@ -31,19 +31,29 @@
 ROW_BLOCK = 8
 
 
-def conv_norm_kernel(x_ref, k_ref, db_ref, g_ref, nb_ref, o_ref, kf_ref, sh_ref):
-    rows_p = x_ref.shape[0]
+def conv_norm_kernel(
+    c_ref, t_ref, b_ref, l_ref, r_ref, k_ref, db_ref, g_ref, nb_ref, o_ref, kf_ref, sh_ref
+):
     tile_rows, tile_cols, channels = o_ref.shape
+    halo = t_ref.shape[0]
+    rows_p = tile_rows + 2 * halo
     for a in range(TAPS):
         kf_ref[a, pl.ds(0, TAPS), :] = k_ref[a].astype(jnp.float32)
 
-    def widen(r, carry):
-        row = x_ref[r].astype(jnp.float32)
+    def put(r, mid):
+        row = jnp.concatenate([l_ref[r], mid, r_ref[r]], axis=0).astype(jnp.float32)
         for b in range(TAPS):
             sh_ref[b, r] = row[b : b + tile_cols]
+
+    for r in range(halo):
+        put(r, t_ref[r])
+        put(rows_p - halo + r, b_ref[r])
+
+    def widen(r, carry):
+        put(r, c_ref[r - halo])
         return carry
 
-    lax.fori_loop(0, rows_p, widen, 0)
+    lax.fori_loop(halo, rows_p - halo, widen, 0)
     db = db_ref[...]
     g = g_ref[...]
     nb = nb_ref[...]
@@ -126,8 +136,8 @@
 
 
 def block_kernel(
-    x_ref, k_ref, db_ref, g_ref, nb_ref, f_ref, we_hbm, be_ref, wr_hbm, br_ref, ls_ref, wq_hbm,
-    o_ref, q_ref, s_ref, kf_ref, sh_ref, n_ref, we_ref, wr_ref, wq_ref, sem,
+    c_ref, t_ref, b_ref, l_ref, r_ref, k_ref, db_ref, g_ref, nb_ref, f_ref, we_hbm, be_ref, wr_hbm,
+    br_ref, ls_ref, wq_hbm, o_ref, q_ref, s_ref, kf_ref, sh_ref, n_ref, we_ref, wr_ref, wq_ref, sem,
 ):
     loads = [
         pltpu.make_async_copy(source, target, sem.at[i])
@@ -135,7 +145,7 @@
     ]
     for load in loads:
         load.start()
-    conv_norm_kernel(x_ref, k_ref, db_ref, g_ref, nb_ref, n_ref, kf_ref, sh_ref)
+    conv_norm_kernel(c_ref, t_ref, b_ref, l_ref, r_ref, k_ref, db_ref, g_ref, nb_ref, n_ref, kf_ref, sh_ref)
     for load in loads:
         load.wait()
     tile_rows, tile_cols, channels = n_ref.shape
@@ -152,11 +162,12 @@
 
 
 def block_call(
-    padded, features, dw_kernel, dw_bias, norm_gain, norm_bias, w_expand, b_expand, w_reduce,
+    pieces, features, dw_kernel, dw_bias, norm_gain, norm_bias, w_expand, b_expand, w_reduce,
     b_reduce, layer_scale, w_query, copies,
 ):
-    rows_p, cols_p, channels = padded.shape
-    tile_rows, tile_cols = features.shape[:2]
+    tile_rows, tile_cols, channels = features.shape
+    rows_p = tile_rows + 2 * pieces[0].shape[0]
+    cols_p = tile_cols + 2 * pieces[0].shape[0]
     pixels = tile_rows * tile_cols
     hidden_total = w_expand.shape[1]
     tokens = pixels // 64
@@ -169,7 +180,7 @@
             jax.ShapeDtypeStruct((tokens, channels), jnp.float32),
             jax.ShapeDtypeStruct((copies, tokens, channels), jnp.bfloat16),
         ),
-        in_specs=[vmem] * 6 + [anywhere, vmem, anywhere, vmem, vmem, anywhere],
+        in_specs=[vmem] * 10 + [anywhere, vmem, anywhere, vmem, vmem, anywhere],
         out_specs=(vmem, vmem, vmem),
         scratch_shapes=[
             pltpu.VMEM((TAPS, 8, channels), jnp.float32),
@@ -186,7 +197,8 @@
             transcendentals=2 * pixels * hidden_total,
         ),
     )(
-        padded,
+        features,
+        *pieces,
         dw_kernel,
         dw_bias.reshape(1, channels),
         norm_gain.reshape(1, channels),
@@ -216,13 +228,8 @@
     copies,
 ):
     tile_rows, tile_cols, channels = features.shape
-    top, bottom, left, right = pieces
-    extended = jnp.concatenate([top, features, bottom], axis=0)
-    padded = jnp.concatenate(
-        [left, extended, right, jnp.zeros_like(right)[:, : -(tile_cols + 3 * 3) % 8]], axis=1
-    )
     summed, queries, sent = block_call(
-        padded,
+        pieces,
         features,
         dw_kernel,
         dw_bias,

time: 56.2 us -> 58.1 us (1.034)
  the two profiles are of different devices: /device:TPU:113 before, /device:TPU:129 now
where the time goes in v14:
time: 58.1 us; the launch traced here: 57.6 us
  starting transfers between devices  19.7 us (34%)
  Pallas kernels  15.6 us (27%)
  waiting for transfers between devices  13 us (22%)
  local copies, waits for them, and re-layouts  6.82 us (12%)
  other arithmetic  1.33 us (2%)
  matrix products  0.8 us (1%)
    pallas_call x1, Pallas kernels, block_call(): pl.pallas_call(block_kernel, out_shape=(jax.ShapeDtypeStruct((pixels, cha...  15.6 us
    ppermute x4, starting transfers between devices, shifted(): return (lax.ppermute(piece, axis, up), lax.ppermute(piece, axis, down))  13 us
    ppermute x4, waiting for transfers between devices, shifted(): return (lax.ppermute(piece, axis, up), lax.ppermute(piece, axis, down))  7.79 us
    all_to_all x1, starting transfers between devices, shards(): band_pooled = lax.all_to_all(sent, 'col', 0, 0)  6.76 us
    all_to_all x1, waiting for transfers between devices, shards(): band_pooled = lax.all_to_all(sent, 'col', 0, 0)  5.23 us
    unnamed x18, local copies, waits for them, and re-layouts  3.82 us
  transfers between devices with their start and end apart: 5, of which 3 were waited for; matrix products, arithmetic and copies ran while one was open for 3% of the time, Pallas kernels for 0%

profile of v14, /device:TPU:129, one launch (start us, length us, event | category | flops | bytes accessed | tf_op | source)
XLA Modules:
  0.0 57.6 jit_solution(17065287602725095485)
XLA Ops:
  0.0 0.9 %fusion.12 = (bf16[3,32,256]{2,1,0:T(8,128)(2,1)S(1)}, bf16[3,32,256]{2,1,0:T(8,128)(2,1)S(1)}) fusion(bf16[32,32,256]{2,1,0:T(8,128)(2,1)} %c_ref.1), kind=kLoop, calls=%fused_computation.41 | loop fusion | bytes 196608 | tf_op jit(solution)/shard_map/slice | solution.py:21
  0.9 4.4 %collective-permute-start.1 = (bf16[3,32,256]{2,1,0:T(8,128)(2,1)S(1)}, bf16[3,32,256]{2,1,0:T(8,128)(2,1)S(1)}, u32[]{:S(2)}, u32[]{:S(2)}) collective-permute-start(bf16[3,32,256]{2,1,0:T(8,128)(2,1)S(1)} %get-tuple-element.13), channel_id=1, source_target_pairs={{16,0},{32,16},{48,32},{64,48},{80,64},{96,80},{112,96},{128,112},... | collective-permute-start | bytes 147464 | tf_op jit(solution)/shard_map/ppermute | solution.py:15
  5.2 2.4 %collective-permute-start = (bf16[3,32,256]{2,1,0:T(8,128)(2,1)S(1)}, bf16[3,32,256]{2,1,0:T(8,128)(2,1)S(1)}, u32[]{:S(2)}, u32[]{:S(2)}) collective-permute-start(bf16[3,32,256]{2,1,0:T(8,128)(2,1)S(1)} %get-tuple-element.14), channel_id=1, source_target_pairs={{0,16},{16,32},{32,48},{48,64},{64,80},{80,96},{96,112},{112,128},... | collective-permute-start | bytes 147464 | tf_op jit(solution)/shard_map/ppermute | solution.py:15
  7.7 1.0 %fusion.11 = (bf16[32,3,256]{2,1,0:T(4,128)(2,1)S(1)}, bf16[32,3,256]{2,1,0:T(4,128)(2,1)S(1)}) fusion(bf16[32,32,256]{2,1,0:T(8,128)(2,1)} %c_ref.1), kind=kLoop, calls=%fused_computation.40 | loop fusion | bytes 196608 | tf_op jit(solution)/shard_map/slice | solution.py:25
  8.7 0.7 %copy-done.1 = f32[8,7,127]{2,0,1:T(8,128)S(1)} copy-done((f32[8,7,127]{2,0,1:T(8,128)S(1)}, f32[8,7,127]{2,0,1:T(8,128)}, u32[]{:S(2)}) %copy-start.1) | copy-done | bytes 28472
  9.5 0.1 dynamic-slice_bitcast_fusion.15
  9.6 4.0 %collective-permute-done.t_ref = bf16[3,32,256]{2,1,0:T(8,128)(2,1)S(1)} collective-permute-done((bf16[3,32,256]{2,1,0:T(8,128)(2,1)S(1)}, bf16[3,32,256]{2,1,0:T(8,128)(2,1)S(1)}, u32[]{:S(2)}, u32[]{:S(2)}) %collective-permute-start) | collective-permute-done | bytes 49184 | tf_op jit(solution)/shard_map/ppermute | solution.py:15
  13.8 0.5 copy-done.6
  14.3 4.3 %collective-permute-start.2 = (bf16[38,3,256]{2,1,0:T(4,128)(2,1)S(1)}, bf16[38,3,256]{2,1,0:T(4,128)(2,1)S(1)}, u32[]{:S(2)}, u32[]{:S(2)}) collective-permute-start(bf16[38,3,256]{2,1,0:T(4,128)(2,1)S(1)} %pad_maximum_fusion.1), channel_id=1, source_target_pairs={{0,1},{1,2},{2,3},{3,4},{4,5},{5,6},{6,7},{7,8},{8,9},{9,10},{10,1... | collective-permute-start | bytes 175112 | tf_op jit(solution)/shard_map/ppermute | solution.py:15
  18.7 1.9 %collective-permute-start.3 = (bf16[38,3,256]{2,1,0:T(4,128)(2,1)S(1)}, bf16[38,3,256]{2,1,0:T(4,128)(2,1)S(1)}, u32[]{:S(2)}, u32[]{:S(2)}) collective-permute-start(bf16[38,3,256]{2,1,0:T(4,128)(2,1)S(1)} %pad_maximum_fusion.2), channel_id=1, source_target_pairs={{1,0},{2,1},{3,2},{4,3},{5,4},{6,5},{7,6},{8,7},{9,8},{10,9},{11,1... | collective-permute-start | bytes 175112 | tf_op jit(solution)/shard_map/ppermute | solution.py:15
  20.6 3.7 %collective-permute-done.3.r_ref = bf16[38,3,256]{2,1,0:T(4,128)(2,1)S(1)} collective-permute-done((bf16[38,3,256]{2,1,0:T(4,128)(2,1)S(1)}, bf16[38,3,256]{2,1,0:T(4,128)(2,1)S(1)}, u32[]{:S(2)}, u32[]{:S(2)}) %collective-permute-start.3) | collective-permute-done | bytes 58400 | tf_op jit(solution)/shard_map/ppermute | solution.py:15
  24.4 0.6 %copy-done.8 = bf16[38,3,256]{2,1,0:T(4,128)(2,1)} copy-done((bf16[38,3,256]{2,1,0:T(4,128)(2,1)}, bf16[38,3,256]{2,1,0:T(4,128)(2,1)S(1)}, u32[]{:S(2)}) %copy-start.8) | copy-done | bytes 58392
  25.0 15.6 %shard_map.136 = (bf16[1024,256]{1,0:T(8,128)(2,1)}, f32[16,256]{1,0:T(8,128)}, bf16[16,16,256]{2,1,0:T(8,128)(2,1)}) custom-call(bf16[32,32,256]{2,1,0:T(8,128)(2,1)} %c_ref.1, bf16[3,32,256]{2,1,0:T(8,128)(2,1)} %copy-done.6, bf16[3,32,256]{2,1,0:T(8,128)(2,1)} %copy-done.5, bf16[38,3,256]{2,1,0:T(4,128)(2,1)} %copy-done.7, bf16[38,3,256]{2,1,0:T(4,128)(2,1)} %copy-done.8, ...), custom_call_target="tpu_custom_call" | custom-call | flops 1099431936 | bytes 2836480 | tf_op jit(solution)/shard_map/pallas_call | solution.py:176
  40.6 6.8 %all-to-all-start = ((bf16[16,16,256]{2,1,0:T(8,128)(2,1)}), bf16[16,16,256]{2,1,0:T(8,128)(2,1)S(1)}, u32[]{:S(2)}, u32[]{:S(2)}) async-start(bf16[16,16,256]{2,1,0:T(8,128)(2,1)} %get-tuple-element.9), calls=%async_computation | async-start | bytes 262144 | tf_op jit(solution)/shard_map/all_to_all | solution.py:290
  47.5 0.2 reshape.73
  47.7 0.5 copy-done.4
  48.3 5.2 %all-to-all-done = bf16[16,16,256]{2,1,0:T(8,128)(2,1)S(1)} async-done(((bf16[16,16,256]{2,1,0:T(8,128)(2,1)}), bf16[16,16,256]{2,1,0:T(8,128)(2,1)S(1)}, u32[]{:S(2)}, u32[]{:S(2)}) %all-to-all-start) | async-done | bytes 131104 | tf_op jit(solution)/shard_map/all_to_all | solution.py:290
  53.7 0.2 convolution_convert_fusion
  54.1 0.1 fusion.3
  54.2 0.2 fusion.16
  54.5 0.3 fusion.4
  54.9 0.5 copy-done.3
  55.7 0.9 %copy-done.2 = bf16[1024,256]{1,0:T(8,128)(2,1)S(1)} copy-done((bf16[1024,256]{1,0:T(8,128)(2,1)S(1)}, bf16[1024,256]{1,0:T(8,128)(2,1)}, u32[]{:S(2)}) %copy-start.2) | copy-done | bytes 524312
  56.6 1.0 %fusion.5 = bf16[32,32,256]{2,1,0:T(8,128)(2,1)} fusion(f32[32,32,256]{2,1,0:T(8,128)S(1)} %bitcast.67, bf16[32,32,256]{2,1,0:T(8,128)(2,1)S(1)} %bitcast.70), kind=kLoop, calls=%fused_computation.9 | loop fusion | flops 786432 | bytes 2097152 | tf_op jit(solution)/shard_map/convert_element_type | solution.py:330
  (34 shorter events, 1.1 us)
Async XLA Ops:
  0.0 53.7 %copy-start = (bf16[256,512]{1,0:T(8,128)(2,1)S(1)}, bf16[256,512]{1,0:T(8,128)(2,1)}, u32[]{:S(2)}) copy-start(bf16[256,512]{1,0:T(8,128)(2,1)} %param.25) | copy-start | bytes 786436
  0.9 8.7 %collective-permute-start.1 = (bf16[3,32,256]{2,1,0:T(8,128)(2,1)S(1)}, bf16[3,32,256]{2,1,0:T(8,128)(2,1)S(1)}, u32[]{:S(2)}, u32[]{:S(2)}) collective-permute-start(bf16[3,32,256]{2,1,0:T(8,128)(2,1)S(1)} %get-tuple-element.13), channel_id=1, source_target_pairs={{16,0},{32,16},{48,32},{64,48},{80,64},{96,80},{112,96},{128,112},... | collective-permute-start | bytes 147464 | tf_op jit(solution)/shard_map/ppermute | solution.py:15
  5.2 8.4 %collective-permute-start = (bf16[3,32,256]{2,1,0:T(8,128)(2,1)S(1)}, bf16[3,32,256]{2,1,0:T(8,128)(2,1)S(1)}, u32[]{:S(2)}, u32[]{:S(2)}) collective-permute-start(bf16[3,32,256]{2,1,0:T(8,128)(2,1)S(1)} %get-tuple-element.14), channel_id=1, source_target_pairs={{0,16},{16,32},{32,48},{48,64},{64,80},{80,96},{96,112},{112,128},... | collective-permute-start | bytes 147464 | tf_op jit(solution)/shard_map/ppermute | solution.py:15
  8.7 0.8 %copy-start.1 = (f32[8,7,127]{2,0,1:T(8,128)S(1)}, f32[8,7,127]{2,0,1:T(8,128)}, u32[]{:S(2)}) copy-start(f32[8,7,127]{2,0,1:T(8,128)} %param.26) | copy-start | bytes 85348
  9.6 4.2 %copy-start.5 = (bf16[3,32,256]{2,1,0:T(8,128)(2,1)}, bf16[3,32,256]{2,1,0:T(8,128)(2,1)S(1)}, u32[]{:S(2)}) copy-start(bf16[3,32,256]{2,1,0:T(8,128)(2,1)S(1)} %collective-permute-done.1.b_ref) | copy-start | bytes 147460
  13.7 0.6 %copy-start.6 = (bf16[3,32,256]{2,1,0:T(8,128)(2,1)}, bf16[3,32,256]{2,1,0:T(8,128)(2,1)S(1)}, u32[]{:S(2)}) copy-start(bf16[3,32,256]{2,1,0:T(8,128)(2,1)S(1)} %collective-permute-done.t_ref) | copy-start | bytes 147460
  14.3 6.3 %collective-permute-start.2 = (bf16[38,3,256]{2,1,0:T(4,128)(2,1)S(1)}, bf16[38,3,256]{2,1,0:T(4,128)(2,1)S(1)}, u32[]{:S(2)}, u32[]{:S(2)}) collective-permute-start(bf16[38,3,256]{2,1,0:T(4,128)(2,1)S(1)} %pad_maximum_fusion.1), channel_id=1, source_target_pairs={{0,1},{1,2},{2,3},{3,4},{4,5},{5,6},{6,7},{7,8},{8,9},{9,10},{10,1... | collective-permute-start | bytes 175112 | tf_op jit(solution)/shard_map/ppermute | solution.py:15
  18.7 5.7 %collective-permute-start.3 = (bf16[38,3,256]{2,1,0:T(4,128)(2,1)S(1)}, bf16[38,3,256]{2,1,0:T(4,128)(2,1)S(1)}, u32[]{:S(2)}, u32[]{:S(2)}) collective-permute-start(bf16[38,3,256]{2,1,0:T(4,128)(2,1)S(1)} %pad_maximum_fusion.2), channel_id=1, source_target_pairs={{1,0},{2,1},{3,2},{4,3},{5,4},{6,5},{7,6},{8,7},{9,8},{10,9},{11,1... | collective-permute-start | bytes 175112 | tf_op jit(solution)/shard_map/ppermute | solution.py:15
  20.6 3.8 %copy-start.7 = (bf16[38,3,256]{2,1,0:T(4,128)(2,1)}, bf16[38,3,256]{2,1,0:T(4,128)(2,1)S(1)}, u32[]{:S(2)}) copy-start(bf16[38,3,256]{2,1,0:T(4,128)(2,1)S(1)} %collective-permute-done.2.l_ref) | copy-start | bytes 175108
  24.4 0.6 %copy-start.8 = (bf16[38,3,256]{2,1,0:T(4,128)(2,1)}, bf16[38,3,256]{2,1,0:T(4,128)(2,1)S(1)}, u32[]{:S(2)}) copy-start(bf16[38,3,256]{2,1,0:T(4,128)(2,1)S(1)} %collective-permute-done.3.r_ref) | copy-start | bytes 175108
  40.6 12.9 %all-to-all-start = ((bf16[16,16,256]{2,1,0:T(8,128)(2,1)}), bf16[16,16,256]{2,1,0:T(8,128)(2,1)S(1)}, u32[]{:S(2)}, u32[]{:S(2)}) async-start(bf16[16,16,256]{2,1,0:T(8,128)(2,1)} %get-tuple-element.9), calls=%async_computation | async-start | bytes 262144 | tf_op jit(solution)/shard_map/all_to_all | solution.py:290
  47.5 0.7 %copy-start.4 = (f32[16,256]{1,0:T(8,128)S(1)}, f32[16,256]{1,0:T(8,128)}, u32[]{:S(2)}) copy-start(f32[16,256]{1,0:T(8,128)} %get-tuple-element.10) | copy-start | bytes 49156
  54.5 0.9 %copy-start.3 = (bf16[256,256]{1,0:T(8,128)(2,1)S(1)}, bf16[256,256]{1,0:T(8,128)(2,1)}, u32[]{:S(2)}) copy-start(bf16[256,256]{1,0:T(8,128)(2,1)} %param.27) | copy-start | bytes 393220
  55.5 1.1 %copy-start.2 = (bf16[1024,256]{1,0:T(8,128)(2,1)S(1)}, bf16[1024,256]{1,0:T(8,128)(2,1)}, u32[]{:S(2)}) copy-start(bf16[1024,256]{1,0:T(8,128)(2,1)} %get-tuple-element.8) | copy-start | bytes 1572868

commit v15 on v13

--- a/solution.py
+++ b/solution.py
@@ -88,15 +88,17 @@
 HIDDEN_BLOCK = 256
 
 
+LOG2E = 1.4426950408889634
+
+
 def gelu_exact(pre):
-    z = jnp.abs(pre) * jnp.float32(0.7071067811865476)
-    t = 1.0 / (1.0 + 0.5 * z)
-    poly = jnp.float32(ERFC_COEFFS[-1])
-    for coeff in ERFC_COEFFS[-2::-1]:
-        poly = poly * t + jnp.float32(coeff)
-    tail = t * jnp.exp(poly - z * z)
-    one_plus_erf = jnp.where(pre >= 0, 2.0 - tail, tail)
-    return 0.5 * pre * one_plus_erf
+    t = 1.0 / (1.0 + jnp.abs(pre) * jnp.float32(0.5 * 0.7071067811865476))
+    poly = jnp.float32(ERFC_COEFFS[-1] * LOG2E)
+    for coeff in ERFC_COEFFS[-2:0:-1]:
+        poly = poly * t + jnp.float32(coeff * LOG2E)
+    poly = poly * t + jnp.float32(ERFC_COEFFS[0] * LOG2E - 1.0)
+    half_tail = t * jnp.exp2(poly - (pre * pre) * jnp.float32(0.5 * LOG2E))
+    return pre * jnp.where(pre >= 0, 1.0 - half_tail, half_tail)
 
 
 def mlp_block(normed, features, we_ref, be_ref, wr_ref, br_ref, ls_ref, out_dtype):

time: 56.2 us -> 55.9 us (level)
  no operation moved by 1% of the time
where the time goes in v15:
time: 55.9 us; the launch traced here: 55.5 us
  starting transfers between devices  21 us (38%)
  Pallas kernels  15.2 us (27%)
  waiting for transfers between devices  10.7 us (19%)
  local copies, waits for them, and re-layouts  4.8 us (9%)
  other arithmetic  2.72 us (5%)
  matrix products  0.79 us (1%)
    pallas_call x1, Pallas kernels, block_call(): pl.pallas_call(block_kernel, out_shape=(jax.ShapeDtypeStruct((pixels, cha...  15.2 us
    ppermute x4, starting transfers between devices, shifted(): return (lax.ppermute(piece, axis, up), lax.ppermute(piece, axis, down))  14.5 us
    all_to_all x1, starting transfers between devices, shards(): band_pooled = lax.all_to_all(sent, 'col', 0, 0)  6.53 us
    all_to_all x1, waiting for transfers between devices, shards(): band_pooled = lax.all_to_all(sent, 'col', 0, 0)  5.74 us
    ppermute x4, waiting for transfers between devices, shifted(): return (lax.ppermute(piece, axis, up), lax.ppermute(piece, axis, down))  4.99 us
    another operation x1, local copies, waits for them, and re-layouts, shards(): rows_of.append(jnp.stack(per_col, axis=1))  1.45 us
    concatenate x1, other arithmetic, block_pass(): jnp.concatenate([left, extended, right, jnp.zeros_like(right)[:, :-(tile_...  1.4 us
  transfers between devices with their start and end apart: 5, of which 3 were waited for; matrix products, arithmetic and copies ran while one was open for 5% of the time, Pallas kernels for 0%

profile of v15, /device:TPU:113, one launch (start us, length us, event | category | flops | bytes accessed | tf_op | source)
XLA Modules:
  0.0 55.5 jit_solution(10732661244577119968)
XLA Ops:
  0.0 0.9 %fusion.12 = (bf16[3,32,256]{2,1,0:T(8,128)(2,1)S(1)}, bf16[3,32,256]{2,1,0:T(8,128)(2,1)S(1)}) fusion(bf16[32,32,256]{2,1,0:T(8,128)(2,1)} %param.14), kind=kLoop, calls=%fused_computation.42 | loop fusion | bytes 196608 | tf_op jit(solution)/shard_map/slice | solution.py:20
  0.9 4.5 %collective-permute-start = (bf16[3,32,256]{2,1,0:T(8,128)(2,1)S(1)}, bf16[3,32,256]{2,1,0:T(8,128)(2,1)S(1)}, u32[]{:S(2)}, u32[]{:S(2)}) collective-permute-start(bf16[3,32,256]{2,1,0:T(8,128)(2,1)S(1)} %get-tuple-element.13), channel_id=1, source_target_pairs={{0,16},{16,32},{32,48},{48,64},{64,80},{80,96},{96,112},{112,128},... | collective-permute-start | bytes 147464 | tf_op jit(solution)/shard_map/ppermute | solution.py:15
  5.4 2.3 %collective-permute-start.1 = (bf16[3,32,256]{2,1,0:T(8,128)(2,1)S(1)}, bf16[3,32,256]{2,1,0:T(8,128)(2,1)S(1)}, u32[]{:S(2)}, u32[]{:S(2)}) collective-permute-start(bf16[3,32,256]{2,1,0:T(8,128)(2,1)S(1)} %get-tuple-element.14), channel_id=1, source_target_pairs={{16,0},{32,16},{48,32},{64,48},{80,64},{96,80},{112,96},{128,112},... | collective-permute-start | bytes 147464 | tf_op jit(solution)/shard_map/ppermute | solution.py:15
  7.7 1.0 %fusion.11 = (bf16[32,3,256]{2,1,0:T(4,128)(2,1)S(1)}, bf16[32,3,256]{2,1,0:T(4,128)(2,1)S(1)}) fusion(bf16[32,32,256]{2,1,0:T(8,128)(2,1)} %param.14), kind=kLoop, calls=%fused_computation.41 | loop fusion | bytes 196608 | tf_op jit(solution)/shard_map/slice | solution.py:23
  8.7 1.4 %dynamic-slice_bitcast_fusion.15 = (f32[8,1,4,64]{3,0,2,1:T(8,128)S(1)}, f32[8,1,4,64]{3,0,2,1:T(8,128)S(1)}, f32[8,1,4,64]{3,0,2,1:T(8,128)S(1)}, f32[8,1,4,64]...) fusion(f32[8,7,127]{2,0,1:T(8,128)} %param.26, ...), kind=kLoop, calls=%fused_computation.39 | loop fusion | bytes 262172 | tf_op jit(solution)/shard_map/stack | solution.py:303
  10.3 3.6 %collective-permute-done.1 = bf16[3,32,256]{2,1,0:T(8,128)(2,1)S(1)} collective-permute-done((bf16[3,32,256]{2,1,0:T(8,128)(2,1)S(1)}, bf16[3,32,256]{2,1,0:T(8,128)(2,1)S(1)}, u32[]{:S(2)}, u32[]{:S(2)}) %collective-permute-start.1) | collective-permute-done | bytes 49184 | tf_op jit(solution)/shard_map/ppermute | solution.py:15
  14.0 4.0 %collective-permute-start.3 = (bf16[38,3,256]{2,1,0:T(4,128)(2,1)S(1)}, bf16[38,3,256]{2,1,0:T(4,128)(2,1)S(1)}, u32[]{:S(2)}, u32[]{:S(2)}) collective-permute-start(bf16[38,3,256]{2,1,0:T(4,128)(2,1)S(1)} %pad_maximum_fusion.2), channel_id=1, source_target_pairs={{1,0},{2,1},{3,2},{4,3},{5,4},{6,5},{7,6},{8,7},{9,8},{10,9},{11,1... | collective-permute-start | bytes 175112 | tf_op jit(solution)/shard_map/ppermute | solution.py:15
  18.1 3.7 %collective-permute-start.2 = (bf16[38,3,256]{2,1,0:T(4,128)(2,1)S(1)}, bf16[38,3,256]{2,1,0:T(4,128)(2,1)S(1)}, u32[]{:S(2)}, u32[]{:S(2)}) collective-permute-start(bf16[38,3,256]{2,1,0:T(4,128)(2,1)S(1)} %pad_maximum_fusion.1), channel_id=1, source_target_pairs={{0,1},{1,2},{2,3},{3,4},{4,5},{5,6},{6,7},{7,8},{8,9},{9,10},{10,1... | collective-permute-start | bytes 175112 | tf_op jit(solution)/shard_map/ppermute | solution.py:15
  21.8 1.4 %collective-permute-done.2 = bf16[38,3,256]{2,1,0:T(4,128)(2,1)S(1)} collective-permute-done((bf16[38,3,256]{2,1,0:T(4,128)(2,1)S(1)}, bf16[38,3,256]{2,1,0:T(4,128)(2,1)S(1)}, u32[]{:S(2)}, u32[]{:S(2)}) %collective-permute-start.2) | collective-permute-done | bytes 58400 | tf_op jit(solution)/shard_map/ppermute | solution.py:15
  23.2 1.4 %maximum_maximum_fusion.x_ref = bf16[38,41,256]{2,1,0:T(8,128)(2,1)} fusion(bf16[38,3,256]{2,1,0:T(4,128)(2,1)S(1)} %collective-permute-done.3, bf16[3,32,256]{2,1,0:T(8,128)(2,1)S(1)} %collective-permute-done.1, bf16[32,32,256]{2,1,0:T(8,128)(2,1)S(1)} %copy-done.1, bf16[3,32,256]{2,1,0:T(8,128)(2,1)S(1)} %collective-permute-done, ...), kind=kLoop, calls=%fused_computation.10 | loop fusion | flops 4786176 | bytes 1537106 | tf_op jit(solution)/shard_map/concatenate | solution.py:223
  24.6 15.2 %shard_map.136 = (bf16[1024,256]{1,0:T(8,128)(2,1)}, f32[16,256]{1,0:T(8,128)}, bf16[16,16,256]{2,1,0:T(8,128)(2,1)}) custom-call(bf16[38,41,256]{2,1,0:T(8,128)(2,1)} %maximum_maximum_fusion.x_ref, bf16[7,7,256]{2,1,0:T(8,128)(2,1)} %k_ref.1, f32[1,256]{1,0:T(1,128)} %bitcast.74, f32[1,256]{1,0:T(1,128)} %bitcast.75, f32[1,256]{1,0:T(1,128)} %bitcast.76, ...), custom_call_target="tpu_custom_call" | custom-call | flops 1099431936 | bytes 2894848 | tf_op jit(solution)/shard_map/pallas_call | solution.py:167
  39.8 6.5 %all-to-all-start = ((bf16[16,16,256]{2,1,0:T(8,128)(2,1)}), bf16[16,16,256]{2,1,0:T(8,128)(2,1)S(1)}, u32[]{:S(2)}, u32[]{:S(2)}) async-start(bf16[16,16,256]{2,1,0:T(8,128)(2,1)} %get-tuple-element.9), calls=%async_computation | async-start | bytes 262144 | tf_op jit(solution)/shard_map/all_to_all | solution.py:285
  46.4 0.2 reshape.73
  46.7 5.7 %all-to-all-done = bf16[16,16,256]{2,1,0:T(8,128)(2,1)S(1)} async-done(((bf16[16,16,256]{2,1,0:T(8,128)(2,1)}), bf16[16,16,256]{2,1,0:T(8,128)(2,1)S(1)}, u32[]{:S(2)}, u32[]{:S(2)}) %all-to-all-start) | async-done | bytes 131104 | tf_op jit(solution)/shard_map/all_to_all | solution.py:285
  52.6 0.2 convolution_convert_fusion
  52.9 0.1 copy.21
  53.0 0.1 fusion.3
  53.1 0.2 fusion.16
  53.3 0.1 copy.20
  53.4 0.3 fusion.4
  53.9 0.1 fusion.6
  54.0 0.1 broadcast_in_dim.5
  54.1 0.4 copy-done.2
  54.5 1.0 %fusion.5 = bf16[32,32,256]{2,1,0:T(8,128)(2,1)} fusion(f32[32,32,256]{2,1,0:T(8,128)S(1)} %bitcast.67, bf16[32,32,256]{2,1,0:T(8,128)(2,1)S(1)} %bitcast.71), kind=kLoop, calls=%fused_computation.9 | loop fusion | flops 786432 | bytes 2097152 | tf_op jit(solution)/shard_map/convert_element_type | solution.py:325
  (29 shorter events, 0.8 us)
Async XLA Ops:
  0.0 52.6 %copy-start = (bf16[256,512]{1,0:T(8,128)(2,1)S(1)}, bf16[256,512]{1,0:T(8,128)(2,1)}, u32[]{:S(2)}) copy-start(bf16[256,512]{1,0:T(8,128)(2,1)} %param.25) | copy-start | bytes 786436
  0.0 23.2 %copy-start.1 = (bf16[32,32,256]{2,1,0:T(8,128)(2,1)S(1)}, bf16[32,32,256]{2,1,0:T(8,128)(2,1)}, u32[]{:S(2)}) copy-start(bf16[32,32,256]{2,1,0:T(8,128)(2,1)} %param.14) | copy-start | bytes 1572868
  0.9 9.4 %collective-permute-start = (bf16[3,32,256]{2,1,0:T(8,128)(2,1)S(1)}, bf16[3,32,256]{2,1,0:T(8,128)(2,1)S(1)}, u32[]{:S(2)}, u32[]{:S(2)}) collective-permute-start(bf16[3,32,256]{2,1,0:T(8,128)(2,1)S(1)} %get-tuple-element.13), channel_id=1, source_target_pairs={{0,16},{16,32},{32,48},{48,64},{64,80},{80,96},{96,112},{112,128},... | collective-permute-start | bytes 147464 | tf_op jit(solution)/shard_map/ppermute | solution.py:15
  5.4 8.4 %collective-permute-start.1 = (bf16[3,32,256]{2,1,0:T(8,128)(2,1)S(1)}, bf16[3,32,256]{2,1,0:T(8,128)(2,1)S(1)}, u32[]{:S(2)}, u32[]{:S(2)}) collective-permute-start(bf16[3,32,256]{2,1,0:T(8,128)(2,1)S(1)} %get-tuple-element.14), channel_id=1, source_target_pairs={{16,0},{32,16},{48,32},{64,48},{80,64},{96,80},{112,96},{128,112},... | collective-permute-start | bytes 147464 | tf_op jit(solution)/shard_map/ppermute | solution.py:15
  14.0 7.9 %collective-permute-start.3 = (bf16[38,3,256]{2,1,0:T(4,128)(2,1)S(1)}, bf16[38,3,256]{2,1,0:T(4,128)(2,1)S(1)}, u32[]{:S(2)}, u32[]{:S(2)}) collective-permute-start(bf16[38,3,256]{2,1,0:T(4,128)(2,1)S(1)} %pad_maximum_fusion.2), channel_id=1, source_target_pairs={{1,0},{2,1},{3,2},{4,3},{5,4},{6,5},{7,6},{8,7},{9,8},{10,9},{11,1... | collective-permute-start | bytes 175112 | tf_op jit(solution)/shard_map/ppermute | solution.py:15
  18.1 5.1 %collective-permute-start.2 = (bf16[38,3,256]{2,1,0:T(4,128)(2,1)S(1)}, bf16[38,3,256]{2,1,0:T(4,128)(2,1)S(1)}, u32[]{:S(2)}, u32[]{:S(2)}) collective-permute-start(bf16[38,3,256]{2,1,0:T(4,128)(2,1)S(1)} %pad_maximum_fusion.1), channel_id=1, source_target_pairs={{0,1},{1,2},{2,3},{3,4},{4,5},{5,6},{6,7},{7,8},{8,9},{9,10},{10,1... | collective-permute-start | bytes 175112 | tf_op jit(solution)/shard_map/ppermute | solution.py:15
  39.8 6.9 %copy-start.4 = (f32[16,256]{1,0:T(8,128)S(1)}, f32[16,256]{1,0:T(8,128)}, u32[]{:S(2)}) copy-start(f32[16,256]{1,0:T(8,128)} %get-tuple-element.10) | copy-start | bytes 49156
  39.8 12.7 %all-to-all-start = ((bf16[16,16,256]{2,1,0:T(8,128)(2,1)}), bf16[16,16,256]{2,1,0:T(8,128)(2,1)S(1)}, u32[]{:S(2)}, u32[]{:S(2)}) async-start(bf16[16,16,256]{2,1,0:T(8,128)(2,1)} %get-tuple-element.9), calls=%async_computation | async-start | bytes 262144 | tf_op jit(solution)/shard_map/all_to_all | solution.py:285
  52.9 1.0 %copy-start.3 = (bf16[256,256]{1,0:T(8,128)(2,1)S(1)}, bf16[256,256]{1,0:T(8,128)(2,1)}, u32[]{:S(2)}) copy-start(bf16[256,256]{1,0:T(8,128)(2,1)} %param.27) | copy-start | bytes 393220
  53.4 1.1 %copy-start.2 = (bf16[1024,256]{1,0:T(8,128)(2,1)S(1)}, bf16[1024,256]{1,0:T(8,128)(2,1)}, u32[]{:S(2)}) copy-start(bf16[1024,256]{1,0:T(8,128)(2,1)} %get-tuple-element.8) | copy-start | bytes 1572868

commit v16 on v15

--- a/solution.py
+++ b/solution.py
@@ -202,6 +202,31 @@
         w_query,
     )
 
+def spread_kernel(bo_ref, lifted_ref, o_ref):
+    tile_rows, tile_cols, channels = o_ref.shape
+    per_row = tile_cols // 8
+    lifted = lifted_ref[...]
+    for i in range(tile_rows // 8):
+        spread = jnp.broadcast_to(
+            lifted[i * per_row : (i + 1) * per_row][:, None, :], (per_row, 8, channels)
+        ).reshape(tile_cols, channels)
+        rows = pl.ds(i * 8, 8)
+        o_ref[rows] = (bo_ref[rows].astype(jnp.float32) + spread[None]).astype(o_ref.dtype)
+
+
+def spread_add(block_out, lifted):
+    vmem = pl.BlockSpec(memory_space=pltpu.VMEM)
+    return pl.pallas_call(
+        spread_kernel,
+        out_shape=jax.ShapeDtypeStruct(block_out.shape, jnp.bfloat16),
+        in_specs=[vmem, vmem],
+        out_specs=vmem,
+        cost_estimate=pl.CostEstimate(
+            flops=block_out.size, bytes_accessed=4 * block_out.size, transcendentals=0
+        ),
+    )(block_out, lifted)
+
+
 def block_pass(
     pieces,
     features,
@@ -316,13 +341,8 @@
         .reshape(local_count, channels)
         .astype(jnp.bfloat16)
     )
-    lifted = jnp.dot(context, w_out, preferred_element_type=jnp.float32).reshape(
-        region_side, 1, region_side, 1, channels
-    )
-    spread = jnp.broadcast_to(lifted, (region_side, 8, region_side, 8, channels)).reshape(
-        tile_rows, tile_cols, channels
-    )
-    return (block_out.astype(jnp.float32) + spread).astype(jnp.bfloat16)
+    lifted = jnp.dot(context, w_out, preferred_element_type=jnp.float32)
+    return spread_add(block_out, lifted)
 
 
 def solution(mesh):

time: 55.9 us -> 56.2 us (level)
  the two profiles are of different devices: /device:TPU:113 before, /device:TPU:129 now
where the time goes in v16:
time: 56.2 us; the launch traced here: 55.7 us
  starting transfers between devices  20.3 us (36%)
  Pallas kernels  17.1 us (30%)
  waiting for transfers between devices  10.6 us (19%)
  local copies, waits for them, and re-layouts  4.3 us (8%)
  other arithmetic  1.76 us (3%)
  matrix products  1.41 us (3%)
    pallas_call x1, Pallas kernels, block_call(): pl.pallas_call(block_kernel, out_shape=(jax.ShapeDtypeStruct((pixels, cha...  15.2 us
    ppermute x4, starting transfers between devices, shifted(): return (lax.ppermute(piece, axis, up), lax.ppermute(piece, axis, down))  13 us
    all_to_all x1, starting transfers between devices, shards(): band_pooled = lax.all_to_all(sent, 'col', 0, 0)  7.32 us
    all_to_all x1, waiting for transfers between devices, shards(): band_pooled = lax.all_to_all(sent, 'col', 0, 0)  5.74 us
    ppermute x4, waiting for transfers between devices, shifted(): return (lax.ppermute(piece, axis, up), lax.ppermute(piece, axis, down))  4.83 us
    pallas_call x1, Pallas kernels, spread_add(): pl.pallas_call(spread_kernel, out_shape=jax.ShapeDtypeStruct(block_out.sh...  1.93 us
    another operation x1, local copies, waits for them, and re-layouts, shards(): rows_of.append(jnp.stack(per_col, axis=1))  1.44 us
    concatenate x1, other arithmetic, block_pass(): jnp.concatenate([left, extended, right, jnp.zeros_like(right)[:, :-(tile_...  1.4 us
  transfers between devices with their start and end apart: 5, of which 3 were waited for; matrix products, arithmetic and copies ran while one was open for 5% of the time, Pallas kernels for 0%

profile of v16, /device:TPU:129, one launch (start us, length us, event | category | flops | bytes accessed | tf_op | source)
XLA Modules:
  0.0 55.7 jit_solution(13540925734766702293)
XLA Ops:
  0.0 0.9 %fusion.9 = (bf16[3,32,256]{2,1,0:T(8,128)(2,1)S(1)}, bf16[3,32,256]{2,1,0:T(8,128)(2,1)S(1)}) fusion(bf16[32,32,256]{2,1,0:T(8,128)(2,1)} %param.14), kind=kLoop, calls=%fused_computation.38 | loop fusion | bytes 196608 | tf_op jit(solution)/shard_map/slice | solution.py:20
  0.9 4.4 %collective-permute-start.1 = (bf16[3,32,256]{2,1,0:T(8,128)(2,1)S(1)}, bf16[3,32,256]{2,1,0:T(8,128)(2,1)S(1)}, u32[]{:S(2)}, u32[]{:S(2)}) collective-permute-start(bf16[3,32,256]{2,1,0:T(8,128)(2,1)S(1)} %get-tuple-element.14), channel_id=1, source_target_pairs={{16,0},{32,16},{48,32},{64,48},{80,64},{96,80},{112,96},{128,112},... | collective-permute-start | bytes 147464 | tf_op jit(solution)/shard_map/ppermute | solution.py:15
  5.3 2.4 %collective-permute-start = (bf16[3,32,256]{2,1,0:T(8,128)(2,1)S(1)}, bf16[3,32,256]{2,1,0:T(8,128)(2,1)S(1)}, u32[]{:S(2)}, u32[]{:S(2)}) collective-permute-start(bf16[3,32,256]{2,1,0:T(8,128)(2,1)S(1)} %get-tuple-element.13), channel_id=1, source_target_pairs={{0,16},{16,32},{32,48},{48,64},{64,80},{80,96},{96,112},{112,128},... | collective-permute-start | bytes 147464 | tf_op jit(solution)/shard_map/ppermute | solution.py:15
  7.7 1.0 %fusion.8 = (bf16[32,3,256]{2,1,0:T(4,128)(2,1)S(1)}, bf16[32,3,256]{2,1,0:T(4,128)(2,1)S(1)}) fusion(bf16[32,32,256]{2,1,0:T(8,128)(2,1)} %param.14), kind=kLoop, calls=%fused_computation.37 | loop fusion | bytes 196608 | tf_op jit(solution)/shard_map/slice | solution.py:23
  8.7 1.4 %dynamic-slice_bitcast_fusion.15 = (f32[8,1,4,64]{3,0,2,1:T(8,128)S(1)}, f32[8,1,4,64]{3,0,2,1:T(8,128)S(1)}, f32[8,1,4,64]{3,0,2,1:T(8,128)S(1)}, f32[8,1,4,64]...) fusion(f32[8,7,127]{2,0,1:T(8,128)} %param.26, ...), kind=kLoop, calls=%fused_computation.35 | loop fusion | bytes 262172 | tf_op jit(solution)/shard_map/stack | solution.py:328
  10.3 3.4 %collective-permute-done = bf16[3,32,256]{2,1,0:T(8,128)(2,1)S(1)} collective-permute-done((bf16[3,32,256]{2,1,0:T(8,128)(2,1)S(1)}, bf16[3,32,256]{2,1,0:T(8,128)(2,1)S(1)}, u32[]{:S(2)}, u32[]{:S(2)}) %collective-permute-start) | collective-permute-done | bytes 49184 | tf_op jit(solution)/shard_map/ppermute | solution.py:15
  13.8 4.0 %collective-permute-start.3 = (bf16[38,3,256]{2,1,0:T(4,128)(2,1)S(1)}, bf16[38,3,256]{2,1,0:T(4,128)(2,1)S(1)}, u32[]{:S(2)}, u32[]{:S(2)}) collective-permute-start(bf16[38,3,256]{2,1,0:T(4,128)(2,1)S(1)} %pad_maximum_fusion.2), channel_id=1, source_target_pairs={{1,0},{2,1},{3,2},{4,3},{5,4},{6,5},{7,6},{8,7},{9,8},{10,9},{11,1... | collective-permute-start | bytes 175112 | tf_op jit(solution)/shard_map/ppermute | solution.py:15
  17.9 2.2 %collective-permute-start.2 = (bf16[38,3,256]{2,1,0:T(4,128)(2,1)S(1)}, bf16[38,3,256]{2,1,0:T(4,128)(2,1)S(1)}, u32[]{:S(2)}, u32[]{:S(2)}) collective-permute-start(bf16[38,3,256]{2,1,0:T(4,128)(2,1)S(1)} %pad_maximum_fusion.1), channel_id=1, source_target_pairs={{0,1},{1,2},{2,3},{3,4},{4,5},{5,6},{6,7},{7,8},{8,9},{9,10},{10,1... | collective-permute-start | bytes 175112 | tf_op jit(solution)/shard_map/ppermute | solution.py:15
  20.2 1.4 %collective-permute-done.2 = bf16[38,3,256]{2,1,0:T(4,128)(2,1)S(1)} collective-permute-done((bf16[38,3,256]{2,1,0:T(4,128)(2,1)S(1)}, bf16[38,3,256]{2,1,0:T(4,128)(2,1)S(1)}, u32[]{:S(2)}, u32[]{:S(2)}) %collective-permute-start.2) | collective-permute-done | bytes 58400 | tf_op jit(solution)/shard_map/ppermute | solution.py:15
  21.5 1.4 %maximum_maximum_fusion.x_ref = bf16[38,41,256]{2,1,0:T(8,128)(2,1)} fusion(bf16[38,3,256]{2,1,0:T(4,128)(2,1)S(1)} %collective-permute-done.3, bf16[3,32,256]{2,1,0:T(8,128)(2,1)S(1)} %collective-permute-done.1, bf16[32,32,256]{2,1,0:T(8,128)(2,1)S(1)} %copy-done.1, bf16[3,32,256]{2,1,0:T(8,128)(2,1)S(1)} %collective-permute-done, ...), kind=kLoop, calls=%fused_computation.8 | loop fusion | flops 4786176 | bytes 1537106 | tf_op jit(solution)/shard_map/concatenate | solution.py:248
  22.9 15.2 %shard_map.136 = (bf16[1024,256]{1,0:T(8,128)(2,1)}, f32[16,256]{1,0:T(8,128)}, bf16[16,16,256]{2,1,0:T(8,128)(2,1)}) custom-call(bf16[38,41,256]{2,1,0:T(8,128)(2,1)} %maximum_maximum_fusion.x_ref, bf16[7,7,256]{2,1,0:T(8,128)(2,1)} %k_ref.1, f32[1,256]{1,0:T(1,128)} %bitcast.69, f32[1,256]{1,0:T(1,128)} %bitcast.70, f32[1,256]{1,0:T(1,128)} %bitcast.71, ...), custom_call_target="tpu_custom_call" | custom-call | flops 1099431936 | bytes 2894848 | tf_op jit(solution)/shard_map/pallas_call | solution.py:167
  38.1 7.3 %all-to-all-start = ((bf16[16,16,256]{2,1,0:T(8,128)(2,1)}), bf16[16,16,256]{2,1,0:T(8,128)(2,1)S(1)}, u32[]{:S(2)}, u32[]{:S(2)}) async-start(bf16[16,16,256]{2,1,0:T(8,128)(2,1)} %get-tuple-element.9), calls=%async_computation | async-start | bytes 262144 | tf_op jit(solution)/shard_map/all_to_all | solution.py:310
  45.6 0.2 reshape.59
  45.8 0.1 reshape.57
  45.9 5.7 %all-to-all-done = bf16[16,16,256]{2,1,0:T(8,128)(2,1)S(1)} async-done(((bf16[16,16,256]{2,1,0:T(8,128)(2,1)}), bf16[16,16,256]{2,1,0:T(8,128)(2,1)S(1)}, u32[]{:S(2)}, u32[]{:S(2)}) %all-to-all-start) | async-done | bytes 131104 | tf_op jit(solution)/shard_map/all_to_all | solution.py:310
  51.8 0.2 convolution_convert_fusion
  52.0 0.1 copy.20
  52.1 0.1 copy.21
  52.2 0.1 fusion.3
  52.4 0.2 fusion.13
  52.6 0.3 fusion.4
  52.9 0.1 convert_element_type.23
  53.0 0.8 %fusion.14.lifted_ref = f32[16,256]{1,0:T(8,128)} fusion(bf16[16,256]{1,0:T(8,128)(2,1)S(1)} %convert_element_type.23, bf16[256,256]{1,0:T(8,128)(2,1)S(1)} %copy-done.2), kind=kOutput, calls=%fused_computation.43 | convolution fusion | flops 2097152 | bytes 155648 | tf_op jit(solution)/shard_map/dot_general | solution.py:344
  53.7 1.9 %shard_map.137 = bf16[32,32,256]{2,1,0:T(8,128)(2,1)} custom-call(bf16[32,32,256]{2,1,0:T(8,128)(2,1)} %bitcast.64, f32[16,256]{1,0:T(8,128)} %fusion.14.lifted_ref), custom_call_target="tpu_custom_call" | custom-call | flops 262144 | bytes 1048576 | tf_op jit(solution)/shard_map/pallas_call | solution.py:219
  (26 shorter events, 0.6 us)
Async XLA Ops:
  0.0 51.8 %copy-start = (bf16[256,512]{1,0:T(8,128)(2,1)S(1)}, bf16[256,512]{1,0:T(8,128)(2,1)}, u32[]{:S(2)}) copy-start(bf16[256,512]{1,0:T(8,128)(2,1)} %param.25) | copy-start | bytes 786436
  0.0 21.5 %copy-start.1 = (bf16[32,32,256]{2,1,0:T(8,128)(2,1)S(1)}, bf16[32,32,256]{2,1,0:T(8,128)(2,1)}, u32[]{:S(2)}) copy-start(bf16[32,32,256]{2,1,0:T(8,128)(2,1)} %param.14) | copy-start | bytes 1572868
  0.9 9.4 %collective-permute-start.1 = (bf16[3,32,256]{2,1,0:T(8,128)(2,1)S(1)}, bf16[3,32,256]{2,1,0:T(8,128)(2,1)S(1)}, u32[]{:S(2)}, u32[]{:S(2)}) collective-permute-start(bf16[3,32,256]{2,1,0:T(8,128)(2,1)S(1)} %get-tuple-element.14), channel_id=1, source_target_pairs={{16,0},{32,16},{48,32},{64,48},{80,64},{96,80},{112,96},{128,112},... | collective-permute-start | bytes 147464 | tf_op jit(solution)/shard_map/ppermute | solution.py:15
  5.3 8.4 %collective-permute-start = (bf16[3,32,256]{2,1,0:T(8,128)(2,1)S(1)}, bf16[3,32,256]{2,1,0:T(8,128)(2,1)S(1)}, u32[]{:S(2)}, u32[]{:S(2)}) collective-permute-start(bf16[3,32,256]{2,1,0:T(8,128)(2,1)S(1)} %get-tuple-element.13), channel_id=1, source_target_pairs={{0,16},{16,32},{32,48},{48,64},{64,80},{80,96},{96,112},{112,128},... | collective-permute-start | bytes 147464 | tf_op jit(solution)/shard_map/ppermute | solution.py:15
  13.8 6.4 %collective-permute-start.3 = (bf16[38,3,256]{2,1,0:T(4,128)(2,1)S(1)}, bf16[38,3,256]{2,1,0:T(4,128)(2,1)S(1)}, u32[]{:S(2)}, u32[]{:S(2)}) collective-permute-start(bf16[38,3,256]{2,1,0:T(4,128)(2,1)S(1)} %pad_maximum_fusion.2), channel_id=1, source_target_pairs={{1,0},{2,1},{3,2},{4,3},{5,4},{6,5},{7,6},{8,7},{9,8},{10,9},{11,1... | collective-permute-start | bytes 175112 | tf_op jit(solution)/shard_map/ppermute | solution.py:15
  17.9 3.6 %collective-permute-start.2 = (bf16[38,3,256]{2,1,0:T(4,128)(2,1)S(1)}, bf16[38,3,256]{2,1,0:T(4,128)(2,1)S(1)}, u32[]{:S(2)}, u32[]{:S(2)}) collective-permute-start(bf16[38,3,256]{2,1,0:T(4,128)(2,1)S(1)} %pad_maximum_fusion.1), channel_id=1, source_target_pairs={{0,1},{1,2},{2,3},{3,4},{4,5},{5,6},{6,7},{7,8},{8,9},{9,10},{10,1... | collective-permute-start | bytes 175112 | tf_op jit(solution)/shard_map/ppermute | solution.py:15
  38.1 7.7 %copy-start.3 = (f32[16,256]{1,0:T(8,128)S(1)}, f32[16,256]{1,0:T(8,128)}, u32[]{:S(2)}) copy-start(f32[16,256]{1,0:T(8,128)} %get-tuple-element.10) | copy-start | bytes 49156
  38.1 13.5 %all-to-all-start = ((bf16[16,16,256]{2,1,0:T(8,128)(2,1)}), bf16[16,16,256]{2,1,0:T(8,128)(2,1)S(1)}, u32[]{:S(2)}, u32[]{:S(2)}) async-start(bf16[16,16,256]{2,1,0:T(8,128)(2,1)} %get-tuple-element.9), calls=%async_computation | async-start | bytes 262144 | tf_op jit(solution)/shard_map/all_to_all | solution.py:310
  52.0 1.0 %copy-start.2 = (bf16[256,256]{1,0:T(8,128)(2,1)S(1)}, bf16[256,256]{1,0:T(8,128)(2,1)}, u32[]{:S(2)}) copy-start(bf16[256,256]{1,0:T(8,128)(2,1)} %param.27) | copy-start | bytes 393220

commit v17 on v15

--- a/solution.py
+++ b/solution.py
@@ -128,12 +128,14 @@
 
 
 def block_kernel(
-    x_ref, k_ref, db_ref, g_ref, nb_ref, f_ref, we_hbm, be_ref, wr_hbm, br_ref, ls_ref, wq_hbm,
-    o_ref, q_ref, s_ref, kf_ref, sh_ref, n_ref, we_ref, wr_ref, wq_ref, sem,
+    x_ref, k_ref, db_ref, g_ref, nb_ref, f_hbm, we_hbm, be_ref, wr_hbm, br_ref, ls_ref, wq_hbm,
+    o_hbm, q_ref, s_ref, kf_ref, sh_ref, n_ref, we_ref, wr_ref, wq_ref, f_ref, o_ref, sem, out_sem,
 ):
     loads = [
         pltpu.make_async_copy(source, target, sem.at[i])
-        for i, (source, target) in enumerate(((we_hbm, we_ref), (wr_hbm, wr_ref), (wq_hbm, wq_ref)))
+        for i, (source, target) in enumerate(
+            ((we_hbm, we_ref), (wr_hbm, wr_ref), (wq_hbm, wq_ref), (f_hbm, f_ref))
+        )
     ]
     for load in loads:
         load.start()
@@ -143,14 +145,20 @@
     tile_rows, tile_cols, channels = n_ref.shape
     per_row = tile_cols // 8
     block = 8 * tile_cols
+    stores = []
     for step in range(tile_rows // 8):
         rows = pl.ds(step * block, block)
         normed = n_ref[pl.ds(step * 8, 8)].reshape(block, channels)
         out = mlp_block(normed, f_ref[rows], we_ref, be_ref, wr_ref, br_ref, ls_ref, o_ref.dtype)
         o_ref[rows] = out
+        store = pltpu.make_async_copy(o_ref.at[rows], o_hbm.at[rows], out_sem.at[step])
+        store.start()
+        stores.append(store)
         queries, copies = region_tokens(out, wq_ref, s_ref.shape[0])
         q_ref[pl.ds(step * per_row, per_row), :] = queries
         s_ref[:, pl.ds(step * per_row, per_row), :] = copies
+    for store in stores:
+        store.wait()
 
 
 def block_call(
@@ -171,8 +179,8 @@
             jax.ShapeDtypeStruct((tokens, channels), jnp.float32),
             jax.ShapeDtypeStruct((copies, tokens, channels), jnp.bfloat16),
         ),
-        in_specs=[vmem] * 6 + [anywhere, vmem, anywhere, vmem, vmem, anywhere],
-        out_specs=(vmem, vmem, vmem),
+        in_specs=[vmem] * 5 + [anywhere, anywhere, vmem, anywhere, vmem, vmem, anywhere],
+        out_specs=(anywhere, vmem, vmem),
         scratch_shapes=[
             pltpu.VMEM((TAPS, 8, channels), jnp.float32),
             pltpu.VMEM((TAPS, rows_p, tile_cols, channels), jnp.float32),
@@ -180,7 +188,10 @@
             pltpu.VMEM((channels, hidden_total), jnp.bfloat16),
             pltpu.VMEM((hidden_total, channels), jnp.bfloat16),
             pltpu.VMEM((channels, channels), jnp.bfloat16),
-            pltpu.SemaphoreType.DMA((3,)),
+            pltpu.VMEM((pixels, channels), jnp.bfloat16),
+            pltpu.VMEM((pixels, channels), jnp.bfloat16),
+            pltpu.SemaphoreType.DMA((4,)),
+            pltpu.SemaphoreType.DMA((tile_rows // 8,)),
         ],
         cost_estimate=pl.CostEstimate(
             flops=2 * TAPS * TAPS * pixels * channels + 4 * pixels * channels * hidden_total,

time: 55.9 us -> 56.3 us (level)
  no operation moved by 1% of the time
where the time goes in v17:
time: 56.3 us; the launch traced here: 55.8 us
  starting transfers between devices  21 us (37%)
  Pallas kernels  15.5 us (28%)
  waiting for transfers between devices  10.7 us (19%)
  local copies, waits for them, and re-layouts  4.8 us (9%)
  other arithmetic  2.72 us (5%)
  matrix products  0.79 us (1%)
    pallas_call x1, Pallas kernels, block_call(): pl.pallas_call(block_kernel, out_shape=(jax.ShapeDtypeStruct((pixels, cha...  15.5 us
    ppermute x4, starting transfers between devices, shifted(): return (lax.ppermute(piece, axis, up), lax.ppermute(piece, axis, down))  14.5 us
    all_to_all x1, starting transfers between devices, shards(): band_pooled = lax.all_to_all(sent, 'col', 0, 0)  6.53 us
    all_to_all x1, waiting for transfers between devices, shards(): band_pooled = lax.all_to_all(sent, 'col', 0, 0)  5.74 us
    ppermute x4, waiting for transfers between devices, shifted(): return (lax.ppermute(piece, axis, up), lax.ppermute(piece, axis, down))  4.99 us
    another operation x1, local copies, waits for them, and re-layouts, shards(): rows_of.append(jnp.stack(per_col, axis=1))  1.45 us
    concatenate x1, other arithmetic, block_pass(): jnp.concatenate([left, extended, right, jnp.zeros_like(right)[:, :-(tile_...  1.4 us
  transfers between devices with their start and end apart: 5, of which 3 were waited for; matrix products, arithmetic and copies ran while one was open for 5% of the time, Pallas kernels for 0%

profile of v17, /device:TPU:113, one launch (start us, length us, event | category | flops | bytes accessed | tf_op | source)
XLA Modules:
  0.0 55.8 jit_solution(9036042199536627465)
XLA Ops:
  0.0 0.9 %fusion.12 = (bf16[3,32,256]{2,1,0:T(8,128)(2,1)S(1)}, bf16[3,32,256]{2,1,0:T(8,128)(2,1)S(1)}) fusion(bf16[32,32,256]{2,1,0:T(8,128)(2,1)} %param.14), kind=kLoop, calls=%fused_computation.42 | loop fusion | bytes 196608 | tf_op jit(solution)/shard_map/slice | solution.py:20
  0.9 4.5 %collective-permute-start = (bf16[3,32,256]{2,1,0:T(8,128)(2,1)S(1)}, bf16[3,32,256]{2,1,0:T(8,128)(2,1)S(1)}, u32[]{:S(2)}, u32[]{:S(2)}) collective-permute-start(bf16[3,32,256]{2,1,0:T(8,128)(2,1)S(1)} %get-tuple-element.13), channel_id=1, source_target_pairs={{0,16},{16,32},{32,48},{48,64},{64,80},{80,96},{96,112},{112,128},... | collective-permute-start | bytes 147464 | tf_op jit(solution)/shard_map/ppermute | solution.py:15
  5.4 2.3 %collective-permute-start.1 = (bf16[3,32,256]{2,1,0:T(8,128)(2,1)S(1)}, bf16[3,32,256]{2,1,0:T(8,128)(2,1)S(1)}, u32[]{:S(2)}, u32[]{:S(2)}) collective-permute-start(bf16[3,32,256]{2,1,0:T(8,128)(2,1)S(1)} %get-tuple-element.14), channel_id=1, source_target_pairs={{16,0},{32,16},{48,32},{64,48},{80,64},{96,80},{112,96},{128,112},... | collective-permute-start | bytes 147464 | tf_op jit(solution)/shard_map/ppermute | solution.py:15
  7.7 1.0 %fusion.11 = (bf16[32,3,256]{2,1,0:T(4,128)(2,1)S(1)}, bf16[32,3,256]{2,1,0:T(4,128)(2,1)S(1)}) fusion(bf16[32,32,256]{2,1,0:T(8,128)(2,1)} %param.14), kind=kLoop, calls=%fused_computation.41 | loop fusion | bytes 196608 | tf_op jit(solution)/shard_map/slice | solution.py:23
  8.7 1.4 %dynamic-slice_bitcast_fusion.15 = (f32[8,1,4,64]{3,0,2,1:T(8,128)S(1)}, f32[8,1,4,64]{3,0,2,1:T(8,128)S(1)}, f32[8,1,4,64]{3,0,2,1:T(8,128)S(1)}, f32[8,1,4,64]...) fusion(f32[8,7,127]{2,0,1:T(8,128)} %param.26, ...), kind=kLoop, calls=%fused_computation.39 | loop fusion | bytes 262172 | tf_op jit(solution)/shard_map/stack | solution.py:314
  10.3 3.6 %collective-permute-done.1 = bf16[3,32,256]{2,1,0:T(8,128)(2,1)S(1)} collective-permute-done((bf16[3,32,256]{2,1,0:T(8,128)(2,1)S(1)}, bf16[3,32,256]{2,1,0:T(8,128)(2,1)S(1)}, u32[]{:S(2)}, u32[]{:S(2)}) %collective-permute-start.1) | collective-permute-done | bytes 49184 | tf_op jit(solution)/shard_map/ppermute | solution.py:15
  14.0 4.0 %collective-permute-start.3 = (bf16[38,3,256]{2,1,0:T(4,128)(2,1)S(1)}, bf16[38,3,256]{2,1,0:T(4,128)(2,1)S(1)}, u32[]{:S(2)}, u32[]{:S(2)}) collective-permute-start(bf16[38,3,256]{2,1,0:T(4,128)(2,1)S(1)} %pad_maximum_fusion.2), channel_id=1, source_target_pairs={{1,0},{2,1},{3,2},{4,3},{5,4},{6,5},{7,6},{8,7},{9,8},{10,9},{11,1... | collective-permute-start | bytes 175112 | tf_op jit(solution)/shard_map/ppermute | solution.py:15
  18.1 3.7 %collective-permute-start.2 = (bf16[38,3,256]{2,1,0:T(4,128)(2,1)S(1)}, bf16[38,3,256]{2,1,0:T(4,128)(2,1)S(1)}, u32[]{:S(2)}, u32[]{:S(2)}) collective-permute-start(bf16[38,3,256]{2,1,0:T(4,128)(2,1)S(1)} %pad_maximum_fusion.1), channel_id=1, source_target_pairs={{0,1},{1,2},{2,3},{3,4},{4,5},{5,6},{6,7},{7,8},{8,9},{9,10},{10,1... | collective-permute-start | bytes 175112 | tf_op jit(solution)/shard_map/ppermute | solution.py:15
  21.8 1.4 %collective-permute-done.2 = bf16[38,3,256]{2,1,0:T(4,128)(2,1)S(1)} collective-permute-done((bf16[38,3,256]{2,1,0:T(4,128)(2,1)S(1)}, bf16[38,3,256]{2,1,0:T(4,128)(2,1)S(1)}, u32[]{:S(2)}, u32[]{:S(2)}) %collective-permute-start.2) | collective-permute-done | bytes 58400 | tf_op jit(solution)/shard_map/ppermute | solution.py:15
  23.2 1.4 %maximum_maximum_fusion.x_ref = bf16[38,41,256]{2,1,0:T(8,128)(2,1)} fusion(bf16[38,3,256]{2,1,0:T(4,128)(2,1)S(1)} %collective-permute-done.3, bf16[3,32,256]{2,1,0:T(8,128)(2,1)S(1)} %collective-permute-done.1, bf16[32,32,256]{2,1,0:T(8,128)(2,1)S(1)} %copy-done.1, bf16[3,32,256]{2,1,0:T(8,128)(2,1)S(1)} %collective-permute-done, ...), kind=kLoop, calls=%fused_computation.10 | loop fusion | flops 4786176 | bytes 1537106 | tf_op jit(solution)/shard_map/concatenate | solution.py:234
  24.6 15.5 %shard_map.136 = (bf16[1024,256]{1,0:T(8,128)(2,1)}, f32[16,256]{1,0:T(8,128)}, bf16[16,16,256]{2,1,0:T(8,128)(2,1)}) custom-call(bf16[38,41,256]{2,1,0:T(8,128)(2,1)} %maximum_maximum_fusion.x_ref, bf16[7,7,256]{2,1,0:T(8,128)(2,1)} %k_ref.1, f32[1,256]{1,0:T(1,128)} %bitcast.74, f32[1,256]{1,0:T(1,128)} %bitcast.75, f32[1,256]{1,0:T(1,128)} %bitcast.76, ...), custom_call_target="tpu_custom_call" | custom-call | flops 1099431936 | bytes 2894848 | tf_op jit(solution)/shard_map/pallas_call | solution.py:175
  40.1 6.5 %all-to-all-start = ((bf16[16,16,256]{2,1,0:T(8,128)(2,1)}), bf16[16,16,256]{2,1,0:T(8,128)(2,1)S(1)}, u32[]{:S(2)}, u32[]{:S(2)}) async-start(bf16[16,16,256]{2,1,0:T(8,128)(2,1)} %get-tuple-element.9), calls=%async_computation | async-start | bytes 262144 | tf_op jit(solution)/shard_map/all_to_all | solution.py:296
  46.8 0.2 reshape.73
  47.1 5.7 %all-to-all-done = bf16[16,16,256]{2,1,0:T(8,128)(2,1)S(1)} async-done(((bf16[16,16,256]{2,1,0:T(8,128)(2,1)}), bf16[16,16,256]{2,1,0:T(8,128)(2,1)S(1)}, u32[]{:S(2)}, u32[]{:S(2)}) %all-to-all-start) | async-done | bytes 131104 | tf_op jit(solution)/shard_map/all_to_all | solution.py:296
  53.0 0.2 convolution_convert_fusion
  53.3 0.1 copy.21
  53.4 0.1 fusion.3
  53.5 0.2 fusion.16
  53.7 0.1 copy.20
  53.8 0.3 fusion.4
  54.2 0.1 fusion.6
  54.4 0.1 broadcast_in_dim.5
  54.5 0.4 copy-done.2
  54.9 1.0 %fusion.5 = bf16[32,32,256]{2,1,0:T(8,128)(2,1)} fusion(f32[32,32,256]{2,1,0:T(8,128)S(1)} %bitcast.67, bf16[32,32,256]{2,1,0:T(8,128)(2,1)S(1)} %bitcast.71), kind=kLoop, calls=%fused_computation.9 | loop fusion | flops 786432 | bytes 2097152 | tf_op jit(solution)/shard_map/convert_element_type | solution.py:336
  (29 shorter events, 0.8 us)
Async XLA Ops:
  0.0 53.0 %copy-start = (bf16[256,512]{1,0:T(8,128)(2,1)S(1)}, bf16[256,512]{1,0:T(8,128)(2,1)}, u32[]{:S(2)}) copy-start(bf16[256,512]{1,0:T(8,128)(2,1)} %param.25) | copy-start | bytes 786436
  0.0 23.2 %copy-start.1 = (bf16[32,32,256]{2,1,0:T(8,128)(2,1)S(1)}, bf16[32,32,256]{2,1,0:T(8,128)(2,1)}, u32[]{:S(2)}) copy-start(bf16[32,32,256]{2,1,0:T(8,128)(2,1)} %param.14) | copy-start | bytes 1572868
  0.9 9.4 %collective-permute-start = (bf16[3,32,256]{2,1,0:T(8,128)(2,1)S(1)}, bf16[3,32,256]{2,1,0:T(8,128)(2,1)S(1)}, u32[]{:S(2)}, u32[]{:S(2)}) collective-permute-start(bf16[3,32,256]{2,1,0:T(8,128)(2,1)S(1)} %get-tuple-element.13), channel_id=1, source_target_pairs={{0,16},{16,32},{32,48},{48,64},{64,80},{80,96},{96,112},{112,128},... | collective-permute-start | bytes 147464 | tf_op jit(solution)/shard_map/ppermute | solution.py:15
  5.4 8.4 %collective-permute-start.1 = (bf16[3,32,256]{2,1,0:T(8,128)(2,1)S(1)}, bf16[3,32,256]{2,1,0:T(8,128)(2,1)S(1)}, u32[]{:S(2)}, u32[]{:S(2)}) collective-permute-start(bf16[3,32,256]{2,1,0:T(8,128)(2,1)S(1)} %get-tuple-element.14), channel_id=1, source_target_pairs={{16,0},{32,16},{48,32},{64,48},{80,64},{96,80},{112,96},{128,112},... | collective-permute-start | bytes 147464 | tf_op jit(solution)/shard_map/ppermute | solution.py:15
  14.0 7.9 %collective-permute-start.3 = (bf16[38,3,256]{2,1,0:T(4,128)(2,1)S(1)}, bf16[38,3,256]{2,1,0:T(4,128)(2,1)S(1)}, u32[]{:S(2)}, u32[]{:S(2)}) collective-permute-start(bf16[38,3,256]{2,1,0:T(4,128)(2,1)S(1)} %pad_maximum_fusion.2), channel_id=1, source_target_pairs={{1,0},{2,1},{3,2},{4,3},{5,4},{6,5},{7,6},{8,7},{9,8},{10,9},{11,1... | collective-permute-start | bytes 175112 | tf_op jit(solution)/shard_map/ppermute | solution.py:15
  18.1 5.1 %collective-permute-start.2 = (bf16[38,3,256]{2,1,0:T(4,128)(2,1)S(1)}, bf16[38,3,256]{2,1,0:T(4,128)(2,1)S(1)}, u32[]{:S(2)}, u32[]{:S(2)}) collective-permute-start(bf16[38,3,256]{2,1,0:T(4,128)(2,1)S(1)} %pad_maximum_fusion.1), channel_id=1, source_target_pairs={{0,1},{1,2},{2,3},{3,4},{4,5},{5,6},{6,7},{7,8},{8,9},{9,10},{10,1... | collective-permute-start | bytes 175112 | tf_op jit(solution)/shard_map/ppermute | solution.py:15
  40.1 6.9 %copy-start.4 = (f32[16,256]{1,0:T(8,128)S(1)}, f32[16,256]{1,0:T(8,128)}, u32[]{:S(2)}) copy-start(f32[16,256]{1,0:T(8,128)} %get-tuple-element.10) | copy-start | bytes 49156
  40.1 12.7 %all-to-all-start = ((bf16[16,16,256]{2,1,0:T(8,128)(2,1)}), bf16[16,16,256]{2,1,0:T(8,128)(2,1)S(1)}, u32[]{:S(2)}, u32[]{:S(2)}) async-start(bf16[16,16,256]{2,1,0:T(8,128)(2,1)} %get-tuple-element.9), calls=%async_computation | async-start | bytes 262144 | tf_op jit(solution)/shard_map/all_to_all | solution.py:296
  53.2 1.0 %copy-start.3 = (bf16[256,256]{1,0:T(8,128)(2,1)S(1)}, bf16[256,256]{1,0:T(8,128)(2,1)}, u32[]{:S(2)}) copy-start(bf16[256,256]{1,0:T(8,128)(2,1)} %param.27) | copy-start | bytes 393220
  53.8 1.1 %copy-start.2 = (bf16[1024,256]{1,0:T(8,128)(2,1)S(1)}, bf16[1024,256]{1,0:T(8,128)(2,1)}, u32[]{:S(2)}) copy-start(bf16[1024,256]{1,0:T(8,128)(2,1)} %get-tuple-element.8) | copy-start | bytes 1572868

commit v18 on v15

--- a/solution.py
+++ b/solution.py
@@ -221,7 +221,7 @@
     top, bottom, left, right = pieces
     extended = jnp.concatenate([top, features, bottom], axis=0)
     padded = jnp.concatenate(
-        [left, extended, right, jnp.zeros_like(right)[:, : -(tile_cols + 3 * 3) % 8]], axis=1
+        [left, extended, right], axis=1
     )
     summed, queries, sent = block_call(
         padded,

time: 55.9 us -> 55.8 us (level)
  no operation moved by 1% of the time
where the time goes in v18:
time: 55.8 us; the launch traced here: 55.3 us
  starting transfers between devices  21 us (38%)
  Pallas kernels  15.1 us (27%)
  waiting for transfers between devices  10.8 us (19%)
  local copies, waits for them, and re-layouts  4.72 us (8%)
  other arithmetic  2.65 us (5%)
  matrix products  0.8 us (1%)
    pallas_call x1, Pallas kernels, block_call(): pl.pallas_call(block_kernel, out_shape=(jax.ShapeDtypeStruct((pixels, cha...  15.1 us
    ppermute x4, starting transfers between devices, shifted(): return (lax.ppermute(piece, axis, up), lax.ppermute(piece, axis, down))  14.5 us
    all_to_all x1, starting transfers between devices, shards(): band_pooled = lax.all_to_all(sent, 'col', 0, 0)  6.53 us
    all_to_all x1, waiting for transfers between devices, shards(): band_pooled = lax.all_to_all(sent, 'col', 0, 0)  5.74 us
    ppermute x4, waiting for transfers between devices, shifted(): return (lax.ppermute(piece, axis, up), lax.ppermute(piece, axis, down))  5.06 us
    another operation x1, local copies, waits for them, and re-layouts, shards(): rows_of.append(jnp.stack(per_col, axis=1))  1.45 us
    concatenate x1, other arithmetic, block_pass(): padded = jnp.concatenate([left, extended, right], axis=1)  1.33 us
  transfers between devices with their start and end apart: 5, of which 3 were waited for; matrix products, arithmetic and copies ran while one was open for 5% of the time, Pallas kernels for 0%

profile of v18, /device:TPU:113, one launch (start us, length us, event | category | flops | bytes accessed | tf_op | source)
XLA Modules:
  0.0 55.3 jit_solution(5097102246668208184)
XLA Ops:
  0.0 0.9 %fusion.12 = (bf16[3,32,256]{2,1,0:T(8,128)(2,1)S(1)}, bf16[3,32,256]{2,1,0:T(8,128)(2,1)S(1)}) fusion(bf16[32,32,256]{2,1,0:T(8,128)(2,1)} %param.14), kind=kLoop, calls=%fused_computation.42 | loop fusion | bytes 196608 | tf_op jit(solution)/shard_map/slice | solution.py:20
  0.9 4.5 %collective-permute-start = (bf16[3,32,256]{2,1,0:T(8,128)(2,1)S(1)}, bf16[3,32,256]{2,1,0:T(8,128)(2,1)S(1)}, u32[]{:S(2)}, u32[]{:S(2)}) collective-permute-start(bf16[3,32,256]{2,1,0:T(8,128)(2,1)S(1)} %get-tuple-element.13), channel_id=1, source_target_pairs={{0,16},{16,32},{32,48},{48,64},{64,80},{80,96},{96,112},{112,128},... | collective-permute-start | bytes 147464 | tf_op jit(solution)/shard_map/ppermute | solution.py:15
  5.4 2.3 %collective-permute-start.1 = (bf16[3,32,256]{2,1,0:T(8,128)(2,1)S(1)}, bf16[3,32,256]{2,1,0:T(8,128)(2,1)S(1)}, u32[]{:S(2)}, u32[]{:S(2)}) collective-permute-start(bf16[3,32,256]{2,1,0:T(8,128)(2,1)S(1)} %get-tuple-element.14), channel_id=1, source_target_pairs={{16,0},{32,16},{48,32},{64,48},{80,64},{96,80},{112,96},{128,112},... | collective-permute-start | bytes 147464 | tf_op jit(solution)/shard_map/ppermute | solution.py:15
  7.7 1.0 %fusion.11 = (bf16[32,3,256]{2,1,0:T(4,128)(2,1)S(1)}, bf16[32,3,256]{2,1,0:T(4,128)(2,1)S(1)}) fusion(bf16[32,32,256]{2,1,0:T(8,128)(2,1)} %param.14), kind=kLoop, calls=%fused_computation.41 | loop fusion | bytes 196608 | tf_op jit(solution)/shard_map/slice | solution.py:23
  8.7 1.4 %dynamic-slice_bitcast_fusion.15 = (f32[8,1,4,64]{3,0,2,1:T(8,128)S(1)}, f32[8,1,4,64]{3,0,2,1:T(8,128)S(1)}, f32[8,1,4,64]{3,0,2,1:T(8,128)S(1)}, f32[8,1,4,64]...) fusion(f32[8,7,127]{2,0,1:T(8,128)} %param.26, ...), kind=kLoop, calls=%fused_computation.39 | loop fusion | bytes 262172 | tf_op jit(solution)/shard_map/stack | solution.py:303
  10.2 3.7 %collective-permute-done.1 = bf16[3,32,256]{2,1,0:T(8,128)(2,1)S(1)} collective-permute-done((bf16[3,32,256]{2,1,0:T(8,128)(2,1)S(1)}, bf16[3,32,256]{2,1,0:T(8,128)(2,1)S(1)}, u32[]{:S(2)}, u32[]{:S(2)}) %collective-permute-start.1) | collective-permute-done | bytes 49184 | tf_op jit(solution)/shard_map/ppermute | solution.py:15
  14.0 4.0 %collective-permute-start.3 = (bf16[38,3,256]{2,1,0:T(4,128)(2,1)S(1)}, bf16[38,3,256]{2,1,0:T(4,128)(2,1)S(1)}, u32[]{:S(2)}, u32[]{:S(2)}) collective-permute-start(bf16[38,3,256]{2,1,0:T(4,128)(2,1)S(1)} %pad_maximum_fusion.3), channel_id=1, source_target_pairs={{1,0},{2,1},{3,2},{4,3},{5,4},{6,5},{7,6},{8,7},{9,8},{10,9},{11,1... | collective-permute-start | bytes 175112 | tf_op jit(solution)/shard_map/ppermute | solution.py:15
  18.1 3.7 %collective-permute-start.2 = (bf16[38,3,256]{2,1,0:T(4,128)(2,1)S(1)}, bf16[38,3,256]{2,1,0:T(4,128)(2,1)S(1)}, u32[]{:S(2)}, u32[]{:S(2)}) collective-permute-start(bf16[38,3,256]{2,1,0:T(4,128)(2,1)S(1)} %pad_maximum_fusion.2), channel_id=1, source_target_pairs={{0,1},{1,2},{2,3},{3,4},{4,5},{5,6},{6,7},{7,8},{8,9},{9,10},{10,1... | collective-permute-start | bytes 175112 | tf_op jit(solution)/shard_map/ppermute | solution.py:15
  21.8 1.4 %collective-permute-done.2 = bf16[38,3,256]{2,1,0:T(4,128)(2,1)S(1)} collective-permute-done((bf16[38,3,256]{2,1,0:T(4,128)(2,1)S(1)}, bf16[38,3,256]{2,1,0:T(4,128)(2,1)S(1)}, u32[]{:S(2)}, u32[]{:S(2)}) %collective-permute-start.2) | collective-permute-done | bytes 58400 | tf_op jit(solution)/shard_map/ppermute | solution.py:15
  23.2 1.3 %pad_maximum_fusion.x_ref = bf16[38,38,256]{2,1,0:T(8,128)(2,1)} fusion(bf16[38,3,256]{2,1,0:T(4,128)(2,1)S(1)} %collective-permute-done.3, bf16[3,32,256]{2,1,0:T(8,128)(2,1)S(1)} %collective-permute-done.1, bf16[32,32,256]{2,1,0:T(8,128)(2,1)S(1)} %copy-done.1, bf16[3,32,256]{2,1,0:T(8,128)(2,1)S(1)} %collective-permute-done, ...), kind=kLoop, calls=%fused_computation.10 | loop fusion | flops 3696640 | bytes 1478656 | tf_op jit(solution)/shard_map/concatenate | solution.py:223
  24.5 15.1 %shard_map.136 = (bf16[1024,256]{1,0:T(8,128)(2,1)}, f32[16,256]{1,0:T(8,128)}, bf16[16,16,256]{2,1,0:T(8,128)(2,1)}) custom-call(bf16[38,38,256]{2,1,0:T(8,128)(2,1)} %pad_maximum_fusion.x_ref, bf16[7,7,256]{2,1,0:T(8,128)(2,1)} %k_ref.1, f32[1,256]{1,0:T(1,128)} %bitcast.74, f32[1,256]{1,0:T(1,128)} %bitcast.75, f32[1,256]{1,0:T(1,128)} %bitcast.76, ...), custom_call_target="tpu_custom_call" | custom-call | flops 1099431936 | bytes 2836480 | tf_op jit(solution)/shard_map/pallas_call | solution.py:167
  39.6 6.5 %all-to-all-start = ((bf16[16,16,256]{2,1,0:T(8,128)(2,1)}), bf16[16,16,256]{2,1,0:T(8,128)(2,1)S(1)}, u32[]{:S(2)}, u32[]{:S(2)}) async-start(bf16[16,16,256]{2,1,0:T(8,128)(2,1)} %get-tuple-element.9), calls=%async_computation | async-start | bytes 262144 | tf_op jit(solution)/shard_map/all_to_all | solution.py:285
  46.3 0.2 reshape.73
  46.6 5.7 %all-to-all-done = bf16[16,16,256]{2,1,0:T(8,128)(2,1)S(1)} async-done(((bf16[16,16,256]{2,1,0:T(8,128)(2,1)}), bf16[16,16,256]{2,1,0:T(8,128)(2,1)S(1)}, u32[]{:S(2)}, u32[]{:S(2)}) %all-to-all-start) | async-done | bytes 131104 | tf_op jit(solution)/shard_map/all_to_all | solution.py:285
  52.5 0.2 convolution_convert_fusion
  52.8 0.1 copy.21
  52.9 0.1 fusion.3
  53.0 0.2 fusion.16
  53.2 0.1 copy.20
  53.3 0.3 fusion.4
  53.7 0.1 fusion.6
  53.9 0.1 broadcast_in_dim.2
  54.0 0.4 copy-done.2
  54.4 1.0 %fusion.5 = bf16[32,32,256]{2,1,0:T(8,128)(2,1)} fusion(f32[32,32,256]{2,1,0:T(8,128)S(1)} %bitcast.67, bf16[32,32,256]{2,1,0:T(8,128)(2,1)S(1)} %bitcast.71), kind=kLoop, calls=%fused_computation.9 | loop fusion | flops 786432 | bytes 2097152 | tf_op jit(solution)/shard_map/convert_element_type | solution.py:325
  (27 shorter events, 0.7 us)
Async XLA Ops:
  0.0 52.5 %copy-start = (bf16[256,512]{1,0:T(8,128)(2,1)S(1)}, bf16[256,512]{1,0:T(8,128)(2,1)}, u32[]{:S(2)}) copy-start(bf16[256,512]{1,0:T(8,128)(2,1)} %param.25) | copy-start | bytes 786436
  0.0 23.2 %copy-start.1 = (bf16[32,32,256]{2,1,0:T(8,128)(2,1)S(1)}, bf16[32,32,256]{2,1,0:T(8,128)(2,1)}, u32[]{:S(2)}) copy-start(bf16[32,32,256]{2,1,0:T(8,128)(2,1)} %param.14) | copy-start | bytes 1572868
  0.9 9.3 %collective-permute-start = (bf16[3,32,256]{2,1,0:T(8,128)(2,1)S(1)}, bf16[3,32,256]{2,1,0:T(8,128)(2,1)S(1)}, u32[]{:S(2)}, u32[]{:S(2)}) collective-permute-start(bf16[3,32,256]{2,1,0:T(8,128)(2,1)S(1)} %get-tuple-element.13), channel_id=1, source_target_pairs={{0,16},{16,32},{32,48},{48,64},{64,80},{80,96},{96,112},{112,128},... | collective-permute-start | bytes 147464 | tf_op jit(solution)/shard_map/ppermute | solution.py:15
  5.4 8.4 %collective-permute-start.1 = (bf16[3,32,256]{2,1,0:T(8,128)(2,1)S(1)}, bf16[3,32,256]{2,1,0:T(8,128)(2,1)S(1)}, u32[]{:S(2)}, u32[]{:S(2)}) collective-permute-start(bf16[3,32,256]{2,1,0:T(8,128)(2,1)S(1)} %get-tuple-element.14), channel_id=1, source_target_pairs={{16,0},{32,16},{48,32},{64,48},{80,64},{96,80},{112,96},{128,112},... | collective-permute-start | bytes 147464 | tf_op jit(solution)/shard_map/ppermute | solution.py:15
  14.0 7.9 %collective-permute-start.3 = (bf16[38,3,256]{2,1,0:T(4,128)(2,1)S(1)}, bf16[38,3,256]{2,1,0:T(4,128)(2,1)S(1)}, u32[]{:S(2)}, u32[]{:S(2)}) collective-permute-start(bf16[38,3,256]{2,1,0:T(4,128)(2,1)S(1)} %pad_maximum_fusion.3), channel_id=1, source_target_pairs={{1,0},{2,1},{3,2},{4,3},{5,4},{6,5},{7,6},{8,7},{9,8},{10,9},{11,1... | collective-permute-start | bytes 175112 | tf_op jit(solution)/shard_map/ppermute | solution.py:15
  18.1 5.1 %collective-permute-start.2 = (bf16[38,3,256]{2,1,0:T(4,128)(2,1)S(1)}, bf16[38,3,256]{2,1,0:T(4,128)(2,1)S(1)}, u32[]{:S(2)}, u32[]{:S(2)}) collective-permute-start(bf16[38,3,256]{2,1,0:T(4,128)(2,1)S(1)} %pad_maximum_fusion.2), channel_id=1, source_target_pairs={{0,1},{1,2},{2,3},{3,4},{4,5},{5,6},{6,7},{7,8},{8,9},{9,10},{10,1... | collective-permute-start | bytes 175112 | tf_op jit(solution)/shard_map/ppermute | solution.py:15
  39.6 6.9 %copy-start.4 = (f32[16,256]{1,0:T(8,128)S(1)}, f32[16,256]{1,0:T(8,128)}, u32[]{:S(2)}) copy-start(f32[16,256]{1,0:T(8,128)} %get-tuple-element.10) | copy-start | bytes 49156
  39.6 12.7 %all-to-all-start = ((bf16[16,16,256]{2,1,0:T(8,128)(2,1)}), bf16[16,16,256]{2,1,0:T(8,128)(2,1)S(1)}, u32[]{:S(2)}, u32[]{:S(2)}) async-start(bf16[16,16,256]{2,1,0:T(8,128)(2,1)} %get-tuple-element.9), calls=%async_computation | async-start | bytes 262144 | tf_op jit(solution)/shard_map/all_to_all | solution.py:285
  52.8 1.0 %copy-start.3 = (bf16[256,256]{1,0:T(8,128)(2,1)S(1)}, bf16[256,256]{1,0:T(8,128)(2,1)}, u32[]{:S(2)}) copy-start(bf16[256,256]{1,0:T(8,128)(2,1)} %param.27) | copy-start | bytes 393220
  53.3 1.1 %copy-start.2 = (bf16[1024,256]{1,0:T(8,128)(2,1)S(1)}, bf16[1024,256]{1,0:T(8,128)(2,1)}, u32[]{:S(2)}) copy-start(bf16[1024,256]{1,0:T(8,128)(2,1)} %get-tuple-element.8) | copy-start | bytes 1572868

commit v19 on v18

--- a/solution.py
+++ b/solution.py
@@ -17,15 +17,12 @@
 
 def halo_pieces(features, width):
     rows, cols = features.shape[:2]
-    top, _ = shifted(features[rows - width :], "row")
-    _, bottom = shifted(features[:width], "row")
-    last_cols = jnp.concatenate(
-        [top[:, cols - width :], features[:, cols - width :], bottom[:, cols - width :]], axis=0
-    )
-    first_cols = jnp.concatenate([top[:, :width], features[:, :width], bottom[:, :width]], axis=0)
-    left, _ = shifted(last_cols, "col")
-    _, right = shifted(first_cols, "col")
-    return top, bottom, left, right
+    left, _ = shifted(features[:, cols - width :], "col")
+    _, right = shifted(features[:, :width], "col")
+    extended = jnp.concatenate([left, features, right], axis=1)
+    top, _ = shifted(extended[rows - width :], "row")
+    _, bottom = shifted(extended[:width], "row")
+    return extended, top, bottom
 
 TAPS = 7
 ROW_BLOCK = 8
@@ -218,11 +215,8 @@
     copies,
 ):
     tile_rows, tile_cols, channels = features.shape
-    top, bottom, left, right = pieces
-    extended = jnp.concatenate([top, features, bottom], axis=0)
-    padded = jnp.concatenate(
-        [left, extended, right], axis=1
-    )
+    extended, top, bottom = pieces
+    padded = jnp.concatenate([top, extended, bottom], axis=0)
     summed, queries, sent = block_call(
         padded,
         features,

time: 55.8 us -> 56.1 us (level)
  waiting for transfers between devices: 10.8 us -> 14.5 us
  starting transfers between devices: 21 us -> 18.6 us
  local copies, waits for them, and re-layouts: 4.72 us -> 3.86 us
    ppermute x4, waiting for transfers between devices: 5.06 us -> 8.77 us  [shifted(): return (lax.ppermute(piece, axis, up), lax.ppermute(piece, axis, down))]
    ppermute x4, starting transfers between devices: 14.5 us -> 12.2 us  [shifted(): return (lax.ppermute(piece, axis, up), lax.ppermute(piece, axis, down))]
    slice x4 -> x1, local copies, waits for them, and re-layouts: 1.95 us -> 1.1 us  [halo_pieces(): left, _ = shifted(features[:, cols - width:], 'col')]
    concatenate x3 -> x1, other arithmetic: 1.46 us -> 1.26 us  [block_pass(): padded = jnp.concatenate([top, extended, bottom], axis=0)]
  transfers between devices with their start and end apart: 5 -> 5, of which waited for: 3 -> 3; matrix products, arithmetic and copies ran while one was open for 5% -> 3% of each run, Pallas kernels for 0% -> 0%
where the time goes in v19:
time: 56.1 us; the launch traced here: 55.6 us
  starting transfers between devices  18.6 us (33%)
  Pallas kernels  15.1 us (27%)
  waiting for transfers between devices  14.5 us (26%)
  local copies, waits for them, and re-layouts  3.86 us (7%)
  other arithmetic  2.5 us (4%)
  matrix products  0.79 us (1%)
    pallas_call x1, Pallas kernels, block_call(): pl.pallas_call(block_kernel, out_shape=(jax.ShapeDtypeStruct((pixels, cha...  15.1 us
    ppermute x4, starting transfers between devices, shifted(): return (lax.ppermute(piece, axis, up), lax.ppermute(piece, axis, down))  12.2 us
    ppermute x4, waiting for transfers between devices, shifted(): return (lax.ppermute(piece, axis, up), lax.ppermute(piece, axis, down))  8.77 us
    all_to_all x1, starting transfers between devices, shards(): band_pooled = lax.all_to_all(sent, 'col', 0, 0)  6.46 us
    all_to_all x1, waiting for transfers between devices, shards(): band_pooled = lax.all_to_all(sent, 'col', 0, 0)  5.74 us
    another operation x1, local copies, waits for them, and re-layouts, shards(): rows_of.append(jnp.stack(per_col, axis=1))  1.44 us
    concatenate x1, other arithmetic, block_pass(): padded = jnp.concatenate([top, extended, bottom], axis=0)  1.26 us
  transfers between devices with their start and end apart: 5, of which 3 were waited for; matrix products, arithmetic and copies ran while one was open for 3% of the time, Pallas kernels for 0%

profile of v19, /device:TPU:113, one launch (start us, length us, event | category | flops | bytes accessed | tf_op | source)
XLA Modules:
  0.0 55.6 jit_solution(8897348029159027588)
XLA Ops:
  0.0 1.1 %fusion.11 = (bf16[32,3,256]{2,1,0:T(4,128)(2,1)S(1)}, bf16[32,3,256]{2,1,0:T(4,128)(2,1)S(1)}) fusion(bf16[32,32,256]{2,1,0:T(8,128)(2,1)} %param.14), kind=kLoop, calls=%fused_computation.42 | loop fusion | bytes 196608 | tf_op jit(solution)/shard_map/slice | solution.py:20
  1.1 3.5 %collective-permute-start = (bf16[32,3,256]{2,1,0:T(4,128)(2,1)S(1)}, bf16[32,3,256]{2,1,0:T(4,128)(2,1)S(1)}, u32[]{:S(2)}, u32[]{:S(2)}) collective-permute-start(bf16[32,3,256]{2,1,0:T(4,128)(2,1)S(1)} %get-tuple-element.13), channel_id=1, source_target_pairs={{0,1},{1,2},{2,3},{3,4},{4,5},{5,6},{6,7},{7,8},{8,9},{9,10},{10,1... | collective-permute-start | bytes 147464 | tf_op jit(solution)/shard_map/ppermute | solution.py:15
  4.6 1.9 %collective-permute-start.1 = (bf16[32,3,256]{2,1,0:T(4,128)(2,1)S(1)}, bf16[32,3,256]{2,1,0:T(4,128)(2,1)S(1)}, u32[]{:S(2)}, u32[]{:S(2)}) collective-permute-start(bf16[32,3,256]{2,1,0:T(4,128)(2,1)S(1)} %get-tuple-element.14), channel_id=1, source_target_pairs={{1,0},{2,1},{3,2},{4,3},{5,4},{6,5},{7,6},{8,7},{9,8},{10,9},{11,1... | collective-permute-start | bytes 147464 | tf_op jit(solution)/shard_map/ppermute | solution.py:15
  6.5 1.4 %dynamic-slice_bitcast_fusion.15 = (f32[8,1,4,64]{3,0,2,1:T(8,128)S(1)}, f32[8,1,4,64]{3,0,2,1:T(8,128)S(1)}, f32[8,1,4,64]{3,0,2,1:T(8,128)S(1)}, f32[8,1,4,64]...) fusion(f32[8,7,127]{2,0,1:T(8,128)} %param.26, ...), kind=kLoop, calls=%fused_computation.40 | loop fusion | bytes 262172 | tf_op jit(solution)/shard_map/stack | solution.py:297
  8.0 2.2 %collective-permute-done.1 = bf16[32,3,256]{2,1,0:T(4,128)(2,1)S(1)} collective-permute-done((bf16[32,3,256]{2,1,0:T(4,128)(2,1)S(1)}, bf16[32,3,256]{2,1,0:T(4,128)(2,1)S(1)}, u32[]{:S(2)}, u32[]{:S(2)}) %collective-permute-start.1) | collective-permute-done | bytes 49184 | tf_op jit(solution)/shard_map/ppermute | solution.py:15
  10.2 4.8 %collective-permute-start.2 = (bf16[3,38,256]{2,1,0:T(8,128)(2,1)S(1)}, bf16[3,38,256]{2,1,0:T(8,128)(2,1)S(1)}, u32[]{:S(2)}, u32[]{:S(2)}) collective-permute-start(bf16[3,38,256]{2,1,0:T(8,128)(2,1)S(1)} %get-tuple-element.11), channel_id=1, source_target_pairs={{0,16},{16,32},{32,48},{48,64},{64,80},{80,96},{96,112},{112,128},... | collective-permute-start | bytes 175112 | tf_op jit(solution)/shard_map/ppermute | solution.py:15
  15.0 2.0 %collective-permute-start.3 = (bf16[3,38,256]{2,1,0:T(8,128)(2,1)S(1)}, bf16[3,38,256]{2,1,0:T(8,128)(2,1)S(1)}, u32[]{:S(2)}, u32[]{:S(2)}) collective-permute-start(bf16[3,38,256]{2,1,0:T(8,128)(2,1)S(1)} %get-tuple-element.12), channel_id=1, source_target_pairs={{16,0},{32,16},{48,32},{64,48},{80,64},{96,80},{112,96},{128,112},... | collective-permute-start | bytes 175112 | tf_op jit(solution)/shard_map/ppermute | solution.py:15
  17.1 6.6 %collective-permute-done.3 = bf16[3,38,256]{2,1,0:T(8,128)(2,1)S(1)} collective-permute-done((bf16[3,38,256]{2,1,0:T(8,128)(2,1)S(1)}, bf16[3,38,256]{2,1,0:T(8,128)(2,1)S(1)}, u32[]{:S(2)}, u32[]{:S(2)}) %collective-permute-start.3) | collective-permute-done | bytes 58400 | tf_op jit(solution)/shard_map/ppermute | solution.py:15
  23.6 1.3 %pad_maximum_fusion.x_ref = bf16[38,38,256]{2,1,0:T(8,128)(2,1)} fusion(bf16[3,38,256]{2,1,0:T(8,128)(2,1)S(1)} %collective-permute-done.3, bf16[32,3,256]{2,1,0:T(4,128)(2,1)S(1)} %collective-permute-done.1, bf16[32,32,256]{2,1,0:T(8,128)(2,1)S(1)} %copy-done.1, bf16[32,3,256]{2,1,0:T(4,128)(2,1)S(1)} %collective-permute-done, ...), kind=kLoop, calls=%fused_computation.10 | loop fusion | flops 3696640 | bytes 1478656 | tf_op jit(solution)/shard_map/concatenate | solution.py:219
  24.9 15.1 %shard_map.136 = (bf16[1024,256]{1,0:T(8,128)(2,1)}, f32[16,256]{1,0:T(8,128)}, bf16[16,16,256]{2,1,0:T(8,128)(2,1)}) custom-call(bf16[38,38,256]{2,1,0:T(8,128)(2,1)} %pad_maximum_fusion.x_ref, bf16[7,7,256]{2,1,0:T(8,128)(2,1)} %k_ref.1, f32[1,256]{1,0:T(1,128)} %bitcast.74, f32[1,256]{1,0:T(1,128)} %bitcast.75, f32[1,256]{1,0:T(1,128)} %bitcast.76, ...), custom_call_target="tpu_custom_call" | custom-call | flops 1099431936 | bytes 2836480 | tf_op jit(solution)/shard_map/pallas_call | solution.py:164
  40.0 6.5 %all-to-all-start = ((bf16[16,16,256]{2,1,0:T(8,128)(2,1)}), bf16[16,16,256]{2,1,0:T(8,128)(2,1)S(1)}, u32[]{:S(2)}, u32[]{:S(2)}) async-start(bf16[16,16,256]{2,1,0:T(8,128)(2,1)} %get-tuple-element.9), calls=%async_computation | async-start | bytes 262144 | tf_op jit(solution)/shard_map/all_to_all | solution.py:279
  46.6 0.2 reshape.73
  46.9 5.7 %all-to-all-done = bf16[16,16,256]{2,1,0:T(8,128)(2,1)S(1)} async-done(((bf16[16,16,256]{2,1,0:T(8,128)(2,1)}), bf16[16,16,256]{2,1,0:T(8,128)(2,1)S(1)}, u32[]{:S(2)}, u32[]{:S(2)}) %all-to-all-start) | async-done | bytes 131104 | tf_op jit(solution)/shard_map/all_to_all | solution.py:279
  52.8 0.2 convolution_convert_fusion
  53.0 0.1 copy.21
  53.2 0.1 fusion.3
  53.3 0.2 fusion.13
  53.5 0.1 copy.20
  53.6 0.3 fusion.4
  53.9 0.1 reshape.74
  54.0 0.1 fusion.6
  54.2 0.1 broadcast_in_dim.2
  54.3 0.4 copy-done.2
  54.6 1.0 %fusion.5 = bf16[32,32,256]{2,1,0:T(8,128)(2,1)} fusion(f32[32,32,256]{2,1,0:T(8,128)S(1)} %bitcast.67, bf16[32,32,256]{2,1,0:T(8,128)(2,1)S(1)} %bitcast.71), kind=kLoop, calls=%fused_computation.9 | loop fusion | flops 786432 | bytes 2097152 | tf_op jit(solution)/shard_map/convert_element_type | solution.py:319
  (23 shorter events, 0.4 us)
Async XLA Ops:
  0.0 52.8 %copy-start = (bf16[256,512]{1,0:T(8,128)(2,1)S(1)}, bf16[256,512]{1,0:T(8,128)(2,1)}, u32[]{:S(2)}) copy-start(bf16[256,512]{1,0:T(8,128)(2,1)} %param.25) | copy-start | bytes 786436
  0.0 10.2 %copy-start.1 = (bf16[32,32,256]{2,1,0:T(8,128)(2,1)S(1)}, bf16[32,32,256]{2,1,0:T(8,128)(2,1)}, u32[]{:S(2)}) copy-start(bf16[32,32,256]{2,1,0:T(8,128)(2,1)} %param.14) | copy-start | bytes 1572868
  1.1 6.9 %collective-permute-start = (bf16[32,3,256]{2,1,0:T(4,128)(2,1)S(1)}, bf16[32,3,256]{2,1,0:T(4,128)(2,1)S(1)}, u32[]{:S(2)}, u32[]{:S(2)}) collective-permute-start(bf16[32,3,256]{2,1,0:T(4,128)(2,1)S(1)} %get-tuple-element.13), channel_id=1, source_target_pairs={{0,1},{1,2},{2,3},{3,4},{4,5},{5,6},{6,7},{7,8},{8,9},{9,10},{10,1... | collective-permute-start | bytes 147464 | tf_op jit(solution)/shard_map/ppermute | solution.py:15
  4.6 5.6 %collective-permute-start.1 = (bf16[32,3,256]{2,1,0:T(4,128)(2,1)S(1)}, bf16[32,3,256]{2,1,0:T(4,128)(2,1)S(1)}, u32[]{:S(2)}, u32[]{:S(2)}) collective-permute-start(bf16[32,3,256]{2,1,0:T(4,128)(2,1)S(1)} %get-tuple-element.14), channel_id=1, source_target_pairs={{1,0},{2,1},{3,2},{4,3},{5,4},{6,5},{7,6},{8,7},{9,8},{10,9},{11,1... | collective-permute-start | bytes 147464 | tf_op jit(solution)/shard_map/ppermute | solution.py:15
  10.2 6.8 %collective-permute-start.2 = (bf16[3,38,256]{2,1,0:T(8,128)(2,1)S(1)}, bf16[3,38,256]{2,1,0:T(8,128)(2,1)S(1)}, u32[]{:S(2)}, u32[]{:S(2)}) collective-permute-start(bf16[3,38,256]{2,1,0:T(8,128)(2,1)S(1)} %get-tuple-element.11), channel_id=1, source_target_pairs={{0,16},{16,32},{32,48},{48,64},{64,80},{80,96},{96,112},{112,128},... | collective-permute-start | bytes 175112 | tf_op jit(solution)/shard_map/ppermute | solution.py:15
  15.0 8.6 %collective-permute-start.3 = (bf16[3,38,256]{2,1,0:T(8,128)(2,1)S(1)}, bf16[3,38,256]{2,1,0:T(8,128)(2,1)S(1)}, u32[]{:S(2)}, u32[]{:S(2)}) collective-permute-start(bf16[3,38,256]{2,1,0:T(8,128)(2,1)S(1)} %get-tuple-element.12), channel_id=1, source_target_pairs={{16,0},{32,16},{48,32},{64,48},{80,64},{96,80},{112,96},{128,112},... | collective-permute-start | bytes 175112 | tf_op jit(solution)/shard_map/ppermute | solution.py:15
  40.0 6.8 %copy-start.4 = (f32[16,256]{1,0:T(8,128)S(1)}, f32[16,256]{1,0:T(8,128)}, u32[]{:S(2)}) copy-start(f32[16,256]{1,0:T(8,128)} %get-tuple-element.10) | copy-start | bytes 49156
  40.0 12.6 %all-to-all-start = ((bf16[16,16,256]{2,1,0:T(8,128)(2,1)}), bf16[16,16,256]{2,1,0:T(8,128)(2,1)S(1)}, u32[]{:S(2)}, u32[]{:S(2)}) async-start(bf16[16,16,256]{2,1,0:T(8,128)(2,1)} %get-tuple-element.9), calls=%async_computation | async-start | bytes 262144 | tf_op jit(solution)/shard_map/all_to_all | solution.py:279
  53.0 1.0 %copy-start.3 = (bf16[256,256]{1,0:T(8,128)(2,1)S(1)}, bf16[256,256]{1,0:T(8,128)(2,1)}, u32[]{:S(2)}) copy-start(bf16[256,256]{1,0:T(8,128)(2,1)} %param.27) | copy-start | bytes 393220
  53.6 1.1 %copy-start.2 = (bf16[1024,256]{1,0:T(8,128)(2,1)S(1)}, bf16[1024,256]{1,0:T(8,128)(2,1)}, u32[]{:S(2)}) copy-start(bf16[1024,256]{1,0:T(8,128)(2,1)} %get-tuple-element.8) | copy-start | bytes 1572868

commit v20 on v18

--- a/solution.py
+++ b/solution.py
@@ -28,7 +28,7 @@
     return top, bottom, left, right
 
 TAPS = 7
-ROW_BLOCK = 8
+ROW_BLOCK = 16
 
 
 def conv_norm_kernel(x_ref, k_ref, db_ref, g_ref, nb_ref, o_ref, kf_ref, sh_ref):

time: 55.8 us -> 55.3 us (level)
  no operation moved by 1% of the time
where the time goes in v20:
time: 55.3 us; the launch traced here: 54.9 us
  starting transfers between devices  21 us (38%)
  Pallas kernels  14.6 us (26%)
  waiting for transfers between devices  10.8 us (20%)
  local copies, waits for them, and re-layouts  4.72 us (9%)
  other arithmetic  2.65 us (5%)
  matrix products  0.8 us (1%)
    pallas_call x1, Pallas kernels, block_call(): pl.pallas_call(block_kernel, out_shape=(jax.ShapeDtypeStruct((pixels, cha...  14.6 us
    ppermute x4, starting transfers between devices, shifted(): return (lax.ppermute(piece, axis, up), lax.ppermute(piece, axis, down))  14.5 us
    all_to_all x1, starting transfers between devices, shards(): band_pooled = lax.all_to_all(sent, 'col', 0, 0)  6.53 us
    all_to_all x1, waiting for transfers between devices, shards(): band_pooled = lax.all_to_all(sent, 'col', 0, 0)  5.74 us
    ppermute x4, waiting for transfers between devices, shifted(): return (lax.ppermute(piece, axis, up), lax.ppermute(piece, axis, down))  5.06 us
    another operation x1, local copies, waits for them, and re-layouts, shards(): rows_of.append(jnp.stack(per_col, axis=1))  1.45 us
    concatenate x1, other arithmetic, block_pass(): padded = jnp.concatenate([left, extended, right], axis=1)  1.33 us
  transfers between devices with their start and end apart: 5, of which 3 were waited for; matrix products, arithmetic and copies ran while one was open for 5% of the time, Pallas kernels for 0%

profile of v20, /device:TPU:113, one launch (start us, length us, event | category | flops | bytes accessed | tf_op | source)
XLA Modules:
  0.0 54.9 jit_solution(7047993525385032187)
XLA Ops:
  0.0 0.9 %fusion.12 = (bf16[3,32,256]{2,1,0:T(8,128)(2,1)S(1)}, bf16[3,32,256]{2,1,0:T(8,128)(2,1)S(1)}) fusion(bf16[32,32,256]{2,1,0:T(8,128)(2,1)} %param.14), kind=kLoop, calls=%fused_computation.42 | loop fusion | bytes 196608 | tf_op jit(solution)/shard_map/slice | solution.py:20
  0.9 4.5 %collective-permute-start = (bf16[3,32,256]{2,1,0:T(8,128)(2,1)S(1)}, bf16[3,32,256]{2,1,0:T(8,128)(2,1)S(1)}, u32[]{:S(2)}, u32[]{:S(2)}) collective-permute-start(bf16[3,32,256]{2,1,0:T(8,128)(2,1)S(1)} %get-tuple-element.13), channel_id=1, source_target_pairs={{0,16},{16,32},{32,48},{48,64},{64,80},{80,96},{96,112},{112,128},... | collective-permute-start | bytes 147464 | tf_op jit(solution)/shard_map/ppermute | solution.py:15
  5.4 2.3 %collective-permute-start.1 = (bf16[3,32,256]{2,1,0:T(8,128)(2,1)S(1)}, bf16[3,32,256]{2,1,0:T(8,128)(2,1)S(1)}, u32[]{:S(2)}, u32[]{:S(2)}) collective-permute-start(bf16[3,32,256]{2,1,0:T(8,128)(2,1)S(1)} %get-tuple-element.14), channel_id=1, source_target_pairs={{16,0},{32,16},{48,32},{64,48},{80,64},{96,80},{112,96},{128,112},... | collective-permute-start | bytes 147464 | tf_op jit(solution)/shard_map/ppermute | solution.py:15
  7.7 1.0 %fusion.11 = (bf16[32,3,256]{2,1,0:T(4,128)(2,1)S(1)}, bf16[32,3,256]{2,1,0:T(4,128)(2,1)S(1)}) fusion(bf16[32,32,256]{2,1,0:T(8,128)(2,1)} %param.14), kind=kLoop, calls=%fused_computation.41 | loop fusion | bytes 196608 | tf_op jit(solution)/shard_map/slice | solution.py:23
  8.7 1.4 %dynamic-slice_bitcast_fusion.15 = (f32[8,1,4,64]{3,0,2,1:T(8,128)S(1)}, f32[8,1,4,64]{3,0,2,1:T(8,128)S(1)}, f32[8,1,4,64]{3,0,2,1:T(8,128)S(1)}, f32[8,1,4,64]...) fusion(f32[8,7,127]{2,0,1:T(8,128)} %param.26, ...), kind=kLoop, calls=%fused_computation.39 | loop fusion | bytes 262172 | tf_op jit(solution)/shard_map/stack | solution.py:303
  10.2 3.7 %collective-permute-done.1 = bf16[3,32,256]{2,1,0:T(8,128)(2,1)S(1)} collective-permute-done((bf16[3,32,256]{2,1,0:T(8,128)(2,1)S(1)}, bf16[3,32,256]{2,1,0:T(8,128)(2,1)S(1)}, u32[]{:S(2)}, u32[]{:S(2)}) %collective-permute-start.1) | collective-permute-done | bytes 49184 | tf_op jit(solution)/shard_map/ppermute | solution.py:15
  14.0 4.0 %collective-permute-start.3 = (bf16[38,3,256]{2,1,0:T(4,128)(2,1)S(1)}, bf16[38,3,256]{2,1,0:T(4,128)(2,1)S(1)}, u32[]{:S(2)}, u32[]{:S(2)}) collective-permute-start(bf16[38,3,256]{2,1,0:T(4,128)(2,1)S(1)} %pad_maximum_fusion.3), channel_id=1, source_target_pairs={{1,0},{2,1},{3,2},{4,3},{5,4},{6,5},{7,6},{8,7},{9,8},{10,9},{11,1... | collective-permute-start | bytes 175112 | tf_op jit(solution)/shard_map/ppermute | solution.py:15
  18.1 3.7 %collective-permute-start.2 = (bf16[38,3,256]{2,1,0:T(4,128)(2,1)S(1)}, bf16[38,3,256]{2,1,0:T(4,128)(2,1)S(1)}, u32[]{:S(2)}, u32[]{:S(2)}) collective-permute-start(bf16[38,3,256]{2,1,0:T(4,128)(2,1)S(1)} %pad_maximum_fusion.2), channel_id=1, source_target_pairs={{0,1},{1,2},{2,3},{3,4},{4,5},{5,6},{6,7},{7,8},{8,9},{9,10},{10,1... | collective-permute-start | bytes 175112 | tf_op jit(solution)/shard_map/ppermute | solution.py:15
  21.8 1.4 %collective-permute-done.2 = bf16[38,3,256]{2,1,0:T(4,128)(2,1)S(1)} collective-permute-done((bf16[38,3,256]{2,1,0:T(4,128)(2,1)S(1)}, bf16[38,3,256]{2,1,0:T(4,128)(2,1)S(1)}, u32[]{:S(2)}, u32[]{:S(2)}) %collective-permute-start.2) | collective-permute-done | bytes 58400 | tf_op jit(solution)/shard_map/ppermute | solution.py:15
  23.2 1.3 %pad_maximum_fusion.x_ref = bf16[38,38,256]{2,1,0:T(8,128)(2,1)} fusion(bf16[38,3,256]{2,1,0:T(4,128)(2,1)S(1)} %collective-permute-done.3, bf16[3,32,256]{2,1,0:T(8,128)(2,1)S(1)} %collective-permute-done.1, bf16[32,32,256]{2,1,0:T(8,128)(2,1)S(1)} %copy-done.1, bf16[3,32,256]{2,1,0:T(8,128)(2,1)S(1)} %collective-permute-done, ...), kind=kLoop, calls=%fused_computation.10 | loop fusion | flops 3696640 | bytes 1478656 | tf_op jit(solution)/shard_map/concatenate | solution.py:223
  24.5 14.6 %shard_map.136 = (bf16[1024,256]{1,0:T(8,128)(2,1)}, f32[16,256]{1,0:T(8,128)}, bf16[16,16,256]{2,1,0:T(8,128)(2,1)}) custom-call(bf16[38,38,256]{2,1,0:T(8,128)(2,1)} %pad_maximum_fusion.x_ref, bf16[7,7,256]{2,1,0:T(8,128)(2,1)} %k_ref.1, f32[1,256]{1,0:T(1,128)} %bitcast.74, f32[1,256]{1,0:T(1,128)} %bitcast.75, f32[1,256]{1,0:T(1,128)} %bitcast.76, ...), custom_call_target="tpu_custom_call" | custom-call | flops 1099431936 | bytes 2836480 | tf_op jit(solution)/shard_map/pallas_call | solution.py:167
  39.2 6.5 %all-to-all-start = ((bf16[16,16,256]{2,1,0:T(8,128)(2,1)}), bf16[16,16,256]{2,1,0:T(8,128)(2,1)S(1)}, u32[]{:S(2)}, u32[]{:S(2)}) async-start(bf16[16,16,256]{2,1,0:T(8,128)(2,1)} %get-tuple-element.9), calls=%async_computation | async-start | bytes 262144 | tf_op jit(solution)/shard_map/all_to_all | solution.py:285
  45.8 0.2 reshape.73
  46.1 5.7 %all-to-all-done = bf16[16,16,256]{2,1,0:T(8,128)(2,1)S(1)} async-done(((bf16[16,16,256]{2,1,0:T(8,128)(2,1)}), bf16[16,16,256]{2,1,0:T(8,128)(2,1)S(1)}, u32[]{:S(2)}, u32[]{:S(2)}) %all-to-all-start) | async-done | bytes 131104 | tf_op jit(solution)/shard_map/all_to_all | solution.py:285
  52.0 0.2 convolution_convert_fusion
  52.3 0.1 copy.21
  52.4 0.1 fusion.3
  52.5 0.2 fusion.16
  52.7 0.1 copy.20
  52.8 0.3 fusion.4
  53.2 0.1 fusion.6
  53.4 0.1 broadcast_in_dim.2
  53.5 0.4 copy-done.2
  53.9 1.0 %fusion.5 = bf16[32,32,256]{2,1,0:T(8,128)(2,1)} fusion(f32[32,32,256]{2,1,0:T(8,128)S(1)} %bitcast.67, bf16[32,32,256]{2,1,0:T(8,128)(2,1)S(1)} %bitcast.71), kind=kLoop, calls=%fused_computation.9 | loop fusion | flops 786432 | bytes 2097152 | tf_op jit(solution)/shard_map/convert_element_type | solution.py:325
  (27 shorter events, 0.7 us)
Async XLA Ops:
  0.0 52.0 %copy-start = (bf16[256,512]{1,0:T(8,128)(2,1)S(1)}, bf16[256,512]{1,0:T(8,128)(2,1)}, u32[]{:S(2)}) copy-start(bf16[256,512]{1,0:T(8,128)(2,1)} %param.25) | copy-start | bytes 786436
  0.0 23.2 %copy-start.1 = (bf16[32,32,256]{2,1,0:T(8,128)(2,1)S(1)}, bf16[32,32,256]{2,1,0:T(8,128)(2,1)}, u32[]{:S(2)}) copy-start(bf16[32,32,256]{2,1,0:T(8,128)(2,1)} %param.14) | copy-start | bytes 1572868
  0.9 9.3 %collective-permute-start = (bf16[3,32,256]{2,1,0:T(8,128)(2,1)S(1)}, bf16[3,32,256]{2,1,0:T(8,128)(2,1)S(1)}, u32[]{:S(2)}, u32[]{:S(2)}) collective-permute-start(bf16[3,32,256]{2,1,0:T(8,128)(2,1)S(1)} %get-tuple-element.13), channel_id=1, source_target_pairs={{0,16},{16,32},{32,48},{48,64},{64,80},{80,96},{96,112},{112,128},... | collective-permute-start | bytes 147464 | tf_op jit(solution)/shard_map/ppermute | solution.py:15
  5.4 8.4 %collective-permute-start.1 = (bf16[3,32,256]{2,1,0:T(8,128)(2,1)S(1)}, bf16[3,32,256]{2,1,0:T(8,128)(2,1)S(1)}, u32[]{:S(2)}, u32[]{:S(2)}) collective-permute-start(bf16[3,32,256]{2,1,0:T(8,128)(2,1)S(1)} %get-tuple-element.14), channel_id=1, source_target_pairs={{16,0},{32,16},{48,32},{64,48},{80,64},{96,80},{112,96},{128,112},... | collective-permute-start | bytes 147464 | tf_op jit(solution)/shard_map/ppermute | solution.py:15
  14.0 7.9 %collective-permute-start.3 = (bf16[38,3,256]{2,1,0:T(4,128)(2,1)S(1)}, bf16[38,3,256]{2,1,0:T(4,128)(2,1)S(1)}, u32[]{:S(2)}, u32[]{:S(2)}) collective-permute-start(bf16[38,3,256]{2,1,0:T(4,128)(2,1)S(1)} %pad_maximum_fusion.3), channel_id=1, source_target_pairs={{1,0},{2,1},{3,2},{4,3},{5,4},{6,5},{7,6},{8,7},{9,8},{10,9},{11,1... | collective-permute-start | bytes 175112 | tf_op jit(solution)/shard_map/ppermute | solution.py:15
  18.1 5.1 %collective-permute-start.2 = (bf16[38,3,256]{2,1,0:T(4,128)(2,1)S(1)}, bf16[38,3,256]{2,1,0:T(4,128)(2,1)S(1)}, u32[]{:S(2)}, u32[]{:S(2)}) collective-permute-start(bf16[38,3,256]{2,1,0:T(4,128)(2,1)S(1)} %pad_maximum_fusion.2), channel_id=1, source_target_pairs={{0,1},{1,2},{2,3},{3,4},{4,5},{5,6},{6,7},{7,8},{8,9},{9,10},{10,1... | collective-permute-start | bytes 175112 | tf_op jit(solution)/shard_map/ppermute | solution.py:15
  39.2 6.9 %copy-start.4 = (f32[16,256]{1,0:T(8,128)S(1)}, f32[16,256]{1,0:T(8,128)}, u32[]{:S(2)}) copy-start(f32[16,256]{1,0:T(8,128)} %get-tuple-element.10) | copy-start | bytes 49156
  39.2 12.7 %all-to-all-start = ((bf16[16,16,256]{2,1,0:T(8,128)(2,1)}), bf16[16,16,256]{2,1,0:T(8,128)(2,1)S(1)}, u32[]{:S(2)}, u32[]{:S(2)}) async-start(bf16[16,16,256]{2,1,0:T(8,128)(2,1)} %get-tuple-element.9), calls=%async_computation | async-start | bytes 262144 | tf_op jit(solution)/shard_map/all_to_all | solution.py:285
  52.3 1.0 %copy-start.3 = (bf16[256,256]{1,0:T(8,128)(2,1)S(1)}, bf16[256,256]{1,0:T(8,128)(2,1)}, u32[]{:S(2)}) copy-start(bf16[256,256]{1,0:T(8,128)(2,1)} %param.27) | copy-start | bytes 393220
  52.8 1.1 %copy-start.2 = (bf16[1024,256]{1,0:T(8,128)(2,1)S(1)}, bf16[1024,256]{1,0:T(8,128)(2,1)}, u32[]{:S(2)}) copy-start(bf16[1024,256]{1,0:T(8,128)(2,1)} %get-tuple-element.8) | copy-start | bytes 1572868
